TPU v7x, 128 devices: a whole 4x4x4 slice. The times are simulated.
128 devices in a mesh: blk: 32 (over x, z, y_hi), band: 4 (over y_lo, core).
Axes of the slice: x: 4, y: 4 (y_hi: 2, y_lo: 2; y = y_hi * 2 + y_lo), z: 4, core: 2. Of those that a mesh axis runs over, the one named last changes fastest.
Arguments:
- coarse_kernel: bfloat16 [64, 512, 512], P('blk'), may hold values from -6 to 6
- interp_index: int32 [256, 8, 4], P('blk'), may hold values from 0 to 63, as said below
- interp_weight: float32 [256, 8, 4], P('blk'), may hold values from 0.1 to 1
- stop_order: int32 [8], replicated, may hold values from 0 to 7, each once
- intersection: bfloat16 [256, 512, 512], P('blk'), may hold values from -0.25 to 0.25
- trial_vectors: bfloat16 [256, 512, 128], P('blk', 'band'), may hold values from -0.09375 to 0.09375
Outputs:
- hamiltonian: bfloat16 [256, 8, 512, 512], P('blk', None, None, 'band')
- kernel_product: bfloat16 [256, 512, 128], P('blk', 'band')
Inputs may be any that keep to these rules, and one draw needn't show every extreme that they name: `interp_index`: A fine k-point k lies on blk index i = k // 8; blk index j holds the coarse k-points j * 2 to (j + 1) * 2 - 1. The four coarse k-points named for k (j = 0, 1, 2, 3) lie on blk indices i - 1, i, i, i + 1, taken modulo the number of blk indices. `stop_order`: each of 0 to 7 once.
All inputs are finite; a program needn't handle non-finite values.
Results may differ from a plain program's by a relative error of at most 0.015.
Values may be sent and summed in bfloat16 or wider, within the bound.
No kernel may reach another device: no remote copies, remote signals or barrier semaphores. Data moves between devices by JAX's collectives and lax.ppermute only.
A program may use at most 128 MiB of HBM per device.

v0:
```python
import functools

import jax
import jax.numpy as jnp
from jax import lax
from jax.experimental import pallas as pl
from jax.experimental.pallas import tpu as pltpu
from jax.sharding import PartitionSpec as P


def shifted(value, axis, steps):
    count = lax.axis_size(axis)
    pairs = [(source, (source + steps) % count) for source in range(count)]
    return lax.ppermute(value, axis, pairs)


def sandwich_kernel(slot_ref, band_ref, weight_ref, before_ref, local_ref, after_ref,
                    inter_ref, right_ref, ham_ref, prod_ref, left_ref,
                    *, blocks_dev, stop_count, corner_count):
    k = pl.program_id(0)
    s = pl.program_id(1)

    @pl.when(s == 0)
    def _():
        right = right_ref[0]
        for slot in range(blocks_dev):
            for group, source in enumerate((before_ref, local_ref, after_ref)):
                prod_ref[group * blocks_dev + slot] = jnp.dot(
                    source[slot], right, preferred_element_type=jnp.float32)
        left_ref[...] = inter_ref[0].T

    base = (k * stop_count + s) * corner_count
    rotated = weight_ref[base] * prod_ref[slot_ref[base]]
    for j in range(1, corner_count):
        rotated = rotated + weight_ref[base + j] * prod_ref[slot_ref[base + j]]
    rotated = rotated.astype(jnp.bfloat16)
    ham_ref[0, 0] = jnp.dot(
        left_ref[...], rotated, preferred_element_type=jnp.float32).astype(jnp.bfloat16)


def product_kernel(ham_ref, trial_ref, part_ref, *, stop_count):
    acc = jnp.dot(ham_ref[0, 0], trial_ref[0, 0], preferred_element_type=jnp.float32)
    for s in range(1, stop_count):
        acc = acc + jnp.dot(ham_ref[0, s], trial_ref[s, 0], preferred_element_type=jnp.float32)
    part_ref[0] = acc.astype(jnp.bfloat16)


def on_device(coarse_kernel, interp_index, interp_weight, stop_order, intersection, trial_vectors):
    blocks_dev = coarse_kernel.shape[0]
    fine_dev = intersection.shape[0]
    column_count = trial_vectors.shape[1]
    vector_count = trial_vectors.shape[2]
    block_order = intersection.shape[1]
    stop_count = stop_order.shape[0]
    corner_count = interp_index.shape[2]
    cycle_length = lax.axis_size("blk")
    total_coarse = blocks_dev * cycle_length
    position = lax.axis_index("blk")
    band = lax.axis_index("band")

    before = shifted(coarse_kernel, "blk", 1)
    after = shifted(coarse_kernel, "blk", -1)
    before, after, trial_vectors = lax.optimization_barrier((before, after, trial_vectors))
    sources = jnp.stack(
        [shifted(trial_vectors, "blk", station + 1) for station in range(stop_count)])

    order_index = jnp.take(interp_index, stop_order, axis=1)
    order_weight = jnp.take(interp_weight, stop_order, axis=1)
    window_slots = 3 * blocks_dev
    local_index = jnp.mod(order_index - (position - 1) * blocks_dev, total_coarse)
    slot_group = local_index // blocks_dev
    slot_index = jnp.clip(slot_group, 0, 2) * blocks_dev + jnp.mod(local_index, blocks_dev)
    slot_index = jnp.clip(slot_index, 0, window_slots - 1).astype(jnp.int32).reshape(-1)
    weights = order_weight.astype(jnp.float32).reshape(-1)
    band_index = jnp.reshape(band, (1,)).astype(jnp.int32)

    kernel = functools.partial(
        sandwich_kernel, blocks_dev=blocks_dev, stop_count=stop_count, corner_count=corner_count)
    whole = pl.BlockSpec((blocks_dev, block_order, block_order), lambda k, s, sl, bd: (0, 0, 0))
    grid_spec = pltpu.PrefetchScalarGridSpec(
        num_scalar_prefetch=2,
        grid=(fine_dev, stop_count),
        in_specs=[
            pl.BlockSpec(memory_space=pltpu.SMEM),
            whole,
            whole,
            whole,
            pl.BlockSpec((1, block_order, block_order), lambda k, s, sl, bd: (k, 0, 0)),
            pl.BlockSpec((1, block_order, column_count), lambda k, s, sl, bd: (k, 0, bd[0])),
        ],
        out_specs=pl.BlockSpec((1, 1, block_order, column_count), lambda k, s, sl, bd: (k, s, 0, 0)),
        scratch_shapes=[
            pltpu.VMEM((window_slots, block_order, column_count), jnp.float32),
            pltpu.VMEM((block_order, block_order), jnp.bfloat16),
        ],
    )
    hamiltonian = pl.pallas_call(
        kernel,
        grid_spec=grid_spec,
        out_shape=jax.ShapeDtypeStruct(
            (fine_dev, stop_count, block_order, column_count), jnp.bfloat16),
        compiler_params=pltpu.CompilerParams(
            dimension_semantics=("arbitrary", "arbitrary"), vmem_limit_bytes=48 * 1024 * 1024),
    )(slot_index, band_index, weights, before, coarse_kernel, after, intersection, intersection)
    partial_value = pl.pallas_call(
        functools.partial(product_kernel, stop_count=stop_count),
        grid=(fine_dev,),
        in_specs=[
            pl.BlockSpec((1, stop_count, block_order, column_count), lambda k: (k, 0, 0, 0)),
            pl.BlockSpec((stop_count, 1, column_count, vector_count), lambda k: (0, k, 0, 0)),
        ],
        out_specs=pl.BlockSpec((1, block_order, vector_count), lambda k: (k, 0, 0)),
        out_shape=jax.ShapeDtypeStruct((fine_dev, block_order, vector_count), jnp.bfloat16),
    )(hamiltonian, sources)
    product_share = lax.psum_scatter(partial_value, "band", scatter_dimension=1, tiled=True)
    return (hamiltonian, product_share)


def solution(mesh):
    placed = (
        P("blk", None, None),
        P("blk", None, None),
        P("blk", None, None),
        P(),
        P("blk", None, None),
        P("blk", "band", None),
    )
    return jax.shard_map(
        on_device,
        mesh=mesh,
        in_specs=placed,
        out_specs=(P("blk", None, None, "band"), P("blk", "band", None)),
        check_vma=False,
    )
```

profile of v0, /device:TPU:1, one launch (start us, length us, event | category | flops | bytes accessed | tf_op | source)
XLA Modules:
  0.0 178.4 jit_solution(11351659161042178504)
XLA Ops:
  7.2 3.8 %collective-permute-start = (bf16[2,512,512]{2,1,0:T(8,128)(2,1)}, bf16[2,512,512]{2,1,0:T(8,128)(2,1)S(1)}, u32[]{:S(2)}, u32[]{:S(2)}) collective-permute-start(bf16[2,512,512]{2,1,0:T(8,128)(2,1)} %local_ref.1), channel_id=1, source_target_pairs={{0,4},{4,8},{8,12},{12,16},{16,20},{20,24},{24,28},{28,32},{32,36}... | collective-permute-start | bytes 3145736 | tf_op jit(solution)/shard_map/ppermute | solution.py:14
  11.0 5.8 %collective-permute-start.1 = (bf16[2,512,512]{2,1,0:T(8,128)(2,1)}, bf16[2,512,512]{2,1,0:T(8,128)(2,1)S(1)}, u32[]{:S(2)}, u32[]{:S(2)}) collective-permute-start(bf16[2,512,512]{2,1,0:T(8,128)(2,1)} %local_ref.1), channel_id=1, source_target_pairs={{0,124},{4,0},{8,4},{12,8},{16,12},{20,16},{24,20},{28,24},{32,28}... | collective-permute-start | bytes 3145736 | tf_op jit(solution)/shard_map/ppermute | solution.py:14
  16.8 0.8 copy.8
  17.6 0.8 copy.10
  18.3 0.7 compare_select_fusion
  19.0 0.6 gather_fusion
  19.6 0.6 gather_fusion.1
  20.2 0.7 compare_and_fusion
  20.9 34.7 %collective-permute-done.before_ref = bf16[2,512,512]{2,1,0:T(8,128)(2,1)S(1)} collective-permute-done((bf16[2,512,512]{2,1,0:T(8,128)(2,1)}, bf16[2,512,512]{2,1,0:T(8,128)(2,1)S(1)}, u32[]{:S(2)}, u32[]{:S(2)}) %collective-permute-start) | collective-permute-done | bytes 1048608 | tf_op jit(solution)/shard_map/ppermute | solution.py:14
  55.6 2.0 %collective-permute-done.1.after_ref = bf16[2,512,512]{2,1,0:T(8,128)(2,1)S(1)} collective-permute-done((bf16[2,512,512]{2,1,0:T(8,128)(2,1)}, bf16[2,512,512]{2,1,0:T(8,128)(2,1)S(1)}, u32[]{:S(2)}, u32[]{:S(2)}) %collective-permute-start.1) | collective-permute-done | bytes 1048608 | tf_op jit(solution)/shard_map/ppermute | solution.py:14
  57.7 2.9 %collective-permute-start.2 = (bf16[8,128,128]{2,1,0:T(8,128)(2,1)}, bf16[8,128,128]{2,1,0:T(8,128)(2,1)S(1)}, u32[]{:S(2)}, u32[]{:S(2)}) collective-permute-start(bf16[8,128,128]{2,1,0:T(8,128)(2,1)} %param.11), channel_id=1, source_target_pairs={{0,4},{4,8},{8,12},{12,16},{16,20},{20,24},{24,28},{28,32},{32,36}... | collective-permute-start | bytes 786440 | tf_op jit(solution)/shard_map/ppermute | solution.py:14
  60.9 1.7 collective-permute-start.3
  62.9 1.3 collective-permute-start.9
  64.2 3.1 %collective-permute-start.8 = (bf16[8,128,128]{2,1,0:T(8,128)(2,1)}, bf16[8,128,128]{2,1,0:T(8,128)(2,1)S(1)}, u32[]{:S(2)}, u32[]{:S(2)}) collective-permute-start(bf16[8,128,128]{2,1,0:T(8,128)(2,1)} %param.11), channel_id=1, source_target_pairs={{0,28},{4,32},{8,36},{12,40},{16,44},{20,48},{24,52},{28,56},{32,6... | collective-permute-start | bytes 786440 | tf_op jit(solution)/shard_map/ppermute | solution.py:14
  67.8 1.2 copy-done
  69.0 45.5 %shard_map.77.ham_ref = bf16[8,8,512,128]{3,2,1,0:T(8,128)(2,1)} custom-call(s32[256]{0:T(256)S(1)} %fusion.2.slot_ref, s32[1]{0:T(128)} %bitcast.1.band_ref, f32[256]{0:T(256)S(1)} %select_n.46.weight_ref, bf16[2,512,512]{2,1,0:T(8,128)(2,1)S(1)} %collective-permute-done.before_ref, bf16[2,512,512]{2,1,0:T(8,128)(2,1)S(1)} %copy-done, ...), custom_call_target="tpu_custom_call" | custom-call | tf_op jit(solution)/shard_map/pallas_call | solution.py:97
  114.5 2.2 %collective-permute-start.4 = (bf16[8,128,128]{2,1,0:T(8,128)(2,1)S(1)}, bf16[8,128,128]{2,1,0:T(8,128)(2,1)S(1)}, u32[]{:S(2)}, u32[]{:S(2)}) collective-permute-start(bf16[8,128,128]{2,1,0:T(8,128)(2,1)S(1)} %copy-done.2), channel_id=1, source_target_pairs={{0,12},{4,16},{8,20},{12,24},{16,28},{20,32},{24,36},{28,40},{32,4... | collective-permute-start | bytes 786440 | tf_op jit(solution)/shard_map/ppermute | solution.py:14
  116.7 1.7 collective-permute-start.5
  118.5 9.9 %collective-permute-done.4 = bf16[8,128,128]{2,1,0:T(8,128)(2,1)S(1)} collective-permute-done((bf16[8,128,128]{2,1,0:T(8,128)(2,1)S(1)}, bf16[8,128,128]{2,1,0:T(8,128)(2,1)S(1)}, u32[]{:S(2)}, u32[]{:S(2)}) %collective-permute-start.4) | collective-permute-done | bytes 262176 | tf_op jit(solution)/shard_map/ppermute | solution.py:14
  128.4 1.1 collective-permute-done.5
  129.6 8.6 %collective-permute-done.6 = bf16[8,128,128]{2,1,0:T(8,128)(2,1)S(1)} collective-permute-done((bf16[8,128,128]{2,1,0:T(8,128)(2,1)S(1)}, bf16[8,128,128]{2,1,0:T(8,128)(2,1)S(1)}, u32[]{:S(2)}, u32[]{:S(2)}) %collective-permute-start.6) | collective-permute-done | bytes 262176 | tf_op jit(solution)/shard_map/ppermute | solution.py:14
  138.4 1.3 copy-done.1
  139.7 8.4 %shard_map.78 = bf16[8,512,128]{2,1,0:T(8,128)(2,1)} custom-call(bf16[8,8,512,128]{3,2,1,0:T(8,128)(2,1)} %shard_map.77.ham_ref, bf16[8,8,128,128]{3,2,1,0:T(8,128)(2,1)} %copy-done.1), custom_call_target="tpu_custom_call" | custom-call | tf_op jit(solution)/shard_map/pallas_call | solution.py:105
  148.1 23.4 %reduce-scatter.2.cloned.1.call-done = bf16[8,128,128]{2,1,0:T(8,128)(2,1)} async-done(((bf16[8,512,128]{2,1,0:T(8,128)(2,1)}), bf16[8,128,128]{2,1,0:T(8,128)(2,1)}) %reduce-scatter.2.cloned.1.call-update) | async-done | bytes 262160 | tf_op jit(solution)/shard_map/reduce_scatter | solution.py:115
  (29 shorter events, 1.5 us)
Async XLA Ops:
  7.2 164.4 %reduce-scatter.2.cloned.1.call-start = ((), (), s32[]{:S(2)}) async-start(), calls=%async_computation.1 | async-start | bytes 1310720 | tf_op jit(solution)/shard_map/reduce_scatter | solution.py:115
  7.2 48.4 %collective-permute-start = (bf16[2,512,512]{2,1,0:T(8,128)(2,1)}, bf16[2,512,512]{2,1,0:T(8,128)(2,1)S(1)}, u32[]{:S(2)}, u32[]{:S(2)}) collective-permute-start(bf16[2,512,512]{2,1,0:T(8,128)(2,1)} %local_ref.1), channel_id=1, source_target_pairs={{0,4},{4,8},{8,12},{12,16},{16,20},{20,24},{24,28},{28,32},{32,36}... | collective-permute-start | bytes 3145736 | tf_op jit(solution)/shard_map/ppermute | solution.py:14
  11.0 46.7 %collective-permute-start.1 = (bf16[2,512,512]{2,1,0:T(8,128)(2,1)}, bf16[2,512,512]{2,1,0:T(8,128)(2,1)S(1)}, u32[]{:S(2)}, u32[]{:S(2)}) collective-permute-start(bf16[2,512,512]{2,1,0:T(8,128)(2,1)} %local_ref.1), channel_id=1, source_target_pairs={{0,124},{4,0},{8,4},{12,8},{16,12},{20,16},{24,20},{28,24},{32,28}... | collective-permute-start | bytes 3145736 | tf_op jit(solution)/shard_map/ppermute | solution.py:14
  57.7 56.8 %collective-permute-start.2 = (bf16[8,128,128]{2,1,0:T(8,128)(2,1)}, bf16[8,128,128]{2,1,0:T(8,128)(2,1)S(1)}, u32[]{:S(2)}, u32[]{:S(2)}) collective-permute-start(bf16[8,128,128]{2,1,0:T(8,128)(2,1)} %param.11), channel_id=1, source_target_pairs={{0,4},{4,8},{8,12},{12,16},{16,20},{20,24},{24,28},{28,32},{32,36}... | collective-permute-start | bytes 786440 | tf_op jit(solution)/shard_map/ppermute | solution.py:14
  60.9 55.8 %collective-permute-start.3 = (bf16[8,128,128]{2,1,0:T(8,128)(2,1)}, bf16[8,128,128]{2,1,0:T(8,128)(2,1)S(1)}, u32[]{:S(2)}, u32[]{:S(2)}) collective-permute-start(bf16[8,128,128]{2,1,0:T(8,128)(2,1)} %param.11), channel_id=1, source_target_pairs={{0,8},{4,12},{8,16},{12,20},{16,24},{20,28},{24,32},{28,36},{32,40... | collective-permute-start | bytes 786440 | tf_op jit(solution)/shard_map/ppermute | solution.py:14
  62.9 75.4 %collective-permute-start.9 = (bf16[8,128,128]{2,1,0:T(8,128)(2,1)}, bf16[8,128,128]{2,1,0:T(8,128)(2,1)S(1)}, u32[]{:S(2)}, u32[]{:S(2)}) collective-permute-start(bf16[8,128,128]{2,1,0:T(8,128)(2,1)} %param.11), channel_id=1, source_target_pairs={{0,32},{4,36},{8,40},{12,44},{16,48},{20,52},{24,56},{28,60},{32,6... | collective-permute-start | bytes 786440 | tf_op jit(solution)/shard_map/ppermute | solution.py:14
  64.2 74.1 %collective-permute-start.8 = (bf16[8,128,128]{2,1,0:T(8,128)(2,1)}, bf16[8,128,128]{2,1,0:T(8,128)(2,1)S(1)}, u32[]{:S(2)}, u32[]{:S(2)}) collective-permute-start(bf16[8,128,128]{2,1,0:T(8,128)(2,1)} %param.11), channel_id=1, source_target_pairs={{0,28},{4,32},{8,36},{12,40},{16,44},{20,48},{24,52},{28,56},{32,6... | collective-permute-start | bytes 786440 | tf_op jit(solution)/shard_map/ppermute | solution.py:14
  67.3 70.9 %collective-permute-start.7 = (bf16[8,128,128]{2,1,0:T(8,128)(2,1)}, bf16[8,128,128]{2,1,0:T(8,128)(2,1)S(1)}, u32[]{:S(2)}, u32[]{:S(2)}) collective-permute-start(bf16[8,128,128]{2,1,0:T(8,128)(2,1)} %param.11), channel_id=1, source_target_pairs={{0,24},{4,28},{8,32},{12,36},{16,40},{20,44},{24,48},{28,52},{32,5... | collective-permute-start | bytes 786440 | tf_op jit(solution)/shard_map/ppermute | solution.py:14
  67.8 1.2 copy-start
  69.0 45.5 %copy-start.2 = (bf16[8,128,128]{2,1,0:T(8,128)(2,1)S(1)}, bf16[8,128,128]{2,1,0:T(8,128)(2,1)}, u32[]{:S(2)}) copy-start(bf16[8,128,128]{2,1,0:T(8,128)(2,1)} %param.11) | copy-start | bytes 786436
  114.5 13.9 %collective-permute-start.4 = (bf16[8,128,128]{2,1,0:T(8,128)(2,1)S(1)}, bf16[8,128,128]{2,1,0:T(8,128)(2,1)S(1)}, u32[]{:S(2)}, u32[]{:S(2)}) collective-permute-start(bf16[8,128,128]{2,1,0:T(8,128)(2,1)S(1)} %copy-done.2), channel_id=1, source_target_pairs={{0,12},{4,16},{8,20},{12,24},{16,28},{20,32},{24,36},{28,40},{32,4... | collective-permute-start | bytes 786440 | tf_op jit(solution)/shard_map/ppermute | solution.py:14
  116.7 12.8 %collective-permute-start.5 = (bf16[8,128,128]{2,1,0:T(8,128)(2,1)S(1)}, bf16[8,128,128]{2,1,0:T(8,128)(2,1)S(1)}, u32[]{:S(2)}, u32[]{:S(2)}) collective-permute-start(bf16[8,128,128]{2,1,0:T(8,128)(2,1)S(1)} %copy-done.2), channel_id=1, source_target_pairs={{0,16},{4,20},{8,24},{12,28},{16,32},{20,36},{24,40},{28,44},{32,4... | collective-permute-start | bytes 786440 | tf_op jit(solution)/shard_map/ppermute | solution.py:14
  128.4 9.7 %collective-permute-start.6 = (bf16[8,128,128]{2,1,0:T(8,128)(2,1)S(1)}, bf16[8,128,128]{2,1,0:T(8,128)(2,1)S(1)}, u32[]{:S(2)}, u32[]{:S(2)}) collective-permute-start(bf16[8,128,128]{2,1,0:T(8,128)(2,1)S(1)} %copy-done.2), channel_id=1, source_target_pairs={{0,20},{4,24},{8,28},{12,32},{16,36},{20,40},{24,44},{28,48},{32,5... | collective-permute-start | bytes 786440 | tf_op jit(solution)/shard_map/ppermute | solution.py:14
  138.3 1.3 copy-start.1
Sparse Core Ops, SparseCore 0:
  148.3 23.2 reduce-scatter.1
where the time goes:
time: 179 us; the launch traced here: 178 us
  waiting for transfers between devices  79.8 us (45%)
  Pallas kernels  53.9 us (30%)
  starting transfers between devices  23 us (13%)
  between operations  14.1 us (8%)
  local copies, waits for them, and re-layouts  6.02 us (3%)
    ppermute x10, waiting for transfers between devices, shifted(): return lax.ppermute(value, axis, pairs)  56.4 us
    pallas_call x1, Pallas kernels, on_device(): pl.pallas_call(kernel, grid_spec=grid_spec, out_shape=jax.ShapeDtypeStruc...  45.5 us
    reduce_scatter x1, waiting for transfers between devices, on_device(): lax.psum_scatter(partial_value, 'band', scatter_dimension=1, tiled=True)  23.4 us
    ppermute x10, starting transfers between devices, shifted(): return lax.ppermute(value, axis, pairs)  23 us
    pallas_call x1, Pallas kernels, on_device(): pl.pallas_call(functools.partial(product_kernel, stop_count=stop_count),...  8.45 us
    unnamed x15, local copies, waits for them, and re-layouts  4.36 us
  transfers between devices with their start and end apart: 11, of which 6 were waited for; matrix products, arithmetic and copies ran while one was open for 3% of the time, Pallas kernels for 25%

commit v1 on v0

v1 whole, which is shorter than its diff:
```python
import functools

import jax
import jax.numpy as jnp
from jax import lax
from jax.experimental import pallas as pl
from jax.experimental.pallas import tpu as pltpu
from jax.sharding import PartitionSpec as P


def shifted(value, axis, steps):
    count = lax.axis_size(axis)
    pairs = [(source, (source + steps) % count) for source in range(count)]
    return lax.ppermute(value, axis, pairs)


def sandwich_kernel(slot_ref, band_ref, weight_ref, halo_ref, local_ref, inter_ref, right_ref,
                    ham_ref, prod_ref, rot_ref, *, blocks_dev, stop_count, corner_count):
    k = pl.program_id(0)
    column_count = right_ref.shape[2]
    right = right_ref[0]
    sources = [halo_ref.at[slot] for slot in range(blocks_dev)]
    sources += [local_ref.at[slot] for slot in range(blocks_dev)]
    sources += [halo_ref.at[blocks_dev + slot] for slot in range(blocks_dev)]
    for slot, source in enumerate(sources):
        prod_ref[slot] = jnp.dot(source[...], right, preferred_element_type=jnp.float32)
    for s in range(stop_count):
        base = (k * stop_count + s) * corner_count
        rotated = weight_ref[base] * prod_ref[slot_ref[base]]
        for j in range(1, corner_count):
            rotated = rotated + weight_ref[base + j] * prod_ref[slot_ref[base + j]]
        rot_ref[:, s * column_count:(s + 1) * column_count] = rotated.astype(jnp.bfloat16)
    left = inter_ref[0].T
    half = stop_count // 2
    for part in range(2):
        ham = jnp.dot(left, rot_ref[:, part * half * column_count:(part + 1) * half * column_count],
                      preferred_element_type=jnp.float32)
        for s in range(half):
            ham_ref[0, part * half + s] = ham[:, s * column_count:(s + 1) * column_count].astype(
                jnp.bfloat16)


def product_kernel(ham_ref, trial_ref, part_ref, *, stop_count):
    wide = jnp.concatenate([ham_ref[0, s] for s in range(stop_count)], axis=1)
    tall = jnp.concatenate([trial_ref[s, 0] for s in range(stop_count)], axis=0)
    part_ref[0] = jnp.dot(wide, tall, preferred_element_type=jnp.float32).astype(jnp.bfloat16)


def on_device(coarse_kernel, interp_index, interp_weight, stop_order, intersection, trial_vectors):
    blocks_dev = coarse_kernel.shape[0]
    fine_dev = intersection.shape[0]
    column_count = trial_vectors.shape[1]
    vector_count = trial_vectors.shape[2]
    block_order = intersection.shape[1]
    stop_count = stop_order.shape[0]
    corner_count = interp_index.shape[2]
    cycle_length = lax.axis_size("blk")
    total_coarse = blocks_dev * cycle_length
    position = lax.axis_index("blk")
    band = lax.axis_index("band")

    band_count = lax.axis_size("band")
    assert band_count == 2 * blocks_dev
    piece = lax.dynamic_index_in_dim(coarse_kernel, band % blocks_dev, 0, keepdims=True)
    pairs = []
    for i in range(cycle_length):
        for b in range(band_count):
            target = (i + 1) % cycle_length if b < blocks_dev else (i - 1) % cycle_length
            pairs.append((i * band_count + b, target * band_count + b))
    piece = lax.ppermute(piece, ("blk", "band"), pairs)
    halo = lax.all_gather(piece, "band", axis=0, tiled=True)
    halo, trial_vectors = lax.optimization_barrier((halo, trial_vectors))
    sources = jnp.stack(
        [shifted(trial_vectors, "blk", station + 1) for station in range(stop_count)])

    order_index = jnp.take(interp_index, stop_order, axis=1)
    order_weight = jnp.take(interp_weight, stop_order, axis=1)
    window_slots = 3 * blocks_dev
    local_index = jnp.mod(order_index - (position - 1) * blocks_dev, total_coarse)
    slot_group = local_index // blocks_dev
    slot_index = jnp.clip(slot_group, 0, 2) * blocks_dev + jnp.mod(local_index, blocks_dev)
    slot_index = jnp.clip(slot_index, 0, window_slots - 1).astype(jnp.int32).reshape(-1)
    weights = order_weight.astype(jnp.float32).reshape(-1)
    band_index = jnp.reshape(band, (1,)).astype(jnp.int32)

    kernel = functools.partial(
        sandwich_kernel, blocks_dev=blocks_dev, stop_count=stop_count, corner_count=corner_count)
    grid_spec = pltpu.PrefetchScalarGridSpec(
        num_scalar_prefetch=2,
        grid=(fine_dev,),
        in_specs=[
            pl.BlockSpec(memory_space=pltpu.SMEM),
            pl.BlockSpec((2 * blocks_dev, block_order, block_order), lambda k, sl, bd: (0, 0, 0)),
            pl.BlockSpec((blocks_dev, block_order, block_order), lambda k, sl, bd: (0, 0, 0)),
            pl.BlockSpec((1, block_order, block_order), lambda k, sl, bd: (k, 0, 0)),
            pl.BlockSpec((1, block_order, column_count), lambda k, sl, bd: (k, 0, bd[0])),
        ],
        out_specs=pl.BlockSpec(
            (1, stop_count, block_order, column_count), lambda k, sl, bd: (k, 0, 0, 0)),
        scratch_shapes=[
            pltpu.VMEM((window_slots, block_order, column_count), jnp.float32),
            pltpu.VMEM((block_order, stop_count * column_count), jnp.bfloat16),
        ],
    )
    hamiltonian = pl.pallas_call(
        kernel,
        grid_spec=grid_spec,
        out_shape=jax.ShapeDtypeStruct(
            (fine_dev, stop_count, block_order, column_count), jnp.bfloat16),
        compiler_params=pltpu.CompilerParams(
            dimension_semantics=("arbitrary",), vmem_limit_bytes=48 * 1024 * 1024),
    )(slot_index, band_index, weights, halo, coarse_kernel, intersection, intersection)
    partial_value = pl.pallas_call(
        functools.partial(product_kernel, stop_count=stop_count),
        grid=(fine_dev,),
        in_specs=[
            pl.BlockSpec((1, stop_count, block_order, column_count), lambda k: (k, 0, 0, 0)),
            pl.BlockSpec((stop_count, 1, column_count, vector_count), lambda k: (0, k, 0, 0)),
        ],
        out_specs=pl.BlockSpec((1, block_order, vector_count), lambda k: (k, 0, 0)),
        out_shape=jax.ShapeDtypeStruct((fine_dev, block_order, vector_count), jnp.bfloat16),
    )(hamiltonian, sources)
    product_share = lax.psum_scatter(partial_value, "band", scatter_dimension=1, tiled=True)
    return (hamiltonian, product_share)


def solution(mesh):
    placed = (
        P("blk", None, None),
        P("blk", None, None),
        P("blk", None, None),
        P(),
        P("blk", None, None),
        P("blk", "band", None),
    )
    return jax.shard_map(
        on_device,
        mesh=mesh,
        in_specs=placed,
        out_specs=(P("blk", None, None, "band"), P("blk", "band", None)),
        check_vma=False,
    )
```

time: 179 us -> 155 us (0.87)
  Pallas kernels: 53.9 us -> 28.6 us
  starting transfers between devices: 23 us -> 17.3 us
  waiting for transfers between devices: 79.8 us -> 84.6 us
  local copies, waits for them, and re-layouts: 6.02 us -> 8.36 us
    ppermute x10 -> x8, waiting for transfers between devices: 56.4 us -> 21.3 us  [shifted(): return lax.ppermute(value, axis, pairs)]
    all_gather x0 -> x1, waiting for transfers between devices: none -> 26.6 us  [on_device(): halo = lax.all_gather(piece, 'band', axis=0, tiled=True)]
    pallas_call x1, Pallas kernels: 45.5 us -> 20.1 us  [on_device(): pl.pallas_call(kernel, grid_spec=grid_spec, out_shape=jax.ShapeDtypeStruc...]
    ppermute x0 -> x1, waiting for transfers between devices: none -> 17.3 us  [on_device(): piece = lax.ppermute(piece, ('blk', 'band'), pairs)]
    ppermute x10 -> x8, starting transfers between devices: 23 us -> 13.4 us  [shifted(): return lax.ppermute(value, axis, pairs)]
    reduce_scatter x1, waiting for transfers between devices: 23.4 us -> 19.3 us  [on_device(): lax.psum_scatter(partial_value, 'band', scatter_dimension=1, tiled=True)]
    ppermute x0 -> x1, starting transfers between devices: none -> 3.8 us  [on_device(): piece = lax.ppermute(piece, ('blk', 'band'), pairs)]
    unnamed x15 -> x19, local copies, waits for them, and re-layouts: 4.36 us -> 5.55 us
  transfers between devices with their start and end apart: 11 -> 11, of which waited for: 6 -> 5; matrix products, arithmetic and copies ran while one was open for 3% -> 3% of each run, Pallas kernels for 25% -> 13%
where the time goes in v1:
time: 155 us; the launch traced here: 154 us
  waiting for transfers between devices  84.6 us (55%)
  Pallas kernels  28.6 us (18%)
  starting transfers between devices  17.3 us (11%)
  between operations  14.2 us (9%)
  local copies, waits for them, and re-layouts  8.36 us (5%)
    all_gather x1, waiting for transfers between devices, on_device(): halo = lax.all_gather(piece, 'band', axis=0, tiled=True)  26.6 us
    ppermute x8, waiting for transfers between devices, shifted(): return lax.ppermute(value, axis, pairs)  21.3 us
    pallas_call x1, Pallas kernels, on_device(): pl.pallas_call(kernel, grid_spec=grid_spec, out_shape=jax.ShapeDtypeStruc...  20.1 us
    reduce_scatter x1, waiting for transfers between devices, on_device(): lax.psum_scatter(partial_value, 'band', scatter_dimension=1, tiled=True)  19.3 us
    ppermute x1, waiting for transfers between devices, on_device(): piece = lax.ppermute(piece, ('blk', 'band'), pairs)  17.3 us
    ppermute x8, starting transfers between devices, shifted(): return lax.ppermute(value, axis, pairs)  13.4 us
    pallas_call x1, Pallas kernels, on_device(): pl.pallas_call(functools.partial(product_kernel, stop_count=stop_count),...  8.52 us
    unnamed x19, local copies, waits for them, and re-layouts  5.55 us
  transfers between devices with their start and end apart: 11, of which 5 were waited for; matrix products, arithmetic and copies ran while one was open for 3% of the time, Pallas kernels for 13%

profile of v1, /device:TPU:1, one launch (start us, length us, event | category | flops | bytes accessed | tf_op | source)
XLA Modules:
  0.0 154.5 jit_solution(4766795305280976302)
XLA Ops:
  7.2 1.2 constant_dynamic-slice_fusion
  8.4 3.8 %collective-permute-start = (bf16[1,512,512]{2,1,0:T(8,128)(2,1)S(1)}, bf16[1,512,512]{2,1,0:T(8,128)(2,1)S(1)}, u32[]{:S(2)}, u32[]{:S(2)}) collective-permute-start(bf16[1,512,512]{2,1,0:T(8,128)(2,1)S(1)} %constant_dynamic-slice_fusion), channel_id=1, source_target_pairs={{0,4},{1,5},{2,126},{3,127},{4,8},{5,9},{6,2},{7,3},{8,12},{9,13},... | collective-permute-start | bytes 1572872 | tf_op jit(solution)/shard_map/ppermute | solution.py:70
  12.2 17.3 %collective-permute-done = bf16[1,512,512]{2,1,0:T(8,128)(2,1)S(1)} collective-permute-done((bf16[1,512,512]{2,1,0:T(8,128)(2,1)S(1)}, bf16[1,512,512]{2,1,0:T(8,128)(2,1)S(1)}, u32[]{:S(2)}, u32[]{:S(2)}) %collective-permute-start) | collective-permute-done | bytes 524320 | tf_op jit(solution)/shard_map/ppermute | solution.py:70
  29.5 0.8 copy-done.3
  30.4 0.8 copy.12
  31.2 0.8 copy.14
  32.0 0.7 compare_select_fusion
  33.2 0.6 gather_fusion.1
  33.8 0.7 compare_and_fusion
  34.5 26.6 %all-gather.2.cloned.1.call-done.halo_ref = bf16[4,512,512]{2,1,0:T(8,128)(2,1)} async-done(((bf16[1,512,512]{2,1,0:T(8,128)(2,1)}), bf16[4,512,512]{2,1,0:T(8,128)(2,1)}) %all-gather.2.cloned.1.call-update) | async-done | bytes 2097168 | tf_op jit(solution)/shard_map/all_gather | solution.py:71
  61.1 2.4 %collective-permute-start.1 = (bf16[8,128,128]{2,1,0:T(8,128)(2,1)}, bf16[8,128,128]{2,1,0:T(8,128)(2,1)S(1)}, u32[]{:S(2)}, u32[]{:S(2)}) collective-permute-start(bf16[8,128,128]{2,1,0:T(8,128)(2,1)} %param.11), channel_id=1, source_target_pairs={{0,4},{4,8},{8,12},{12,16},{16,20},{20,24},{24,28},{28,32},{32,36}... | collective-permute-start | bytes 786440 | tf_op jit(solution)/shard_map/ppermute | solution.py:14
  63.8 1.3 collective-permute-start.2
  65.4 1.3 collective-permute-start.8
  66.7 3.5 %collective-permute-start.7 = (bf16[8,128,128]{2,1,0:T(8,128)(2,1)}, bf16[8,128,128]{2,1,0:T(8,128)(2,1)S(1)}, u32[]{:S(2)}, u32[]{:S(2)}) collective-permute-start(bf16[8,128,128]{2,1,0:T(8,128)(2,1)} %param.11), channel_id=1, source_target_pairs={{0,28},{4,32},{8,36},{12,40},{16,44},{20,48},{24,52},{28,56},{32,6... | collective-permute-start | bytes 786440 | tf_op jit(solution)/shard_map/ppermute | solution.py:14
  70.2 0.8 collective-permute-start.6
  71.0 1.6 %copy-done.1 = bf16[4,512,512]{2,1,0:T(8,128)(2,1)S(1)} copy-done((bf16[4,512,512]{2,1,0:T(8,128)(2,1)S(1)}, bf16[4,512,512]{2,1,0:T(8,128)(2,1)}, u32[]{:S(2)}) %copy-start.1) | copy-done | bytes 2097176
  72.6 20.1 %shard_map.77.ham_ref = bf16[8,8,512,128]{3,2,1,0:T(8,128)(2,1)} custom-call(s32[256]{0:T(256)S(1)} %fusion.2.slot_ref, s32[1]{0:T(128)} %bitcast.1.band_ref, f32[256]{0:T(256)S(1)} %select_n.56.weight_ref, bf16[4,512,512]{2,1,0:T(8,128)(2,1)S(1)} %copy-done.1, bf16[2,512,512]{2,1,0:T(8,128)(2,1)S(1)} %copy-done, bf16[8,512,512]{2,1,0:T(8,128)(2,1)} %right_ref.1, ...), custom_call_target="tpu_custom_call" | custom-call | tf_op jit(solution)/shard_map/pallas_call | solution.py:105
  92.7 1.4 collective-permute-start.3
  94.1 2.6 %collective-permute-start.4 = (bf16[8,128,128]{2,1,0:T(8,128)(2,1)S(1)}, bf16[8,128,128]{2,1,0:T(8,128)(2,1)S(1)}, u32[]{:S(2)}, u32[]{:S(2)}) collective-permute-start(bf16[8,128,128]{2,1,0:T(8,128)(2,1)S(1)} %copy-done.4), channel_id=1, source_target_pairs={{0,16},{4,20},{8,24},{12,28},{16,32},{20,36},{24,40},{28,44},{32,4... | collective-permute-start | bytes 786440 | tf_op jit(solution)/shard_map/ppermute | solution.py:14
  96.8 11.7 %collective-permute-done.3 = bf16[8,128,128]{2,1,0:T(8,128)(2,1)S(1)} collective-permute-done((bf16[8,128,128]{2,1,0:T(8,128)(2,1)S(1)}, bf16[8,128,128]{2,1,0:T(8,128)(2,1)S(1)}, u32[]{:S(2)}, u32[]{:S(2)}) %collective-permute-start.3) | collective-permute-done | bytes 262176 | tf_op jit(solution)/shard_map/ppermute | solution.py:14
  108.6 9.6 %collective-permute-done.5 = bf16[8,128,128]{2,1,0:T(8,128)(2,1)S(1)} collective-permute-done((bf16[8,128,128]{2,1,0:T(8,128)(2,1)S(1)}, bf16[8,128,128]{2,1,0:T(8,128)(2,1)S(1)}, u32[]{:S(2)}, u32[]{:S(2)}) %collective-permute-start.5) | collective-permute-done | bytes 262176 | tf_op jit(solution)/shard_map/ppermute | solution.py:14
  118.4 1.3 copy-done.2
  119.8 8.5 %shard_map.78 = bf16[8,512,128]{2,1,0:T(8,128)(2,1)} custom-call(bf16[8,8,512,128]{3,2,1,0:T(8,128)(2,1)} %shard_map.77.ham_ref, bf16[8,8,128,128]{3,2,1,0:T(8,128)(2,1)} %copy-done.2), custom_call_target="tpu_custom_call" | custom-call | tf_op jit(solution)/shard_map/pallas_call | solution.py:113
  128.3 19.3 %reduce-scatter.2.cloned.1.call-done = bf16[8,128,128]{2,1,0:T(8,128)(2,1)} async-done(((bf16[8,512,128]{2,1,0:T(8,128)(2,1)}), bf16[8,128,128]{2,1,0:T(8,128)(2,1)}) %reduce-scatter.2.cloned.1.call-update) | async-done | bytes 262160 | tf_op jit(solution)/shard_map/reduce_scatter | solution.py:123
  (35 shorter events, 1.6 us)
Async XLA Ops:
  7.2 63.9 %copy-start = (bf16[2,512,512]{2,1,0:T(8,128)(2,1)S(1)}, bf16[2,512,512]{2,1,0:T(8,128)(2,1)}, u32[]{:S(2)}) copy-start(bf16[2,512,512]{2,1,0:T(8,128)(2,1)} %local_ref.1) | copy-start | bytes 3145732
  7.2 53.9 %all-gather.2.cloned.1.call-start = ((), (), s32[]{:S(2)}) async-start(), calls=%async_computation.1 | async-start | bytes 2621440 | tf_op jit(solution)/shard_map/all_gather | solution.py:71
  8.4 21.1 %collective-permute-start = (bf16[1,512,512]{2,1,0:T(8,128)(2,1)S(1)}, bf16[1,512,512]{2,1,0:T(8,128)(2,1)S(1)}, u32[]{:S(2)}, u32[]{:S(2)}) collective-permute-start(bf16[1,512,512]{2,1,0:T(8,128)(2,1)S(1)} %constant_dynamic-slice_fusion), channel_id=1, source_target_pairs={{0,4},{1,5},{2,126},{3,127},{4,8},{5,9},{6,2},{7,3},{8,12},{9,13},... | collective-permute-start | bytes 1572872 | tf_op jit(solution)/shard_map/ppermute | solution.py:70
  29.5 0.8 copy-start.3
  30.3 117.3 %reduce-scatter.2.cloned.1.call-start = ((), (), s32[]{:S(2)}) async-start(), calls=%async_computation.2 | async-start | bytes 1310720 | tf_op jit(solution)/shard_map/reduce_scatter | solution.py:123
  61.1 31.6 %collective-permute-start.1 = (bf16[8,128,128]{2,1,0:T(8,128)(2,1)}, bf16[8,128,128]{2,1,0:T(8,128)(2,1)S(1)}, u32[]{:S(2)}, u32[]{:S(2)}) collective-permute-start(bf16[8,128,128]{2,1,0:T(8,128)(2,1)} %param.11), channel_id=1, source_target_pairs={{0,4},{4,8},{8,12},{12,16},{16,20},{20,24},{24,28},{28,32},{32,36}... | collective-permute-start | bytes 786440 | tf_op jit(solution)/shard_map/ppermute | solution.py:14
  63.8 30.3 %collective-permute-start.2 = (bf16[8,128,128]{2,1,0:T(8,128)(2,1)}, bf16[8,128,128]{2,1,0:T(8,128)(2,1)S(1)}, u32[]{:S(2)}, u32[]{:S(2)}) collective-permute-start(bf16[8,128,128]{2,1,0:T(8,128)(2,1)} %param.11), channel_id=1, source_target_pairs={{0,8},{4,12},{8,16},{12,20},{16,24},{20,28},{24,32},{28,36},{32,40... | collective-permute-start | bytes 786440 | tf_op jit(solution)/shard_map/ppermute | solution.py:14
  65.4 52.9 %collective-permute-start.8 = (bf16[8,128,128]{2,1,0:T(8,128)(2,1)}, bf16[8,128,128]{2,1,0:T(8,128)(2,1)S(1)}, u32[]{:S(2)}, u32[]{:S(2)}) collective-permute-start(bf16[8,128,128]{2,1,0:T(8,128)(2,1)} %param.11), channel_id=1, source_target_pairs={{0,32},{4,36},{8,40},{12,44},{16,48},{20,52},{24,56},{28,60},{32,6... | collective-permute-start | bytes 786440 | tf_op jit(solution)/shard_map/ppermute | solution.py:14
  66.7 51.6 %collective-permute-start.7 = (bf16[8,128,128]{2,1,0:T(8,128)(2,1)}, bf16[8,128,128]{2,1,0:T(8,128)(2,1)S(1)}, u32[]{:S(2)}, u32[]{:S(2)}) collective-permute-start(bf16[8,128,128]{2,1,0:T(8,128)(2,1)} %param.11), channel_id=1, source_target_pairs={{0,28},{4,32},{8,36},{12,40},{16,44},{20,48},{24,52},{28,56},{32,6... | collective-permute-start | bytes 786440 | tf_op jit(solution)/shard_map/ppermute | solution.py:14
  70.2 48.0 %collective-permute-start.6 = (bf16[8,128,128]{2,1,0:T(8,128)(2,1)}, bf16[8,128,128]{2,1,0:T(8,128)(2,1)S(1)}, u32[]{:S(2)}, u32[]{:S(2)}) collective-permute-start(bf16[8,128,128]{2,1,0:T(8,128)(2,1)} %param.11), channel_id=1, source_target_pairs={{0,24},{4,28},{8,32},{12,36},{16,40},{20,44},{24,48},{28,52},{32,5... | collective-permute-start | bytes 786440 | tf_op jit(solution)/shard_map/ppermute | solution.py:14
  71.0 1.6 %copy-start.1 = (bf16[4,512,512]{2,1,0:T(8,128)(2,1)S(1)}, bf16[4,512,512]{2,1,0:T(8,128)(2,1)}, u32[]{:S(2)}) copy-start(bf16[4,512,512]{2,1,0:T(8,128)(2,1)} %all-gather.2.cloned.1.call-done.halo_ref) | copy-start | bytes 6291460
  72.6 20.1 %copy-start.4 = (bf16[8,128,128]{2,1,0:T(8,128)(2,1)S(1)}, bf16[8,128,128]{2,1,0:T(8,128)(2,1)}, u32[]{:S(2)}) copy-start(bf16[8,128,128]{2,1,0:T(8,128)(2,1)} %param.11) | copy-start | bytes 786436
  92.7 15.8 %collective-permute-start.3 = (bf16[8,128,128]{2,1,0:T(8,128)(2,1)S(1)}, bf16[8,128,128]{2,1,0:T(8,128)(2,1)S(1)}, u32[]{:S(2)}, u32[]{:S(2)}) collective-permute-start(bf16[8,128,128]{2,1,0:T(8,128)(2,1)S(1)} %copy-done.4), channel_id=1, source_target_pairs={{0,12},{4,16},{8,20},{12,24},{16,28},{20,32},{24,36},{28,40},{32,4... | collective-permute-start | bytes 786440 | tf_op jit(solution)/shard_map/ppermute | solution.py:14
  94.1 14.4 %collective-permute-start.4 = (bf16[8,128,128]{2,1,0:T(8,128)(2,1)S(1)}, bf16[8,128,128]{2,1,0:T(8,128)(2,1)S(1)}, u32[]{:S(2)}, u32[]{:S(2)}) collective-permute-start(bf16[8,128,128]{2,1,0:T(8,128)(2,1)S(1)} %copy-done.4), channel_id=1, source_target_pairs={{0,16},{4,20},{8,24},{12,28},{16,32},{20,36},{24,40},{28,44},{32,4... | collective-permute-start | bytes 786440 | tf_op jit(solution)/shard_map/ppermute | solution.py:14
  108.5 9.7 %collective-permute-start.5 = (bf16[8,128,128]{2,1,0:T(8,128)(2,1)S(1)}, bf16[8,128,128]{2,1,0:T(8,128)(2,1)S(1)}, u32[]{:S(2)}, u32[]{:S(2)}) collective-permute-start(bf16[8,128,128]{2,1,0:T(8,128)(2,1)S(1)} %copy-done.4), channel_id=1, source_target_pairs={{0,20},{4,24},{8,28},{12,32},{16,36},{20,40},{24,44},{28,48},{32,5... | collective-permute-start | bytes 786440 | tf_op jit(solution)/shard_map/ppermute | solution.py:14
  118.4 1.3 copy-start.2
Sparse Core Ops, SparseCore 0:
  30.4 30.6 all-gather.1
  128.4 19.1 reduce-scatter.1

commit v2 on v1

--- a/solution.py
+++ b/solution.py
@@ -60,15 +60,15 @@
     band = lax.axis_index("band")
 
     band_count = lax.axis_size("band")
-    assert band_count == 2 * blocks_dev
-    piece = lax.dynamic_index_in_dim(coarse_kernel, band % blocks_dev, 0, keepdims=True)
+    core = band % 2
     pairs = []
     for i in range(cycle_length):
         for b in range(band_count):
-            target = (i + 1) % cycle_length if b < blocks_dev else (i - 1) % cycle_length
+            target = (i + 1) % cycle_length if b % 2 == 0 else (i - 1) % cycle_length
             pairs.append((i * band_count + b, target * band_count + b))
-    piece = lax.ppermute(piece, ("blk", "band"), pairs)
-    halo = lax.all_gather(piece, "band", axis=0, tiled=True)
+    near = lax.ppermute(coarse_kernel, ("blk", "band"), pairs)
+    far = lax.ppermute(near, "band", [(b, b ^ 1) for b in range(band_count)])
+    halo = jnp.concatenate([near, far], axis=0)
     halo, trial_vectors = lax.optimization_barrier((halo, trial_vectors))
     sources = jnp.stack(
         [shifted(trial_vectors, "blk", station + 1) for station in range(stop_count)])
@@ -77,8 +77,9 @@
     order_weight = jnp.take(interp_weight, stop_order, axis=1)
     window_slots = 3 * blocks_dev
     local_index = jnp.mod(order_index - (position - 1) * blocks_dev, total_coarse)
-    slot_group = local_index // blocks_dev
-    slot_index = jnp.clip(slot_group, 0, 2) * blocks_dev + jnp.mod(local_index, blocks_dev)
+    slot_group = jnp.clip(local_index // blocks_dev, 0, 2)
+    slot_group = jnp.where(core == 0, slot_group, 2 - slot_group)
+    slot_index = slot_group * blocks_dev + jnp.mod(local_index, blocks_dev)
     slot_index = jnp.clip(slot_index, 0, window_slots - 1).astype(jnp.int32).reshape(-1)
     weights = order_weight.astype(jnp.float32).reshape(-1)
     band_index = jnp.reshape(band, (1,)).astype(jnp.int32)

time: 155 us -> 136 us (0.88)
  waiting for transfers between devices: 84.6 us -> 56.4 us
  starting transfers between devices: 17.3 us -> 27.7 us
  local copies, waits for them, and re-layouts: 8.36 us -> 5.76 us
  other arithmetic: 1.5 us -> 3.31 us
    all_gather x1 -> x0, waiting for transfers between devices: 26.6 us -> none  [on_device(): halo = lax.all_gather(piece, 'band', axis=0, tiled=True)]
    ppermute x1 -> x2, starting transfers between devices: 3.8 us -> 13.2 us  [the longest x1 9.47 us: on_device(): near = lax.ppermute(coarse_kernel, ('blk', 'band'), pairs)]
    ppermute x1 -> x2, waiting for transfers between devices: 17.3 us -> 15.4 us  [the longest x1 15.4 us: on_device(): near = lax.ppermute(coarse_kernel, ('blk', 'band'), pairs)]
    concatenate x0 -> x1, other arithmetic: none -> 1.81 us  [on_device(): halo = jnp.concatenate([near, far], axis=0)]
    reduce_scatter x1, waiting for transfers between devices: 19.3 us -> 21.1 us  [on_device(): lax.psum_scatter(partial_value, 'band', scatter_dimension=1, tiled=True)]
    unnamed x19 -> x15, local copies, waits for them, and re-layouts: 5.55 us -> 4.1 us
  transfers between devices with their start and end apart: 11 -> 11, of which waited for: 5 -> 4; matrix products, arithmetic and copies ran while one was open for 3% -> 4% of each run, Pallas kernels for 13% -> 15%
where the time goes in v2:
time: 136 us
  waiting for transfers between devices  56.4 us (41%)
  Pallas kernels  28.6 us (21%)
  starting transfers between devices  27.7 us (20%)
  between operations  14.2 us (10%)
  local copies, waits for them, and re-layouts  5.76 us (4%)
  other arithmetic  3.31 us (2%)
    reduce_scatter x1, waiting for transfers between devices, on_device(): lax.psum_scatter(partial_value, 'band', scatter_dimension=1, tiled=True)  21.1 us
    pallas_call x1, Pallas kernels, on_device(): pl.pallas_call(kernel, grid_spec=grid_spec, out_shape=jax.ShapeDtypeStruc...  20.1 us
    ppermute x8, waiting for transfers between devices, shifted(): return lax.ppermute(value, axis, pairs)  19.9 us
    ppermute x1, waiting for transfers between devices, on_device(): near = lax.ppermute(coarse_kernel, ('blk', 'band'), pairs)  15.4 us
    ppermute x8, starting transfers between devices, shifted(): return lax.ppermute(value, axis, pairs)  14.5 us
    ppermute x1, starting transfers between devices, on_device(): near = lax.ppermute(coarse_kernel, ('blk', 'band'), pairs)  9.47 us
    pallas_call x1, Pallas kernels, on_device(): pl.pallas_call(functools.partial(product_kernel, stop_count=stop_count),...  8.52 us
    unnamed x15, local copies, waits for them, and re-layouts  4.1 us
  transfers between devices with their start and end apart: 11, of which 4 were waited for; matrix products, arithmetic and copies ran while one was open for 4% of the time, Pallas kernels for 15%

profile of v2, /device:TPU:1, one launch (start us, length us, event | category | flops | bytes accessed | tf_op | source)
XLA Modules:
  0.0 135.9 jit_solution(8558878911254235871)
XLA Ops:
  7.2 9.5 %collective-permute-start = (bf16[2,512,512]{2,1,0:T(8,128)(2,1)}, bf16[2,512,512]{2,1,0:T(8,128)(2,1)S(1)}, u32[]{:S(2)}, u32[]{:S(2)}) collective-permute-start(bf16[2,512,512]{2,1,0:T(8,128)(2,1)} %local_ref.1), channel_id=1, source_target_pairs={{0,4},{1,125},{2,6},{3,127},{4,8},{5,1},{6,10},{7,3},{8,12},{9,5},... | collective-permute-start | bytes 3145736 | tf_op jit(solution)/shard_map/ppermute | solution.py:69
  16.7 15.4 %collective-permute-done = bf16[2,512,512]{2,1,0:T(8,128)(2,1)S(1)} collective-permute-done((bf16[2,512,512]{2,1,0:T(8,128)(2,1)}, bf16[2,512,512]{2,1,0:T(8,128)(2,1)S(1)}, u32[]{:S(2)}, u32[]{:S(2)}) %collective-permute-start) | collective-permute-done | bytes 1048608 | tf_op jit(solution)/shard_map/ppermute | solution.py:69
  32.1 3.7 %collective-permute-start.1 = (bf16[2,512,512]{2,1,0:T(8,128)(2,1)S(1)}, bf16[2,512,512]{2,1,0:T(8,128)(2,1)}, u32[]{:S(2)}, u32[]{:S(2)}) collective-permute-start(bf16[2,512,512]{2,1,0:T(8,128)(2,1)S(1)} %collective-permute-done), channel_id=1, source_target_pairs={{0,1},{1,0},{2,3},{3,2},{4,5},{5,4},{6,7},{7,6},{8,9},{9,8},{10,11... | collective-permute-start | bytes 3145736 | tf_op jit(solution)/shard_map/ppermute | solution.py:70
  35.8 0.8 copy.8
  36.6 0.8 copy.10
  37.4 0.7 compare_select_fusion
  38.1 0.6 gather_fusion
  38.7 0.6 gather_fusion.1
  39.2 0.7 compare_and_fusion
  40.0 1.8 %pad_maximum_fusion.halo_ref = bf16[4,512,512]{2,1,0:T(8,128)(2,1)S(1)} fusion(bf16[2,512,512]{2,1,0:T(8,128)(2,1)} %collective-permute-done.1, bf16[2,512,512]{2,1,0:T(8,128)(2,1)} %copy-done.2), kind=kLoop, calls=%fused_computation.2 | loop fusion | flops 1048576 | bytes 4194304 | tf_op jit(solution)/shard_map/concatenate | solution.py:71
  41.8 3.7 %collective-permute-start.2 = (bf16[8,128,128]{2,1,0:T(8,128)(2,1)}, bf16[8,128,128]{2,1,0:T(8,128)(2,1)S(1)}, u32[]{:S(2)}, u32[]{:S(2)}) collective-permute-start(bf16[8,128,128]{2,1,0:T(8,128)(2,1)} %param.11), channel_id=1, source_target_pairs={{0,4},{4,8},{8,12},{12,16},{16,20},{20,24},{24,28},{28,32},{32,36}... | collective-permute-start | bytes 786440 | tf_op jit(solution)/shard_map/ppermute | solution.py:14
  45.6 0.1 copy.9
  46.2 1.3 collective-permute-start.9
  47.5 3.3 %collective-permute-start.8 = (bf16[8,128,128]{2,1,0:T(8,128)(2,1)}, bf16[8,128,128]{2,1,0:T(8,128)(2,1)S(1)}, u32[]{:S(2)}, u32[]{:S(2)}) collective-permute-start(bf16[8,128,128]{2,1,0:T(8,128)(2,1)} %param.11), channel_id=1, source_target_pairs={{0,28},{4,32},{8,36},{12,40},{16,44},{20,48},{24,52},{28,56},{32,6... | collective-permute-start | bytes 786440 | tf_op jit(solution)/shard_map/ppermute | solution.py:14
  50.8 1.2 collective-permute-start.7
  52.0 20.1 %shard_map.77.ham_ref = bf16[8,8,512,128]{3,2,1,0:T(8,128)(2,1)} custom-call(s32[256]{0:T(256)S(1)} %fusion.2.slot_ref, s32[1]{0:T(128)} %bitcast.1.band_ref, f32[256]{0:T(256)S(1)} %select_n.64.weight_ref, bf16[4,512,512]{2,1,0:T(8,128)(2,1)S(1)} %pad_maximum_fusion.halo_ref, bf16[2,512,512]{2,1,0:T(8,128)(2,1)S(1)} %copy-done, ...), custom_call_target="tpu_custom_call" | custom-call | tf_op jit(solution)/shard_map/pallas_call | solution.py:106
  72.1 1.2 collective-permute-start.4
  73.3 3.7 %collective-permute-start.5 = (bf16[8,128,128]{2,1,0:T(8,128)(2,1)}, bf16[8,128,128]{2,1,0:T(8,128)(2,1)S(1)}, u32[]{:S(2)}, u32[]{:S(2)}) collective-permute-start(bf16[8,128,128]{2,1,0:T(8,128)(2,1)} %param.11), channel_id=1, source_target_pairs={{0,16},{4,20},{8,24},{12,28},{16,32},{20,36},{24,40},{28,44},{32,4... | collective-permute-start | bytes 786440 | tf_op jit(solution)/shard_map/ppermute | solution.py:14
  77.0 1.0 bitcast_dynamic-update-slice_fusion.6
  78.0 10.0 %collective-permute-done.4 = bf16[8,128,128]{2,1,0:T(8,128)(2,1)S(1)} collective-permute-done((bf16[8,128,128]{2,1,0:T(8,128)(2,1)}, bf16[8,128,128]{2,1,0:T(8,128)(2,1)S(1)}, u32[]{:S(2)}, u32[]{:S(2)}) %collective-permute-start.4) | collective-permute-done | bytes 262176 | tf_op jit(solution)/shard_map/ppermute | solution.py:14
  88.1 9.8 %collective-permute-done.6 = bf16[8,128,128]{2,1,0:T(8,128)(2,1)S(1)} collective-permute-done((bf16[8,128,128]{2,1,0:T(8,128)(2,1)}, bf16[8,128,128]{2,1,0:T(8,128)(2,1)S(1)}, u32[]{:S(2)}, u32[]{:S(2)}) %collective-permute-start.6) | collective-permute-done | bytes 262176 | tf_op jit(solution)/shard_map/ppermute | solution.py:14
  98.2 1.3 copy-done.1
  99.5 8.5 %shard_map.78 = bf16[8,512,128]{2,1,0:T(8,128)(2,1)} custom-call(bf16[8,8,512,128]{3,2,1,0:T(8,128)(2,1)} %shard_map.77.ham_ref, bf16[8,8,128,128]{3,2,1,0:T(8,128)(2,1)} %copy-done.1), custom_call_target="tpu_custom_call" | custom-call | tf_op jit(solution)/shard_map/pallas_call | solution.py:114
  108.0 21.1 %reduce-scatter.2.cloned.1.call-done = bf16[8,128,128]{2,1,0:T(8,128)(2,1)} async-done(((bf16[8,512,128]{2,1,0:T(8,128)(2,1)}), bf16[8,128,128]{2,1,0:T(8,128)(2,1)}) %reduce-scatter.2.cloned.1.call-update) | async-done | bytes 262160 | tf_op jit(solution)/shard_map/reduce_scatter | solution.py:124
  (30 shorter events, 1.0 us)
Async XLA Ops:
  7.2 121.9 %reduce-scatter.2.cloned.1.call-start = ((), (), s32[]{:S(2)}) async-start(), calls=%async_computation.1 | async-start | bytes 1310720 | tf_op jit(solution)/shard_map/reduce_scatter | solution.py:124
  7.2 24.9 %collective-permute-start = (bf16[2,512,512]{2,1,0:T(8,128)(2,1)}, bf16[2,512,512]{2,1,0:T(8,128)(2,1)S(1)}, u32[]{:S(2)}, u32[]{:S(2)}) collective-permute-start(bf16[2,512,512]{2,1,0:T(8,128)(2,1)} %local_ref.1), channel_id=1, source_target_pairs={{0,4},{1,125},{2,6},{3,127},{4,8},{5,1},{6,10},{7,3},{8,12},{9,5},... | collective-permute-start | bytes 3145736 | tf_op jit(solution)/shard_map/ppermute | solution.py:69
  32.1 7.9 %copy-start.2 = (bf16[2,512,512]{2,1,0:T(8,128)(2,1)}, bf16[2,512,512]{2,1,0:T(8,128)(2,1)S(1)}, u32[]{:S(2)}) copy-start(bf16[2,512,512]{2,1,0:T(8,128)(2,1)S(1)} %collective-permute-done) | copy-start | bytes 3145732
  32.1 7.9 %collective-permute-start.1 = (bf16[2,512,512]{2,1,0:T(8,128)(2,1)S(1)}, bf16[2,512,512]{2,1,0:T(8,128)(2,1)}, u32[]{:S(2)}, u32[]{:S(2)}) collective-permute-start(bf16[2,512,512]{2,1,0:T(8,128)(2,1)S(1)} %collective-permute-done), channel_id=1, source_target_pairs={{0,1},{1,0},{2,3},{3,2},{4,5},{5,4},{6,7},{7,6},{8,9},{9,8},{10,11... | collective-permute-start | bytes 3145736 | tf_op jit(solution)/shard_map/ppermute | solution.py:70
  40.0 12.0 %copy-start = (bf16[2,512,512]{2,1,0:T(8,128)(2,1)S(1)}, bf16[2,512,512]{2,1,0:T(8,128)(2,1)}, u32[]{:S(2)}) copy-start(bf16[2,512,512]{2,1,0:T(8,128)(2,1)} %local_ref.1) | copy-start | bytes 3145732
  41.8 30.3 %collective-permute-start.2 = (bf16[8,128,128]{2,1,0:T(8,128)(2,1)}, bf16[8,128,128]{2,1,0:T(8,128)(2,1)S(1)}, u32[]{:S(2)}, u32[]{:S(2)}) collective-permute-start(bf16[8,128,128]{2,1,0:T(8,128)(2,1)} %param.11), channel_id=1, source_target_pairs={{0,4},{4,8},{8,12},{12,16},{16,20},{20,24},{24,28},{28,32},{32,36}... | collective-permute-start | bytes 786440 | tf_op jit(solution)/shard_map/ppermute | solution.py:14
  45.8 27.5 %collective-permute-start.3 = (bf16[8,128,128]{2,1,0:T(8,128)(2,1)}, bf16[8,128,128]{2,1,0:T(8,128)(2,1)}, u32[]{:S(2)}, u32[]{:S(2)}) collective-permute-start(bf16[8,128,128]{2,1,0:T(8,128)(2,1)} %param.11), channel_id=1, source_target_pairs={{0,8},{4,12},{8,16},{12,20},{16,24},{20,28},{24,32},{28,36},{32,40... | collective-permute-start | bytes 786440 | tf_op jit(solution)/shard_map/ppermute | solution.py:14
  46.2 51.9 %collective-permute-start.9 = (bf16[8,128,128]{2,1,0:T(8,128)(2,1)}, bf16[8,128,128]{2,1,0:T(8,128)(2,1)S(1)}, u32[]{:S(2)}, u32[]{:S(2)}) collective-permute-start(bf16[8,128,128]{2,1,0:T(8,128)(2,1)} %param.11), channel_id=1, source_target_pairs={{0,32},{4,36},{8,40},{12,44},{16,48},{20,52},{24,56},{28,60},{32,6... | collective-permute-start | bytes 786440 | tf_op jit(solution)/shard_map/ppermute | solution.py:14
  47.5 50.6 %collective-permute-start.8 = (bf16[8,128,128]{2,1,0:T(8,128)(2,1)}, bf16[8,128,128]{2,1,0:T(8,128)(2,1)S(1)}, u32[]{:S(2)}, u32[]{:S(2)}) collective-permute-start(bf16[8,128,128]{2,1,0:T(8,128)(2,1)} %param.11), channel_id=1, source_target_pairs={{0,28},{4,32},{8,36},{12,40},{16,44},{20,48},{24,52},{28,56},{32,6... | collective-permute-start | bytes 786440 | tf_op jit(solution)/shard_map/ppermute | solution.py:14
  50.8 47.2 %collective-permute-start.7 = (bf16[8,128,128]{2,1,0:T(8,128)(2,1)}, bf16[8,128,128]{2,1,0:T(8,128)(2,1)S(1)}, u32[]{:S(2)}, u32[]{:S(2)}) collective-permute-start(bf16[8,128,128]{2,1,0:T(8,128)(2,1)} %param.11), channel_id=1, source_target_pairs={{0,24},{4,28},{8,32},{12,36},{16,40},{20,44},{24,48},{28,52},{32,5... | collective-permute-start | bytes 786440 | tf_op jit(solution)/shard_map/ppermute | solution.py:14
  72.1 15.9 %collective-permute-start.4 = (bf16[8,128,128]{2,1,0:T(8,128)(2,1)}, bf16[8,128,128]{2,1,0:T(8,128)(2,1)S(1)}, u32[]{:S(2)}, u32[]{:S(2)}) collective-permute-start(bf16[8,128,128]{2,1,0:T(8,128)(2,1)} %param.11), channel_id=1, source_target_pairs={{0,12},{4,16},{8,20},{12,24},{16,28},{20,32},{24,36},{28,40},{32,4... | collective-permute-start | bytes 786440 | tf_op jit(solution)/shard_map/ppermute | solution.py:14
  73.3 14.7 %collective-permute-start.5 = (bf16[8,128,128]{2,1,0:T(8,128)(2,1)}, bf16[8,128,128]{2,1,0:T(8,128)(2,1)S(1)}, u32[]{:S(2)}, u32[]{:S(2)}) collective-permute-start(bf16[8,128,128]{2,1,0:T(8,128)(2,1)} %param.11), channel_id=1, source_target_pairs={{0,16},{4,20},{8,24},{12,28},{16,32},{20,36},{24,40},{28,44},{32,4... | collective-permute-start | bytes 786440 | tf_op jit(solution)/shard_map/ppermute | solution.py:14
  88.0 9.9 %collective-permute-start.6 = (bf16[8,128,128]{2,1,0:T(8,128)(2,1)}, bf16[8,128,128]{2,1,0:T(8,128)(2,1)S(1)}, u32[]{:S(2)}, u32[]{:S(2)}) collective-permute-start(bf16[8,128,128]{2,1,0:T(8,128)(2,1)} %param.11), channel_id=1, source_target_pairs={{0,20},{4,24},{8,28},{12,32},{16,36},{20,40},{24,44},{28,48},{32,5... | collective-permute-start | bytes 786440 | tf_op jit(solution)/shard_map/ppermute | solution.py:14
  98.2 1.3 copy-start.1
Sparse Core Ops, SparseCore 0:
  108.2 20.8 reduce-scatter.1

commit v3 on v2

--- a/solution.py
+++ b/solution.py
@@ -15,7 +15,8 @@
 
 
 def sandwich_kernel(slot_ref, band_ref, weight_ref, halo_ref, local_ref, inter_ref, right_ref,
-                    ham_ref, prod_ref, rot_ref, *, blocks_dev, stop_count, corner_count):
+                    trial_ref, ham_ref, part_ref, prod_ref, rot_ref, wide_ref,
+                    *, blocks_dev, stop_count, corner_count):
     k = pl.program_id(0)
     column_count = right_ref.shape[2]
     right = right_ref[0]
@@ -35,15 +36,13 @@
     for part in range(2):
         ham = jnp.dot(left, rot_ref[:, part * half * column_count:(part + 1) * half * column_count],
                       preferred_element_type=jnp.float32)
+        ham = ham.astype(jnp.bfloat16)
+        wide_ref[:, part * half * column_count:(part + 1) * half * column_count] = ham
         for s in range(half):
-            ham_ref[0, part * half + s] = ham[:, s * column_count:(s + 1) * column_count].astype(
-                jnp.bfloat16)
-
-
-def product_kernel(ham_ref, trial_ref, part_ref, *, stop_count):
-    wide = jnp.concatenate([ham_ref[0, s] for s in range(stop_count)], axis=1)
-    tall = jnp.concatenate([trial_ref[s, 0] for s in range(stop_count)], axis=0)
-    part_ref[0] = jnp.dot(wide, tall, preferred_element_type=jnp.float32).astype(jnp.bfloat16)
+            ham_ref[0, part * half + s] = ham[:, s * column_count:(s + 1) * column_count]
+    tall = trial_ref[:, 0].reshape(stop_count * column_count, trial_ref.shape[3])
+    part_ref[0] = jnp.dot(wide_ref[...], tall, preferred_element_type=jnp.float32).astype(
+        jnp.bfloat16)
 
 
 def on_device(coarse_kernel, interp_index, interp_weight, stop_order, intersection, trial_vectors):
@@ -69,7 +68,6 @@
     near = lax.ppermute(coarse_kernel, ("blk", "band"), pairs)
     far = lax.ppermute(near, "band", [(b, b ^ 1) for b in range(band_count)])
     halo = jnp.concatenate([near, far], axis=0)
-    halo, trial_vectors = lax.optimization_barrier((halo, trial_vectors))
     sources = jnp.stack(
         [shifted(trial_vectors, "blk", station + 1) for station in range(stop_count)])
 
@@ -95,32 +93,30 @@
             pl.BlockSpec((blocks_dev, block_order, block_order), lambda k, sl, bd: (0, 0, 0)),
             pl.BlockSpec((1, block_order, block_order), lambda k, sl, bd: (k, 0, 0)),
             pl.BlockSpec((1, block_order, column_count), lambda k, sl, bd: (k, 0, bd[0])),
+            pl.BlockSpec(
+                (stop_count, 1, column_count, vector_count), lambda k, sl, bd: (0, k, 0, 0)),
         ],
-        out_specs=pl.BlockSpec(
-            (1, stop_count, block_order, column_count), lambda k, sl, bd: (k, 0, 0, 0)),
+        out_specs=[
+            pl.BlockSpec(
+                (1, stop_count, block_order, column_count), lambda k, sl, bd: (k, 0, 0, 0)),
+            pl.BlockSpec((1, block_order, vector_count), lambda k, sl, bd: (k, 0, 0)),
+        ],
         scratch_shapes=[
             pltpu.VMEM((window_slots, block_order, column_count), jnp.float32),
             pltpu.VMEM((block_order, stop_count * column_count), jnp.bfloat16),
+            pltpu.VMEM((block_order, stop_count * column_count), jnp.bfloat16),
         ],
     )
-    hamiltonian = pl.pallas_call(
+    hamiltonian, partial_value = pl.pallas_call(
         kernel,
         grid_spec=grid_spec,
-        out_shape=jax.ShapeDtypeStruct(
-            (fine_dev, stop_count, block_order, column_count), jnp.bfloat16),
+        out_shape=[
+            jax.ShapeDtypeStruct((fine_dev, stop_count, block_order, column_count), jnp.bfloat16),
+            jax.ShapeDtypeStruct((fine_dev, block_order, vector_count), jnp.bfloat16),
+        ],
         compiler_params=pltpu.CompilerParams(
             dimension_semantics=("arbitrary",), vmem_limit_bytes=48 * 1024 * 1024),
-    )(slot_index, band_index, weights, halo, coarse_kernel, intersection, intersection)
-    partial_value = pl.pallas_call(
-        functools.partial(product_kernel, stop_count=stop_count),
-        grid=(fine_dev,),
-        in_specs=[
-            pl.BlockSpec((1, stop_count, block_order, column_count), lambda k: (k, 0, 0, 0)),
-            pl.BlockSpec((stop_count, 1, column_count, vector_count), lambda k: (0, k, 0, 0)),
-        ],
-        out_specs=pl.BlockSpec((1, block_order, vector_count), lambda k: (k, 0, 0)),
-        out_shape=jax.ShapeDtypeStruct((fine_dev, block_order, vector_count), jnp.bfloat16),
-    )(hamiltonian, sources)
+    )(slot_index, band_index, weights, halo, coarse_kernel, intersection, intersection, sources)
     product_share = lax.psum_scatter(partial_value, "band", scatter_dimension=1, tiled=True)
     return (hamiltonian, product_share)
 

time: 136 us -> 137 us (level)
  waiting for transfers between devices: 56.4 us -> 65.5 us
  Pallas kernels: 28.6 us -> 26.3 us
  local copies, waits for them, and re-layouts: 5.76 us -> 3.49 us
  starting transfers between devices: 27.7 us -> 25.6 us
  other arithmetic: 3.31 us -> 1.68 us
    ppermute x1, waiting for transfers between devices: 15.4 us -> 0.01 us  [on_device(): near = lax.ppermute(coarse_kernel, ('blk', 'band'), pairs)]
    ppermute x8, waiting for transfers between devices: 19.9 us -> 31.8 us  [shifted(): return lax.ppermute(value, axis, pairs)]
    reduce_scatter x1, waiting for transfers between devices: 21.1 us -> 31.7 us  [on_device(): lax.psum_scatter(partial_value, 'band', scatter_dimension=1, tiled=True)]
    ppermute x1, starting transfers between devices: 9.47 us -> 6.37 us  [on_device(): near = lax.ppermute(coarse_kernel, ('blk', 'band'), pairs)]
    pallas_call x2 -> x1, Pallas kernels: 28.6 us -> 26.3 us  [on_device(): pl.pallas_call(kernel, grid_spec=grid_spec, out_shape=[jax.ShapeDtypeStru...]
    unnamed x15 -> x13, local copies, waits for them, and re-layouts: 4.1 us -> 1.83 us
    ppermute x1, waiting for transfers between devices: 0.01 us -> 2.01 us  [on_device(): far = lax.ppermute(near, 'band', [(b, b ^ 1) for b in range(band_count)])]
    concatenate x1, other arithmetic: 1.81 us -> 0.18 us  [on_device(): halo = jnp.concatenate([near, far], axis=0)]
  transfers between devices with their start and end apart: 11 -> 11, of which waited for: 4 -> 4; matrix products, arithmetic and copies ran while one was open for 4% -> 4% of each run, Pallas kernels for 15% -> 0%
where the time goes in v3:
time: 137 us
  waiting for transfers between devices  65.5 us (48%)
  Pallas kernels  26.3 us (19%)
  starting transfers between devices  25.6 us (19%)
  between operations  14.2 us (10%)
  local copies, waits for them, and re-layouts  3.49 us (3%)
  other arithmetic  1.68 us (1%)
    ppermute x8, waiting for transfers between devices, shifted(): return lax.ppermute(value, axis, pairs)  31.8 us
    reduce_scatter x1, waiting for transfers between devices, on_device(): lax.psum_scatter(partial_value, 'band', scatter_dimension=1, tiled=True)  31.7 us
    pallas_call x1, Pallas kernels, on_device(): pl.pallas_call(kernel, grid_spec=grid_spec, out_shape=[jax.ShapeDtypeStru...  26.3 us
    ppermute x8, starting transfers between devices, shifted(): return lax.ppermute(value, axis, pairs)  15.1 us
    ppermute x1, starting transfers between devices, on_device(): near = lax.ppermute(coarse_kernel, ('blk', 'band'), pairs)  6.37 us
    ppermute x1, starting transfers between devices, on_device(): far = lax.ppermute(near, 'band', [(b, b ^ 1) for b in range(band_count)])  4.06 us
  transfers between devices with their start and end apart: 11, of which 4 were waited for; matrix products, arithmetic and copies ran while one was open for 4% of the time, Pallas kernels for 0%

profile of v3, /device:TPU:1, one launch (start us, length us, event | category | flops | bytes accessed | tf_op | source)
XLA Modules:
  0.0 136.7 jit_solution(288979259831687160)
XLA Ops:
  7.2 4.6 %collective-permute-start.7 = (bf16[8,128,128]{2,1,0:T(8,128)(2,1)}, bf16[8,128,128]{2,1,0:T(8,128)(2,1)S(1)}, u32[]{:S(2)}, u32[]{:S(2)}) collective-permute-start(bf16[8,128,128]{2,1,0:T(8,128)(2,1)} %param.11), channel_id=1, source_target_pairs={{0,24},{4,28},{8,32},{12,36},{16,40},{20,44},{24,48},{28,52},{32,5... | collective-permute-start | bytes 786440 | tf_op jit(solution)/shard_map/ppermute | solution.py:14
  11.9 3.2 %collective-permute-start.6 = (bf16[8,128,128]{2,1,0:T(8,128)(2,1)}, bf16[8,128,128]{2,1,0:T(8,128)(2,1)S(1)}, u32[]{:S(2)}, u32[]{:S(2)}) collective-permute-start(bf16[8,128,128]{2,1,0:T(8,128)(2,1)} %param.11), channel_id=1, source_target_pairs={{0,20},{4,24},{8,28},{12,32},{16,36},{20,40},{24,44},{28,48},{32,5... | collective-permute-start | bytes 786440 | tf_op jit(solution)/shard_map/ppermute | solution.py:14
  15.1 1.0 collective-permute-start.3
  16.1 0.8 collective-permute-start.2
  16.9 6.4 %collective-permute-start = (bf16[2,512,512]{2,1,0:T(8,128)(2,1)}, bf16[2,512,512]{2,1,0:T(8,128)(2,1)S(1)}, u32[]{:S(2)}, u32[]{:S(2)}) collective-permute-start(bf16[2,512,512]{2,1,0:T(8,128)(2,1)} %local_ref.1), channel_id=1, source_target_pairs={{0,4},{1,125},{2,6},{3,127},{4,8},{5,1},{6,10},{7,3},{8,12},{9,5},... | collective-permute-start | bytes 3145736 | tf_op jit(solution)/shard_map/ppermute | solution.py:68
  23.3 0.7 compare_and_fusion
  24.0 0.7 compare_select_fusion
  24.6 0.8 copy.8
  25.4 0.8 copy.10
  26.2 0.6 gather_fusion
  26.8 0.6 gather_fusion.1
  27.5 0.1 copy.9
  27.7 0.1 sub.26
  27.8 0.1 copy.11
  27.9 0.1 select_n.64.weight_ref
  28.0 11.6 %collective-permute-done.2 = bf16[8,128,128]{2,1,0:T(8,128)(2,1)S(1)} collective-permute-done((bf16[8,128,128]{2,1,0:T(8,128)(2,1)}, bf16[8,128,128]{2,1,0:T(8,128)(2,1)S(1)}, u32[]{:S(2)}, u32[]{:S(2)}) %collective-permute-start.2) | collective-permute-done | bytes 262176 | tf_op jit(solution)/shard_map/ppermute | solution.py:14
  39.6 0.1 collective-permute-start.5
  39.8 20.2 %collective-permute-done.4 = bf16[8,128,128]{2,1,0:T(8,128)(2,1)S(1)} collective-permute-done((bf16[8,128,128]{2,1,0:T(8,128)(2,1)}, bf16[8,128,128]{2,1,0:T(8,128)(2,1)S(1)}, u32[]{:S(2)}, u32[]{:S(2)}) %collective-permute-start.4) | collective-permute-done | bytes 262176 | tf_op jit(solution)/shard_map/ppermute | solution.py:14
  60.0 5.3 %collective-permute-start.8 = (bf16[8,128,128]{2,1,0:T(8,128)(2,1)}, bf16[8,128,128]{2,1,0:T(8,128)(2,1)S(1)}, u32[]{:S(2)}, u32[]{:S(2)}) collective-permute-start(bf16[8,128,128]{2,1,0:T(8,128)(2,1)} %param.11), channel_id=1, source_target_pairs={{0,28},{4,32},{8,36},{12,40},{16,44},{20,48},{24,52},{28,56},{32,6... | collective-permute-start | bytes 786440 | tf_op jit(solution)/shard_map/ppermute | solution.py:14
  65.3 4.1 %collective-permute-start.1 = (bf16[2,512,512]{2,1,0:T(8,128)(2,1)S(1)}, bf16[2,512,512]{2,1,0:T(8,128)(2,1)S(1)}, u32[]{:S(2)}, u32[]{:S(2)}) collective-permute-start(bf16[2,512,512]{2,1,0:T(8,128)(2,1)S(1)} %collective-permute-done), channel_id=1, source_target_pairs={{0,1},{1,0},{2,3},{3,2},{4,5},{5,4},{6,7},{7,6},{8,9},{9,8},{10,11... | collective-permute-start | bytes 3145736 | tf_op jit(solution)/shard_map/ppermute | solution.py:69
  69.6 2.0 %collective-permute-done.1 = bf16[2,512,512]{2,1,0:T(8,128)(2,1)S(1)} collective-permute-done((bf16[2,512,512]{2,1,0:T(8,128)(2,1)S(1)}, bf16[2,512,512]{2,1,0:T(8,128)(2,1)S(1)}, u32[]{:S(2)}, u32[]{:S(2)}) %collective-permute-start.1) | collective-permute-done | bytes 1048608 | tf_op jit(solution)/shard_map/ppermute | solution.py:69
  71.6 0.2 pad_maximum_fusion.halo_ref
  71.8 26.3 %shard_map.77 = (bf16[8,8,512,128]{3,2,1,0:T(8,128)(2,1)}, bf16[8,512,128]{2,1,0:T(8,128)(2,1)}) custom-call(s32[256]{0:T(256)S(1)} %fusion.2.slot_ref, s32[1]{0:T(128)} %bitcast.1.band_ref, f32[256]{0:T(256)S(1)} %select_n.64.weight_ref, bf16[4,512,512]{2,1,0:T(8,128)(2,1)S(1)} %pad_maximum_fusion.halo_ref, bf16[2,512,512]{2,1,0:T(8,128)(2,1)S(1)} %copy-done, ...), custom_call_target="tpu_custom_call" | custom-call | tf_op jit(solution)/shard_map/pallas_call | solution.py:110
  98.2 31.7 %reduce-scatter.2.cloned.1.call-done = bf16[8,128,128]{2,1,0:T(8,128)(2,1)} async-done(((bf16[8,512,128]{2,1,0:T(8,128)(2,1)}), bf16[8,128,128]{2,1,0:T(8,128)(2,1)}) %reduce-scatter.2.cloned.1.call-update) | async-done | bytes 262160 | tf_op jit(solution)/shard_map/reduce_scatter | solution.py:120
  (27 shorter events, 0.5 us)
Async XLA Ops:
  7.2 122.7 %reduce-scatter.2.cloned.1.call-start = ((), (), s32[]{:S(2)}) async-start(), calls=%async_computation.1 | async-start | bytes 1310720 | tf_op jit(solution)/shard_map/reduce_scatter | solution.py:120
  7.2 62.2 %collective-permute-start.7 = (bf16[8,128,128]{2,1,0:T(8,128)(2,1)}, bf16[8,128,128]{2,1,0:T(8,128)(2,1)S(1)}, u32[]{:S(2)}, u32[]{:S(2)}) collective-permute-start(bf16[8,128,128]{2,1,0:T(8,128)(2,1)} %param.11), channel_id=1, source_target_pairs={{0,24},{4,28},{8,32},{12,36},{16,40},{20,44},{24,48},{28,52},{32,5... | collective-permute-start | bytes 786440 | tf_op jit(solution)/shard_map/ppermute | solution.py:14
  11.9 57.5 %collective-permute-start.6 = (bf16[8,128,128]{2,1,0:T(8,128)(2,1)}, bf16[8,128,128]{2,1,0:T(8,128)(2,1)S(1)}, u32[]{:S(2)}, u32[]{:S(2)}) collective-permute-start(bf16[8,128,128]{2,1,0:T(8,128)(2,1)} %param.11), channel_id=1, source_target_pairs={{0,20},{4,24},{8,28},{12,32},{16,36},{20,40},{24,44},{28,48},{32,5... | collective-permute-start | bytes 786440 | tf_op jit(solution)/shard_map/ppermute | solution.py:14
  15.1 24.5 %collective-permute-start.3 = (bf16[8,128,128]{2,1,0:T(8,128)(2,1)}, bf16[8,128,128]{2,1,0:T(8,128)(2,1)S(1)}, u32[]{:S(2)}, u32[]{:S(2)}) collective-permute-start(bf16[8,128,128]{2,1,0:T(8,128)(2,1)} %param.11), channel_id=1, source_target_pairs={{0,8},{4,12},{8,16},{12,20},{16,24},{20,28},{24,32},{28,36},{32,40... | collective-permute-start | bytes 786440 | tf_op jit(solution)/shard_map/ppermute | solution.py:14
  16.1 23.5 %collective-permute-start.2 = (bf16[8,128,128]{2,1,0:T(8,128)(2,1)}, bf16[8,128,128]{2,1,0:T(8,128)(2,1)S(1)}, u32[]{:S(2)}, u32[]{:S(2)}) collective-permute-start(bf16[8,128,128]{2,1,0:T(8,128)(2,1)} %param.11), channel_id=1, source_target_pairs={{0,4},{4,8},{8,12},{12,16},{16,20},{20,24},{24,28},{28,32},{32,36}... | collective-permute-start | bytes 786440 | tf_op jit(solution)/shard_map/ppermute | solution.py:14
  16.9 48.4 %collective-permute-start = (bf16[2,512,512]{2,1,0:T(8,128)(2,1)}, bf16[2,512,512]{2,1,0:T(8,128)(2,1)S(1)}, u32[]{:S(2)}, u32[]{:S(2)}) collective-permute-start(bf16[2,512,512]{2,1,0:T(8,128)(2,1)} %local_ref.1), channel_id=1, source_target_pairs={{0,4},{1,125},{2,6},{3,127},{4,8},{5,1},{6,10},{7,3},{8,12},{9,5},... | collective-permute-start | bytes 3145736 | tf_op jit(solution)/shard_map/ppermute | solution.py:68
  39.6 20.4 %collective-permute-start.4 = (bf16[8,128,128]{2,1,0:T(8,128)(2,1)}, bf16[8,128,128]{2,1,0:T(8,128)(2,1)S(1)}, u32[]{:S(2)}, u32[]{:S(2)}) collective-permute-start(bf16[8,128,128]{2,1,0:T(8,128)(2,1)} %param.11), channel_id=1, source_target_pairs={{0,12},{4,16},{8,20},{12,24},{16,28},{20,32},{24,36},{28,40},{32,4... | collective-permute-start | bytes 786440 | tf_op jit(solution)/shard_map/ppermute | solution.py:14
  39.6 20.4 %collective-permute-start.5 = (bf16[8,128,128]{2,1,0:T(8,128)(2,1)}, bf16[8,128,128]{2,1,0:T(8,128)(2,1)S(1)}, u32[]{:S(2)}, u32[]{:S(2)}) collective-permute-start(bf16[8,128,128]{2,1,0:T(8,128)(2,1)} %param.11), channel_id=1, source_target_pairs={{0,16},{4,20},{8,24},{12,28},{16,32},{20,36},{24,40},{28,44},{32,4... | collective-permute-start | bytes 786440 | tf_op jit(solution)/shard_map/ppermute | solution.py:14
  60.0 9.6 %collective-permute-start.9 = (bf16[8,128,128]{2,1,0:T(8,128)(2,1)}, bf16[8,128,128]{2,1,0:T(8,128)(2,1)S(1)}, u32[]{:S(2)}, u32[]{:S(2)}) collective-permute-start(bf16[8,128,128]{2,1,0:T(8,128)(2,1)} %param.11), channel_id=1, source_target_pairs={{0,32},{4,36},{8,40},{12,44},{16,48},{20,52},{24,56},{28,60},{32,6... | collective-permute-start | bytes 786440 | tf_op jit(solution)/shard_map/ppermute | solution.py:14
  60.0 9.5 %collective-permute-start.8 = (bf16[8,128,128]{2,1,0:T(8,128)(2,1)}, bf16[8,128,128]{2,1,0:T(8,128)(2,1)S(1)}, u32[]{:S(2)}, u32[]{:S(2)}) collective-permute-start(bf16[8,128,128]{2,1,0:T(8,128)(2,1)} %param.11), channel_id=1, source_target_pairs={{0,28},{4,32},{8,36},{12,40},{16,44},{20,48},{24,52},{28,56},{32,6... | collective-permute-start | bytes 786440 | tf_op jit(solution)/shard_map/ppermute | solution.py:14
  65.3 6.3 %collective-permute-start.1 = (bf16[2,512,512]{2,1,0:T(8,128)(2,1)S(1)}, bf16[2,512,512]{2,1,0:T(8,128)(2,1)S(1)}, u32[]{:S(2)}, u32[]{:S(2)}) collective-permute-start(bf16[2,512,512]{2,1,0:T(8,128)(2,1)S(1)} %collective-permute-done), channel_id=1, source_target_pairs={{0,1},{1,0},{2,3},{3,2},{4,5},{5,4},{6,7},{7,6},{8,9},{9,8},{10,11... | collective-permute-start | bytes 3145736 | tf_op jit(solution)/shard_map/ppermute | solution.py:69
  69.6 2.2 %copy-start.1 = (bf16[8,8,128,128]{3,2,1,0:T(8,128)(2,1)}, bf16[8,8,128,128]{3,2,1,0:T(8,128)(2,1)S(1)}, u32[]{:S(2)}) copy-start(bf16[8,8,128,128]{3,2,1,0:T(8,128)(2,1)S(1)} %bitcast_dynamic-update-slice_fusion.trial_ref) | copy-start | bytes 6291460
  69.6 2.2 %copy-start = (bf16[2,512,512]{2,1,0:T(8,128)(2,1)S(1)}, bf16[2,512,512]{2,1,0:T(8,128)(2,1)}, u32[]{:S(2)}) copy-start(bf16[2,512,512]{2,1,0:T(8,128)(2,1)} %local_ref.1) | copy-start | bytes 3145732
Sparse Core Ops, SparseCore 0:
  98.3 31.5 reduce-scatter.1

commit v4 on v3

--- a/solution.py
+++ b/solution.py
@@ -41,8 +41,7 @@
         for s in range(half):
             ham_ref[0, part * half + s] = ham[:, s * column_count:(s + 1) * column_count]
     tall = trial_ref[:, 0].reshape(stop_count * column_count, trial_ref.shape[3])
-    part_ref[0] = jnp.dot(wide_ref[...], tall, preferred_element_type=jnp.float32).astype(
-        jnp.bfloat16)
+    part_ref[0] = jnp.dot(wide_ref[...], tall, preferred_element_type=jnp.float32)
 
 
 def on_device(coarse_kernel, interp_index, interp_weight, stop_order, intersection, trial_vectors):
@@ -112,12 +111,24 @@
         grid_spec=grid_spec,
         out_shape=[
             jax.ShapeDtypeStruct((fine_dev, stop_count, block_order, column_count), jnp.bfloat16),
-            jax.ShapeDtypeStruct((fine_dev, block_order, vector_count), jnp.bfloat16),
+            jax.ShapeDtypeStruct((fine_dev, block_order, vector_count), jnp.float32),
         ],
         compiler_params=pltpu.CompilerParams(
             dimension_semantics=("arbitrary",), vmem_limit_bytes=48 * 1024 * 1024),
     )(slot_index, band_index, weights, halo, coarse_kernel, intersection, intersection, sources)
-    product_share = lax.psum_scatter(partial_value, "band", scatter_dimension=1, tiled=True)
+    row_block = block_order // band_count
+    halves = partial_value.reshape(fine_dev, 2, 2, row_block, vector_count)
+    send = lax.dynamic_index_in_dim(halves, 1 - core, 2, keepdims=False)
+    keep = lax.dynamic_index_in_dim(halves, core, 2, keepdims=False)
+    swap = [(b, b ^ 1) for b in range(band_count)]
+    pair_sum = keep + lax.ppermute(send.astype(jnp.bfloat16), "band", swap).astype(jnp.float32)
+    level = band // 2
+    send = lax.dynamic_index_in_dim(pair_sum, 1 - level, 1, keepdims=False)
+    keep = lax.dynamic_index_in_dim(pair_sum, level, 1, keepdims=False)
+    swap = [(b, b ^ 2) for b in range(band_count)]
+    product_share = (
+        keep + lax.ppermute(send.astype(jnp.bfloat16), "band", swap).astype(jnp.float32)
+    ).astype(jnp.bfloat16)
     return (hamiltonian, product_share)
 
 

time: 137 us -> 116 us (0.85)
  the two profiles are of different devices: /device:TPU:1 before, /device:TPU:56 now
where the time goes in v4:
time: 116 us; the launch traced here: 115 us
  waiting for transfers between devices  62.5 us (54%)
  Pallas kernels  26 us (22%)
  starting transfers between devices  17.2 us (15%)
  local copies, waits for them, and re-layouts  5.39 us (5%)
  other arithmetic  3.6 us (3%)
    ppermute x8, waiting for transfers between devices, shifted(): return lax.ppermute(value, axis, pairs)  52.1 us
    pallas_call x1, Pallas kernels, on_device(): pl.pallas_call(kernel, grid_spec=grid_spec, out_shape=[jax.ShapeDtypeStru...  26 us
    ppermute x8, starting transfers between devices, shifted(): return lax.ppermute(value, axis, pairs)  16.4 us
    ppermute x2, waiting for transfers between devices, on_device(): lax.ppermute(send.astype(jnp.bfloat16), 'band', swap).astype(jnp.float32)  10.3 us
    unnamed x13, local copies, waits for them, and re-layouts  3.59 us
  transfers between devices with their start and end apart: 12, of which 6 were waited for; matrix products, arithmetic and copies ran while one was open for 4% of the time, Pallas kernels for 0%

profile of v4, /device:TPU:56, one launch (start us, length us, event | category | flops | bytes accessed | tf_op | source)
XLA Modules:
  0.0 115.5 jit_solution(14224497984029386539)
XLA Ops:
  0.6 1.1 collective-permute-start.7
  1.7 4.7 %collective-permute-start.6 = (bf16[8,128,128]{2,1,0:T(8,128)(2,1)}, bf16[8,128,128]{2,1,0:T(8,128)(2,1)S(1)}, u32[]{:S(2)}, u32[]{:S(2)}) collective-permute-start(bf16[8,128,128]{2,1,0:T(8,128)(2,1)} %param.11), channel_id=1, source_target_pairs={{0,20},{4,24},{8,28},{12,32},{16,36},{20,40},{24,44},{28,48},{32,5... | collective-permute-start | bytes 786440 | tf_op jit(solution)/shard_map/ppermute | solution.py:14
  6.4 3.2 %collective-permute-start.2 = (bf16[8,128,128]{2,1,0:T(8,128)(2,1)}, bf16[8,128,128]{2,1,0:T(8,128)(2,1)S(1)}, u32[]{:S(2)}, u32[]{:S(2)}) collective-permute-start(bf16[8,128,128]{2,1,0:T(8,128)(2,1)} %param.11), channel_id=1, source_target_pairs={{0,4},{4,8},{8,12},{12,16},{16,20},{20,24},{24,28},{28,32},{32,36}... | collective-permute-start | bytes 786440 | tf_op jit(solution)/shard_map/ppermute | solution.py:14
  9.6 0.6 collective-permute-start
  10.2 0.7 compare_and_fusion
  10.9 0.7 compare_select_fusion
  11.6 0.8 copy.10
  12.4 0.8 copy.12
  13.2 0.6 gather_fusion
  13.7 0.6 gather_fusion.1
  15.0 7.3 %collective-permute-done.2 = bf16[8,128,128]{2,1,0:T(8,128)(2,1)S(1)} collective-permute-done((bf16[8,128,128]{2,1,0:T(8,128)(2,1)}, bf16[8,128,128]{2,1,0:T(8,128)(2,1)S(1)}, u32[]{:S(2)}, u32[]{:S(2)}) %collective-permute-start.2) | collective-permute-done | bytes 262176 | tf_op jit(solution)/shard_map/ppermute | solution.py:14
  22.3 4.2 %collective-permute-start.4 = (bf16[8,128,128]{2,1,0:T(8,128)(2,1)}, bf16[8,128,128]{2,1,0:T(8,128)(2,1)S(1)}, u32[]{:S(2)}, u32[]{:S(2)}) collective-permute-start(bf16[8,128,128]{2,1,0:T(8,128)(2,1)} %param.11), channel_id=1, source_target_pairs={{0,12},{4,16},{8,20},{12,24},{16,28},{20,32},{24,36},{28,40},{32,4... | collective-permute-start | bytes 786440 | tf_op jit(solution)/shard_map/ppermute | solution.py:14
  26.6 1.9 %collective-permute-start.5 = (bf16[8,128,128]{2,1,0:T(8,128)(2,1)}, bf16[8,128,128]{2,1,0:T(8,128)(2,1)S(1)}, u32[]{:S(2)}, u32[]{:S(2)}) collective-permute-start(bf16[8,128,128]{2,1,0:T(8,128)(2,1)} %param.11), channel_id=1, source_target_pairs={{0,16},{4,20},{8,24},{12,28},{16,32},{20,36},{24,40},{28,44},{32,4... | collective-permute-start | bytes 786440 | tf_op jit(solution)/shard_map/ppermute | solution.py:14
  28.5 19.8 %collective-permute-done.4 = bf16[8,128,128]{2,1,0:T(8,128)(2,1)S(1)} collective-permute-done((bf16[8,128,128]{2,1,0:T(8,128)(2,1)}, bf16[8,128,128]{2,1,0:T(8,128)(2,1)S(1)}, u32[]{:S(2)}, u32[]{:S(2)}) %collective-permute-start.4) | collective-permute-done | bytes 262176 | tf_op jit(solution)/shard_map/ppermute | solution.py:14
  48.3 1.3 %collective-permute-start.9 = (bf16[8,128,128]{2,1,0:T(8,128)(2,1)}, bf16[8,128,128]{2,1,0:T(8,128)(2,1)S(1)}, u32[]{:S(2)}, u32[]{:S(2)}) collective-permute-start(bf16[8,128,128]{2,1,0:T(8,128)(2,1)} %param.11), channel_id=1, source_target_pairs={{0,32},{4,36},{8,40},{12,44},{16,48},{20,52},{24,56},{28,60},{32,6... | collective-permute-start | bytes 786440 | tf_op jit(solution)/shard_map/ppermute | solution.py:14
  49.6 14.1 %collective-permute-done.5 = bf16[8,128,128]{2,1,0:T(8,128)(2,1)S(1)} collective-permute-done((bf16[8,128,128]{2,1,0:T(8,128)(2,1)}, bf16[8,128,128]{2,1,0:T(8,128)(2,1)S(1)}, u32[]{:S(2)}, u32[]{:S(2)}) %collective-permute-start.5) | collective-permute-done | bytes 262176 | tf_op jit(solution)/shard_map/ppermute | solution.py:14
  63.9 10.9 %collective-permute-done.8 = bf16[8,128,128]{2,1,0:T(8,128)(2,1)S(1)} collective-permute-done((bf16[8,128,128]{2,1,0:T(8,128)(2,1)}, bf16[8,128,128]{2,1,0:T(8,128)(2,1)S(1)}, u32[]{:S(2)}, u32[]{:S(2)}) %collective-permute-start.8) | collective-permute-done | bytes 262176 | tf_op jit(solution)/shard_map/ppermute | solution.py:14
  75.1 1.1 copy-done.1
  76.2 0.7 copy-done
  76.9 26.0 %shard_map.77 = (bf16[8,8,512,128]{3,2,1,0:T(8,128)(2,1)}, f32[8,512,128]{2,1,0:T(8,128)S(1)}) custom-call(s32[256]{0:T(256)S(1)} %fusion.5.slot_ref, s32[1]{0:T(128)} %bitcast.1.band_ref, f32[256]{0:T(256)S(1)} %select_n.82.weight_ref, bf16[4,512,512]{2,1,0:T(8,128)(2,1)S(1)} %pad_maximum_fusion.halo_ref, bf16[2,512,512]{2,1,0:T(8,128)(2,1)S(1)} %copy-done, ...), custom_call_target="tpu_custom_call" | custom-call | tf_op jit(solution)/shard_map/pallas_call | solution.py:109
  103.1 2.0 %collective-permute-done.10 = bf16[8,2,128,128]{3,2,0,1:T(8,128)(2,1)} collective-permute-done((bf16[8,2,128,128]{3,2,0,1:T(8,128)(2,1)S(1)}, bf16[8,2,128,128]{3,2,0,1:T(8,128)(2,1)}, u32[]{:S(2)}, u32[]{:S(2)}) %collective-permute-start.10) | collective-permute-done | bytes 524320 | tf_op jit(solution)/shard_map/ppermute | solution.py:124
  105.1 1.1 bitcast_add_fusion
  106.4 8.3 %collective-permute-done.11 = bf16[8,128,128]{2,1,0:T(8,128)(2,1)S(1)} collective-permute-done((bf16[8,128,128]{2,1,0:T(8,128)(2,1)S(1)}, bf16[8,128,128]{2,1,0:T(8,128)(2,1)S(1)}, u32[]{:S(2)}, u32[]{:S(2)}) %collective-permute-start.11) | collective-permute-done | bytes 262176 | tf_op jit(solution)/shard_map/ppermute | solution.py:130
  114.7 0.8 fusion.1
  (32 shorter events, 1.4 us)
Async XLA Ops:
  0.6 63.2 %collective-permute-start.7 = (bf16[8,128,128]{2,1,0:T(8,128)(2,1)}, bf16[8,128,128]{2,1,0:T(8,128)(2,1)S(1)}, u32[]{:S(2)}, u32[]{:S(2)}) collective-permute-start(bf16[8,128,128]{2,1,0:T(8,128)(2,1)} %param.11), channel_id=1, source_target_pairs={{0,24},{4,28},{8,32},{12,36},{16,40},{20,44},{24,48},{28,52},{32,5... | collective-permute-start | bytes 786440 | tf_op jit(solution)/shard_map/ppermute | solution.py:14
  1.7 62.0 %collective-permute-start.6 = (bf16[8,128,128]{2,1,0:T(8,128)(2,1)}, bf16[8,128,128]{2,1,0:T(8,128)(2,1)S(1)}, u32[]{:S(2)}, u32[]{:S(2)}) collective-permute-start(bf16[8,128,128]{2,1,0:T(8,128)(2,1)} %param.11), channel_id=1, source_target_pairs={{0,20},{4,24},{8,28},{12,32},{16,36},{20,40},{24,44},{28,48},{32,5... | collective-permute-start | bytes 786440 | tf_op jit(solution)/shard_map/ppermute | solution.py:14
  6.4 20.1 %collective-permute-start.3 = (bf16[8,128,128]{2,1,0:T(8,128)(2,1)}, bf16[8,128,128]{2,1,0:T(8,128)(2,1)S(1)}, u32[]{:S(2)}, u32[]{:S(2)}) collective-permute-start(bf16[8,128,128]{2,1,0:T(8,128)(2,1)} %param.11), channel_id=1, source_target_pairs={{0,8},{4,12},{8,16},{12,20},{16,24},{20,28},{24,32},{28,36},{32,40... | collective-permute-start | bytes 786440 | tf_op jit(solution)/shard_map/ppermute | solution.py:14
  6.4 15.9 %collective-permute-start.2 = (bf16[8,128,128]{2,1,0:T(8,128)(2,1)}, bf16[8,128,128]{2,1,0:T(8,128)(2,1)S(1)}, u32[]{:S(2)}, u32[]{:S(2)}) collective-permute-start(bf16[8,128,128]{2,1,0:T(8,128)(2,1)} %param.11), channel_id=1, source_target_pairs={{0,4},{4,8},{8,12},{12,16},{16,20},{20,24},{24,28},{28,32},{32,36}... | collective-permute-start | bytes 786440 | tf_op jit(solution)/shard_map/ppermute | solution.py:14
  9.6 54.1 %collective-permute-start = (bf16[2,512,512]{2,1,0:T(8,128)(2,1)}, bf16[2,512,512]{2,1,0:T(8,128)(2,1)S(1)}, u32[]{:S(2)}, u32[]{:S(2)}) collective-permute-start(bf16[2,512,512]{2,1,0:T(8,128)(2,1)} %local_ref.1), channel_id=1, source_target_pairs={{0,4},{1,125},{2,6},{3,127},{4,8},{5,1},{6,10},{7,3},{8,12},{9,5},... | collective-permute-start | bytes 3145736 | tf_op jit(solution)/shard_map/ppermute | solution.py:67
  22.3 26.0 %collective-permute-start.4 = (bf16[8,128,128]{2,1,0:T(8,128)(2,1)}, bf16[8,128,128]{2,1,0:T(8,128)(2,1)S(1)}, u32[]{:S(2)}, u32[]{:S(2)}) collective-permute-start(bf16[8,128,128]{2,1,0:T(8,128)(2,1)} %param.11), channel_id=1, source_target_pairs={{0,12},{4,16},{8,20},{12,24},{16,28},{20,32},{24,36},{28,40},{32,4... | collective-permute-start | bytes 786440 | tf_op jit(solution)/shard_map/ppermute | solution.py:14
  26.6 37.1 %collective-permute-start.5 = (bf16[8,128,128]{2,1,0:T(8,128)(2,1)}, bf16[8,128,128]{2,1,0:T(8,128)(2,1)S(1)}, u32[]{:S(2)}, u32[]{:S(2)}) collective-permute-start(bf16[8,128,128]{2,1,0:T(8,128)(2,1)} %param.11), channel_id=1, source_target_pairs={{0,16},{4,20},{8,24},{12,28},{16,32},{20,36},{24,40},{28,44},{32,4... | collective-permute-start | bytes 786440 | tf_op jit(solution)/shard_map/ppermute | solution.py:14
  48.3 26.6 %collective-permute-start.9 = (bf16[8,128,128]{2,1,0:T(8,128)(2,1)}, bf16[8,128,128]{2,1,0:T(8,128)(2,1)S(1)}, u32[]{:S(2)}, u32[]{:S(2)}) collective-permute-start(bf16[8,128,128]{2,1,0:T(8,128)(2,1)} %param.11), channel_id=1, source_target_pairs={{0,32},{4,36},{8,40},{12,44},{16,48},{20,52},{24,56},{28,60},{32,6... | collective-permute-start | bytes 786440 | tf_op jit(solution)/shard_map/ppermute | solution.py:14
  63.7 11.1 %collective-permute-start.8 = (bf16[8,128,128]{2,1,0:T(8,128)(2,1)}, bf16[8,128,128]{2,1,0:T(8,128)(2,1)S(1)}, u32[]{:S(2)}, u32[]{:S(2)}) collective-permute-start(bf16[8,128,128]{2,1,0:T(8,128)(2,1)} %param.11), channel_id=1, source_target_pairs={{0,28},{4,32},{8,36},{12,40},{16,44},{20,48},{24,52},{28,56},{32,6... | collective-permute-start | bytes 786440 | tf_op jit(solution)/shard_map/ppermute | solution.py:14
  63.7 11.2 %collective-permute-start.1 = (bf16[2,512,512]{2,1,0:T(8,128)(2,1)S(1)}, bf16[2,512,512]{2,1,0:T(8,128)(2,1)S(1)}, u32[]{:S(2)}, u32[]{:S(2)}) collective-permute-start(bf16[2,512,512]{2,1,0:T(8,128)(2,1)S(1)} %collective-permute-done), channel_id=1, source_target_pairs={{0,1},{1,0},{2,3},{3,2},{4,5},{5,4},{6,7},{7,6},{8,9},{9,8},{10,11... | collective-permute-start | bytes 3145736 | tf_op jit(solution)/shard_map/ppermute | solution.py:68
  74.9 1.3 %copy-start.1 = (bf16[8,8,128,128]{3,2,1,0:T(8,128)(2,1)}, bf16[8,8,128,128]{3,2,1,0:T(8,128)(2,1)S(1)}, u32[]{:S(2)}) copy-start(bf16[8,8,128,128]{3,2,1,0:T(8,128)(2,1)S(1)} %bitcast_dynamic-update-slice_fusion.trial_ref) | copy-start | bytes 6291460
  74.9 2.0 %copy-start = (bf16[2,512,512]{2,1,0:T(8,128)(2,1)S(1)}, bf16[2,512,512]{2,1,0:T(8,128)(2,1)}, u32[]{:S(2)}) copy-start(bf16[2,512,512]{2,1,0:T(8,128)(2,1)} %local_ref.1) | copy-start | bytes 3145732
  103.0 2.1 %collective-permute-start.10 = (bf16[8,2,128,128]{3,2,0,1:T(8,128)(2,1)S(1)}, bf16[8,2,128,128]{3,2,0,1:T(8,128)(2,1)}, u32[]{:S(2)}, u32[]{:S(2)}) collective-permute-start(bf16[8,2,128,128]{3,2,0,1:T(8,128)(2,1)S(1)} %fusion), channel_id=1, source_target_pairs={{0,1},{1,0},{2,3},{3,2},{4,5},{5,4},{6,7},{7,6},{8,9},{9,8},{10,11... | collective-permute-start | bytes 1572872 | tf_op jit(solution)/shard_map/ppermute | solution.py:124
  106.3 8.4 %collective-permute-start.11 = (bf16[8,128,128]{2,1,0:T(8,128)(2,1)S(1)}, bf16[8,128,128]{2,1,0:T(8,128)(2,1)S(1)}, u32[]{:S(2)}, u32[]{:S(2)}) collective-permute-start(bf16[8,128,128]{2,1,0:T(8,128)(2,1)S(1)} %fusion.2), channel_id=1, source_target_pairs={{0,2},{1,3},{2,0},{3,1},{4,6},{5,7},{6,4},{7,5},{8,10},{9,11},{10,... | collective-permute-start | bytes 786440 | tf_op jit(solution)/shard_map/ppermute | solution.py:130

commit v5 on v2

--- a/solution.py
+++ b/solution.py
@@ -35,15 +35,16 @@
     for part in range(2):
         ham = jnp.dot(left, rot_ref[:, part * half * column_count:(part + 1) * half * column_count],
                       preferred_element_type=jnp.float32)
+        ham = ham.astype(jnp.bfloat16)
         for s in range(half):
-            ham_ref[0, part * half + s] = ham[:, s * column_count:(s + 1) * column_count].astype(
-                jnp.bfloat16)
+            ham_ref[0, part * half + s] = ham[:, s * column_count:(s + 1) * column_count]
 
 
-def product_kernel(ham_ref, trial_ref, part_ref, *, stop_count):
+def product_kernel(ham_ref, *refs, stop_count):
+    trial_refs, part_ref = refs[:stop_count], refs[stop_count]
     wide = jnp.concatenate([ham_ref[0, s] for s in range(stop_count)], axis=1)
-    tall = jnp.concatenate([trial_ref[s, 0] for s in range(stop_count)], axis=0)
-    part_ref[0] = jnp.dot(wide, tall, preferred_element_type=jnp.float32).astype(jnp.bfloat16)
+    tall = jnp.concatenate([trial_refs[s][0] for s in range(stop_count)], axis=0)
+    part_ref[0] = jnp.dot(wide, tall, preferred_element_type=jnp.float32)
 
 
 def on_device(coarse_kernel, interp_index, interp_weight, stop_order, intersection, trial_vectors):
@@ -69,9 +70,7 @@
     near = lax.ppermute(coarse_kernel, ("blk", "band"), pairs)
     far = lax.ppermute(near, "band", [(b, b ^ 1) for b in range(band_count)])
     halo = jnp.concatenate([near, far], axis=0)
-    halo, trial_vectors = lax.optimization_barrier((halo, trial_vectors))
-    sources = jnp.stack(
-        [shifted(trial_vectors, "blk", station + 1) for station in range(stop_count)])
+    sources = [shifted(trial_vectors, "blk", station + 1) for station in range(stop_count)]
 
     order_index = jnp.take(interp_index, stop_order, axis=1)
     order_weight = jnp.take(interp_weight, stop_order, axis=1)
@@ -110,18 +109,37 @@
             (fine_dev, stop_count, block_order, column_count), jnp.bfloat16),
         compiler_params=pltpu.CompilerParams(
             dimension_semantics=("arbitrary",), vmem_limit_bytes=48 * 1024 * 1024),
+        cost_estimate=pl.CostEstimate(
+            flops=2 * fine_dev * block_order * block_order * column_count * (window_slots + stop_count),
+            transcendentals=0,
+            bytes_accessed=2 * fine_dev * block_order * (block_order + stop_count * column_count)),
     )(slot_index, band_index, weights, halo, coarse_kernel, intersection, intersection)
     partial_value = pl.pallas_call(
         functools.partial(product_kernel, stop_count=stop_count),
         grid=(fine_dev,),
         in_specs=[
             pl.BlockSpec((1, stop_count, block_order, column_count), lambda k: (k, 0, 0, 0)),
-            pl.BlockSpec((stop_count, 1, column_count, vector_count), lambda k: (0, k, 0, 0)),
-        ],
+        ] + [pl.BlockSpec((1, column_count, vector_count), lambda k: (k, 0, 0))] * stop_count,
         out_specs=pl.BlockSpec((1, block_order, vector_count), lambda k: (k, 0, 0)),
-        out_shape=jax.ShapeDtypeStruct((fine_dev, block_order, vector_count), jnp.bfloat16),
-    )(hamiltonian, sources)
-    product_share = lax.psum_scatter(partial_value, "band", scatter_dimension=1, tiled=True)
+        out_shape=jax.ShapeDtypeStruct((fine_dev, block_order, vector_count), jnp.float32),
+        cost_estimate=pl.CostEstimate(
+            flops=2 * fine_dev * stop_count * block_order * column_count * vector_count,
+            transcendentals=0,
+            bytes_accessed=2 * fine_dev * stop_count * block_order * column_count),
+    )(hamiltonian, *sources)
+    row_block = block_order // band_count
+    halves = partial_value.reshape(fine_dev, 2, 2, row_block, vector_count)
+    send = lax.dynamic_index_in_dim(halves, 1 - core, 2, keepdims=False)
+    keep = lax.dynamic_index_in_dim(halves, core, 2, keepdims=False)
+    swap = [(b, b ^ 1) for b in range(band_count)]
+    pair_sum = keep + lax.ppermute(send.astype(jnp.bfloat16), "band", swap).astype(jnp.float32)
+    level = band // 2
+    send = lax.dynamic_index_in_dim(pair_sum, 1 - level, 1, keepdims=False)
+    keep = lax.dynamic_index_in_dim(pair_sum, level, 1, keepdims=False)
+    swap = [(b, b ^ 2) for b in range(band_count)]
+    product_share = (
+        keep + lax.ppermute(send.astype(jnp.bfloat16), "band", swap).astype(jnp.float32)
+    ).astype(jnp.bfloat16)
     return (hamiltonian, product_share)
 
 

time: 136 us -> 114 us (0.84)
  the two profiles are of different devices: /device:TPU:1 before, /device:TPU:74 now
where the time goes in v5:
time: 114 us; the launch traced here: 113 us
  starting transfers between devices  44.7 us (39%)
  Pallas kernels  29 us (25%)
  waiting for transfers between devices  28.1 us (25%)
  local copies, waits for them, and re-layouts  6.81 us (6%)
  other arithmetic  3.78 us (3%)
    ppermute x8, starting transfers between devices, shifted(): return lax.ppermute(value, axis, pairs)  27.2 us
    pallas_call x1, Pallas kernels, on_device(): pl.pallas_call(kernel, grid_spec=grid_spec, out_shape=jax.ShapeDtypeStruc...  20.1 us
    ppermute x1, waiting for transfers between devices, on_device(): near = lax.ppermute(coarse_kernel, ('blk', 'band'), pairs)  17.9 us
    ppermute x1, starting transfers between devices, on_device(): far = lax.ppermute(near, 'band', [(b, b ^ 1) for b in range(band_count)])  15 us
    ppermute x2, waiting for transfers between devices, on_device(): lax.ppermute(send.astype(jnp.bfloat16), 'band', swap).astype(jnp.float32)  10.2 us
    pallas_call x1, Pallas kernels, on_device(): pl.pallas_call(functools.partial(product_kernel, stop_count=stop_count),...  8.88 us
    unnamed x22, local copies, waits for them, and re-layouts  3.83 us
    ppermute x1, starting transfers between devices, on_device(): near = lax.ppermute(coarse_kernel, ('blk', 'band'), pairs)  2.36 us
  transfers between devices with their start and end apart: 12, of which 3 were waited for; matrix products, arithmetic and copies ran while one was open for 4% of the time, Pallas kernels for 18%

profile of v5, /device:TPU:74, one launch (start us, length us, event | category | flops | bytes accessed | tf_op | source)
XLA Modules:
  0.0 113.2 jit_solution(9920183102572627082)
XLA Ops:
  0.6 2.4 %collective-permute-start = (bf16[2,512,512]{2,1,0:T(8,128)(2,1)}, bf16[2,512,512]{2,1,0:T(8,128)(2,1)S(1)}, u32[]{:S(2)}, u32[]{:S(2)}) collective-permute-start(bf16[2,512,512]{2,1,0:T(8,128)(2,1)} %local_ref.1), channel_id=1, source_target_pairs={{0,4},{1,125},{2,6},{3,127},{4,8},{5,1},{6,10},{7,3},{8,12},{9,5},... | collective-permute-start | bytes 3145736 | tf_op jit(solution)/shard_map/ppermute | solution.py:70
  3.0 2.3 %collective-permute-start.2 = (bf16[8,128,128]{2,1,0:T(8,128)(2,1)}, bf16[8,128,128]{2,1,0:T(8,128)(2,1)S(1)}, u32[]{:S(2)}, u32[]{:S(2)}) collective-permute-start(bf16[8,128,128]{2,1,0:T(8,128)(2,1)} %param.11), channel_id=1, source_target_pairs={{0,4},{4,8},{8,12},{12,16},{16,20},{20,24},{24,28},{28,32},{32,36}... | collective-permute-start | bytes 786440 | tf_op jit(solution)/shard_map/ppermute | solution.py:14
  5.4 3.6 %collective-permute-start.4 = (bf16[8,128,128]{2,1,0:T(8,128)(2,1)}, bf16[8,128,128]{2,1,0:T(8,128)(2,1)S(1)}, u32[]{:S(2)}, u32[]{:S(2)}) collective-permute-start(bf16[8,128,128]{2,1,0:T(8,128)(2,1)} %param.11), channel_id=1, source_target_pairs={{0,12},{4,16},{8,20},{12,24},{16,28},{20,32},{24,36},{28,40},{32,4... | collective-permute-start | bytes 786440 | tf_op jit(solution)/shard_map/ppermute | solution.py:14
  9.1 2.4 %collective-permute-start.5 = (bf16[8,128,128]{2,1,0:T(8,128)(2,1)}, bf16[8,128,128]{2,1,0:T(8,128)(2,1)S(1)}, u32[]{:S(2)}, u32[]{:S(2)}) collective-permute-start(bf16[8,128,128]{2,1,0:T(8,128)(2,1)} %param.11), channel_id=1, source_target_pairs={{0,16},{4,20},{8,24},{12,28},{16,32},{20,36},{24,40},{28,44},{32,4... | collective-permute-start | bytes 786440 | tf_op jit(solution)/shard_map/ppermute | solution.py:14
  11.4 17.9 %collective-permute-done = bf16[2,512,512]{2,1,0:T(8,128)(2,1)S(1)} collective-permute-done((bf16[2,512,512]{2,1,0:T(8,128)(2,1)}, bf16[2,512,512]{2,1,0:T(8,128)(2,1)S(1)}, u32[]{:S(2)}, u32[]{:S(2)}) %collective-permute-start) | collective-permute-done | bytes 1048608 | tf_op jit(solution)/shard_map/ppermute | solution.py:70
  29.3 15.0 %collective-permute-start.1 = (bf16[2,512,512]{2,1,0:T(8,128)(2,1)S(1)}, bf16[2,512,512]{2,1,0:T(8,128)(2,1)S(1)}, u32[]{:S(2)}, u32[]{:S(2)}) collective-permute-start(bf16[2,512,512]{2,1,0:T(8,128)(2,1)S(1)} %collective-permute-done), channel_id=1, source_target_pairs={{0,1},{1,0},{2,3},{3,2},{4,5},{5,4},{6,7},{7,6},{8,9},{9,8},{10,11... | collective-permute-start | bytes 3145736 | tf_op jit(solution)/shard_map/ppermute | solution.py:71
  44.3 0.7 compare_select_fusion
  45.0 0.8 copy.10
  45.8 0.6 gather_fusion
  46.4 0.7 compare_and_fusion
  47.3 0.8 copy.12
  49.4 0.6 copy-done.9
  50.0 11.8 %collective-permute-start.7 = (bf16[8,128,128]{2,1,0:T(8,128)(2,1)S(1)}, bf16[8,128,128]{2,1,0:T(8,128)(2,1)S(1)}, u32[]{:S(2)}, u32[]{:S(2)}) collective-permute-start(bf16[8,128,128]{2,1,0:T(8,128)(2,1)S(1)} %copy-done.9), channel_id=1, source_target_pairs={{0,24},{4,28},{8,32},{12,36},{16,40},{20,44},{24,48},{28,52},{32,5... | collective-permute-start | bytes 786440 | tf_op jit(solution)/shard_map/ppermute | solution.py:14
  61.8 4.9 %collective-permute-start.8 = (bf16[8,128,128]{2,1,0:T(8,128)(2,1)S(1)}, bf16[8,128,128]{2,1,0:T(8,128)(2,1)S(1)}, u32[]{:S(2)}, u32[]{:S(2)}) collective-permute-start(bf16[8,128,128]{2,1,0:T(8,128)(2,1)S(1)} %copy-done.9), channel_id=1, source_target_pairs={{0,28},{4,32},{8,36},{12,40},{16,44},{20,48},{24,52},{28,56},{32,6... | collective-permute-start | bytes 786440 | tf_op jit(solution)/shard_map/ppermute | solution.py:14
  66.7 2.0 %collective-permute-start.9 = (bf16[8,128,128]{2,1,0:T(8,128)(2,1)S(1)}, bf16[8,128,128]{2,1,0:T(8,128)(2,1)S(1)}, u32[]{:S(2)}, u32[]{:S(2)}) collective-permute-start(bf16[8,128,128]{2,1,0:T(8,128)(2,1)S(1)} %copy-done.9), channel_id=1, source_target_pairs={{0,32},{4,36},{8,40},{12,44},{16,48},{20,52},{24,56},{28,60},{32,6... | collective-permute-start | bytes 786440 | tf_op jit(solution)/shard_map/ppermute | solution.py:14
  68.7 20.1 %shard_map.77.ham_ref = bf16[8,8,512,128]{3,2,1,0:T(8,128)(2,1)} custom-call(s32[256]{0:T(256)S(1)} %fusion.5.slot_ref, s32[1]{0:T(128)} %bitcast.1.band_ref, f32[256]{0:T(256)S(1)} %select_n.82.weight_ref, bf16[4,512,512]{2,1,0:T(8,128)(2,1)S(1)} %pad_maximum_fusion.halo_ref, bf16[2,512,512]{2,1,0:T(8,128)(2,1)S(1)} %copy-done, ...), custom_call_target="tpu_custom_call" | custom-call | flops 7516192768 | bytes 12582912 | tf_op jit(solution)/shard_map/pallas_call | solution.py:105
  88.9 0.6 copy-done.4
  89.8 0.7 copy-done.8
  90.5 8.9 %shard_map.78 = f32[8,512,128]{2,1,0:T(8,128)} custom-call(bf16[8,8,512,128]{3,2,1,0:T(8,128)(2,1)} %shard_map.77.ham_ref, bf16[8,128,128]{2,1,0:T(8,128)(2,1)} %copy-done.1, bf16[8,128,128]{2,1,0:T(8,128)(2,1)} %copy-done.2, bf16[8,128,128]{2,1,0:T(8,128)(2,1)} %copy-done.3, bf16[8,128,128]{2,1,0:T(8,128)(2,1)} %copy-done.4, ...), custom_call_target="tpu_custom_call" | custom-call | flops 1073741824 | bytes 8388608 | tf_op jit(solution)/shard_map/pallas_call | solution.py:117
  99.3 1.3 %fusion = bf16[8,2,128,128]{3,2,0,1:T(8,128)(2,1)S(1)} fusion(f32[8,2,2,128,128]{4,3,2,1,0:T(8,128)} %bitcast.16, s32[]{:T(128)S(6)} %select_n.84), kind=kLoop, calls=%fused_computation.5 | loop fusion | bytes 1048580 | tf_op jit(solution)/shard_map/convert_element_type | solution.py:135
  100.8 1.9 %collective-permute-done.10 = bf16[8,2,128,128]{3,2,0,1:T(8,128)(2,1)S(1)} collective-permute-done((bf16[8,2,128,128]{3,2,0,1:T(8,128)(2,1)S(1)}, bf16[8,2,128,128]{3,2,0,1:T(8,128)(2,1)S(1)}, u32[]{:S(2)}, u32[]{:S(2)}) %collective-permute-start.10) | collective-permute-done | bytes 524320 | tf_op jit(solution)/shard_map/ppermute | solution.py:135
  102.6 1.3 %bitcast_add_fusion = f32[8,2,128,128]{3,2,0,1:T(8,128)S(1)} fusion(bf16[8,2,128,128]{3,2,0,1:T(8,128)(2,1)S(1)} %collective-permute-done.10, f32[8,2,2,128,128]{4,3,2,1,0:T(8,128)} %bitcast.17, s32[]{:T(128)S(6)} %select_n.83), kind=kLoop, calls=%fused_computation.4 | loop fusion | flops 524288 | bytes 2621444 | tf_op jit(solution)/shard_map/add | solution.py:135
  104.1 8.3 %collective-permute-done.11 = bf16[8,128,128]{2,1,0:T(8,128)(2,1)S(1)} collective-permute-done((bf16[8,128,128]{2,1,0:T(8,128)(2,1)S(1)}, bf16[8,128,128]{2,1,0:T(8,128)(2,1)S(1)}, u32[]{:S(2)}, u32[]{:S(2)}) %collective-permute-start.11) | collective-permute-done | bytes 262176 | tf_op jit(solution)/shard_map/ppermute | solution.py:141
  112.5 0.8 fusion.1
  (41 shorter events, 2.1 us)
Async XLA Ops:
  0.6 28.7 %collective-permute-start = (bf16[2,512,512]{2,1,0:T(8,128)(2,1)}, bf16[2,512,512]{2,1,0:T(8,128)(2,1)S(1)}, u32[]{:S(2)}, u32[]{:S(2)}) collective-permute-start(bf16[2,512,512]{2,1,0:T(8,128)(2,1)} %local_ref.1), channel_id=1, source_target_pairs={{0,4},{1,125},{2,6},{3,127},{4,8},{5,1},{6,10},{7,3},{8,12},{9,5},... | collective-permute-start | bytes 3145736 | tf_op jit(solution)/shard_map/ppermute | solution.py:70
  3.0 46.4 %collective-permute-start.2 = (bf16[8,128,128]{2,1,0:T(8,128)(2,1)}, bf16[8,128,128]{2,1,0:T(8,128)(2,1)S(1)}, u32[]{:S(2)}, u32[]{:S(2)}) collective-permute-start(bf16[8,128,128]{2,1,0:T(8,128)(2,1)} %param.11), channel_id=1, source_target_pairs={{0,4},{4,8},{8,12},{12,16},{16,20},{20,24},{24,28},{28,32},{32,36}... | collective-permute-start | bytes 786440 | tf_op jit(solution)/shard_map/ppermute | solution.py:14
  5.3 56.5 %collective-permute-start.3 = (bf16[8,128,128]{2,1,0:T(8,128)(2,1)}, bf16[8,128,128]{2,1,0:T(8,128)(2,1)S(1)}, u32[]{:S(2)}, u32[]{:S(2)}) collective-permute-start(bf16[8,128,128]{2,1,0:T(8,128)(2,1)} %param.11), channel_id=1, source_target_pairs={{0,8},{4,12},{8,16},{12,20},{16,24},{20,28},{24,32},{28,36},{32,40... | collective-permute-start | bytes 786440 | tf_op jit(solution)/shard_map/ppermute | solution.py:14
  5.4 61.3 %collective-permute-start.4 = (bf16[8,128,128]{2,1,0:T(8,128)(2,1)}, bf16[8,128,128]{2,1,0:T(8,128)(2,1)S(1)}, u32[]{:S(2)}, u32[]{:S(2)}) collective-permute-start(bf16[8,128,128]{2,1,0:T(8,128)(2,1)} %param.11), channel_id=1, source_target_pairs={{0,12},{4,16},{8,20},{12,24},{16,28},{20,32},{24,36},{28,40},{32,4... | collective-permute-start | bytes 786440 | tf_op jit(solution)/shard_map/ppermute | solution.py:14
  9.1 79.7 %collective-permute-start.5 = (bf16[8,128,128]{2,1,0:T(8,128)(2,1)}, bf16[8,128,128]{2,1,0:T(8,128)(2,1)S(1)}, u32[]{:S(2)}, u32[]{:S(2)}) collective-permute-start(bf16[8,128,128]{2,1,0:T(8,128)(2,1)} %param.11), channel_id=1, source_target_pairs={{0,16},{4,20},{8,24},{12,28},{16,32},{20,36},{24,40},{28,44},{32,4... | collective-permute-start | bytes 786440 | tf_op jit(solution)/shard_map/ppermute | solution.py:14
  29.3 19.7 %collective-permute-start.1 = (bf16[2,512,512]{2,1,0:T(8,128)(2,1)S(1)}, bf16[2,512,512]{2,1,0:T(8,128)(2,1)S(1)}, u32[]{:S(2)}, u32[]{:S(2)}) collective-permute-start(bf16[2,512,512]{2,1,0:T(8,128)(2,1)S(1)} %collective-permute-done), channel_id=1, source_target_pairs={{0,1},{1,0},{2,3},{3,2},{4,5},{5,4},{6,7},{7,6},{8,9},{9,8},{10,11... | collective-permute-start | bytes 3145736 | tf_op jit(solution)/shard_map/ppermute | solution.py:71
  49.1 1.0 copy-start.9
  49.1 19.6 %copy-start = (bf16[2,512,512]{2,1,0:T(8,128)(2,1)S(1)}, bf16[2,512,512]{2,1,0:T(8,128)(2,1)}, u32[]{:S(2)}) copy-start(bf16[2,512,512]{2,1,0:T(8,128)(2,1)} %local_ref.1) | copy-start | bytes 3145732
  49.1 39.7 %collective-permute-start.6 = (bf16[8,128,128]{2,1,0:T(8,128)(2,1)}, bf16[8,128,128]{2,1,0:T(8,128)(2,1)S(1)}, u32[]{:S(2)}, u32[]{:S(2)}) collective-permute-start(bf16[8,128,128]{2,1,0:T(8,128)(2,1)} %param.11), channel_id=1, source_target_pairs={{0,20},{4,24},{8,28},{12,32},{16,36},{20,40},{24,44},{28,48},{32,5... | collective-permute-start | bytes 786440 | tf_op jit(solution)/shard_map/ppermute | solution.py:14
  50.0 38.7 %copy-start.1 = (bf16[8,128,128]{2,1,0:T(8,128)(2,1)}, bf16[8,128,128]{2,1,0:T(8,128)(2,1)S(1)}, u32[]{:S(2)}) copy-start(bf16[8,128,128]{2,1,0:T(8,128)(2,1)S(1)} %collective-permute-done.2.refs_0_) | copy-start | bytes 786436
  50.0 38.8 %collective-permute-start.7 = (bf16[8,128,128]{2,1,0:T(8,128)(2,1)S(1)}, bf16[8,128,128]{2,1,0:T(8,128)(2,1)S(1)}, u32[]{:S(2)}, u32[]{:S(2)}) collective-permute-start(bf16[8,128,128]{2,1,0:T(8,128)(2,1)S(1)} %copy-done.9), channel_id=1, source_target_pairs={{0,24},{4,28},{8,32},{12,36},{16,40},{20,44},{24,48},{28,52},{32,5... | collective-permute-start | bytes 786440 | tf_op jit(solution)/shard_map/ppermute | solution.py:14
  61.8 27.0 %copy-start.2 = (bf16[8,128,128]{2,1,0:T(8,128)(2,1)}, bf16[8,128,128]{2,1,0:T(8,128)(2,1)S(1)}, u32[]{:S(2)}) copy-start(bf16[8,128,128]{2,1,0:T(8,128)(2,1)S(1)} %collective-permute-done.3.refs_1_) | copy-start | bytes 786436
  61.8 27.1 %collective-permute-start.8 = (bf16[8,128,128]{2,1,0:T(8,128)(2,1)S(1)}, bf16[8,128,128]{2,1,0:T(8,128)(2,1)S(1)}, u32[]{:S(2)}, u32[]{:S(2)}) collective-permute-start(bf16[8,128,128]{2,1,0:T(8,128)(2,1)S(1)} %copy-done.9), channel_id=1, source_target_pairs={{0,28},{4,32},{8,36},{12,40},{16,44},{20,48},{24,52},{28,56},{32,6... | collective-permute-start | bytes 786440 | tf_op jit(solution)/shard_map/ppermute | solution.py:14
  66.7 22.1 %copy-start.3 = (bf16[8,128,128]{2,1,0:T(8,128)(2,1)}, bf16[8,128,128]{2,1,0:T(8,128)(2,1)S(1)}, u32[]{:S(2)}) copy-start(bf16[8,128,128]{2,1,0:T(8,128)(2,1)S(1)} %collective-permute-done.4.refs_2_) | copy-start | bytes 786436
  66.7 22.1 %collective-permute-start.9 = (bf16[8,128,128]{2,1,0:T(8,128)(2,1)S(1)}, bf16[8,128,128]{2,1,0:T(8,128)(2,1)S(1)}, u32[]{:S(2)}, u32[]{:S(2)}) collective-permute-start(bf16[8,128,128]{2,1,0:T(8,128)(2,1)S(1)} %copy-done.9), channel_id=1, source_target_pairs={{0,32},{4,36},{8,40},{12,44},{16,48},{20,52},{24,56},{28,60},{32,6... | collective-permute-start | bytes 786440 | tf_op jit(solution)/shard_map/ppermute | solution.py:14
  88.8 0.7 copy-start.4
  88.8 0.8 copy-start.5
  88.8 0.8 copy-start.6
  88.9 0.9 copy-start.7
  89.8 0.7 copy-start.8
  100.7 2.0 %collective-permute-start.10 = (bf16[8,2,128,128]{3,2,0,1:T(8,128)(2,1)S(1)}, bf16[8,2,128,128]{3,2,0,1:T(8,128)(2,1)S(1)}, u32[]{:S(2)}, u32[]{:S(2)}) collective-permute-start(bf16[8,2,128,128]{3,2,0,1:T(8,128)(2,1)S(1)} %fusion), channel_id=1, source_target_pairs={{0,1},{1,0},{2,3},{3,2},{4,5},{5,4},{6,7},{7,6},{8,9},{9,8},{10,11... | collective-permute-start | bytes 1572872 | tf_op jit(solution)/shard_map/ppermute | solution.py:135
  104.0 8.4 %collective-permute-start.11 = (bf16[8,128,128]{2,1,0:T(8,128)(2,1)S(1)}, bf16[8,128,128]{2,1,0:T(8,128)(2,1)S(1)}, u32[]{:S(2)}, u32[]{:S(2)}) collective-permute-start(bf16[8,128,128]{2,1,0:T(8,128)(2,1)S(1)} %fusion.2), channel_id=1, source_target_pairs={{0,2},{1,3},{2,0},{3,1},{4,6},{5,7},{6,4},{7,5},{8,10},{9,11},{10,... | collective-permute-start | bytes 786440 | tf_op jit(solution)/shard_map/ppermute | solution.py:141

commit v6 on v5

--- a/solution.py
+++ b/solution.py
@@ -66,7 +66,7 @@
     for i in range(cycle_length):
         for b in range(band_count):
             target = (i + 1) % cycle_length if b % 2 == 0 else (i - 1) % cycle_length
-            pairs.append((i * band_count + b, target * band_count + b))
+            pairs.append((i * band_count + b, target * band_count + (b ^ 2)))
     near = lax.ppermute(coarse_kernel, ("blk", "band"), pairs)
     far = lax.ppermute(near, "band", [(b, b ^ 1) for b in range(band_count)])
     halo = jnp.concatenate([near, far], axis=0)

time: 114 us -> 118 us (1.035)
  the two profiles are of different devices: /device:TPU:74 before, /device:TPU:64 now
where the time goes in v6:
time: 118 us; the launch traced here: 117 us
  starting transfers between devices  40.7 us (34%)
  waiting for transfers between devices  36 us (31%)
  Pallas kernels  29 us (25%)
  local copies, waits for them, and re-layouts  6.81 us (6%)
  other arithmetic  3.78 us (3%)
    ppermute x1, waiting for transfers between devices, on_device(): near = lax.ppermute(coarse_kernel, ('blk', 'band'), pairs)  25.8 us
    ppermute x8, starting transfers between devices, shifted(): return lax.ppermute(value, axis, pairs)  20.5 us
    pallas_call x1, Pallas kernels, on_device(): pl.pallas_call(kernel, grid_spec=grid_spec, out_shape=jax.ShapeDtypeStruc...  20.1 us
    ppermute x1, starting transfers between devices, on_device(): far = lax.ppermute(near, 'band', [(b, b ^ 1) for b in range(band_count)])  17 us
    ppermute x2, waiting for transfers between devices, on_device(): lax.ppermute(send.astype(jnp.bfloat16), 'band', swap).astype(jnp.float32)  10.2 us
    pallas_call x1, Pallas kernels, on_device(): pl.pallas_call(functools.partial(product_kernel, stop_count=stop_count),...  8.88 us
    unnamed x22, local copies, waits for them, and re-layouts  3.83 us
    ppermute x1, starting transfers between devices, on_device(): near = lax.ppermute(coarse_kernel, ('blk', 'band'), pairs)  3.08 us
  transfers between devices with their start and end apart: 12, of which 3 were waited for; matrix products, arithmetic and copies ran while one was open for 4% of the time, Pallas kernels for 17%

profile of v6, /device:TPU:64, one launch (start us, length us, event | category | flops | bytes accessed | tf_op | source)
XLA Modules:
  0.0 117.1 jit_solution(16511434533815288314)
XLA Ops:
  0.6 3.1 %collective-permute-start = (bf16[2,512,512]{2,1,0:T(8,128)(2,1)}, bf16[2,512,512]{2,1,0:T(8,128)(2,1)S(1)}, u32[]{:S(2)}, u32[]{:S(2)}) collective-permute-start(bf16[2,512,512]{2,1,0:T(8,128)(2,1)} %local_ref.1), channel_id=1, source_target_pairs={{0,6},{1,127},{2,4},{3,125},{4,10},{5,3},{6,8},{7,1},{8,14},{9,7},... | collective-permute-start | bytes 3145736 | tf_op jit(solution)/shard_map/ppermute | solution.py:70
  3.7 1.7 %collective-permute-start.2 = (bf16[8,128,128]{2,1,0:T(8,128)(2,1)}, bf16[8,128,128]{2,1,0:T(8,128)(2,1)S(1)}, u32[]{:S(2)}, u32[]{:S(2)}) collective-permute-start(bf16[8,128,128]{2,1,0:T(8,128)(2,1)} %param.11), channel_id=1, source_target_pairs={{0,4},{4,8},{8,12},{12,16},{16,20},{20,24},{24,28},{28,32},{32,36}... | collective-permute-start | bytes 786440 | tf_op jit(solution)/shard_map/ppermute | solution.py:14
  5.6 4.2 %collective-permute-start.4 = (bf16[8,128,128]{2,1,0:T(8,128)(2,1)}, bf16[8,128,128]{2,1,0:T(8,128)(2,1)S(1)}, u32[]{:S(2)}, u32[]{:S(2)}) collective-permute-start(bf16[8,128,128]{2,1,0:T(8,128)(2,1)} %param.11), channel_id=1, source_target_pairs={{0,12},{4,16},{8,20},{12,24},{16,28},{20,32},{24,36},{28,40},{32,4... | collective-permute-start | bytes 786440 | tf_op jit(solution)/shard_map/ppermute | solution.py:14
  9.8 2.4 %collective-permute-start.5 = (bf16[8,128,128]{2,1,0:T(8,128)(2,1)}, bf16[8,128,128]{2,1,0:T(8,128)(2,1)S(1)}, u32[]{:S(2)}, u32[]{:S(2)}) collective-permute-start(bf16[8,128,128]{2,1,0:T(8,128)(2,1)} %param.11), channel_id=1, source_target_pairs={{0,16},{4,20},{8,24},{12,28},{16,32},{20,36},{24,40},{28,44},{32,4... | collective-permute-start | bytes 786440 | tf_op jit(solution)/shard_map/ppermute | solution.py:14
  12.2 25.8 %collective-permute-done = bf16[2,512,512]{2,1,0:T(8,128)(2,1)S(1)} collective-permute-done((bf16[2,512,512]{2,1,0:T(8,128)(2,1)}, bf16[2,512,512]{2,1,0:T(8,128)(2,1)S(1)}, u32[]{:S(2)}, u32[]{:S(2)}) %collective-permute-start) | collective-permute-done | bytes 1048608 | tf_op jit(solution)/shard_map/ppermute | solution.py:70
  37.9 17.0 %collective-permute-start.1 = (bf16[2,512,512]{2,1,0:T(8,128)(2,1)S(1)}, bf16[2,512,512]{2,1,0:T(8,128)(2,1)S(1)}, u32[]{:S(2)}, u32[]{:S(2)}) collective-permute-start(bf16[2,512,512]{2,1,0:T(8,128)(2,1)S(1)} %collective-permute-done), channel_id=1, source_target_pairs={{0,1},{1,0},{2,3},{3,2},{4,5},{5,4},{6,7},{7,6},{8,9},{9,8},{10,11... | collective-permute-start | bytes 3145736 | tf_op jit(solution)/shard_map/ppermute | solution.py:71
  54.9 0.7 compare_select_fusion
  55.6 0.8 copy.10
  56.4 0.6 gather_fusion
  57.0 0.7 compare_and_fusion
  57.9 0.8 copy.12
  58.7 0.6 gather_fusion.1
  60.0 0.6 copy-done.9
  60.6 11.0 %collective-permute-start.8 = (bf16[8,128,128]{2,1,0:T(8,128)(2,1)S(1)}, bf16[8,128,128]{2,1,0:T(8,128)(2,1)S(1)}, u32[]{:S(2)}, u32[]{:S(2)}) collective-permute-start(bf16[8,128,128]{2,1,0:T(8,128)(2,1)S(1)} %copy-done.9), channel_id=1, source_target_pairs={{0,28},{4,32},{8,36},{12,40},{16,44},{20,48},{24,52},{28,56},{32,6... | collective-permute-start | bytes 786440 | tf_op jit(solution)/shard_map/ppermute | solution.py:14
  71.6 1.0 collective-permute-start.9
  72.6 20.1 %shard_map.77.ham_ref = bf16[8,8,512,128]{3,2,1,0:T(8,128)(2,1)} custom-call(s32[256]{0:T(256)S(1)} %fusion.5.slot_ref, s32[1]{0:T(128)} %bitcast.1.band_ref, f32[256]{0:T(256)S(1)} %select_n.82.weight_ref, bf16[4,512,512]{2,1,0:T(8,128)(2,1)S(1)} %pad_maximum_fusion.halo_ref, bf16[2,512,512]{2,1,0:T(8,128)(2,1)S(1)} %copy-done, ...), custom_call_target="tpu_custom_call" | custom-call | flops 7516192768 | bytes 12582912 | tf_op jit(solution)/shard_map/pallas_call | solution.py:105
  92.8 0.6 copy-done.4
  93.7 0.7 copy-done.8
  94.4 8.9 %shard_map.78 = f32[8,512,128]{2,1,0:T(8,128)} custom-call(bf16[8,8,512,128]{3,2,1,0:T(8,128)(2,1)} %shard_map.77.ham_ref, bf16[8,128,128]{2,1,0:T(8,128)(2,1)} %copy-done.1, bf16[8,128,128]{2,1,0:T(8,128)(2,1)} %copy-done.2, bf16[8,128,128]{2,1,0:T(8,128)(2,1)} %copy-done.3, bf16[8,128,128]{2,1,0:T(8,128)(2,1)} %copy-done.4, ...), custom_call_target="tpu_custom_call" | custom-call | flops 1073741824 | bytes 8388608 | tf_op jit(solution)/shard_map/pallas_call | solution.py:117
  103.2 1.3 %fusion = bf16[8,2,128,128]{3,2,0,1:T(8,128)(2,1)S(1)} fusion(f32[8,2,2,128,128]{4,3,2,1,0:T(8,128)} %bitcast.16, s32[]{:T(128)S(6)} %select_n.84), kind=kLoop, calls=%fused_computation.5 | loop fusion | bytes 1048580 | tf_op jit(solution)/shard_map/convert_element_type | solution.py:135
  104.7 1.9 %collective-permute-done.10 = bf16[8,2,128,128]{3,2,0,1:T(8,128)(2,1)S(1)} collective-permute-done((bf16[8,2,128,128]{3,2,0,1:T(8,128)(2,1)S(1)}, bf16[8,2,128,128]{3,2,0,1:T(8,128)(2,1)S(1)}, u32[]{:S(2)}, u32[]{:S(2)}) %collective-permute-start.10) | collective-permute-done | bytes 524320 | tf_op jit(solution)/shard_map/ppermute | solution.py:135
  106.5 1.3 %bitcast_add_fusion = f32[8,2,128,128]{3,2,0,1:T(8,128)S(1)} fusion(bf16[8,2,128,128]{3,2,0,1:T(8,128)(2,1)S(1)} %collective-permute-done.10, f32[8,2,2,128,128]{4,3,2,1,0:T(8,128)} %bitcast.17, s32[]{:T(128)S(6)} %select_n.83), kind=kLoop, calls=%fused_computation.4 | loop fusion | flops 524288 | bytes 2621444 | tf_op jit(solution)/shard_map/add | solution.py:135
  108.0 8.3 %collective-permute-done.11 = bf16[8,128,128]{2,1,0:T(8,128)(2,1)S(1)} collective-permute-done((bf16[8,128,128]{2,1,0:T(8,128)(2,1)S(1)}, bf16[8,128,128]{2,1,0:T(8,128)(2,1)S(1)}, u32[]{:S(2)}, u32[]{:S(2)}) %collective-permute-start.11) | collective-permute-done | bytes 262176 | tf_op jit(solution)/shard_map/ppermute | solution.py:141
  116.4 0.8 fusion.1
  (41 shorter events, 1.6 us)
Async XLA Ops:
  0.6 37.3 %collective-permute-start = (bf16[2,512,512]{2,1,0:T(8,128)(2,1)}, bf16[2,512,512]{2,1,0:T(8,128)(2,1)S(1)}, u32[]{:S(2)}, u32[]{:S(2)}) collective-permute-start(bf16[2,512,512]{2,1,0:T(8,128)(2,1)} %local_ref.1), channel_id=1, source_target_pairs={{0,6},{1,127},{2,4},{3,125},{4,10},{5,3},{6,8},{7,1},{8,14},{9,7},... | collective-permute-start | bytes 3145736 | tf_op jit(solution)/shard_map/ppermute | solution.py:70
  3.7 56.3 %collective-permute-start.2 = (bf16[8,128,128]{2,1,0:T(8,128)(2,1)}, bf16[8,128,128]{2,1,0:T(8,128)(2,1)S(1)}, u32[]{:S(2)}, u32[]{:S(2)}) collective-permute-start(bf16[8,128,128]{2,1,0:T(8,128)(2,1)} %param.11), channel_id=1, source_target_pairs={{0,4},{4,8},{8,12},{12,16},{16,20},{20,24},{24,28},{28,32},{32,36}... | collective-permute-start | bytes 786440 | tf_op jit(solution)/shard_map/ppermute | solution.py:14
  5.4 55.2 %collective-permute-start.3 = (bf16[8,128,128]{2,1,0:T(8,128)(2,1)}, bf16[8,128,128]{2,1,0:T(8,128)(2,1)S(1)}, u32[]{:S(2)}, u32[]{:S(2)}) collective-permute-start(bf16[8,128,128]{2,1,0:T(8,128)(2,1)} %param.11), channel_id=1, source_target_pairs={{0,8},{4,12},{8,16},{12,20},{16,24},{20,28},{24,32},{28,36},{32,40... | collective-permute-start | bytes 786440 | tf_op jit(solution)/shard_map/ppermute | solution.py:14
  5.6 66.0 %collective-permute-start.4 = (bf16[8,128,128]{2,1,0:T(8,128)(2,1)}, bf16[8,128,128]{2,1,0:T(8,128)(2,1)S(1)}, u32[]{:S(2)}, u32[]{:S(2)}) collective-permute-start(bf16[8,128,128]{2,1,0:T(8,128)(2,1)} %param.11), channel_id=1, source_target_pairs={{0,12},{4,16},{8,20},{12,24},{16,28},{20,32},{24,36},{28,40},{32,4... | collective-permute-start | bytes 786440 | tf_op jit(solution)/shard_map/ppermute | solution.py:14
  9.8 82.9 %collective-permute-start.5 = (bf16[8,128,128]{2,1,0:T(8,128)(2,1)}, bf16[8,128,128]{2,1,0:T(8,128)(2,1)S(1)}, u32[]{:S(2)}, u32[]{:S(2)}) collective-permute-start(bf16[8,128,128]{2,1,0:T(8,128)(2,1)} %param.11), channel_id=1, source_target_pairs={{0,16},{4,20},{8,24},{12,28},{16,32},{20,36},{24,40},{28,44},{32,4... | collective-permute-start | bytes 786440 | tf_op jit(solution)/shard_map/ppermute | solution.py:14
  37.9 21.8 %collective-permute-start.1 = (bf16[2,512,512]{2,1,0:T(8,128)(2,1)S(1)}, bf16[2,512,512]{2,1,0:T(8,128)(2,1)S(1)}, u32[]{:S(2)}, u32[]{:S(2)}) collective-permute-start(bf16[2,512,512]{2,1,0:T(8,128)(2,1)S(1)} %collective-permute-done), channel_id=1, source_target_pairs={{0,1},{1,0},{2,3},{3,2},{4,5},{5,4},{6,7},{7,6},{8,9},{9,8},{10,11... | collective-permute-start | bytes 3145736 | tf_op jit(solution)/shard_map/ppermute | solution.py:71
  59.7 1.0 copy-start.9
  59.7 12.9 %copy-start = (bf16[2,512,512]{2,1,0:T(8,128)(2,1)S(1)}, bf16[2,512,512]{2,1,0:T(8,128)(2,1)}, u32[]{:S(2)}) copy-start(bf16[2,512,512]{2,1,0:T(8,128)(2,1)} %local_ref.1) | copy-start | bytes 3145732
  59.7 33.0 %collective-permute-start.6 = (bf16[8,128,128]{2,1,0:T(8,128)(2,1)}, bf16[8,128,128]{2,1,0:T(8,128)(2,1)S(1)}, u32[]{:S(2)}, u32[]{:S(2)}) collective-permute-start(bf16[8,128,128]{2,1,0:T(8,128)(2,1)} %param.11), channel_id=1, source_target_pairs={{0,20},{4,24},{8,28},{12,32},{16,36},{20,40},{24,44},{28,48},{32,5... | collective-permute-start | bytes 786440 | tf_op jit(solution)/shard_map/ppermute | solution.py:14
  60.6 32.0 %copy-start.1 = (bf16[8,128,128]{2,1,0:T(8,128)(2,1)}, bf16[8,128,128]{2,1,0:T(8,128)(2,1)S(1)}, u32[]{:S(2)}) copy-start(bf16[8,128,128]{2,1,0:T(8,128)(2,1)S(1)} %collective-permute-done.2.refs_0_) | copy-start | bytes 786436
  60.6 32.1 %collective-permute-start.7 = (bf16[8,128,128]{2,1,0:T(8,128)(2,1)S(1)}, bf16[8,128,128]{2,1,0:T(8,128)(2,1)S(1)}, u32[]{:S(2)}, u32[]{:S(2)}) collective-permute-start(bf16[8,128,128]{2,1,0:T(8,128)(2,1)S(1)} %copy-done.9), channel_id=1, source_target_pairs={{0,24},{4,28},{8,32},{12,36},{16,40},{20,44},{24,48},{28,52},{32,5... | collective-permute-start | bytes 786440 | tf_op jit(solution)/shard_map/ppermute | solution.py:14
  60.6 32.0 %copy-start.2 = (bf16[8,128,128]{2,1,0:T(8,128)(2,1)}, bf16[8,128,128]{2,1,0:T(8,128)(2,1)S(1)}, u32[]{:S(2)}) copy-start(bf16[8,128,128]{2,1,0:T(8,128)(2,1)S(1)} %collective-permute-done.3.refs_1_) | copy-start | bytes 786436
  60.6 32.1 %collective-permute-start.8 = (bf16[8,128,128]{2,1,0:T(8,128)(2,1)S(1)}, bf16[8,128,128]{2,1,0:T(8,128)(2,1)S(1)}, u32[]{:S(2)}, u32[]{:S(2)}) collective-permute-start(bf16[8,128,128]{2,1,0:T(8,128)(2,1)S(1)} %copy-done.9), channel_id=1, source_target_pairs={{0,28},{4,32},{8,36},{12,40},{16,44},{20,48},{24,52},{28,56},{32,6... | collective-permute-start | bytes 786440 | tf_op jit(solution)/shard_map/ppermute | solution.py:14
  71.6 21.1 %copy-start.3 = (bf16[8,128,128]{2,1,0:T(8,128)(2,1)}, bf16[8,128,128]{2,1,0:T(8,128)(2,1)S(1)}, u32[]{:S(2)}) copy-start(bf16[8,128,128]{2,1,0:T(8,128)(2,1)S(1)} %collective-permute-done.4.refs_2_) | copy-start | bytes 786436
  71.6 21.2 %collective-permute-start.9 = (bf16[8,128,128]{2,1,0:T(8,128)(2,1)S(1)}, bf16[8,128,128]{2,1,0:T(8,128)(2,1)S(1)}, u32[]{:S(2)}, u32[]{:S(2)}) collective-permute-start(bf16[8,128,128]{2,1,0:T(8,128)(2,1)S(1)} %copy-done.9), channel_id=1, source_target_pairs={{0,32},{4,36},{8,40},{12,44},{16,48},{20,52},{24,56},{28,60},{32,6... | collective-permute-start | bytes 786440 | tf_op jit(solution)/shard_map/ppermute | solution.py:14
  92.7 0.7 copy-start.4
  92.7 0.8 copy-start.5
  92.7 0.8 copy-start.6
  92.8 0.9 copy-start.7
  93.7 0.7 copy-start.8
  104.6 2.0 %collective-permute-start.10 = (bf16[8,2,128,128]{3,2,0,1:T(8,128)(2,1)S(1)}, bf16[8,2,128,128]{3,2,0,1:T(8,128)(2,1)S(1)}, u32[]{:S(2)}, u32[]{:S(2)}) collective-permute-start(bf16[8,2,128,128]{3,2,0,1:T(8,128)(2,1)S(1)} %fusion), channel_id=1, source_target_pairs={{0,1},{1,0},{2,3},{3,2},{4,5},{5,4},{6,7},{7,6},{8,9},{9,8},{10,11... | collective-permute-start | bytes 1572872 | tf_op jit(solution)/shard_map/ppermute | solution.py:135
  107.9 8.4 %collective-permute-start.11 = (bf16[8,128,128]{2,1,0:T(8,128)(2,1)S(1)}, bf16[8,128,128]{2,1,0:T(8,128)(2,1)S(1)}, u32[]{:S(2)}, u32[]{:S(2)}) collective-permute-start(bf16[8,128,128]{2,1,0:T(8,128)(2,1)S(1)} %fusion.2), channel_id=1, source_target_pairs={{0,2},{1,3},{2,0},{3,1},{4,6},{5,7},{6,4},{7,5},{8,10},{9,11},{10,... | collective-permute-start | bytes 786440 | tf_op jit(solution)/shard_map/ppermute | solution.py:141

commit v7 on v5

--- a/solution.py
+++ b/solution.py
@@ -70,7 +70,12 @@
     near = lax.ppermute(coarse_kernel, ("blk", "band"), pairs)
     far = lax.ppermute(near, "band", [(b, b ^ 1) for b in range(band_count)])
     halo = jnp.concatenate([near, far], axis=0)
-    sources = [shifted(trial_vectors, "blk", station + 1) for station in range(stop_count)]
+    assert stop_count == 8
+    first = shifted(trial_vectors, "blk", 1)
+    last = shifted(trial_vectors, "blk", 8)
+    second = shifted(jnp.stack([trial_vectors, first]), "blk", 2)
+    third = shifted(jnp.stack([trial_vectors, first, second[0], second[1]]), "blk", 4)
+    sources = [first, second[0], second[1], third[0], third[1], third[2], third[3], last]
 
     order_index = jnp.take(interp_index, stop_order, axis=1)
     order_weight = jnp.take(interp_weight, stop_order, axis=1)

time: 114 us -> 112 us (0.982)
  the two profiles are of different devices: /device:TPU:74 before, /device:TPU:1 now
where the time goes in v7:
time: 112 us
  waiting for transfers between devices  44.9 us (40%)
  Pallas kernels  29 us (26%)
  starting transfers between devices  23.6 us (21%)
  other arithmetic  6.9 us (6%)
  local copies, waits for them, and re-layouts  6.48 us (6%)
    ppermute x4, waiting for transfers between devices, shifted(): return lax.ppermute(value, axis, pairs)  37.2 us
    pallas_call x1, Pallas kernels, on_device(): pl.pallas_call(kernel, grid_spec=grid_spec, out_shape=jax.ShapeDtypeStruc...  20.1 us
    pallas_call x1, Pallas kernels, on_device(): pl.pallas_call(functools.partial(product_kernel, stop_count=stop_count),...  8.91 us
    ppermute x4, starting transfers between devices, shifted(): return lax.ppermute(value, axis, pairs)  8.21 us
    ppermute x2, waiting for transfers between devices, on_device(): lax.ppermute(send.astype(jnp.bfloat16), 'band', swap).astype(jnp.float32)  7.73 us
    ppermute x2, starting transfers between devices, on_device(): lax.ppermute(send.astype(jnp.bfloat16), 'band', swap).astype(jnp.float32)  7.23 us
    ppermute x1, starting transfers between devices, on_device(): near = lax.ppermute(coarse_kernel, ('blk', 'band'), pairs)  5.75 us
    ppermute x1, starting transfers between devices, on_device(): far = lax.ppermute(near, 'band', [(b, b ^ 1) for b in range(band_count)])  2.37 us
  transfers between devices with their start and end apart: 8, of which 5 were waited for; matrix products, arithmetic and copies ran while one was open for 8% of the time, Pallas kernels for 18%

profile of v7, /device:TPU:1, one launch (start us, length us, event | category | flops | bytes accessed | tf_op | source)
XLA Modules:
  0.0 111.6 jit_solution(7494944883537549086)
XLA Ops:
  0.7 3.8 %collective-permute-start.2 = (bf16[8,128,128]{2,1,0:T(8,128)(2,1)}, bf16[8,128,128]{2,1,0:T(8,128)(2,1)S(1)}, u32[]{:S(2)}, u32[]{:S(2)}) collective-permute-start(bf16[8,128,128]{2,1,0:T(8,128)(2,1)} %param.11), channel_id=1, source_target_pairs={{0,4},{4,8},{8,12},{12,16},{16,20},{20,24},{24,28},{28,32},{32,36}... | collective-permute-start | bytes 786440 | tf_op jit(solution)/shard_map/ppermute | solution.py:14
  4.5 5.8 %collective-permute-start = (bf16[2,512,512]{2,1,0:T(8,128)(2,1)}, bf16[2,512,512]{2,1,0:T(8,128)(2,1)}, u32[]{:S(2)}, u32[]{:S(2)}) collective-permute-start(bf16[2,512,512]{2,1,0:T(8,128)(2,1)} %local_ref.1), channel_id=1, source_target_pairs={{0,4},{1,125},{2,6},{3,127},{4,8},{5,1},{6,10},{7,3},{8,12},{9,5},... | collective-permute-start | bytes 3145736 | tf_op jit(solution)/shard_map/ppermute | solution.py:70
  10.2 6.2 %collective-permute-done.2.refs_0_ = bf16[8,128,128]{2,1,0:T(8,128)(2,1)S(1)} collective-permute-done((bf16[8,128,128]{2,1,0:T(8,128)(2,1)}, bf16[8,128,128]{2,1,0:T(8,128)(2,1)S(1)}, u32[]{:S(2)}, u32[]{:S(2)}) %collective-permute-start.2) | collective-permute-done | bytes 262176 | tf_op jit(solution)/shard_map/ppermute | solution.py:14
  16.4 1.1 pad_maximum_fusion.2
  17.7 0.8 copy.10
  18.5 0.7 compare_select_fusion
  19.7 15.0 %collective-permute-done.3 = bf16[2,8,128,128]{3,2,1,0:T(8,128)(2,1)S(1)} collective-permute-done((bf16[2,8,128,128]{3,2,1,0:T(8,128)(2,1)S(1)}, bf16[2,8,128,128]{3,2,1,0:T(8,128)(2,1)S(1)}, u32[]{:S(2)}, u32[]{:S(2)}) %collective-permute-start.3) | collective-permute-done | bytes 524320 | tf_op jit(solution)/shard_map/ppermute | solution.py:14
  34.7 1.1 pad_maximum_fusion.1
  35.8 4.3 %collective-permute-start.4 = (bf16[4,8,128,128]{3,2,1,0:T(8,128)(2,1)S(1)}, bf16[4,8,128,128]{3,2,1,0:T(8,128)(2,1)S(1)}, u32[]{:S(2)}, u32[]{:S(2)}) collective-permute-start(bf16[4,8,128,128]{3,2,1,0:T(8,128)(2,1)S(1)} %pad_maximum_fusion.1), channel_id=1, source_target_pairs={{0,16},{4,20},{8,24},{12,28},{16,32},{20,36},{24,40},{28,44},{32,4... | collective-permute-start | bytes 3145736 | tf_op jit(solution)/shard_map/ppermute | solution.py:14
  40.1 2.4 %collective-permute-start.1 = (bf16[2,512,512]{2,1,0:T(8,128)(2,1)}, bf16[2,512,512]{2,1,0:T(8,128)(2,1)}, u32[]{:S(2)}, u32[]{:S(2)}) collective-permute-start(bf16[2,512,512]{2,1,0:T(8,128)(2,1)} %collective-permute-done), channel_id=1, source_target_pairs={{0,1},{1,0},{2,3},{3,2},{4,5},{5,4},{6,7},{7,6},{8,9},{9,8},{10,11... | collective-permute-start | bytes 3145736 | tf_op jit(solution)/shard_map/ppermute | solution.py:71
  43.8 0.8 slice_bitcast_fusion.4
  44.6 16.0 %collective-permute-done.4 = bf16[4,8,128,128]{3,2,1,0:T(8,128)(2,1)S(1)} collective-permute-done((bf16[4,8,128,128]{3,2,1,0:T(8,128)(2,1)S(1)}, bf16[4,8,128,128]{3,2,1,0:T(8,128)(2,1)S(1)}, u32[]{:S(2)}, u32[]{:S(2)}) %collective-permute-start.4) | collective-permute-done | bytes 1048608 | tf_op jit(solution)/shard_map/ppermute | solution.py:14
  60.6 1.0 slice_bitcast_fusion
  61.6 1.8 %pad_maximum_fusion.halo_ref = bf16[4,512,512]{2,1,0:T(8,128)(2,1)S(1)} fusion(bf16[2,512,512]{2,1,0:T(8,128)(2,1)} %collective-permute-done.1, bf16[2,512,512]{2,1,0:T(8,128)(2,1)} %collective-permute-done), kind=kLoop, calls=%fused_computation.2 | loop fusion | flops 1048576 | bytes 4194304 | tf_op jit(solution)/shard_map/concatenate | solution.py:72
  63.4 20.1 %shard_map.77.ham_ref = bf16[8,8,512,128]{3,2,1,0:T(8,128)(2,1)} custom-call(s32[256]{0:T(256)S(1)} %fusion.5.slot_ref, s32[1]{0:T(128)} %bitcast.1.band_ref, f32[256]{0:T(256)S(1)} %select_n.82.weight_ref, bf16[4,512,512]{2,1,0:T(8,128)(2,1)S(1)} %pad_maximum_fusion.halo_ref, bf16[2,512,512]{2,1,0:T(8,128)(2,1)S(1)} %copy-done, ...), custom_call_target="tpu_custom_call" | custom-call | flops 7516192768 | bytes 12582912 | tf_op jit(solution)/shard_map/pallas_call | solution.py:110
  83.6 0.7 copy-done.2
  84.3 8.9 %shard_map.78 = f32[8,512,128]{2,1,0:T(8,128)} custom-call(bf16[8,8,512,128]{3,2,1,0:T(8,128)(2,1)} %shard_map.77.ham_ref, bf16[8,128,128]{2,1,0:T(8,128)(2,1)} %copy-done.1, bf16[8,128,128]{2,1,0:T(8,128)(2,1)} %get-tuple-element.7.refs_1_, bf16[8,128,128]{2,1,0:T(8,128)(2,1)} %get-tuple-element.6.refs_2_, bf16[8,128,128]{2,1,0:T(8,128)(2,1)} %get-tuple-element.5.refs_3_, ...), custom_call_target="tpu_custom_call" | custom-call | flops 1073741824 | bytes 8388608 | tf_op jit(solution)/shard_map/pallas_call | solution.py:122
  93.2 1.3 %fusion = bf16[8,2,128,128]{3,2,0,1:T(8,128)(2,1)S(1)} fusion(f32[8,2,2,128,128]{4,3,2,1,0:T(8,128)} %bitcast.30, s32[]{:T(128)S(6)} %select_n.84), kind=kLoop, calls=%fused_computation.6 | loop fusion | bytes 1048580 | tf_op jit(solution)/shard_map/convert_element_type | solution.py:140
  94.5 5.8 %collective-permute-start.6 = (bf16[8,2,128,128]{3,2,0,1:T(8,128)(2,1)S(1)}, bf16[8,2,128,128]{3,2,0,1:T(8,128)(2,1)S(1)}, u32[]{:S(2)}, u32[]{:S(2)}) collective-permute-start(bf16[8,2,128,128]{3,2,0,1:T(8,128)(2,1)S(1)} %fusion), channel_id=1, source_target_pairs={{0,1},{1,0},{2,3},{3,2},{4,5},{5,4},{6,7},{7,6},{8,9},{9,8},{10,11... | collective-permute-start | bytes 1572872 | tf_op jit(solution)/shard_map/ppermute | solution.py:140
  100.4 1.5 %collective-permute-done.6 = bf16[8,2,128,128]{3,2,0,1:T(8,128)(2,1)S(1)} collective-permute-done((bf16[8,2,128,128]{3,2,0,1:T(8,128)(2,1)S(1)}, bf16[8,2,128,128]{3,2,0,1:T(8,128)(2,1)S(1)}, u32[]{:S(2)}, u32[]{:S(2)}) %collective-permute-start.6) | collective-permute-done | bytes 524320 | tf_op jit(solution)/shard_map/ppermute | solution.py:140
  101.9 1.3 %bitcast_add_fusion = f32[8,2,128,128]{3,2,0,1:T(8,128)S(1)} fusion(bf16[8,2,128,128]{3,2,0,1:T(8,128)(2,1)S(1)} %collective-permute-done.6, f32[8,2,2,128,128]{4,3,2,1,0:T(8,128)} %bitcast.31, s32[]{:T(128)S(6)} %select_n.83), kind=kLoop, calls=%fused_computation.5 | loop fusion | flops 524288 | bytes 2621444 | tf_op jit(solution)/shard_map/add | solution.py:140
  103.3 1.4 %collective-permute-start.7 = (bf16[8,128,128]{2,1,0:T(8,128)(2,1)S(1)}, bf16[8,128,128]{2,1,0:T(8,128)(2,1)S(1)}, u32[]{:S(2)}, u32[]{:S(2)}) collective-permute-start(bf16[8,128,128]{2,1,0:T(8,128)(2,1)S(1)} %fusion.2), channel_id=1, source_target_pairs={{0,2},{1,3},{2,0},{3,1},{4,6},{5,7},{6,4},{7,5},{8,10},{9,11},{10,... | collective-permute-start | bytes 786440 | tf_op jit(solution)/shard_map/ppermute | solution.py:146
  104.7 6.2 %collective-permute-done.7 = bf16[8,128,128]{2,1,0:T(8,128)(2,1)S(1)} collective-permute-done((bf16[8,128,128]{2,1,0:T(8,128)(2,1)S(1)}, bf16[8,128,128]{2,1,0:T(8,128)(2,1)S(1)}, u32[]{:S(2)}, u32[]{:S(2)}) %collective-permute-start.7) | collective-permute-done | bytes 262176 | tf_op jit(solution)/shard_map/ppermute | solution.py:146
  110.9 0.8 fusion.1
  (27 shorter events, 2.2 us)
Async XLA Ops:
  0.6 39.4 %copy-start.4 = (s32[8]{0:T(128)S(1)}, s32[8]{0:T(128)}, u32[]{:S(2)}) copy-start(s32[8]{0:T(128)} %param.9) | copy-start | bytes 100
  0.6 42.1 %copy-start.3 = (f32[8,8,4]{1,2,0:T(4,128)S(1)}, f32[8,8,4]{1,2,0:T(4,128)}, u32[]{:S(2)}) copy-start(f32[8,8,4]{1,2,0:T(4,128)} %param.8) | copy-start | bytes 3076
  0.7 15.7 %collective-permute-start.2 = (bf16[8,128,128]{2,1,0:T(8,128)(2,1)}, bf16[8,128,128]{2,1,0:T(8,128)(2,1)S(1)}, u32[]{:S(2)}, u32[]{:S(2)}) collective-permute-start(bf16[8,128,128]{2,1,0:T(8,128)(2,1)} %param.11), channel_id=1, source_target_pairs={{0,4},{4,8},{8,12},{12,16},{16,20},{20,24},{24,28},{28,32},{32,36}... | collective-permute-start | bytes 786440 | tf_op jit(solution)/shard_map/ppermute | solution.py:14
  4.5 35.6 %collective-permute-start = (bf16[2,512,512]{2,1,0:T(8,128)(2,1)}, bf16[2,512,512]{2,1,0:T(8,128)(2,1)}, u32[]{:S(2)}, u32[]{:S(2)}) collective-permute-start(bf16[2,512,512]{2,1,0:T(8,128)(2,1)} %local_ref.1), channel_id=1, source_target_pairs={{0,4},{1,125},{2,6},{3,127},{4,8},{5,1},{6,10},{7,3},{8,12},{9,5},... | collective-permute-start | bytes 3145736 | tf_op jit(solution)/shard_map/ppermute | solution.py:70
  16.4 28.2 %copy-start.1 = (bf16[8,128,128]{2,1,0:T(8,128)(2,1)}, bf16[8,128,128]{2,1,0:T(8,128)(2,1)S(1)}, u32[]{:S(2)}) copy-start(bf16[8,128,128]{2,1,0:T(8,128)(2,1)S(1)} %collective-permute-done.2.refs_0_) | copy-start | bytes 786436
  17.5 17.2 %collective-permute-start.3 = (bf16[2,8,128,128]{3,2,1,0:T(8,128)(2,1)S(1)}, bf16[2,8,128,128]{3,2,1,0:T(8,128)(2,1)S(1)}, u32[]{:S(2)}, u32[]{:S(2)}) collective-permute-start(bf16[2,8,128,128]{3,2,1,0:T(8,128)(2,1)S(1)} %pad_maximum_fusion.2), channel_id=1, source_target_pairs={{0,8},{4,12},{8,16},{12,20},{16,24},{20,28},{24,32},{28,36},{32,40... | collective-permute-start | bytes 1572872 | tf_op jit(solution)/shard_map/ppermute | solution.py:14
  17.6 66.0 %collective-permute-start.5 = (bf16[8,128,128]{2,1,0:T(8,128)(2,1)}, bf16[8,128,128]{2,1,0:T(8,128)(2,1)S(1)}, u32[]{:S(2)}, u32[]{:S(2)}) collective-permute-start(bf16[8,128,128]{2,1,0:T(8,128)(2,1)} %param.11), channel_id=1, source_target_pairs={{0,32},{4,36},{8,40},{12,44},{16,48},{20,52},{24,56},{28,60},{32,6... | collective-permute-start | bytes 786440 | tf_op jit(solution)/shard_map/ppermute | solution.py:14
  35.8 24.8 %collective-permute-start.4 = (bf16[4,8,128,128]{3,2,1,0:T(8,128)(2,1)S(1)}, bf16[4,8,128,128]{3,2,1,0:T(8,128)(2,1)S(1)}, u32[]{:S(2)}, u32[]{:S(2)}) collective-permute-start(bf16[4,8,128,128]{3,2,1,0:T(8,128)(2,1)S(1)} %pad_maximum_fusion.1), channel_id=1, source_target_pairs={{0,16},{4,20},{8,24},{12,28},{16,32},{20,36},{24,40},{28,44},{32,4... | collective-permute-start | bytes 3145736 | tf_op jit(solution)/shard_map/ppermute | solution.py:14
  40.1 21.5 %collective-permute-start.1 = (bf16[2,512,512]{2,1,0:T(8,128)(2,1)}, bf16[2,512,512]{2,1,0:T(8,128)(2,1)}, u32[]{:S(2)}, u32[]{:S(2)}) collective-permute-start(bf16[2,512,512]{2,1,0:T(8,128)(2,1)} %collective-permute-done), channel_id=1, source_target_pairs={{0,1},{1,0},{2,3},{3,2},{4,5},{5,4},{6,7},{7,6},{8,9},{9,8},{10,11... | collective-permute-start | bytes 3145736 | tf_op jit(solution)/shard_map/ppermute | solution.py:71
  61.6 1.9 %copy-start = (bf16[2,512,512]{2,1,0:T(8,128)(2,1)S(1)}, bf16[2,512,512]{2,1,0:T(8,128)(2,1)}, u32[]{:S(2)}) copy-start(bf16[2,512,512]{2,1,0:T(8,128)(2,1)} %local_ref.1) | copy-start | bytes 3145732
  83.5 0.7 copy-start.2
  94.5 7.4 %collective-permute-start.6 = (bf16[8,2,128,128]{3,2,0,1:T(8,128)(2,1)S(1)}, bf16[8,2,128,128]{3,2,0,1:T(8,128)(2,1)S(1)}, u32[]{:S(2)}, u32[]{:S(2)}) collective-permute-start(bf16[8,2,128,128]{3,2,0,1:T(8,128)(2,1)S(1)} %fusion), channel_id=1, source_target_pairs={{0,1},{1,0},{2,3},{3,2},{4,5},{5,4},{6,7},{7,6},{8,9},{9,8},{10,11... | collective-permute-start | bytes 1572872 | tf_op jit(solution)/shard_map/ppermute | solution.py:140
  103.3 7.6 %collective-permute-start.7 = (bf16[8,128,128]{2,1,0:T(8,128)(2,1)S(1)}, bf16[8,128,128]{2,1,0:T(8,128)(2,1)S(1)}, u32[]{:S(2)}, u32[]{:S(2)}) collective-permute-start(bf16[8,128,128]{2,1,0:T(8,128)(2,1)S(1)} %fusion.2), channel_id=1, source_target_pairs={{0,2},{1,3},{2,0},{3,1},{4,6},{5,7},{6,4},{7,5},{8,10},{9,11},{10,... | collective-permute-start | bytes 786440 | tf_op jit(solution)/shard_map/ppermute | solution.py:146

commit v8 on v7

--- a/solution.py
+++ b/solution.py
@@ -40,10 +40,11 @@
             ham_ref[0, part * half + s] = ham[:, s * column_count:(s + 1) * column_count]
 
 
-def product_kernel(ham_ref, *refs, stop_count):
-    trial_refs, part_ref = refs[:stop_count], refs[stop_count]
+def product_kernel(ham_ref, first_ref, second_ref, third_ref, last_ref, part_ref, *, stop_count):
     wide = jnp.concatenate([ham_ref[0, s] for s in range(stop_count)], axis=1)
-    tall = jnp.concatenate([trial_refs[s][0] for s in range(stop_count)], axis=0)
+    pieces = [first_ref[0]] + [second_ref[j, 0] for j in range(second_ref.shape[0])]
+    pieces += [third_ref[j, 0] for j in range(third_ref.shape[0])] + [last_ref[0]]
+    tall = jnp.concatenate(pieces, axis=0)
     part_ref[0] = jnp.dot(wide, tall, preferred_element_type=jnp.float32)
 
 
@@ -75,7 +76,7 @@
     last = shifted(trial_vectors, "blk", 8)
     second = shifted(jnp.stack([trial_vectors, first]), "blk", 2)
     third = shifted(jnp.stack([trial_vectors, first, second[0], second[1]]), "blk", 4)
-    sources = [first, second[0], second[1], third[0], third[1], third[2], third[3], last]
+    sources = [first, second, third, last]
 
     order_index = jnp.take(interp_index, stop_order, axis=1)
     order_weight = jnp.take(interp_weight, stop_order, axis=1)
@@ -124,7 +125,11 @@
         grid=(fine_dev,),
         in_specs=[
             pl.BlockSpec((1, stop_count, block_order, column_count), lambda k: (k, 0, 0, 0)),
-        ] + [pl.BlockSpec((1, column_count, vector_count), lambda k: (k, 0, 0))] * stop_count,
+            pl.BlockSpec((1, column_count, vector_count), lambda k: (k, 0, 0)),
+            pl.BlockSpec((2, 1, column_count, vector_count), lambda k: (0, k, 0, 0)),
+            pl.BlockSpec((4, 1, column_count, vector_count), lambda k: (0, k, 0, 0)),
+            pl.BlockSpec((1, column_count, vector_count), lambda k: (k, 0, 0)),
+        ],
         out_specs=pl.BlockSpec((1, block_order, vector_count), lambda k: (k, 0, 0)),
         out_shape=jax.ShapeDtypeStruct((fine_dev, block_order, vector_count), jnp.float32),
         cost_estimate=pl.CostEstimate(

time: 112 us -> 106 us (0.946)
  starting transfers between devices: 23.6 us -> 20.1 us
  waiting for transfers between devices: 44.9 us -> 43 us
    ppermute x4, waiting for transfers between devices: 37.2 us -> 21.6 us  [shifted(): return lax.ppermute(value, axis, pairs)]
    ppermute x1, waiting for transfers between devices: 0.01 us -> 13.6 us  [on_device(): near = lax.ppermute(coarse_kernel, ('blk', 'band'), pairs)]
    ppermute x4, starting transfers between devices: 8.21 us -> 1.02 us  [shifted(): return lax.ppermute(value, axis, pairs)]
    ppermute x1, starting transfers between devices: 2.37 us -> 6.24 us  [on_device(): far = lax.ppermute(near, 'band', [(b, b ^ 1) for b in range(band_count)])]
    ppermute x2, starting transfers between devices: 7.23 us -> 3.39 us  [on_device(): lax.ppermute(send.astype(jnp.bfloat16), 'band', swap).astype(jnp.float32)]
    ppermute x1, starting transfers between devices: 5.75 us -> 9.47 us  [on_device(): near = lax.ppermute(coarse_kernel, ('blk', 'band'), pairs)]
    squeeze x2 -> x0, local copies, waits for them, and re-layouts: 1.84 us -> none  [the longest x1 1 us: on_device(): third[3]]
  transfers between devices with their start and end apart: 8 -> 8, of which waited for: 5 -> 5; matrix products, arithmetic and copies ran while one was open for 8% -> 8% of each run, Pallas kernels for 18% -> 19%
where the time goes in v8:
time: 106 us
  waiting for transfers between devices  43 us (41%)
  Pallas kernels  28.8 us (27%)
  starting transfers between devices  20.1 us (19%)
  other arithmetic  7.4 us (7%)
  local copies, waits for them, and re-layouts  5.57 us (5%)
    ppermute x4, waiting for transfers between devices, shifted(): return lax.ppermute(value, axis, pairs)  21.6 us
    pallas_call x1, Pallas kernels, on_device(): pl.pallas_call(kernel, grid_spec=grid_spec, out_shape=jax.ShapeDtypeStruc...  20.1 us
    ppermute x1, waiting for transfers between devices, on_device(): near = lax.ppermute(coarse_kernel, ('blk', 'band'), pairs)  13.6 us
    ppermute x1, starting transfers between devices, on_device(): near = lax.ppermute(coarse_kernel, ('blk', 'band'), pairs)  9.47 us
    pallas_call x1, Pallas kernels, on_device(): pl.pallas_call(functools.partial(product_kernel, stop_count=stop_count),...  8.71 us
    ppermute x2, waiting for transfers between devices, on_device(): lax.ppermute(send.astype(jnp.bfloat16), 'band', swap).astype(jnp.float32)  7.73 us
    ppermute x1, starting transfers between devices, on_device(): far = lax.ppermute(near, 'band', [(b, b ^ 1) for b in range(band_count)])  6.24 us
    ppermute x2, starting transfers between devices, on_device(): lax.ppermute(send.astype(jnp.bfloat16), 'band', swap).astype(jnp.float32)  3.39 us
  transfers between devices with their start and end apart: 8, of which 5 were waited for; matrix products, arithmetic and copies ran while one was open for 8% of the time, Pallas kernels for 19%

profile of v8, /device:TPU:1, one launch (start us, length us, event | category | flops | bytes accessed | tf_op | source)
XLA Modules:
  0.0 105.6 jit_solution(3450032800319245002)
XLA Ops:
  0.6 9.5 %collective-permute-start = (bf16[2,512,512]{2,1,0:T(8,128)(2,1)}, bf16[2,512,512]{2,1,0:T(8,128)(2,1)S(1)}, u32[]{:S(2)}, u32[]{:S(2)}) collective-permute-start(bf16[2,512,512]{2,1,0:T(8,128)(2,1)} %local_ref.1), channel_id=1, source_target_pairs={{0,4},{1,125},{2,6},{3,127},{4,8},{5,1},{6,10},{7,3},{8,12},{9,5},... | collective-permute-start | bytes 3145736 | tf_op jit(solution)/shard_map/ppermute | solution.py:71
  10.1 0.7 compare_select_fusion
  10.8 0.8 copy.10
  11.6 0.7 compare_and_fusion
  12.2 13.6 %collective-permute-done = bf16[2,512,512]{2,1,0:T(8,128)(2,1)S(1)} collective-permute-done((bf16[2,512,512]{2,1,0:T(8,128)(2,1)}, bf16[2,512,512]{2,1,0:T(8,128)(2,1)S(1)}, u32[]{:S(2)}, u32[]{:S(2)}) %collective-permute-start) | collective-permute-done | bytes 1048608 | tf_op jit(solution)/shard_map/ppermute | solution.py:71
  25.8 6.2 %collective-permute-start.1 = (bf16[2,512,512]{2,1,0:T(8,128)(2,1)S(1)}, bf16[2,512,512]{2,1,0:T(8,128)(2,1)}, u32[]{:S(2)}, u32[]{:S(2)}) collective-permute-start(bf16[2,512,512]{2,1,0:T(8,128)(2,1)S(1)} %collective-permute-done), channel_id=1, source_target_pairs={{0,1},{1,0},{2,3},{3,2},{4,5},{5,4},{6,7},{7,6},{8,9},{9,8},{10,11... | collective-permute-start | bytes 3145736 | tf_op jit(solution)/shard_map/ppermute | solution.py:72
  32.1 1.1 %pad_maximum_fusion.2 = bf16[2,8,128,128]{3,2,1,0:T(8,128)(2,1)S(1)} fusion(bf16[1,8,128,128]{3,2,1,0:T(8,128)(2,1)S(1)} %bitcast.20, bf16[1,8,128,128]{3,2,1,0:T(8,128)(2,1)} %bitcast.22), kind=kLoop, calls=%fused_computation.7 | loop fusion | flops 262144 | bytes 1048576 | tf_op jit(solution)/shard_map/stack | solution.py:77
  33.2 0.9 collective-permute-start.3
  35.0 0.8 copy.12
  35.8 0.6 gather_fusion.1
  36.7 16.1 %collective-permute-done.3.second_ref = bf16[2,8,128,128]{3,2,1,0:T(8,128)(2,1)S(1)} collective-permute-done((bf16[2,8,128,128]{3,2,1,0:T(8,128)(2,1)S(1)}, bf16[2,8,128,128]{3,2,1,0:T(8,128)(2,1)S(1)}, u32[]{:S(2)}, u32[]{:S(2)}) %collective-permute-start.3) | collective-permute-done | bytes 524320 | tf_op jit(solution)/shard_map/ppermute | solution.py:14
  52.8 1.2 %pad_maximum_fusion.1 = bf16[4,8,128,128]{3,2,1,0:T(8,128)(2,1)S(1)} fusion(bf16[2,8,128,128]{3,2,1,0:T(8,128)(2,1)S(1)} %collective-permute-done.3.second_ref, bf16[1,8,128,128]{3,2,1,0:T(8,128)(2,1)S(1)} %bitcast.21, bf16[1,8,128,128]{3,2,1,0:T(8,128)(2,1)} %bitcast.23), kind=kLoop, calls=%fused_computation.3 | loop fusion | flops 1048576 | bytes 2097152 | tf_op jit(solution)/shard_map/stack | solution.py:78
  54.2 1.5 %pad_maximum_fusion.halo_ref = bf16[4,512,512]{2,1,0:T(8,128)(2,1)S(1)} fusion(bf16[2,512,512]{2,1,0:T(8,128)(2,1)} %collective-permute-done.1, bf16[2,512,512]{2,1,0:T(8,128)(2,1)S(1)} %collective-permute-done), kind=kLoop, calls=%fused_computation.2 | loop fusion | flops 1048576 | bytes 4194304 | tf_op jit(solution)/shard_map/concatenate | solution.py:73
  55.7 20.1 %shard_map.77.ham_ref = bf16[8,8,512,128]{3,2,1,0:T(8,128)(2,1)} custom-call(s32[256]{0:T(256)S(1)} %fusion.5.slot_ref, s32[1]{0:T(128)} %bitcast.1.band_ref, f32[256]{0:T(256)S(1)} %select_n.82.weight_ref, bf16[4,512,512]{2,1,0:T(8,128)(2,1)S(1)} %pad_maximum_fusion.halo_ref, bf16[2,512,512]{2,1,0:T(8,128)(2,1)S(1)} %copy-done, ...), custom_call_target="tpu_custom_call" | custom-call | flops 7516192768 | bytes 12582912 | tf_op jit(solution)/shard_map/pallas_call | solution.py:111
  75.8 5.5 %collective-permute-done.4.third_ref = bf16[4,8,128,128]{3,2,1,0:T(8,128)(2,1)S(1)} collective-permute-done((bf16[4,8,128,128]{3,2,1,0:T(8,128)(2,1)S(1)}, bf16[4,8,128,128]{3,2,1,0:T(8,128)(2,1)S(1)}, u32[]{:S(2)}, u32[]{:S(2)}) %collective-permute-start.4) | collective-permute-done | bytes 1048608 | tf_op jit(solution)/shard_map/ppermute | solution.py:14
  81.3 1.0 copy-done.3
  82.3 8.7 %shard_map.78 = f32[8,512,128]{2,1,0:T(8,128)} custom-call(bf16[8,8,512,128]{3,2,1,0:T(8,128)(2,1)} %shard_map.77.ham_ref, bf16[8,128,128]{2,1,0:T(8,128)(2,1)} %copy-done.1, bf16[2,8,128,128]{3,2,1,0:T(8,128)(2,1)} %copy-done.2, bf16[4,8,128,128]{3,2,1,0:T(8,128)(2,1)} %copy-done.3, bf16[8,128,128]{2,1,0:T(8,128)(2,1)} %copy-done.4), custom_call_target="tpu_custom_call" | custom-call | flops 1073741824 | bytes 8388608 | tf_op jit(solution)/shard_map/pallas_call | solution.py:123
  91.0 1.3 %fusion = bf16[8,2,128,128]{3,2,0,1:T(8,128)(2,1)S(1)} fusion(f32[8,2,2,128,128]{4,3,2,1,0:T(8,128)} %bitcast.18, s32[]{:T(128)S(6)} %select_n.84), kind=kLoop, calls=%fused_computation.6 | loop fusion | bytes 1048580 | tf_op jit(solution)/shard_map/convert_element_type | solution.py:145
  92.4 2.0 %collective-permute-start.6 = (bf16[8,2,128,128]{3,2,0,1:T(8,128)(2,1)S(1)}, bf16[8,2,128,128]{3,2,0,1:T(8,128)(2,1)S(1)}, u32[]{:S(2)}, u32[]{:S(2)}) collective-permute-start(bf16[8,2,128,128]{3,2,0,1:T(8,128)(2,1)S(1)} %fusion), channel_id=1, source_target_pairs={{0,1},{1,0},{2,3},{3,2},{4,5},{5,4},{6,7},{7,6},{8,9},{9,8},{10,11... | collective-permute-start | bytes 1572872 | tf_op jit(solution)/shard_map/ppermute | solution.py:145
  94.4 1.5 %collective-permute-done.6 = bf16[8,2,128,128]{3,2,0,1:T(8,128)(2,1)S(1)} collective-permute-done((bf16[8,2,128,128]{3,2,0,1:T(8,128)(2,1)S(1)}, bf16[8,2,128,128]{3,2,0,1:T(8,128)(2,1)S(1)}, u32[]{:S(2)}, u32[]{:S(2)}) %collective-permute-start.6) | collective-permute-done | bytes 524320 | tf_op jit(solution)/shard_map/ppermute | solution.py:145
  95.9 1.3 %bitcast_add_fusion = f32[8,2,128,128]{3,2,0,1:T(8,128)S(1)} fusion(bf16[8,2,128,128]{3,2,0,1:T(8,128)(2,1)S(1)} %collective-permute-done.6, f32[8,2,2,128,128]{4,3,2,1,0:T(8,128)} %bitcast.19, s32[]{:T(128)S(6)} %select_n.83), kind=kLoop, calls=%fused_computation.5 | loop fusion | flops 524288 | bytes 2621444 | tf_op jit(solution)/shard_map/add | solution.py:145
  97.3 1.4 %collective-permute-start.7 = (bf16[8,128,128]{2,1,0:T(8,128)(2,1)S(1)}, bf16[8,128,128]{2,1,0:T(8,128)(2,1)S(1)}, u32[]{:S(2)}, u32[]{:S(2)}) collective-permute-start(bf16[8,128,128]{2,1,0:T(8,128)(2,1)S(1)} %fusion.2), channel_id=1, source_target_pairs={{0,2},{1,3},{2,0},{3,1},{4,6},{5,7},{6,4},{7,5},{8,10},{9,11},{10,... | collective-permute-start | bytes 786440 | tf_op jit(solution)/shard_map/ppermute | solution.py:151
  98.7 6.2 %collective-permute-done.7 = bf16[8,128,128]{2,1,0:T(8,128)(2,1)S(1)} collective-permute-done((bf16[8,128,128]{2,1,0:T(8,128)(2,1)S(1)}, bf16[8,128,128]{2,1,0:T(8,128)(2,1)S(1)}, u32[]{:S(2)}, u32[]{:S(2)}) %collective-permute-start.7) | collective-permute-done | bytes 262176 | tf_op jit(solution)/shard_map/ppermute | solution.py:151
  104.9 0.8 fusion.1
  (25 shorter events, 1.4 us)
Async XLA Ops:
  0.6 25.2 %collective-permute-start = (bf16[2,512,512]{2,1,0:T(8,128)(2,1)}, bf16[2,512,512]{2,1,0:T(8,128)(2,1)S(1)}, u32[]{:S(2)}, u32[]{:S(2)}) collective-permute-start(bf16[2,512,512]{2,1,0:T(8,128)(2,1)} %local_ref.1), channel_id=1, source_target_pairs={{0,4},{1,125},{2,6},{3,127},{4,8},{5,1},{6,10},{7,3},{8,12},{9,5},... | collective-permute-start | bytes 3145736 | tf_op jit(solution)/shard_map/ppermute | solution.py:71
  10.1 22.0 %collective-permute-start.2 = (bf16[8,128,128]{2,1,0:T(8,128)(2,1)}, bf16[8,128,128]{2,1,0:T(8,128)(2,1)S(1)}, u32[]{:S(2)}, u32[]{:S(2)}) collective-permute-start(bf16[8,128,128]{2,1,0:T(8,128)(2,1)} %param.11), channel_id=1, source_target_pairs={{0,4},{4,8},{8,12},{12,16},{16,20},{20,24},{24,28},{28,32},{32,36}... | collective-permute-start | bytes 786440 | tf_op jit(solution)/shard_map/ppermute | solution.py:14
  10.1 65.7 %collective-permute-start.5 = (bf16[8,128,128]{2,1,0:T(8,128)(2,1)}, bf16[8,128,128]{2,1,0:T(8,128)(2,1)S(1)}, u32[]{:S(2)}, u32[]{:S(2)}) collective-permute-start(bf16[8,128,128]{2,1,0:T(8,128)(2,1)} %param.11), channel_id=1, source_target_pairs={{0,32},{4,36},{8,40},{12,44},{16,48},{20,52},{24,56},{28,60},{32,6... | collective-permute-start | bytes 786440 | tf_op jit(solution)/shard_map/ppermute | solution.py:14
  25.8 28.3 %collective-permute-start.1 = (bf16[2,512,512]{2,1,0:T(8,128)(2,1)S(1)}, bf16[2,512,512]{2,1,0:T(8,128)(2,1)}, u32[]{:S(2)}, u32[]{:S(2)}) collective-permute-start(bf16[2,512,512]{2,1,0:T(8,128)(2,1)S(1)} %collective-permute-done), channel_id=1, source_target_pairs={{0,1},{1,0},{2,3},{3,2},{4,5},{5,4},{6,7},{7,6},{8,9},{9,8},{10,11... | collective-permute-start | bytes 3145736 | tf_op jit(solution)/shard_map/ppermute | solution.py:72
  32.1 23.6 %copy-start.1 = (bf16[8,128,128]{2,1,0:T(8,128)(2,1)}, bf16[8,128,128]{2,1,0:T(8,128)(2,1)S(1)}, u32[]{:S(2)}) copy-start(bf16[8,128,128]{2,1,0:T(8,128)(2,1)S(1)} %collective-permute-done.2.first_ref) | copy-start | bytes 786436
  33.2 19.6 %collective-permute-start.3 = (bf16[2,8,128,128]{3,2,1,0:T(8,128)(2,1)S(1)}, bf16[2,8,128,128]{3,2,1,0:T(8,128)(2,1)S(1)}, u32[]{:S(2)}, u32[]{:S(2)}) collective-permute-start(bf16[2,8,128,128]{3,2,1,0:T(8,128)(2,1)S(1)} %pad_maximum_fusion.2), channel_id=1, source_target_pairs={{0,8},{4,12},{8,16},{12,20},{16,24},{20,28},{24,32},{28,36},{32,40... | collective-permute-start | bytes 1572872 | tf_op jit(solution)/shard_map/ppermute | solution.py:14
  52.8 2.9 %copy-start.2 = (bf16[2,8,128,128]{3,2,1,0:T(8,128)(2,1)}, bf16[2,8,128,128]{3,2,1,0:T(8,128)(2,1)S(1)}, u32[]{:S(2)}) copy-start(bf16[2,8,128,128]{3,2,1,0:T(8,128)(2,1)S(1)} %collective-permute-done.3.second_ref) | copy-start | bytes 1572868
  54.0 27.3 %collective-permute-start.4 = (bf16[4,8,128,128]{3,2,1,0:T(8,128)(2,1)S(1)}, bf16[4,8,128,128]{3,2,1,0:T(8,128)(2,1)S(1)}, u32[]{:S(2)}, u32[]{:S(2)}) collective-permute-start(bf16[4,8,128,128]{3,2,1,0:T(8,128)(2,1)S(1)} %pad_maximum_fusion.1), channel_id=1, source_target_pairs={{0,16},{4,20},{8,24},{12,28},{16,32},{20,36},{24,40},{28,44},{32,4... | collective-permute-start | bytes 3145736 | tf_op jit(solution)/shard_map/ppermute | solution.py:14
  54.1 1.5 %copy-start = (bf16[2,512,512]{2,1,0:T(8,128)(2,1)S(1)}, bf16[2,512,512]{2,1,0:T(8,128)(2,1)}, u32[]{:S(2)}) copy-start(bf16[2,512,512]{2,1,0:T(8,128)(2,1)} %local_ref.1) | copy-start | bytes 3145732
  75.8 5.5 %copy-start.4 = (bf16[8,128,128]{2,1,0:T(8,128)(2,1)}, bf16[8,128,128]{2,1,0:T(8,128)(2,1)S(1)}, u32[]{:S(2)}) copy-start(bf16[8,128,128]{2,1,0:T(8,128)(2,1)S(1)} %collective-permute-done.5.last_ref) | copy-start | bytes 786436
  81.3 1.0 copy-start.3
  92.4 3.6 %collective-permute-start.6 = (bf16[8,2,128,128]{3,2,0,1:T(8,128)(2,1)S(1)}, bf16[8,2,128,128]{3,2,0,1:T(8,128)(2,1)S(1)}, u32[]{:S(2)}, u32[]{:S(2)}) collective-permute-start(bf16[8,2,128,128]{3,2,0,1:T(8,128)(2,1)S(1)} %fusion), channel_id=1, source_target_pairs={{0,1},{1,0},{2,3},{3,2},{4,5},{5,4},{6,7},{7,6},{8,9},{9,8},{10,11... | collective-permute-start | bytes 1572872 | tf_op jit(solution)/shard_map/ppermute | solution.py:145
  97.3 7.6 %collective-permute-start.7 = (bf16[8,128,128]{2,1,0:T(8,128)(2,1)S(1)}, bf16[8,128,128]{2,1,0:T(8,128)(2,1)S(1)}, u32[]{:S(2)}, u32[]{:S(2)}) collective-permute-start(bf16[8,128,128]{2,1,0:T(8,128)(2,1)S(1)} %fusion.2), channel_id=1, source_target_pairs={{0,2},{1,3},{2,0},{3,1},{4,6},{5,7},{6,4},{7,5},{8,10},{9,11},{10,... | collective-permute-start | bytes 786440 | tf_op jit(solution)/shard_map/ppermute | solution.py:151

commit v9 on v8

--- a/solution.py
+++ b/solution.py
@@ -15,8 +15,9 @@
 
 
 def sandwich_kernel(slot_ref, band_ref, weight_ref, halo_ref, local_ref, inter_ref, right_ref,
-                    ham_ref, prod_ref, rot_ref, *, blocks_dev, stop_count, corner_count):
-    k = pl.program_id(0)
+                    *refs, blocks_dev, stop_count, corner_count, offset):
+    ham_ref, prod_ref, rot_ref = refs[-3:]
+    k = pl.program_id(0) + offset
     column_count = right_ref.shape[2]
     right = right_ref[0]
     sources = [halo_ref.at[slot] for slot in range(blocks_dev)]
@@ -40,10 +41,10 @@
             ham_ref[0, part * half + s] = ham[:, s * column_count:(s + 1) * column_count]
 
 
-def product_kernel(ham_ref, first_ref, second_ref, third_ref, last_ref, part_ref, *, stop_count):
+def product_kernel(ham_ref, odd_ref, even_ref, fourth_ref, last_ref, part_ref, *, stop_count):
     wide = jnp.concatenate([ham_ref[0, s] for s in range(stop_count)], axis=1)
-    pieces = [first_ref[0]] + [second_ref[j, 0] for j in range(second_ref.shape[0])]
-    pieces += [third_ref[j, 0] for j in range(third_ref.shape[0])] + [last_ref[0]]
+    pieces = [odd_ref[0, 0], even_ref[0, 0], even_ref[1, 0], fourth_ref[0],
+              odd_ref[1, 0], even_ref[2, 0], even_ref[3, 0], last_ref[0]]
     tall = jnp.concatenate(pieces, axis=0)
     part_ref[0] = jnp.dot(wide, tall, preferred_element_type=jnp.float32)
 
@@ -72,11 +73,10 @@
     far = lax.ppermute(near, "band", [(b, b ^ 1) for b in range(band_count)])
     halo = jnp.concatenate([near, far], axis=0)
     assert stop_count == 8
-    first = shifted(trial_vectors, "blk", 1)
+    fourth = shifted(trial_vectors, "blk", 4)
     last = shifted(trial_vectors, "blk", 8)
-    second = shifted(jnp.stack([trial_vectors, first]), "blk", 2)
-    third = shifted(jnp.stack([trial_vectors, first, second[0], second[1]]), "blk", 4)
-    sources = [first, second, third, last]
+    odd = shifted(jnp.stack([trial_vectors, fourth]), "blk", 1)
+
 
     order_index = jnp.take(interp_index, stop_order, axis=1)
     order_weight = jnp.take(interp_weight, stop_order, axis=1)
@@ -89,45 +89,67 @@
     weights = order_weight.astype(jnp.float32).reshape(-1)
     band_index = jnp.reshape(band, (1,)).astype(jnp.int32)
 
-    kernel = functools.partial(
-        sandwich_kernel, blocks_dev=blocks_dev, stop_count=stop_count, corner_count=corner_count)
-    grid_spec = pltpu.PrefetchScalarGridSpec(
-        num_scalar_prefetch=2,
-        grid=(fine_dev,),
-        in_specs=[
+    half_count = fine_dev // 2
+    hamiltonian = None
+    for offset in (0, half_count):
+        kernel = functools.partial(
+            sandwich_kernel, blocks_dev=blocks_dev, stop_count=stop_count,
+            corner_count=corner_count, offset=offset)
+        in_specs = [
             pl.BlockSpec(memory_space=pltpu.SMEM),
             pl.BlockSpec((2 * blocks_dev, block_order, block_order), lambda k, sl, bd: (0, 0, 0)),
             pl.BlockSpec((blocks_dev, block_order, block_order), lambda k, sl, bd: (0, 0, 0)),
-            pl.BlockSpec((1, block_order, block_order), lambda k, sl, bd: (k, 0, 0)),
-            pl.BlockSpec((1, block_order, column_count), lambda k, sl, bd: (k, 0, bd[0])),
-        ],
-        out_specs=pl.BlockSpec(
-            (1, stop_count, block_order, column_count), lambda k, sl, bd: (k, 0, 0, 0)),
-        scratch_shapes=[
-            pltpu.VMEM((window_slots, block_order, column_count), jnp.float32),
-            pltpu.VMEM((block_order, stop_count * column_count), jnp.bfloat16),
-        ],
-    )
-    hamiltonian = pl.pallas_call(
-        kernel,
-        grid_spec=grid_spec,
-        out_shape=jax.ShapeDtypeStruct(
-            (fine_dev, stop_count, block_order, column_count), jnp.bfloat16),
-        compiler_params=pltpu.CompilerParams(
-            dimension_semantics=("arbitrary",), vmem_limit_bytes=48 * 1024 * 1024),
-        cost_estimate=pl.CostEstimate(
-            flops=2 * fine_dev * block_order * block_order * column_count * (window_slots + stop_count),
-            transcendentals=0,
-            bytes_accessed=2 * fine_dev * block_order * (block_order + stop_count * column_count)),
-    )(slot_index, band_index, weights, halo, coarse_kernel, intersection, intersection)
+            pl.BlockSpec(
+                (1, block_order, block_order), lambda k, sl, bd, o=offset: (k + o, 0, 0)),
+            pl.BlockSpec(
+                (1, block_order, column_count), lambda k, sl, bd, o=offset: (k + o, 0, bd[0])),
+        ]
+        operands = [slot_index, band_index, weights, halo, coarse_kernel, intersection,
+                    intersection]
+        aliases = {}
+        if hamiltonian is not None:
+            in_specs.append(pl.BlockSpec(memory_space=pl.ANY))
+            aliases = {len(operands): 0}
+            operands.append(hamiltonian)
+        grid_spec = pltpu.PrefetchScalarGridSpec(
+            num_scalar_prefetch=2,
+            grid=(half_count,),
+            in_specs=in_specs,
+            out_specs=pl.BlockSpec(
+                (1, stop_count, block_order, column_count),
+                lambda k, sl, bd, o=offset: (k + o, 0, 0, 0)),
+            scratch_shapes=[
+                pltpu.VMEM((window_slots, block_order, column_count), jnp.float32),
+                pltpu.VMEM((block_order, stop_count * column_count), jnp.bfloat16),
+            ],
+        )
+        if hamiltonian is not None:
+            hamiltonian, odd = lax.optimization_barrier((hamiltonian, odd))
+            even = shifted(jnp.stack([trial_vectors, odd[0], fourth, odd[1]]), "blk", 2)
+        hamiltonian = pl.pallas_call(
+            kernel,
+            grid_spec=grid_spec,
+            out_shape=jax.ShapeDtypeStruct(
+                (fine_dev, stop_count, block_order, column_count), jnp.bfloat16),
+            input_output_aliases=aliases,
+            compiler_params=pltpu.CompilerParams(
+                dimension_semantics=("arbitrary",), vmem_limit_bytes=48 * 1024 * 1024),
+            cost_estimate=pl.CostEstimate(
+                flops=half_count * 2 * block_order * block_order * column_count
+                * (window_slots + stop_count),
+                transcendentals=0,
+                bytes_accessed=half_count * 2 * block_order
+                * (block_order + stop_count * column_count)),
+        )(*operands)
+    sources = [odd, even, fourth, last]
     partial_value = pl.pallas_call(
         functools.partial(product_kernel, stop_count=stop_count),
         grid=(fine_dev,),
         in_specs=[
             pl.BlockSpec((1, stop_count, block_order, column_count), lambda k: (k, 0, 0, 0)),
-            pl.BlockSpec((1, column_count, vector_count), lambda k: (k, 0, 0)),
             pl.BlockSpec((2, 1, column_count, vector_count), lambda k: (0, k, 0, 0)),
             pl.BlockSpec((4, 1, column_count, vector_count), lambda k: (0, k, 0, 0)),
+            pl.BlockSpec((1, column_count, vector_count), lambda k: (k, 0, 0)),
             pl.BlockSpec((1, column_count, vector_count), lambda k: (k, 0, 0)),
         ],
         out_specs=pl.BlockSpec((1, block_order, vector_count), lambda k: (k, 0, 0)),

time: 106 us -> 112 us (1.057); the launches traced: 106 us -> 110 us
  starting transfers between devices: 20.1 us -> 24.6 us
  waiting for transfers between devices: 43 us -> 39.4 us
  Pallas kernels: 28.8 us -> 31.3 us
  local copies, waits for them, and re-layouts: 5.57 us -> 7.22 us
    ppermute x4, waiting for transfers between devices: 21.6 us -> 17.6 us  [shifted(): return lax.ppermute(value, axis, pairs)]
    ppermute x4, starting transfers between devices: 1.02 us -> 3.84 us  [shifted(): return lax.ppermute(value, axis, pairs)]
    pallas_call x1 -> x2, Pallas kernels: 20.1 us -> 22.7 us  [on_device(): pl.pallas_call(kernel, grid_spec=grid_spec, out_shape=jax.ShapeDtypeStruc...]
    concatenate x1 -> x0, other arithmetic: 1.49 us -> none  [on_device(): halo = jnp.concatenate([near, far], axis=0)]
    ppermute x1, starting transfers between devices: 6.24 us -> 7.66 us  [on_device(): far = lax.ppermute(near, 'band', [(b, b ^ 1) for b in range(band_count)])]
    concatenate x0 -> x1, local copies, waits for them, and re-layouts: none -> 1.29 us  [on_device(): halo = jnp.concatenate([near, far], axis=0)]
    unnamed x12 -> x11, local copies, waits for them, and re-layouts: 2.58 us -> 2.9 us
  transfers between devices with their start and end apart: 8 -> 8, of which waited for: 5 -> 5; matrix products, arithmetic and copies ran while one was open for 8% -> 8% of each run, Pallas kernels for 19% -> 21%
where the time goes in v9:
time: 112 us; the launch traced here: 110 us
  waiting for transfers between devices  39.4 us (35%)
  Pallas kernels  31.3 us (28%)
  starting transfers between devices  24.6 us (22%)
  local copies, waits for them, and re-layouts  7.22 us (6%)
  other arithmetic  6.89 us (6%)
    pallas_call x2, Pallas kernels, on_device(): pl.pallas_call(kernel, grid_spec=grid_spec, out_shape=jax.ShapeDtypeStruc...  22.7 us
    ppermute x4, waiting for transfers between devices, shifted(): return lax.ppermute(value, axis, pairs)  17.6 us
    ppermute x1, waiting for transfers between devices, on_device(): near = lax.ppermute(coarse_kernel, ('blk', 'band'), pairs)  13.1 us
    ppermute x1, starting transfers between devices, on_device(): near = lax.ppermute(coarse_kernel, ('blk', 'band'), pairs)  9.47 us
    pallas_call x1, Pallas kernels, on_device(): pl.pallas_call(functools.partial(product_kernel, stop_count=stop_count),...  8.66 us
    ppermute x2, waiting for transfers between devices, on_device(): lax.ppermute(send.astype(jnp.bfloat16), 'band', swap).astype(jnp.float32)  8.63 us
    ppermute x1, starting transfers between devices, on_device(): far = lax.ppermute(near, 'band', [(b, b ^ 1) for b in range(band_count)])  7.66 us
    ppermute x4, starting transfers between devices, shifted(): return lax.ppermute(value, axis, pairs)  3.84 us
  transfers between devices with their start and end apart: 8, of which 5 were waited for; matrix products, arithmetic and copies ran while one was open for 8% of the time, Pallas kernels for 21%

profile of v9, /device:TPU:1, one launch (start us, length us, event | category | flops | bytes accessed | tf_op | source)
XLA Modules:
  0.0 110.1 jit_solution(14532250490257917062)
XLA Ops:
  0.6 9.5 %collective-permute-start = (bf16[2,512,512]{2,1,0:T(8,128)(2,1)}, bf16[2,512,512]{2,1,0:T(8,128)(2,1)}, u32[]{:S(2)}, u32[]{:S(2)}) collective-permute-start(bf16[2,512,512]{2,1,0:T(8,128)(2,1)} %local_ref.3), channel_id=1, source_target_pairs={{0,4},{1,125},{2,6},{3,127},{4,8},{5,1},{6,10},{7,3},{8,12},{9,5},... | collective-permute-start | bytes 3145736 | tf_op jit(solution)/shard_map/ppermute | solution.py:72
  10.1 0.8 copy.11
  10.9 0.8 copy.13
  11.7 0.7 compare_select_fusion
  12.3 0.7 compare_and_fusion
  13.0 13.1 %collective-permute-done = bf16[2,512,512]{2,1,0:T(8,128)(2,1)} collective-permute-done((bf16[2,512,512]{2,1,0:T(8,128)(2,1)}, bf16[2,512,512]{2,1,0:T(8,128)(2,1)}, u32[]{:S(2)}, u32[]{:S(2)}) %collective-permute-start) | collective-permute-done | bytes 1048608 | tf_op jit(solution)/shard_map/ppermute | solution.py:72
  26.1 7.7 %collective-permute-start.1 = (bf16[2,512,512]{2,1,0:T(8,128)(2,1)}, bf16[2,512,512]{2,1,0:T(8,128)(2,1)}, u32[]{:S(2)}, u32[]{:S(2)}) collective-permute-start(bf16[2,512,512]{2,1,0:T(8,128)(2,1)} %collective-permute-done), channel_id=1, source_target_pairs={{0,1},{1,0},{2,3},{3,2},{4,5},{5,4},{6,7},{7,6},{8,9},{9,8},{10,11... | collective-permute-start | bytes 3145736 | tf_op jit(solution)/shard_map/ppermute | solution.py:73
  34.3 0.6 gather_fusion.1
  35.6 1.1 pad_maximum_fusion.1
  36.7 3.8 %collective-permute-start.3 = (bf16[2,8,128,128]{3,2,1,0:T(8,128)(2,1)S(1)}, bf16[2,8,128,128]{3,2,1,0:T(8,128)(2,1)S(1)}, u32[]{:S(2)}, u32[]{:S(2)}) collective-permute-start(bf16[2,8,128,128]{3,2,1,0:T(8,128)(2,1)S(1)} %pad_maximum_fusion.1), channel_id=1, source_target_pairs={{0,4},{4,8},{8,12},{12,16},{16,20},{20,24},{24,28},{28,32},{32,36}... | collective-permute-start | bytes 1572872 | tf_op jit(solution)/shard_map/ppermute | solution.py:14
  40.6 1.3 %constant_dynamic-update-slice_fusion.1 = bf16[4,512,512]{2,1,0:T(8,128)(2,1)S(1)} fusion(bf16[2,512,512]{2,1,0:T(8,128)(2,1)} %collective-permute-done), kind=kLoop, calls=%fused_computation.15 | loop fusion | bytes 2097152
  41.9 1.3 %constant_dynamic-update-slice_fusion.halo_ref = bf16[4,512,512]{2,1,0:T(8,128)(2,1)S(1)} fusion(bf16[4,512,512]{2,1,0:T(8,128)(2,1)S(1)} %constant_dynamic-update-slice_fusion.1, bf16[2,512,512]{2,1,0:T(8,128)(2,1)} %collective-permute-done.1), kind=kLoop, calls=%fused_computation.14 | loop fusion | bytes 2097152 | tf_op jit(solution)/shard_map/concatenate | solution.py:74
  43.2 11.3 %shard_map.77.refs_0_ = bf16[8,8,512,128]{3,2,1,0:T(8,128)(2,1)} custom-call(s32[256]{0:T(256)S(1)} %fusion.5.slot_ref, s32[1]{0:T(128)} %bitcast.1.band_ref, f32[256]{0:T(256)S(1)} %select_n.82.weight_ref, bf16[4,512,512]{2,1,0:T(8,128)(2,1)S(1)} %constant_dynamic-update-slice_fusion.halo_ref, bf16[2,512,512]{2,1,0:T(8,128)(2,1)S(1)} %copy-done, ...), custom_call_target="tpu_custom_call" | custom-call | flops 3758096384 | bytes 6291456 | tf_op jit(solution)/shard_map/pallas_call | solution.py:129
  54.5 1.5 %collective-permute-done.3.odd_ref = bf16[2,8,128,128]{3,2,1,0:T(8,128)(2,1)S(1)} collective-permute-done((bf16[2,8,128,128]{3,2,1,0:T(8,128)(2,1)S(1)}, bf16[2,8,128,128]{3,2,1,0:T(8,128)(2,1)S(1)}, u32[]{:S(2)}, u32[]{:S(2)}) %collective-permute-start.3) | collective-permute-done | bytes 524320 | tf_op jit(solution)/shard_map/ppermute | solution.py:14
  56.1 2.2 %pad_maximum_fusion = bf16[4,8,128,128]{3,2,1,0:T(8,128)(2,1)} fusion(bf16[1,8,128,128]{3,2,1,0:T(8,128)(2,1)S(1)} %get-tuple-element.5, bf16[1,8,128,128]{3,2,1,0:T(8,128)(2,1)S(1)} %bitcast.21, bf16[1,8,128,128]{3,2,1,0:T(8,128)(2,1)S(1)} %get-tuple-element.4, bf16[1,8,128,128]{3,2,1,0:T(8,128)(2,1)} %bitcast.3), kind=kLoop, calls=%fused_computation.2 | loop fusion | flops 1572864 | bytes 2097152 | tf_op jit(solution)/shard_map/stack | solution.py:128
  58.3 11.3 %shard_map.78.ham_ref = bf16[8,8,512,128]{3,2,1,0:T(8,128)(2,1)} custom-call(s32[256]{0:T(256)S(1)} %fusion.5.slot_ref, s32[1]{0:T(128)} %bitcast.1.band_ref, f32[256]{0:T(256)S(1)} %select_n.82.weight_ref, bf16[4,512,512]{2,1,0:T(8,128)(2,1)S(1)} %constant_dynamic-update-slice_fusion.halo_ref, ...), custom_call_target="tpu_custom_call", output_to_operand_aliasing={{}: (7, {})} | custom-call | flops 3758096384 | bytes 6291456 | tf_op jit(solution)/shard_map/pallas_call | solution.py:129
  69.6 16.1 %collective-permute-done.4.even_ref = bf16[4,8,128,128]{3,2,1,0:T(8,128)(2,1)} collective-permute-done((bf16[4,8,128,128]{3,2,1,0:T(8,128)(2,1)}, bf16[4,8,128,128]{3,2,1,0:T(8,128)(2,1)}, u32[]{:S(2)}, u32[]{:S(2)}) %collective-permute-start.4) | collective-permute-done | bytes 1048608 | tf_op jit(solution)/shard_map/ppermute | solution.py:14
  85.8 8.7 %shard_map.79 = f32[8,512,128]{2,1,0:T(8,128)} custom-call(bf16[8,8,512,128]{3,2,1,0:T(8,128)(2,1)} %shard_map.78.ham_ref, bf16[2,8,128,128]{3,2,1,0:T(8,128)(2,1)} %copy-done.2, bf16[4,8,128,128]{3,2,1,0:T(8,128)(2,1)} %collective-permute-done.4.even_ref, bf16[8,128,128]{2,1,0:T(8,128)(2,1)} %copy-done.1, bf16[8,128,128]{2,1,0:T(8,128)(2,1)} %copy-done.3), custom_call_target="tpu_custom_call" | custom-call | flops 1073741824 | bytes 8388608 | tf_op jit(solution)/shard_map/pallas_call | solution.py:145
  94.4 1.3 %fusion = bf16[8,2,128,128]{3,2,0,1:T(8,128)(2,1)S(1)} fusion(f32[8,2,2,128,128]{4,3,2,1,0:T(8,128)} %bitcast.18, s32[]{:T(128)S(6)} %select_n.84), kind=kLoop, calls=%fused_computation.5 | loop fusion | bytes 1048580 | tf_op jit(solution)/shard_map/convert_element_type | solution.py:167
  95.7 3.1 %collective-permute-start.6 = (bf16[8,2,128,128]{3,2,0,1:T(8,128)(2,1)S(1)}, bf16[8,2,128,128]{3,2,0,1:T(8,128)(2,1)S(1)}, u32[]{:S(2)}, u32[]{:S(2)}) collective-permute-start(bf16[8,2,128,128]{3,2,0,1:T(8,128)(2,1)S(1)} %fusion), channel_id=1, source_target_pairs={{0,1},{1,0},{2,3},{3,2},{4,5},{5,4},{6,7},{7,6},{8,9},{9,8},{10,11... | collective-permute-start | bytes 1572872 | tf_op jit(solution)/shard_map/ppermute | solution.py:167
  98.9 1.5 %collective-permute-done.6 = bf16[8,2,128,128]{3,2,0,1:T(8,128)(2,1)S(1)} collective-permute-done((bf16[8,2,128,128]{3,2,0,1:T(8,128)(2,1)S(1)}, bf16[8,2,128,128]{3,2,0,1:T(8,128)(2,1)S(1)}, u32[]{:S(2)}, u32[]{:S(2)}) %collective-permute-start.6) | collective-permute-done | bytes 524320 | tf_op jit(solution)/shard_map/ppermute | solution.py:167
  100.4 1.3 %bitcast_add_fusion = f32[8,2,128,128]{3,2,0,1:T(8,128)S(1)} fusion(bf16[8,2,128,128]{3,2,0,1:T(8,128)(2,1)S(1)} %collective-permute-done.6, f32[8,2,2,128,128]{4,3,2,1,0:T(8,128)} %bitcast.19, s32[]{:T(128)S(6)} %select_n.83), kind=kLoop, calls=%fused_computation.4 | loop fusion | flops 524288 | bytes 2621444 | tf_op jit(solution)/shard_map/add | solution.py:167
  102.3 7.1 %collective-permute-done.7 = bf16[8,128,128]{2,1,0:T(8,128)(2,1)S(1)} collective-permute-done((bf16[8,128,128]{2,1,0:T(8,128)(2,1)S(1)}, bf16[8,128,128]{2,1,0:T(8,128)(2,1)S(1)}, u32[]{:S(2)}, u32[]{:S(2)}) %collective-permute-start.7) | collective-permute-done | bytes 262176 | tf_op jit(solution)/shard_map/ppermute | solution.py:173
  109.4 0.8 fusion.1
  (26 shorter events, 1.8 us)
Async XLA Ops:
  0.6 25.5 %collective-permute-start = (bf16[2,512,512]{2,1,0:T(8,128)(2,1)}, bf16[2,512,512]{2,1,0:T(8,128)(2,1)}, u32[]{:S(2)}, u32[]{:S(2)}) collective-permute-start(bf16[2,512,512]{2,1,0:T(8,128)(2,1)} %local_ref.3), channel_id=1, source_target_pairs={{0,4},{1,125},{2,6},{3,127},{4,8},{5,1},{6,10},{7,3},{8,12},{9,5},... | collective-permute-start | bytes 3145736 | tf_op jit(solution)/shard_map/ppermute | solution.py:72
  10.1 25.5 %collective-permute-start.2 = (bf16[8,128,128]{2,1,0:T(8,128)(2,1)}, bf16[8,128,128]{2,1,0:T(8,128)(2,1)S(1)}, u32[]{:S(2)}, u32[]{:S(2)}) collective-permute-start(bf16[8,128,128]{2,1,0:T(8,128)(2,1)} %param.11), channel_id=1, source_target_pairs={{0,16},{4,20},{8,24},{12,28},{16,32},{20,36},{24,40},{28,44},{32,4... | collective-permute-start | bytes 786440 | tf_op jit(solution)/shard_map/ppermute | solution.py:14
  26.1 15.8 %collective-permute-start.1 = (bf16[2,512,512]{2,1,0:T(8,128)(2,1)}, bf16[2,512,512]{2,1,0:T(8,128)(2,1)}, u32[]{:S(2)}, u32[]{:S(2)}) collective-permute-start(bf16[2,512,512]{2,1,0:T(8,128)(2,1)} %collective-permute-done), channel_id=1, source_target_pairs={{0,1},{1,0},{2,3},{3,2},{4,5},{5,4},{6,7},{7,6},{8,9},{9,8},{10,11... | collective-permute-start | bytes 3145736 | tf_op jit(solution)/shard_map/ppermute | solution.py:73
  35.6 20.4 %copy-start.1 = (bf16[8,128,128]{2,1,0:T(8,128)(2,1)}, bf16[8,128,128]{2,1,0:T(8,128)(2,1)S(1)}, u32[]{:S(2)}) copy-start(bf16[8,128,128]{2,1,0:T(8,128)(2,1)S(1)} %collective-permute-done.2.fourth_ref) | copy-start | bytes 786436
  36.7 6.4 %copy-start = (bf16[2,512,512]{2,1,0:T(8,128)(2,1)S(1)}, bf16[2,512,512]{2,1,0:T(8,128)(2,1)}, u32[]{:S(2)}) copy-start(bf16[2,512,512]{2,1,0:T(8,128)(2,1)} %local_ref.3) | copy-start | bytes 3145732
  36.7 19.3 %collective-permute-start.3 = (bf16[2,8,128,128]{3,2,1,0:T(8,128)(2,1)S(1)}, bf16[2,8,128,128]{3,2,1,0:T(8,128)(2,1)S(1)}, u32[]{:S(2)}, u32[]{:S(2)}) collective-permute-start(bf16[2,8,128,128]{3,2,1,0:T(8,128)(2,1)S(1)} %pad_maximum_fusion.1), channel_id=1, source_target_pairs={{0,4},{4,8},{8,12},{12,16},{16,20},{20,24},{24,28},{28,32},{32,36}... | collective-permute-start | bytes 1572872 | tf_op jit(solution)/shard_map/ppermute | solution.py:14
  56.0 2.3 %copy-start.2 = (bf16[2,8,128,128]{3,2,1,0:T(8,128)(2,1)}, bf16[2,8,128,128]{3,2,1,0:T(8,128)(2,1)S(1)}, u32[]{:S(2)}) copy-start(bf16[2,8,128,128]{3,2,1,0:T(8,128)(2,1)S(1)} %collective-permute-done.3.odd_ref) | copy-start | bytes 1572868
  58.3 27.5 %collective-permute-start.4 = (bf16[4,8,128,128]{3,2,1,0:T(8,128)(2,1)}, bf16[4,8,128,128]{3,2,1,0:T(8,128)(2,1)}, u32[]{:S(2)}, u32[]{:S(2)}) collective-permute-start(bf16[4,8,128,128]{3,2,1,0:T(8,128)(2,1)} %pad_maximum_fusion), channel_id=1, source_target_pairs={{0,8},{4,12},{8,16},{12,20},{16,24},{20,28},{24,32},{28,36},{32,40... | collective-permute-start | bytes 3145736 | tf_op jit(solution)/shard_map/ppermute | solution.py:14
  58.3 11.4 %collective-permute-start.5 = (bf16[8,128,128]{2,1,0:T(8,128)(2,1)}, bf16[8,128,128]{2,1,0:T(8,128)(2,1)S(1)}, u32[]{:S(2)}, u32[]{:S(2)}) collective-permute-start(bf16[8,128,128]{2,1,0:T(8,128)(2,1)} %param.11), channel_id=1, source_target_pairs={{0,32},{4,36},{8,40},{12,44},{16,48},{20,52},{24,56},{28,60},{32,6... | collective-permute-start | bytes 786440 | tf_op jit(solution)/shard_map/ppermute | solution.py:14
  69.6 16.1 %copy-start.3 = (bf16[8,128,128]{2,1,0:T(8,128)(2,1)}, bf16[8,128,128]{2,1,0:T(8,128)(2,1)S(1)}, u32[]{:S(2)}) copy-start(bf16[8,128,128]{2,1,0:T(8,128)(2,1)S(1)} %collective-permute-done.5.last_ref) | copy-start | bytes 786436
  95.7 4.7 %collective-permute-start.6 = (bf16[8,2,128,128]{3,2,0,1:T(8,128)(2,1)S(1)}, bf16[8,2,128,128]{3,2,0,1:T(8,128)(2,1)S(1)}, u32[]{:S(2)}, u32[]{:S(2)}) collective-permute-start(bf16[8,2,128,128]{3,2,0,1:T(8,128)(2,1)S(1)} %fusion), channel_id=1, source_target_pairs={{0,1},{1,0},{2,3},{3,2},{4,5},{5,4},{6,7},{7,6},{8,9},{9,8},{10,11... | collective-permute-start | bytes 1572872 | tf_op jit(solution)/shard_map/ppermute | solution.py:167
  101.8 7.6 %collective-permute-start.7 = (bf16[8,128,128]{2,1,0:T(8,128)(2,1)S(1)}, bf16[8,128,128]{2,1,0:T(8,128)(2,1)S(1)}, u32[]{:S(2)}, u32[]{:S(2)}) collective-permute-start(bf16[8,128,128]{2,1,0:T(8,128)(2,1)S(1)} %fusion.2), channel_id=1, source_target_pairs={{0,2},{1,3},{2,0},{3,1},{4,6},{5,7},{6,4},{7,5},{8,10},{9,11},{10,... | collective-permute-start | bytes 786440 | tf_op jit(solution)/shard_map/ppermute | solution.py:173

commit v10 on v7

--- a/solution.py
+++ b/solution.py
@@ -15,7 +15,8 @@
 
 
 def sandwich_kernel(slot_ref, band_ref, weight_ref, halo_ref, local_ref, inter_ref, right_ref,
-                    ham_ref, prod_ref, rot_ref, *, blocks_dev, stop_count, corner_count):
+                    first_ref, second_ref, last_ref, ham_ref, early_ref, prod_ref, rot_ref,
+                    *, blocks_dev, stop_count, corner_count):
     k = pl.program_id(0)
     column_count = right_ref.shape[2]
     right = right_ref[0]
@@ -38,13 +39,20 @@
         ham = ham.astype(jnp.bfloat16)
         for s in range(half):
             ham_ref[0, part * half + s] = ham[:, s * column_count:(s + 1) * column_count]
+        if part == 0:
+            tall = jnp.concatenate([first_ref[0], second_ref[0, 0], second_ref[1, 0]], axis=0)
+            early = jnp.dot(ham[:, :3 * column_count], tall, preferred_element_type=jnp.float32)
+        else:
+            early = early + jnp.dot(ham[:, (half - 1) * column_count:], last_ref[0],
+                                    preferred_element_type=jnp.float32)
+    early_ref[0] = early
 
 
-def product_kernel(ham_ref, *refs, stop_count):
-    trial_refs, part_ref = refs[:stop_count], refs[stop_count]
-    wide = jnp.concatenate([ham_ref[0, s] for s in range(stop_count)], axis=1)
-    tall = jnp.concatenate([trial_refs[s][0] for s in range(stop_count)], axis=0)
-    part_ref[0] = jnp.dot(wide, tall, preferred_element_type=jnp.float32)
+def product_kernel(ham_ref, early_ref, third_ref, part_ref):
+    count = third_ref.shape[0]
+    wide = jnp.concatenate([ham_ref[0, 3 + s] for s in range(count)], axis=1)
+    tall = jnp.concatenate([third_ref[s, 0] for s in range(count)], axis=0)
+    part_ref[0] = early_ref[0] + jnp.dot(wide, tall, preferred_element_type=jnp.float32)
 
 
 def on_device(coarse_kernel, interp_index, interp_weight, stop_order, intersection, trial_vectors):
@@ -75,7 +83,6 @@
     last = shifted(trial_vectors, "blk", 8)
     second = shifted(jnp.stack([trial_vectors, first]), "blk", 2)
     third = shifted(jnp.stack([trial_vectors, first, second[0], second[1]]), "blk", 4)
-    sources = [first, second[0], second[1], third[0], third[1], third[2], third[3], last]
 
     order_index = jnp.take(interp_index, stop_order, axis=1)
     order_weight = jnp.take(interp_weight, stop_order, axis=1)
@@ -99,39 +106,50 @@
             pl.BlockSpec((blocks_dev, block_order, block_order), lambda k, sl, bd: (0, 0, 0)),
             pl.BlockSpec((1, block_order, block_order), lambda k, sl, bd: (k, 0, 0)),
             pl.BlockSpec((1, block_order, column_count), lambda k, sl, bd: (k, 0, bd[0])),
+            pl.BlockSpec((1, column_count, vector_count), lambda k, sl, bd: (k, 0, 0)),
+            pl.BlockSpec((2, 1, column_count, vector_count), lambda k, sl, bd: (0, k, 0, 0)),
+            pl.BlockSpec((1, column_count, vector_count), lambda k, sl, bd: (k, 0, 0)),
         ],
-        out_specs=pl.BlockSpec(
-            (1, stop_count, block_order, column_count), lambda k, sl, bd: (k, 0, 0, 0)),
+        out_specs=[
+            pl.BlockSpec(
+                (1, stop_count, block_order, column_count), lambda k, sl, bd: (k, 0, 0, 0)),
+            pl.BlockSpec((1, block_order, vector_count), lambda k, sl, bd: (k, 0, 0)),
+        ],
         scratch_shapes=[
             pltpu.VMEM((window_slots, block_order, column_count), jnp.float32),
             pltpu.VMEM((block_order, stop_count * column_count), jnp.bfloat16),
         ],
     )
-    hamiltonian = pl.pallas_call(
+    hamiltonian, early_value = pl.pallas_call(
         kernel,
         grid_spec=grid_spec,
-        out_shape=jax.ShapeDtypeStruct(
-            (fine_dev, stop_count, block_order, column_count), jnp.bfloat16),
+        out_shape=[
+            jax.ShapeDtypeStruct((fine_dev, stop_count, block_order, column_count), jnp.bfloat16),
+            jax.ShapeDtypeStruct((fine_dev, block_order, vector_count), jnp.float32),
+        ],
         compiler_params=pltpu.CompilerParams(
             dimension_semantics=("arbitrary",), vmem_limit_bytes=48 * 1024 * 1024),
         cost_estimate=pl.CostEstimate(
             flops=2 * fine_dev * block_order * block_order * column_count * (window_slots + stop_count),
             transcendentals=0,
             bytes_accessed=2 * fine_dev * block_order * (block_order + stop_count * column_count)),
-    )(slot_index, band_index, weights, halo, coarse_kernel, intersection, intersection)
+    )(slot_index, band_index, weights, halo, coarse_kernel, intersection, intersection,
+      first, second, last)
     partial_value = pl.pallas_call(
-        functools.partial(product_kernel, stop_count=stop_count),
+        product_kernel,
         grid=(fine_dev,),
         in_specs=[
             pl.BlockSpec((1, stop_count, block_order, column_count), lambda k: (k, 0, 0, 0)),
-        ] + [pl.BlockSpec((1, column_count, vector_count), lambda k: (k, 0, 0))] * stop_count,
+            pl.BlockSpec((1, block_order, vector_count), lambda k: (k, 0, 0)),
+            pl.BlockSpec((4, 1, column_count, vector_count), lambda k: (0, k, 0, 0)),
+        ],
         out_specs=pl.BlockSpec((1, block_order, vector_count), lambda k: (k, 0, 0)),
         out_shape=jax.ShapeDtypeStruct((fine_dev, block_order, vector_count), jnp.float32),
         cost_estimate=pl.CostEstimate(
             flops=2 * fine_dev * stop_count * block_order * column_count * vector_count,
             transcendentals=0,
             bytes_accessed=2 * fine_dev * stop_count * block_order * column_count),
-    )(hamiltonian, *sources)
+    )(hamiltonian, early_value, third)
     row_block = block_order // band_count
     halves = partial_value.reshape(fine_dev, 2, 2, row_block, vector_count)
     send = lax.dynamic_index_in_dim(halves, 1 - core, 2, keepdims=False)

time: 112 us -> 105 us (0.938)
  waiting for transfers between devices: 44.9 us -> 38.4 us
  starting transfers between devices: 23.6 us -> 20.1 us
  other arithmetic: 6.9 us -> 8.47 us
  Pallas kernels: 29 us -> 30.5 us
    ppermute x4, waiting for transfers between devices: 37.2 us -> 17 us  [shifted(): return lax.ppermute(value, axis, pairs)]
    ppermute x1, waiting for transfers between devices: 0.01 us -> 13.6 us  [on_device(): near = lax.ppermute(coarse_kernel, ('blk', 'band'), pairs)]
    ppermute x4, starting transfers between devices: 8.21 us -> 1.02 us  [shifted(): return lax.ppermute(value, axis, pairs)]
    ppermute x1, starting transfers between devices: 2.37 us -> 6.24 us  [on_device(): far = lax.ppermute(near, 'band', [(b, b ^ 1) for b in range(band_count)])]
    ppermute x2, starting transfers between devices: 7.23 us -> 3.4 us  [on_device(): lax.ppermute(send.astype(jnp.bfloat16), 'band', swap).astype(jnp.float32)]
    ppermute x1, starting transfers between devices: 5.75 us -> 9.47 us  [on_device(): near = lax.ppermute(coarse_kernel, ('blk', 'band'), pairs)]
    squeeze x2 -> x0, local copies, waits for them, and re-layouts: 1.84 us -> none  [the longest x1 1 us: on_device(): third[3]]
    pallas_call x2, Pallas kernels: 29 us -> 30.5 us  [the longest x1 22.2 us: on_device(): pl.pallas_call(kernel, grid_spec=grid_spec, out_shape=[jax.ShapeDtypeStru...]
  transfers between devices with their start and end apart: 8 -> 8, of which waited for: 5 -> 5; matrix products, arithmetic and copies ran while one was open for 8% -> 9% of each run, Pallas kernels for 18% -> 21%
where the time goes in v10:
time: 105 us; the launch traced here: 104 us
  waiting for transfers between devices  38.4 us (37%)
  Pallas kernels  30.5 us (29%)
  starting transfers between devices  20.1 us (19%)
  other arithmetic  8.47 us (8%)
  local copies, waits for them, and re-layouts  5.91 us (6%)
    pallas_call x1, Pallas kernels, on_device(): pl.pallas_call(kernel, grid_spec=grid_spec, out_shape=[jax.ShapeDtypeStru...  22.2 us
    ppermute x4, waiting for transfers between devices, shifted(): return lax.ppermute(value, axis, pairs)  17 us
    ppermute x1, waiting for transfers between devices, on_device(): near = lax.ppermute(coarse_kernel, ('blk', 'band'), pairs)  13.6 us
    ppermute x1, starting transfers between devices, on_device(): near = lax.ppermute(coarse_kernel, ('blk', 'band'), pairs)  9.47 us
    pallas_call x1, Pallas kernels, on_device(): pl.pallas_call(product_kernel, grid=(fine_dev,), in_specs=[pl.BlockSpec((...  8.33 us
    ppermute x2, waiting for transfers between devices, on_device(): lax.ppermute(send.astype(jnp.bfloat16), 'band', swap).astype(jnp.float32)  7.74 us
    ppermute x1, starting transfers between devices, on_device(): far = lax.ppermute(near, 'band', [(b, b ^ 1) for b in range(band_count)])  6.24 us
    ppermute x2, starting transfers between devices, on_device(): lax.ppermute(send.astype(jnp.bfloat16), 'band', swap).astype(jnp.float32)  3.4 us
  transfers between devices with their start and end apart: 8, of which 5 were waited for; matrix products, arithmetic and copies ran while one was open for 9% of the time, Pallas kernels for 21%

profile of v10, /device:TPU:1, one launch (start us, length us, event | category | flops | bytes accessed | tf_op | source)
XLA Modules:
  0.0 104.1 jit_solution(414415788429209499)
XLA Ops:
  0.6 9.5 %collective-permute-start = (bf16[2,512,512]{2,1,0:T(8,128)(2,1)}, bf16[2,512,512]{2,1,0:T(8,128)(2,1)S(1)}, u32[]{:S(2)}, u32[]{:S(2)}) collective-permute-start(bf16[2,512,512]{2,1,0:T(8,128)(2,1)} %local_ref.1), channel_id=1, source_target_pairs={{0,4},{1,125},{2,6},{3,127},{4,8},{5,1},{6,10},{7,3},{8,12},{9,5},... | collective-permute-start | bytes 3145736 | tf_op jit(solution)/shard_map/ppermute | solution.py:78
  10.1 0.7 compare_select_fusion
  10.8 0.8 copy.10
  11.6 0.7 compare_and_fusion
  12.2 13.6 %collective-permute-done = bf16[2,512,512]{2,1,0:T(8,128)(2,1)S(1)} collective-permute-done((bf16[2,512,512]{2,1,0:T(8,128)(2,1)}, bf16[2,512,512]{2,1,0:T(8,128)(2,1)S(1)}, u32[]{:S(2)}, u32[]{:S(2)}) %collective-permute-start) | collective-permute-done | bytes 1048608 | tf_op jit(solution)/shard_map/ppermute | solution.py:78
  25.8 6.2 %collective-permute-start.1 = (bf16[2,512,512]{2,1,0:T(8,128)(2,1)S(1)}, bf16[2,512,512]{2,1,0:T(8,128)(2,1)}, u32[]{:S(2)}, u32[]{:S(2)}) collective-permute-start(bf16[2,512,512]{2,1,0:T(8,128)(2,1)S(1)} %collective-permute-done), channel_id=1, source_target_pairs={{0,1},{1,0},{2,3},{3,2},{4,5},{5,4},{6,7},{7,6},{8,9},{9,8},{10,11... | collective-permute-start | bytes 3145736 | tf_op jit(solution)/shard_map/ppermute | solution.py:79
  32.1 1.0 pad_maximum_fusion.2
  33.1 0.9 collective-permute-start.3
  34.9 0.8 copy.12
  35.7 0.6 gather_fusion.1
  36.4 16.3 %collective-permute-done.3.second_ref = bf16[2,8,128,128]{3,2,1,0:T(8,128)(2,1)S(1)} collective-permute-done((bf16[2,8,128,128]{3,2,1,0:T(8,128)(2,1)S(1)}, bf16[2,8,128,128]{3,2,1,0:T(8,128)(2,1)S(1)}, u32[]{:S(2)}, u32[]{:S(2)}) %collective-permute-start.3) | collective-permute-done | bytes 524320 | tf_op jit(solution)/shard_map/ppermute | solution.py:14
  52.7 1.1 %pad_maximum_fusion.1 = bf16[4,8,128,128]{3,2,1,0:T(8,128)(2,1)S(1)} fusion(bf16[2,8,128,128]{3,2,1,0:T(8,128)(2,1)S(1)} %collective-permute-done.3.second_ref, bf16[1,8,128,128]{3,2,1,0:T(8,128)(2,1)S(1)} %bitcast.19, bf16[1,8,128,128]{3,2,1,0:T(8,128)(2,1)} %bitcast.23), kind=kLoop, calls=%fused_computation.3 | loop fusion | flops 1048576 | bytes 2097152 | tf_op jit(solution)/shard_map/stack | solution.py:85
  54.1 2.8 %pad_maximum_fusion.halo_ref = bf16[4,512,512]{2,1,0:T(8,128)(2,1)} fusion(bf16[2,512,512]{2,1,0:T(8,128)(2,1)} %collective-permute-done.1, bf16[2,512,512]{2,1,0:T(8,128)(2,1)S(1)} %collective-permute-done), kind=kLoop, calls=%fused_computation.2 | loop fusion | flops 1048576 | bytes 4194304 | tf_op jit(solution)/shard_map/concatenate | solution.py:80
  57.0 22.2 %shard_map.77 = (bf16[8,8,512,128]{3,2,1,0:T(8,128)(2,1)}, f32[8,512,128]{2,1,0:T(8,128)S(1)}) custom-call(s32[256]{0:T(256)S(1)} %fusion.5.slot_ref, s32[1]{0:T(128)} %bitcast.1.band_ref, f32[256]{0:T(256)S(1)} %select_n.82.weight_ref, bf16[4,512,512]{2,1,0:T(8,128)(2,1)} %pad_maximum_fusion.halo_ref, bf16[2,512,512]{2,1,0:T(8,128)(2,1)S(1)} %copy-done.1, ...), custom_call_target="tpu_custom_call" | custom-call | flops 7516192768 | bytes 12582912 | tf_op jit(solution)/shard_map/pallas_call | solution.py:123
  79.1 1.3 %copy-done = f32[8,512,128]{2,1,0:T(8,128)} copy-done((f32[8,512,128]{2,1,0:T(8,128)}, f32[8,512,128]{2,1,0:T(8,128)S(1)}, u32[]{:S(2)}) %copy-start) | copy-done | bytes 2097176
  80.5 0.7 collective-permute-done.5.third_ref
  81.2 8.3 %shard_map.78 = f32[8,512,128]{2,1,0:T(8,128)} custom-call(bf16[8,8,512,128]{3,2,1,0:T(8,128)(2,1)} %get-tuple-element.2.ham_ref, f32[8,512,128]{2,1,0:T(8,128)} %copy-done, bf16[4,8,128,128]{3,2,1,0:T(8,128)(2,1)} %collective-permute-done.5.third_ref), custom_call_target="tpu_custom_call" | custom-call | flops 1073741824 | bytes 8388608 | tf_op jit(solution)/shard_map/pallas_call | solution.py:138
  89.5 1.3 %fusion = bf16[8,2,128,128]{3,2,0,1:T(8,128)(2,1)S(1)} fusion(f32[8,2,2,128,128]{4,3,2,1,0:T(8,128)} %bitcast.20, s32[]{:T(128)S(6)} %select_n.84), kind=kLoop, calls=%fused_computation.6 | loop fusion | bytes 1048580 | tf_op jit(solution)/shard_map/convert_element_type | solution.py:158
  90.8 2.0 %collective-permute-start.6 = (bf16[8,2,128,128]{3,2,0,1:T(8,128)(2,1)S(1)}, bf16[8,2,128,128]{3,2,0,1:T(8,128)(2,1)S(1)}, u32[]{:S(2)}, u32[]{:S(2)}) collective-permute-start(bf16[8,2,128,128]{3,2,0,1:T(8,128)(2,1)S(1)} %fusion), channel_id=1, source_target_pairs={{0,1},{1,0},{2,3},{3,2},{4,5},{5,4},{6,7},{7,6},{8,9},{9,8},{10,11... | collective-permute-start | bytes 1572872 | tf_op jit(solution)/shard_map/ppermute | solution.py:158
  92.8 1.5 %collective-permute-done.6 = bf16[8,2,128,128]{3,2,0,1:T(8,128)(2,1)S(1)} collective-permute-done((bf16[8,2,128,128]{3,2,0,1:T(8,128)(2,1)S(1)}, bf16[8,2,128,128]{3,2,0,1:T(8,128)(2,1)S(1)}, u32[]{:S(2)}, u32[]{:S(2)}) %collective-permute-start.6) | collective-permute-done | bytes 524320 | tf_op jit(solution)/shard_map/ppermute | solution.py:158
  94.4 1.3 %bitcast_add_fusion = f32[8,2,128,128]{3,2,0,1:T(8,128)S(1)} fusion(bf16[8,2,128,128]{3,2,0,1:T(8,128)(2,1)S(1)} %collective-permute-done.6, f32[8,2,2,128,128]{4,3,2,1,0:T(8,128)} %bitcast.21, s32[]{:T(128)S(6)} %select_n.83), kind=kLoop, calls=%fused_computation.5 | loop fusion | flops 524288 | bytes 2621444 | tf_op jit(solution)/shard_map/add | solution.py:158
  95.8 1.4 %collective-permute-start.7 = (bf16[8,128,128]{2,1,0:T(8,128)(2,1)S(1)}, bf16[8,128,128]{2,1,0:T(8,128)(2,1)S(1)}, u32[]{:S(2)}, u32[]{:S(2)}) collective-permute-start(bf16[8,128,128]{2,1,0:T(8,128)(2,1)S(1)} %fusion.2), channel_id=1, source_target_pairs={{0,2},{1,3},{2,0},{3,1},{4,6},{5,7},{6,4},{7,5},{8,10},{9,11},{10,... | collective-permute-start | bytes 786440 | tf_op jit(solution)/shard_map/ppermute | solution.py:164
  97.1 6.2 %collective-permute-done.7 = bf16[8,128,128]{2,1,0:T(8,128)(2,1)S(1)} collective-permute-done((bf16[8,128,128]{2,1,0:T(8,128)(2,1)S(1)}, bf16[8,128,128]{2,1,0:T(8,128)(2,1)S(1)}, u32[]{:S(2)}, u32[]{:S(2)}) %collective-permute-start.7) | collective-permute-done | bytes 262176 | tf_op jit(solution)/shard_map/ppermute | solution.py:164
  103.3 0.8 fusion.1
  (19 shorter events, 1.4 us)
Async XLA Ops:
  0.6 25.2 %collective-permute-start = (bf16[2,512,512]{2,1,0:T(8,128)(2,1)}, bf16[2,512,512]{2,1,0:T(8,128)(2,1)S(1)}, u32[]{:S(2)}, u32[]{:S(2)}) collective-permute-start(bf16[2,512,512]{2,1,0:T(8,128)(2,1)} %local_ref.1), channel_id=1, source_target_pairs={{0,4},{1,125},{2,6},{3,127},{4,8},{5,1},{6,10},{7,3},{8,12},{9,5},... | collective-permute-start | bytes 3145736 | tf_op jit(solution)/shard_map/ppermute | solution.py:78
  10.1 22.0 %collective-permute-start.2 = (bf16[8,128,128]{2,1,0:T(8,128)(2,1)}, bf16[8,128,128]{2,1,0:T(8,128)(2,1)S(1)}, u32[]{:S(2)}, u32[]{:S(2)}) collective-permute-start(bf16[8,128,128]{2,1,0:T(8,128)(2,1)} %param.11), channel_id=1, source_target_pairs={{0,4},{4,8},{8,12},{12,16},{16,20},{20,24},{24,28},{28,32},{32,36}... | collective-permute-start | bytes 786440 | tf_op jit(solution)/shard_map/ppermute | solution.py:14
  10.1 46.9 %collective-permute-start.4 = (bf16[8,128,128]{2,1,0:T(8,128)(2,1)}, bf16[8,128,128]{2,1,0:T(8,128)(2,1)S(1)}, u32[]{:S(2)}, u32[]{:S(2)}) collective-permute-start(bf16[8,128,128]{2,1,0:T(8,128)(2,1)} %param.11), channel_id=1, source_target_pairs={{0,32},{4,36},{8,40},{12,44},{16,48},{20,52},{24,56},{28,60},{32,6... | collective-permute-start | bytes 786440 | tf_op jit(solution)/shard_map/ppermute | solution.py:14
  25.8 28.3 %collective-permute-start.1 = (bf16[2,512,512]{2,1,0:T(8,128)(2,1)S(1)}, bf16[2,512,512]{2,1,0:T(8,128)(2,1)}, u32[]{:S(2)}, u32[]{:S(2)}) collective-permute-start(bf16[2,512,512]{2,1,0:T(8,128)(2,1)S(1)} %collective-permute-done), channel_id=1, source_target_pairs={{0,1},{1,0},{2,3},{3,2},{4,5},{5,4},{6,7},{7,6},{8,9},{9,8},{10,11... | collective-permute-start | bytes 3145736 | tf_op jit(solution)/shard_map/ppermute | solution.py:79
  33.1 19.6 %collective-permute-start.3 = (bf16[2,8,128,128]{3,2,1,0:T(8,128)(2,1)S(1)}, bf16[2,8,128,128]{3,2,1,0:T(8,128)(2,1)S(1)}, u32[]{:S(2)}, u32[]{:S(2)}) collective-permute-start(bf16[2,8,128,128]{3,2,1,0:T(8,128)(2,1)S(1)} %pad_maximum_fusion.2), channel_id=1, source_target_pairs={{0,8},{4,12},{8,16},{12,20},{16,24},{20,28},{24,32},{28,36},{32,40... | collective-permute-start | bytes 1572872 | tf_op jit(solution)/shard_map/ppermute | solution.py:14
  53.7 27.4 %collective-permute-start.5 = (bf16[4,8,128,128]{3,2,1,0:T(8,128)(2,1)S(1)}, bf16[4,8,128,128]{3,2,1,0:T(8,128)(2,1)}, u32[]{:S(2)}, u32[]{:S(2)}) collective-permute-start(bf16[4,8,128,128]{3,2,1,0:T(8,128)(2,1)S(1)} %pad_maximum_fusion.1), channel_id=1, source_target_pairs={{0,16},{4,20},{8,24},{12,28},{16,32},{20,36},{24,40},{28,44},{32,4... | collective-permute-start | bytes 3145736 | tf_op jit(solution)/shard_map/ppermute | solution.py:14
  54.1 2.9 %copy-start.1 = (bf16[2,512,512]{2,1,0:T(8,128)(2,1)S(1)}, bf16[2,512,512]{2,1,0:T(8,128)(2,1)}, u32[]{:S(2)}) copy-start(bf16[2,512,512]{2,1,0:T(8,128)(2,1)} %local_ref.1) | copy-start | bytes 3145732
  79.1 1.3 %copy-start = (f32[8,512,128]{2,1,0:T(8,128)}, f32[8,512,128]{2,1,0:T(8,128)S(1)}, u32[]{:S(2)}) copy-start(f32[8,512,128]{2,1,0:T(8,128)S(1)} %get-tuple-element.5.early_ref) | copy-start | bytes 6291460
  90.8 3.6 %collective-permute-start.6 = (bf16[8,2,128,128]{3,2,0,1:T(8,128)(2,1)S(1)}, bf16[8,2,128,128]{3,2,0,1:T(8,128)(2,1)S(1)}, u32[]{:S(2)}, u32[]{:S(2)}) collective-permute-start(bf16[8,2,128,128]{3,2,0,1:T(8,128)(2,1)S(1)} %fusion), channel_id=1, source_target_pairs={{0,1},{1,0},{2,3},{3,2},{4,5},{5,4},{6,7},{7,6},{8,9},{9,8},{10,11... | collective-permute-start | bytes 1572872 | tf_op jit(solution)/shard_map/ppermute | solution.py:158
  95.8 7.6 %collective-permute-start.7 = (bf16[8,128,128]{2,1,0:T(8,128)(2,1)S(1)}, bf16[8,128,128]{2,1,0:T(8,128)(2,1)S(1)}, u32[]{:S(2)}, u32[]{:S(2)}) collective-permute-start(bf16[8,128,128]{2,1,0:T(8,128)(2,1)S(1)} %fusion.2), channel_id=1, source_target_pairs={{0,2},{1,3},{2,0},{3,1},{4,6},{5,7},{6,4},{7,5},{8,10},{9,11},{10,... | collective-permute-start | bytes 786440 | tf_op jit(solution)/shard_map/ppermute | solution.py:164

commit v11 on v10

--- a/solution.py
+++ b/solution.py
@@ -15,7 +15,8 @@
 
 
 def sandwich_kernel(slot_ref, band_ref, weight_ref, halo_ref, local_ref, inter_ref, right_ref,
-                    first_ref, second_ref, last_ref, ham_ref, early_ref, prod_ref, rot_ref,
+                    first_ref, second_ref, third_ref, fourth_ref, ham_ref, early_ref, prod_ref,
+                    rot_ref,
                     *, blocks_dev, stop_count, corner_count):
     k = pl.program_id(0)
     column_count = right_ref.shape[2]
@@ -40,18 +41,15 @@
         for s in range(half):
             ham_ref[0, part * half + s] = ham[:, s * column_count:(s + 1) * column_count]
         if part == 0:
-            tall = jnp.concatenate([first_ref[0], second_ref[0, 0], second_ref[1, 0]], axis=0)
-            early = jnp.dot(ham[:, :3 * column_count], tall, preferred_element_type=jnp.float32)
-        else:
-            early = early + jnp.dot(ham[:, (half - 1) * column_count:], last_ref[0],
-                                    preferred_element_type=jnp.float32)
-    early_ref[0] = early
+            tall = jnp.concatenate(
+                [first_ref[0], second_ref[0], third_ref[0], fourth_ref[0]], axis=0)
+            early_ref[0] = jnp.dot(ham, tall, preferred_element_type=jnp.float32)
 
 
-def product_kernel(ham_ref, early_ref, third_ref, part_ref):
-    count = third_ref.shape[0]
-    wide = jnp.concatenate([ham_ref[0, 3 + s] for s in range(count)], axis=1)
-    tall = jnp.concatenate([third_ref[s, 0] for s in range(count)], axis=0)
+def product_kernel(ham_ref, early_ref, late_ref, part_ref):
+    count = late_ref.shape[0]
+    wide = jnp.concatenate([ham_ref[0, s] for s in range(count)], axis=1)
+    tall = jnp.concatenate([late_ref[s, 0] for s in range(count)], axis=0)
     part_ref[0] = early_ref[0] + jnp.dot(wide, tall, preferred_element_type=jnp.float32)
 
 
@@ -80,9 +78,10 @@
     halo = jnp.concatenate([near, far], axis=0)
     assert stop_count == 8
     first = shifted(trial_vectors, "blk", 1)
-    last = shifted(trial_vectors, "blk", 8)
-    second = shifted(jnp.stack([trial_vectors, first]), "blk", 2)
-    third = shifted(jnp.stack([trial_vectors, first, second[0], second[1]]), "blk", 4)
+    second = shifted(trial_vectors, "blk", 2)
+    fourth = shifted(trial_vectors, "blk", 4)
+    third = shifted(second, "blk", 1)
+    late = shifted(jnp.stack([first, second, third, fourth]), "blk", 4)
 
     order_index = jnp.take(interp_index, stop_order, axis=1)
     order_weight = jnp.take(interp_weight, stop_order, axis=1)
@@ -106,10 +105,7 @@
             pl.BlockSpec((blocks_dev, block_order, block_order), lambda k, sl, bd: (0, 0, 0)),
             pl.BlockSpec((1, block_order, block_order), lambda k, sl, bd: (k, 0, 0)),
             pl.BlockSpec((1, block_order, column_count), lambda k, sl, bd: (k, 0, bd[0])),
-            pl.BlockSpec((1, column_count, vector_count), lambda k, sl, bd: (k, 0, 0)),
-            pl.BlockSpec((2, 1, column_count, vector_count), lambda k, sl, bd: (0, k, 0, 0)),
-            pl.BlockSpec((1, column_count, vector_count), lambda k, sl, bd: (k, 0, 0)),
-        ],
+        ] + [pl.BlockSpec((1, column_count, vector_count), lambda k, sl, bd: (k, 0, 0))] * 4,
         out_specs=[
             pl.BlockSpec(
                 (1, stop_count, block_order, column_count), lambda k, sl, bd: (k, 0, 0, 0)),
@@ -134,14 +130,14 @@
             transcendentals=0,
             bytes_accessed=2 * fine_dev * block_order * (block_order + stop_count * column_count)),
     )(slot_index, band_index, weights, halo, coarse_kernel, intersection, intersection,
-      first, second, last)
+      first, second, third, fourth)
     partial_value = pl.pallas_call(
         product_kernel,
         grid=(fine_dev,),
         in_specs=[
-            pl.BlockSpec((1, stop_count, block_order, column_count), lambda k: (k, 0, 0, 0)),
+            pl.BlockSpec((1, stop_count // 2, block_order, column_count), lambda k: (k, 1, 0, 0)),
             pl.BlockSpec((1, block_order, vector_count), lambda k: (k, 0, 0)),
-            pl.BlockSpec((4, 1, column_count, vector_count), lambda k: (0, k, 0, 0)),
+            pl.BlockSpec((stop_count // 2, 1, column_count, vector_count), lambda k: (0, k, 0, 0)),
         ],
         out_specs=pl.BlockSpec((1, block_order, vector_count), lambda k: (k, 0, 0)),
         out_shape=jax.ShapeDtypeStruct((fine_dev, block_order, vector_count), jnp.float32),
@@ -149,7 +145,7 @@
             flops=2 * fine_dev * stop_count * block_order * column_count * vector_count,
             transcendentals=0,
             bytes_accessed=2 * fine_dev * stop_count * block_order * column_count),
-    )(hamiltonian, early_value, third)
+    )(hamiltonian, early_value, late)
     row_block = block_order // band_count
     halves = partial_value.reshape(fine_dev, 2, 2, row_block, vector_count)
     send = lax.dynamic_index_in_dim(halves, 1 - core, 2, keepdims=False)

time: 105 us -> 108 us (1.029)
  starting transfers between devices: 20.1 us -> 26.9 us
  other arithmetic: 8.47 us -> 5.24 us
  waiting for transfers between devices: 38.4 us -> 36.8 us
    ppermute x1, starting transfers between devices: 6.24 us -> 12.5 us  [on_device(): far = lax.ppermute(near, 'band', [(b, b ^ 1) for b in range(band_count)])]
    ppermute x4 -> x5, waiting for transfers between devices: 17 us -> 13.3 us  [shifted(): return lax.ppermute(value, axis, pairs)]
    another operation x2 -> x1, other arithmetic: 2.05 us -> 0.13 us  [on_device(): late = shifted(jnp.stack([first, second, third, fourth]), 'blk', 4)]
    ppermute x1, waiting for transfers between devices: 13.6 us -> 15.1 us  [on_device(): near = lax.ppermute(coarse_kernel, ('blk', 'band'), pairs)]
    concatenate x1, other arithmetic: 2.83 us -> 1.51 us  [on_device(): halo = jnp.concatenate([near, far], axis=0)]
    ppermute x4 -> x5, starting transfers between devices: 1.02 us -> 2.15 us  [shifted(): return lax.ppermute(value, axis, pairs)]
    unnamed x6 -> x8, local copies, waits for them, and re-layouts: 2.93 us -> 3.89 us
  transfers between devices with their start and end apart: 8 -> 9, of which waited for: 5 -> 5; matrix products, arithmetic and copies ran while one was open for 9% -> 6% of each run, Pallas kernels for 21% -> 22%
where the time goes in v11:
time: 108 us; the launch traced here: 107 us
  waiting for transfers between devices  36.8 us (34%)
  Pallas kernels  30.7 us (28%)
  starting transfers between devices  26.9 us (25%)
  local copies, waits for them, and re-layouts  6.88 us (6%)
  other arithmetic  5.24 us (5%)
    pallas_call x1, Pallas kernels, on_device(): pl.pallas_call(kernel, grid_spec=grid_spec, out_shape=[jax.ShapeDtypeStru...  23.1 us
    ppermute x1, waiting for transfers between devices, on_device(): near = lax.ppermute(coarse_kernel, ('blk', 'band'), pairs)  15.1 us
    ppermute x5, waiting for transfers between devices, shifted(): return lax.ppermute(value, axis, pairs)  13.3 us
    ppermute x1, starting transfers between devices, on_device(): far = lax.ppermute(near, 'band', [(b, b ^ 1) for b in range(band_count)])  12.5 us
    ppermute x1, starting transfers between devices, on_device(): near = lax.ppermute(coarse_kernel, ('blk', 'band'), pairs)  9.47 us
    ppermute x2, waiting for transfers between devices, on_device(): lax.ppermute(send.astype(jnp.bfloat16), 'band', swap).astype(jnp.float32)  8.35 us
    pallas_call x1, Pallas kernels, on_device(): pl.pallas_call(product_kernel, grid=(fine_dev,), in_specs=[pl.BlockSpec((...  7.58 us
    unnamed x8, local copies, waits for them, and re-layouts  3.89 us
  transfers between devices with their start and end apart: 9, of which 5 were waited for; matrix products, arithmetic and copies ran while one was open for 6% of the time, Pallas kernels for 22%

profile of v11, /device:TPU:1, one launch (start us, length us, event | category | flops | bytes accessed | tf_op | source)
XLA Modules:
  0.0 107.2 jit_solution(13238312902673824768)
XLA Ops:
  0.6 9.5 %collective-permute-start = (bf16[2,512,512]{2,1,0:T(8,128)(2,1)}, bf16[2,512,512]{2,1,0:T(8,128)(2,1)S(1)}, u32[]{:S(2)}, u32[]{:S(2)}) collective-permute-start(bf16[2,512,512]{2,1,0:T(8,128)(2,1)} %local_ref.1), channel_id=1, source_target_pairs={{0,4},{1,125},{2,6},{3,127},{4,8},{5,1},{6,10},{7,3},{8,12},{9,5},... | collective-permute-start | bytes 3145736 | tf_op jit(solution)/shard_map/ppermute | solution.py:76
  10.1 0.7 compare_select_fusion
  10.8 15.1 %collective-permute-done = bf16[2,512,512]{2,1,0:T(8,128)(2,1)S(1)} collective-permute-done((bf16[2,512,512]{2,1,0:T(8,128)(2,1)}, bf16[2,512,512]{2,1,0:T(8,128)(2,1)S(1)}, u32[]{:S(2)}, u32[]{:S(2)}) %collective-permute-start) | collective-permute-done | bytes 1048608 | tf_op jit(solution)/shard_map/ppermute | solution.py:76
  25.9 12.5 %collective-permute-start.1 = (bf16[2,512,512]{2,1,0:T(8,128)(2,1)S(1)}, bf16[2,512,512]{2,1,0:T(8,128)(2,1)S(1)}, u32[]{:S(2)}, u32[]{:S(2)}) collective-permute-start(bf16[2,512,512]{2,1,0:T(8,128)(2,1)S(1)} %collective-permute-done), channel_id=1, source_target_pairs={{0,1},{1,0},{2,3},{3,2},{4,5},{5,4},{6,7},{7,6},{8,9},{9,8},{10,11... | collective-permute-start | bytes 3145736 | tf_op jit(solution)/shard_map/ppermute | solution.py:77
  38.4 0.8 copy.10
  39.2 0.6 gather_fusion
  39.8 0.7 compare_and_fusion
  40.4 2.1 %collective-permute-start.4 = (bf16[8,128,128]{2,1,0:T(8,128)(2,1)S(1)}, bf16[8,128,128]{2,1,0:T(8,128)(2,1)S(1)}, u32[]{:S(2)}, u32[]{:S(2)}) collective-permute-start(bf16[8,128,128]{2,1,0:T(8,128)(2,1)S(1)} %collective-permute-done.3.second_ref), channel_id=1, source_target_pairs={{0,4},{4,8},{8,12},{12,16},{16,20},{20,24},{24,28},{28,32},{32,36}... | collective-permute-start | bytes 786440 | tf_op jit(solution)/shard_map/ppermute | solution.py:14
  42.8 0.8 copy.12
  43.6 0.6 gather_fusion.1
  44.5 12.1 %collective-permute-done.4.third_ref = bf16[8,128,128]{2,1,0:T(8,128)(2,1)S(1)} collective-permute-done((bf16[8,128,128]{2,1,0:T(8,128)(2,1)S(1)}, bf16[8,128,128]{2,1,0:T(8,128)(2,1)S(1)}, u32[]{:S(2)}, u32[]{:S(2)}) %collective-permute-start.4) | collective-permute-done | bytes 262176 | tf_op jit(solution)/shard_map/ppermute | solution.py:14
  56.8 1.5 %pad_maximum_fusion.halo_ref = bf16[4,512,512]{2,1,0:T(8,128)(2,1)} fusion(bf16[2,512,512]{2,1,0:T(8,128)(2,1)S(1)} %collective-permute-done.1, bf16[2,512,512]{2,1,0:T(8,128)(2,1)S(1)} %collective-permute-done), kind=kLoop, calls=%fused_computation.2 | loop fusion | flops 1048576 | bytes 4194304 | tf_op jit(solution)/shard_map/concatenate | solution.py:78
  58.4 23.1 %shard_map.77 = (bf16[8,8,512,128]{3,2,1,0:T(8,128)(2,1)}, f32[8,512,128]{2,1,0:T(8,128)S(1)}) custom-call(s32[256]{0:T(256)S(1)} %fusion.5.slot_ref, s32[1]{0:T(128)} %bitcast.1.band_ref, f32[256]{0:T(256)S(1)} %select_n.82.weight_ref, bf16[4,512,512]{2,1,0:T(8,128)(2,1)} %pad_maximum_fusion.halo_ref, bf16[2,512,512]{2,1,0:T(8,128)(2,1)S(1)} %copy-done.1, ...), custom_call_target="tpu_custom_call" | custom-call | flops 7516192768 | bytes 12582912 | tf_op jit(solution)/shard_map/pallas_call | solution.py:119
  81.4 1.3 %copy-done = f32[8,512,128]{2,1,0:T(8,128)} copy-done((f32[8,512,128]{2,1,0:T(8,128)}, f32[8,512,128]{2,1,0:T(8,128)S(1)}, u32[]{:S(2)}) %copy-start) | copy-done | bytes 2097176
  82.8 1.3 %collective-permute-done.6.late_ref = bf16[4,8,128,128]{3,2,1,0:T(8,128)(2,1)S(1)} collective-permute-done((bf16[4,8,128,128]{3,2,1,0:T(8,128)(2,1)S(1)}, bf16[4,8,128,128]{3,2,1,0:T(8,128)(2,1)S(1)}, u32[]{:S(2)}, u32[]{:S(2)}) %collective-permute-start.6) | collective-permute-done | bytes 1048608 | tf_op jit(solution)/shard_map/ppermute | solution.py:14
  84.0 1.0 copy-done.2
  85.0 7.6 %shard_map.78 = f32[8,512,128]{2,1,0:T(8,128)} custom-call(bf16[8,8,512,128]{3,2,1,0:T(8,128)(2,1)} %get-tuple-element.2.ham_ref, f32[8,512,128]{2,1,0:T(8,128)} %copy-done, bf16[4,8,128,128]{3,2,1,0:T(8,128)(2,1)} %copy-done.2), custom_call_target="tpu_custom_call" | custom-call | flops 1073741824 | bytes 8388608 | tf_op jit(solution)/shard_map/pallas_call | solution.py:134
  92.6 1.3 %fusion = bf16[8,2,128,128]{3,2,0,1:T(8,128)(2,1)S(1)} fusion(f32[8,2,2,128,128]{4,3,2,1,0:T(8,128)} %bitcast.24, s32[]{:T(128)S(6)} %select_n.84), kind=kLoop, calls=%fused_computation.6 | loop fusion | bytes 1048580 | tf_op jit(solution)/shard_map/convert_element_type | solution.py:154
  93.9 2.0 %collective-permute-start.7 = (bf16[8,2,128,128]{3,2,0,1:T(8,128)(2,1)S(1)}, bf16[8,2,128,128]{3,2,0,1:T(8,128)(2,1)S(1)}, u32[]{:S(2)}, u32[]{:S(2)}) collective-permute-start(bf16[8,2,128,128]{3,2,0,1:T(8,128)(2,1)S(1)} %fusion), channel_id=1, source_target_pairs={{0,1},{1,0},{2,3},{3,2},{4,5},{5,4},{6,7},{7,6},{8,9},{9,8},{10,11... | collective-permute-start | bytes 1572872 | tf_op jit(solution)/shard_map/ppermute | solution.py:154
  95.9 1.5 %collective-permute-done.7 = bf16[8,2,128,128]{3,2,0,1:T(8,128)(2,1)S(1)} collective-permute-done((bf16[8,2,128,128]{3,2,0,1:T(8,128)(2,1)S(1)}, bf16[8,2,128,128]{3,2,0,1:T(8,128)(2,1)S(1)}, u32[]{:S(2)}, u32[]{:S(2)}) %collective-permute-start.7) | collective-permute-done | bytes 524320 | tf_op jit(solution)/shard_map/ppermute | solution.py:154
  97.5 1.3 %bitcast_add_fusion = f32[8,2,128,128]{3,2,0,1:T(8,128)S(1)} fusion(bf16[8,2,128,128]{3,2,0,1:T(8,128)(2,1)S(1)} %collective-permute-done.7, f32[8,2,2,128,128]{4,3,2,1,0:T(8,128)} %bitcast.25, s32[]{:T(128)S(6)} %select_n.83), kind=kLoop, calls=%fused_computation.5 | loop fusion | flops 524288 | bytes 2621444 | tf_op jit(solution)/shard_map/add | solution.py:154
  98.9 0.8 collective-permute-start.8
  99.6 6.8 %collective-permute-done.8 = bf16[8,128,128]{2,1,0:T(8,128)(2,1)S(1)} collective-permute-done((bf16[8,128,128]{2,1,0:T(8,128)(2,1)S(1)}, bf16[8,128,128]{2,1,0:T(8,128)(2,1)S(1)}, u32[]{:S(2)}, u32[]{:S(2)}) %collective-permute-start.8) | collective-permute-done | bytes 262176 | tf_op jit(solution)/shard_map/ppermute | solution.py:160
  106.4 0.8 fusion.1
  (22 shorter events, 0.9 us)
Async XLA Ops:
  0.6 25.2 %collective-permute-start = (bf16[2,512,512]{2,1,0:T(8,128)(2,1)}, bf16[2,512,512]{2,1,0:T(8,128)(2,1)S(1)}, u32[]{:S(2)}, u32[]{:S(2)}) collective-permute-start(bf16[2,512,512]{2,1,0:T(8,128)(2,1)} %local_ref.1), channel_id=1, source_target_pairs={{0,4},{1,125},{2,6},{3,127},{4,8},{5,1},{6,10},{7,3},{8,12},{9,5},... | collective-permute-start | bytes 3145736 | tf_op jit(solution)/shard_map/ppermute | solution.py:76
  10.1 30.3 %collective-permute-start.3 = (bf16[8,128,128]{2,1,0:T(8,128)(2,1)}, bf16[8,128,128]{2,1,0:T(8,128)(2,1)S(1)}, u32[]{:S(2)}, u32[]{:S(2)}) collective-permute-start(bf16[8,128,128]{2,1,0:T(8,128)(2,1)} %param.11), channel_id=1, source_target_pairs={{0,8},{4,12},{8,16},{12,20},{16,24},{20,28},{24,32},{28,36},{32,40... | collective-permute-start | bytes 786440 | tf_op jit(solution)/shard_map/ppermute | solution.py:14
  10.1 34.4 %collective-permute-start.2 = (bf16[8,128,128]{2,1,0:T(8,128)(2,1)}, bf16[8,128,128]{2,1,0:T(8,128)(2,1)S(1)}, u32[]{:S(2)}, u32[]{:S(2)}) collective-permute-start(bf16[8,128,128]{2,1,0:T(8,128)(2,1)} %param.11), channel_id=1, source_target_pairs={{0,4},{4,8},{8,12},{12,16},{16,20},{20,24},{24,28},{28,32},{32,36}... | collective-permute-start | bytes 786440 | tf_op jit(solution)/shard_map/ppermute | solution.py:14
  10.1 34.4 %collective-permute-start.5 = (bf16[8,128,128]{2,1,0:T(8,128)(2,1)}, bf16[8,128,128]{2,1,0:T(8,128)(2,1)S(1)}, u32[]{:S(2)}, u32[]{:S(2)}) collective-permute-start(bf16[8,128,128]{2,1,0:T(8,128)(2,1)} %param.11), channel_id=1, source_target_pairs={{0,16},{4,20},{8,24},{12,28},{16,32},{20,36},{24,40},{28,44},{32,4... | collective-permute-start | bytes 786440 | tf_op jit(solution)/shard_map/ppermute | solution.py:14
  25.9 31.0 %collective-permute-start.1 = (bf16[2,512,512]{2,1,0:T(8,128)(2,1)S(1)}, bf16[2,512,512]{2,1,0:T(8,128)(2,1)S(1)}, u32[]{:S(2)}, u32[]{:S(2)}) collective-permute-start(bf16[2,512,512]{2,1,0:T(8,128)(2,1)S(1)} %collective-permute-done), channel_id=1, source_target_pairs={{0,1},{1,0},{2,3},{3,2},{4,5},{5,4},{6,7},{7,6},{8,9},{9,8},{10,11... | collective-permute-start | bytes 3145736 | tf_op jit(solution)/shard_map/ppermute | solution.py:77
  40.4 16.2 %collective-permute-start.4 = (bf16[8,128,128]{2,1,0:T(8,128)(2,1)S(1)}, bf16[8,128,128]{2,1,0:T(8,128)(2,1)S(1)}, u32[]{:S(2)}, u32[]{:S(2)}) collective-permute-start(bf16[8,128,128]{2,1,0:T(8,128)(2,1)S(1)} %collective-permute-done.3.second_ref), channel_id=1, source_target_pairs={{0,4},{4,8},{8,12},{12,16},{16,20},{20,24},{24,28},{28,32},{32,36}... | collective-permute-start | bytes 786440 | tf_op jit(solution)/shard_map/ppermute | solution.py:14
  56.7 27.3 %collective-permute-start.6 = (bf16[4,8,128,128]{3,2,1,0:T(8,128)(2,1)S(1)}, bf16[4,8,128,128]{3,2,1,0:T(8,128)(2,1)S(1)}, u32[]{:S(2)}, u32[]{:S(2)}) collective-permute-start(bf16[4,8,128,128]{3,2,1,0:T(8,128)(2,1)S(1)} %pad_maximum_fusion.1), channel_id=1, source_target_pairs={{0,16},{4,20},{8,24},{12,28},{16,32},{20,36},{24,40},{28,44},{32,4... | collective-permute-start | bytes 3145736 | tf_op jit(solution)/shard_map/ppermute | solution.py:14
  56.8 1.5 %copy-start.1 = (bf16[2,512,512]{2,1,0:T(8,128)(2,1)S(1)}, bf16[2,512,512]{2,1,0:T(8,128)(2,1)}, u32[]{:S(2)}) copy-start(bf16[2,512,512]{2,1,0:T(8,128)(2,1)} %local_ref.1) | copy-start | bytes 3145732
  81.4 1.3 %copy-start = (f32[8,512,128]{2,1,0:T(8,128)}, f32[8,512,128]{2,1,0:T(8,128)S(1)}, u32[]{:S(2)}) copy-start(f32[8,512,128]{2,1,0:T(8,128)S(1)} %get-tuple-element.5.early_ref) | copy-start | bytes 6291460
  84.0 1.0 copy-start.2
  93.9 3.6 %collective-permute-start.7 = (bf16[8,2,128,128]{3,2,0,1:T(8,128)(2,1)S(1)}, bf16[8,2,128,128]{3,2,0,1:T(8,128)(2,1)S(1)}, u32[]{:S(2)}, u32[]{:S(2)}) collective-permute-start(bf16[8,2,128,128]{3,2,0,1:T(8,128)(2,1)S(1)} %fusion), channel_id=1, source_target_pairs={{0,1},{1,0},{2,3},{3,2},{4,5},{5,4},{6,7},{7,6},{8,9},{9,8},{10,11... | collective-permute-start | bytes 1572872 | tf_op jit(solution)/shard_map/ppermute | solution.py:154
  98.9 7.6 %collective-permute-start.8 = (bf16[8,128,128]{2,1,0:T(8,128)(2,1)S(1)}, bf16[8,128,128]{2,1,0:T(8,128)(2,1)S(1)}, u32[]{:S(2)}, u32[]{:S(2)}) collective-permute-start(bf16[8,128,128]{2,1,0:T(8,128)(2,1)S(1)} %fusion.2), channel_id=1, source_target_pairs={{0,2},{1,3},{2,0},{3,1},{4,6},{5,7},{6,4},{7,5},{8,10},{9,11},{10,... | collective-permute-start | bytes 786440 | tf_op jit(solution)/shard_map/ppermute | solution.py:160

commit v12 on v10

--- a/solution.py
+++ b/solution.py
@@ -53,6 +53,24 @@
     wide = jnp.concatenate([ham_ref[0, 3 + s] for s in range(count)], axis=1)
     tall = jnp.concatenate([third_ref[s, 0] for s in range(count)], axis=0)
     part_ref[0] = early_ref[0] + jnp.dot(wide, tall, preferred_element_type=jnp.float32)
+
+
+def band_reduce(partial_value, band, band_count):
+    fine_count, block_order, vector_count = partial_value.shape
+    row_block = block_order // band_count
+    core = band % 2
+    halves = partial_value.reshape(fine_count, 2, 2, row_block, vector_count)
+    send = lax.dynamic_index_in_dim(halves, 1 - core, 2, keepdims=False)
+    keep = lax.dynamic_index_in_dim(halves, core, 2, keepdims=False)
+    swap = [(b, b ^ 1) for b in range(band_count)]
+    pair_sum = keep + lax.ppermute(send.astype(jnp.bfloat16), "band", swap).astype(jnp.float32)
+    level = band // 2
+    send = lax.dynamic_index_in_dim(pair_sum, 1 - level, 1, keepdims=False)
+    keep = lax.dynamic_index_in_dim(pair_sum, level, 1, keepdims=False)
+    swap = [(b, b ^ 2) for b in range(band_count)]
+    return (
+        keep + lax.ppermute(send.astype(jnp.bfloat16), "band", swap).astype(jnp.float32)
+    ).astype(jnp.bfloat16)
 
 
 def on_device(coarse_kernel, interp_index, interp_weight, stop_order, intersection, trial_vectors):
@@ -135,34 +153,28 @@
             bytes_accessed=2 * fine_dev * block_order * (block_order + stop_count * column_count)),
     )(slot_index, band_index, weights, halo, coarse_kernel, intersection, intersection,
       first, second, last)
-    partial_value = pl.pallas_call(
-        product_kernel,
-        grid=(fine_dev,),
-        in_specs=[
-            pl.BlockSpec((1, stop_count, block_order, column_count), lambda k: (k, 0, 0, 0)),
-            pl.BlockSpec((1, block_order, vector_count), lambda k: (k, 0, 0)),
-            pl.BlockSpec((4, 1, column_count, vector_count), lambda k: (0, k, 0, 0)),
-        ],
-        out_specs=pl.BlockSpec((1, block_order, vector_count), lambda k: (k, 0, 0)),
-        out_shape=jax.ShapeDtypeStruct((fine_dev, block_order, vector_count), jnp.float32),
-        cost_estimate=pl.CostEstimate(
-            flops=2 * fine_dev * stop_count * block_order * column_count * vector_count,
-            transcendentals=0,
-            bytes_accessed=2 * fine_dev * stop_count * block_order * column_count),
-    )(hamiltonian, early_value, third)
-    row_block = block_order // band_count
-    halves = partial_value.reshape(fine_dev, 2, 2, row_block, vector_count)
-    send = lax.dynamic_index_in_dim(halves, 1 - core, 2, keepdims=False)
-    keep = lax.dynamic_index_in_dim(halves, core, 2, keepdims=False)
-    swap = [(b, b ^ 1) for b in range(band_count)]
-    pair_sum = keep + lax.ppermute(send.astype(jnp.bfloat16), "band", swap).astype(jnp.float32)
-    level = band // 2
-    send = lax.dynamic_index_in_dim(pair_sum, 1 - level, 1, keepdims=False)
-    keep = lax.dynamic_index_in_dim(pair_sum, level, 1, keepdims=False)
-    swap = [(b, b ^ 2) for b in range(band_count)]
-    product_share = (
-        keep + lax.ppermute(send.astype(jnp.bfloat16), "band", swap).astype(jnp.float32)
-    ).astype(jnp.bfloat16)
+    half_count = fine_dev // 2
+    shares = []
+    for offset in (0, half_count):
+        partial_value = pl.pallas_call(
+            product_kernel,
+            grid=(half_count,),
+            in_specs=[
+                pl.BlockSpec((1, stop_count, block_order, column_count),
+                             lambda k, o=offset: (k + o, 0, 0, 0)),
+                pl.BlockSpec((1, block_order, vector_count), lambda k, o=offset: (k + o, 0, 0)),
+                pl.BlockSpec((4, 1, column_count, vector_count),
+                             lambda k, o=offset: (0, k + o, 0, 0)),
+            ],
+            out_specs=pl.BlockSpec((1, block_order, vector_count), lambda k: (k, 0, 0)),
+            out_shape=jax.ShapeDtypeStruct((half_count, block_order, vector_count), jnp.float32),
+            cost_estimate=pl.CostEstimate(
+                flops=2 * half_count * 4 * block_order * column_count * vector_count,
+                transcendentals=0,
+                bytes_accessed=2 * half_count * stop_count * block_order * column_count),
+        )(hamiltonian, early_value, third)
+        shares.append(band_reduce(partial_value, band, band_count))
+    product_share = jnp.concatenate(shares, axis=0)
     return (hamiltonian, product_share)
 
 

time: 105 us -> 105 us (level)
  waiting for transfers between devices: 38.4 us -> 35 us
  local copies, waits for them, and re-layouts: 5.91 us -> 7.83 us
  starting transfers between devices: 20.1 us -> 21.5 us
  Pallas kernels: 30.5 us -> 31.7 us
    ppermute x2 -> x4, waiting for transfers between devices: 7.74 us -> 4.63 us  [band_reduce(): lax.ppermute(send.astype(jnp.bfloat16), 'band', swap).astype(jnp.float32)]
    ppermute x2 -> x4, starting transfers between devices: 3.4 us -> 4.91 us  [band_reduce(): lax.ppermute(send.astype(jnp.bfloat16), 'band', swap).astype(jnp.float32)]
    add x1 -> x2, other arithmetic: 1.33 us -> 0.1 us  [band_reduce(): keep + lax.ppermute(send.astype(jnp.bfloat16), 'band', swap).astype(jnp.f...]
    pallas_call x1 -> x2, Pallas kernels: 8.33 us -> 9.49 us  [on_device(): pl.pallas_call(product_kernel, grid=(half_count,), in_specs=[pl.BlockSpec...]
    unnamed x6 -> x12, local copies, waits for them, and re-layouts: 2.93 us -> 3.91 us
    convert_element_type x2 -> x4, local copies, waits for them, and re-layouts: 1.36 us -> 2.3 us  [band_reduce(): send.astype(jnp.bfloat16)]
  transfers between devices with their start and end apart: 8 -> 10, of which waited for: 5 -> 5; matrix products, arithmetic and copies ran while one was open for 9% -> 11% of each run, Pallas kernels for 21% -> 26%
where the time goes in v12:
time: 105 us; the launch traced here: 104 us
  waiting for transfers between devices  35 us (33%)
  Pallas kernels  31.7 us (30%)
  starting transfers between devices  21.5 us (20%)
  local copies, waits for them, and re-layouts  7.83 us (7%)
  other arithmetic  7.59 us (7%)
    pallas_call x1, Pallas kernels, on_device(): pl.pallas_call(kernel, grid_spec=grid_spec, out_shape=[jax.ShapeDtypeStru...  22.2 us
    ppermute x4, waiting for transfers between devices, shifted(): return lax.ppermute(value, axis, pairs)  16.6 us
    ppermute x1, waiting for transfers between devices, on_device(): near = lax.ppermute(coarse_kernel, ('blk', 'band'), pairs)  13.7 us
    pallas_call x2, Pallas kernels, on_device(): pl.pallas_call(product_kernel, grid=(half_count,), in_specs=[pl.BlockSpec...  9.49 us
    ppermute x1, starting transfers between devices, on_device(): near = lax.ppermute(coarse_kernel, ('blk', 'band'), pairs)  9.47 us
    ppermute x1, starting transfers between devices, on_device(): far = lax.ppermute(near, 'band', [(b, b ^ 1) for b in range(band_count)])  6.13 us
    ppermute x4, starting transfers between devices, band_reduce(): lax.ppermute(send.astype(jnp.bfloat16), 'band', swap).astype(jnp.float32)  4.91 us
    ppermute x4, waiting for transfers between devices, band_reduce(): lax.ppermute(send.astype(jnp.bfloat16), 'band', swap).astype(jnp.float32)  4.63 us
  transfers between devices with their start and end apart: 10, of which 5 were waited for; matrix products, arithmetic and copies ran while one was open for 11% of the time, Pallas kernels for 26%

profile of v12, /device:TPU:1, one launch (start us, length us, event | category | flops | bytes accessed | tf_op | source)
XLA Modules:
  0.0 104.3 jit_solution(14071539522677505455)
XLA Ops:
  0.6 9.5 %collective-permute-start = (bf16[2,512,512]{2,1,0:T(8,128)(2,1)}, bf16[2,512,512]{2,1,0:T(8,128)(2,1)}, u32[]{:S(2)}, u32[]{:S(2)}) collective-permute-start(bf16[2,512,512]{2,1,0:T(8,128)(2,1)} %local_ref.1), channel_id=1, source_target_pairs={{0,4},{1,125},{2,6},{3,127},{4,8},{5,1},{6,10},{7,3},{8,12},{9,5},... | collective-permute-start | bytes 3145736 | tf_op jit(solution)/shard_map/ppermute | solution.py:96
  10.8 0.8 copy.12
  11.6 0.7 compare_and_fusion
  12.2 13.7 %collective-permute-done = bf16[2,512,512]{2,1,0:T(8,128)(2,1)} collective-permute-done((bf16[2,512,512]{2,1,0:T(8,128)(2,1)}, bf16[2,512,512]{2,1,0:T(8,128)(2,1)}, u32[]{:S(2)}, u32[]{:S(2)}) %collective-permute-start) | collective-permute-done | bytes 1048608 | tf_op jit(solution)/shard_map/ppermute | solution.py:96
  25.9 6.1 %collective-permute-start.1 = (bf16[2,512,512]{2,1,0:T(8,128)(2,1)}, bf16[2,512,512]{2,1,0:T(8,128)(2,1)}, u32[]{:S(2)}, u32[]{:S(2)}) collective-permute-start(bf16[2,512,512]{2,1,0:T(8,128)(2,1)} %collective-permute-done), channel_id=1, source_target_pairs={{0,1},{1,0},{2,3},{3,2},{4,5},{5,4},{6,7},{7,6},{8,9},{9,8},{10,11... | collective-permute-start | bytes 3145736 | tf_op jit(solution)/shard_map/ppermute | solution.py:97
  32.1 1.0 pad_maximum_fusion.2
  33.1 0.9 collective-permute-start.3
  34.9 0.8 copy.14
  36.4 16.3 %collective-permute-done.3.second_ref = bf16[2,8,128,128]{3,2,1,0:T(8,128)(2,1)S(1)} collective-permute-done((bf16[2,8,128,128]{3,2,1,0:T(8,128)(2,1)S(1)}, bf16[2,8,128,128]{3,2,1,0:T(8,128)(2,1)S(1)}, u32[]{:S(2)}, u32[]{:S(2)}) %collective-permute-start.3) | collective-permute-done | bytes 524320 | tf_op jit(solution)/shard_map/ppermute | solution.py:14
  52.7 1.1 %pad_maximum_fusion.1 = bf16[4,8,128,128]{3,2,1,0:T(8,128)(2,1)S(1)} fusion(bf16[2,8,128,128]{3,2,1,0:T(8,128)(2,1)S(1)} %collective-permute-done.3.second_ref, bf16[1,8,128,128]{3,2,1,0:T(8,128)(2,1)S(1)} %bitcast.30, bf16[1,8,128,128]{3,2,1,0:T(8,128)(2,1)} %bitcast.36), kind=kLoop, calls=%fused_computation.3 | loop fusion | flops 1048576 | bytes 2097152 | tf_op jit(solution)/shard_map/stack | solution.py:103
  54.1 3.1 %pad_maximum_fusion.halo_ref = bf16[4,512,512]{2,1,0:T(8,128)(2,1)} fusion(bf16[2,512,512]{2,1,0:T(8,128)(2,1)} %collective-permute-done.1, bf16[2,512,512]{2,1,0:T(8,128)(2,1)} %collective-permute-done), kind=kLoop, calls=%fused_computation.2 | loop fusion | flops 1048576 | bytes 4194304 | tf_op jit(solution)/shard_map/concatenate | solution.py:98
  57.3 22.2 %shard_map.77 = (bf16[8,8,512,128]{3,2,1,0:T(8,128)(2,1)}, f32[8,512,128]{2,1,0:T(8,128)S(1)}) custom-call(s32[256]{0:T(256)S(1)} %fusion.8.slot_ref, s32[1]{0:T(128)} %bitcast.1.band_ref, f32[256]{0:T(256)S(1)} %select_n.91.weight_ref, bf16[4,512,512]{2,1,0:T(8,128)(2,1)} %pad_maximum_fusion.halo_ref, bf16[2,512,512]{2,1,0:T(8,128)(2,1)S(1)} %copy-done.1, ...), custom_call_target="tpu_custom_call" | custom-call | flops 7516192768 | bytes 12582912 | tf_op jit(solution)/shard_map/pallas_call | solution.py:141
  79.5 1.3 %copy-done = f32[8,512,128]{2,1,0:T(8,128)} copy-done((f32[8,512,128]{2,1,0:T(8,128)}, f32[8,512,128]{2,1,0:T(8,128)S(1)}, u32[]{:S(2)}) %copy-start) | copy-done | bytes 2097176
  81.1 1.0 copy-done.2
  82.0 4.7 %shard_map.78 = f32[4,512,128]{2,1,0:T(8,128)} custom-call(bf16[8,8,512,128]{3,2,1,0:T(8,128)(2,1)} %get-tuple-element.2.ham_ref, f32[8,512,128]{2,1,0:T(8,128)} %copy-done, bf16[4,8,128,128]{3,2,1,0:T(8,128)(2,1)} %copy-done.2), custom_call_target="tpu_custom_call" | custom-call | flops 268435456 | bytes 4194304 | tf_op jit(solution)/shard_map/pallas_call | solution.py:159
  86.7 1.1 %fusion = bf16[4,2,128,128]{3,2,0,1:T(8,128)(2,1)S(1)} fusion(f32[4,2,2,128,128]{4,3,2,1,0:T(8,128)} %bitcast.31, s32[]{:T(128)S(6)} %select_n.93), kind=kLoop, calls=%fused_computation.9 | loop fusion | bytes 524292 | tf_op jit(solution)/shard_map/convert_element_type | solution.py:66
  87.8 2.0 %collective-permute-start.6 = (bf16[4,2,128,128]{3,2,0,1:T(8,128)(2,1)S(1)}, bf16[4,2,128,128]{3,2,0,1:T(8,128)(2,1)S(1)}, u32[]{:S(2)}, u32[]{:S(2)}) collective-permute-start(bf16[4,2,128,128]{3,2,0,1:T(8,128)(2,1)S(1)} %fusion), channel_id=1, source_target_pairs={{0,1},{1,0},{2,3},{3,2},{4,5},{5,4},{6,7},{7,6},{8,9},{9,8},{10,11... | collective-permute-start | bytes 786440 | tf_op jit(solution)/shard_map/ppermute | solution.py:66
  89.8 4.8 %shard_map.79 = f32[4,512,128]{2,1,0:T(8,128)} custom-call(bf16[8,8,512,128]{3,2,1,0:T(8,128)(2,1)} %get-tuple-element.2.ham_ref, f32[8,512,128]{2,1,0:T(8,128)} %copy-done, bf16[4,8,128,128]{3,2,1,0:T(8,128)(2,1)} %copy-done.2), custom_call_target="tpu_custom_call" | custom-call | flops 268435456 | bytes 4194304 | tf_op jit(solution)/shard_map/pallas_call | solution.py:159
  94.6 1.2 %fusion.1 = bf16[4,2,128,128]{3,2,0,1:T(8,128)(2,1)S(1)} fusion(f32[4,2,2,128,128]{4,3,2,1,0:T(8,128)} %bitcast.33, s32[]{:T(128)S(6)} %select_n.93), kind=kLoop, calls=%fused_computation.10 | loop fusion | bytes 524292 | tf_op jit(solution)/shard_map/convert_element_type | solution.py:66
  96.0 1.4 %collective-permute-start.7 = (bf16[4,128,128]{2,1,0:T(8,128)(2,1)S(1)}, bf16[4,128,128]{2,1,0:T(8,128)(2,1)S(1)}, u32[]{:S(2)}, u32[]{:S(2)}) collective-permute-start(bf16[4,128,128]{2,1,0:T(8,128)(2,1)S(1)} %fusion.4), channel_id=1, source_target_pairs={{0,2},{1,3},{2,0},{3,1},{4,6},{5,7},{6,4},{7,5},{8,10},{9,11},{10,... | collective-permute-start | bytes 393224 | tf_op jit(solution)/shard_map/ppermute | solution.py:72
  97.5 1.4 %collective-permute-start.9 = (bf16[4,128,128]{2,1,0:T(8,128)(2,1)S(1)}, bf16[4,128,128]{2,1,0:T(8,128)(2,1)S(1)}, u32[]{:S(2)}, u32[]{:S(2)}) collective-permute-start(bf16[4,128,128]{2,1,0:T(8,128)(2,1)S(1)} %fusion.5), channel_id=1, source_target_pairs={{0,2},{1,3},{2,0},{3,1},{4,6},{5,7},{6,4},{7,5},{8,10},{9,11},{10,... | collective-permute-start | bytes 393224 | tf_op jit(solution)/shard_map/ppermute | solution.py:72
  98.9 1.8 %collective-permute-done.7 = bf16[4,128,128]{2,1,0:T(8,128)(2,1)S(1)} collective-permute-done((bf16[4,128,128]{2,1,0:T(8,128)(2,1)S(1)}, bf16[4,128,128]{2,1,0:T(8,128)(2,1)S(1)}, u32[]{:S(2)}, u32[]{:S(2)}) %collective-permute-start.7) | collective-permute-done | bytes 131104 | tf_op jit(solution)/shard_map/ppermute | solution.py:72
  100.8 2.8 %collective-permute-done.9 = bf16[4,128,128]{2,1,0:T(8,128)(2,1)S(1)} collective-permute-done((bf16[4,128,128]{2,1,0:T(8,128)(2,1)S(1)}, bf16[4,128,128]{2,1,0:T(8,128)(2,1)S(1)}, u32[]{:S(2)}, u32[]{:S(2)}) %collective-permute-start.9) | collective-permute-done | bytes 131104 | tf_op jit(solution)/shard_map/ppermute | solution.py:72
  103.6 0.7 pad_maximum_fusion.3
  (35 shorter events, 3.2 us)
Async XLA Ops:
  0.6 25.3 %collective-permute-start = (bf16[2,512,512]{2,1,0:T(8,128)(2,1)}, bf16[2,512,512]{2,1,0:T(8,128)(2,1)}, u32[]{:S(2)}, u32[]{:S(2)}) collective-permute-start(bf16[2,512,512]{2,1,0:T(8,128)(2,1)} %local_ref.1), channel_id=1, source_target_pairs={{0,4},{1,125},{2,6},{3,127},{4,8},{5,1},{6,10},{7,3},{8,12},{9,5},... | collective-permute-start | bytes 3145736 | tf_op jit(solution)/shard_map/ppermute | solution.py:96
  10.1 22.0 %collective-permute-start.2 = (bf16[8,128,128]{2,1,0:T(8,128)(2,1)}, bf16[8,128,128]{2,1,0:T(8,128)(2,1)S(1)}, u32[]{:S(2)}, u32[]{:S(2)}) collective-permute-start(bf16[8,128,128]{2,1,0:T(8,128)(2,1)} %param.11), channel_id=1, source_target_pairs={{0,4},{4,8},{8,12},{12,16},{16,20},{20,24},{24,28},{28,32},{32,36}... | collective-permute-start | bytes 786440 | tf_op jit(solution)/shard_map/ppermute | solution.py:14
  10.1 47.2 %collective-permute-start.4 = (bf16[8,128,128]{2,1,0:T(8,128)(2,1)}, bf16[8,128,128]{2,1,0:T(8,128)(2,1)S(1)}, u32[]{:S(2)}, u32[]{:S(2)}) collective-permute-start(bf16[8,128,128]{2,1,0:T(8,128)(2,1)} %param.11), channel_id=1, source_target_pairs={{0,32},{4,36},{8,40},{12,44},{16,48},{20,52},{24,56},{28,60},{32,6... | collective-permute-start | bytes 786440 | tf_op jit(solution)/shard_map/ppermute | solution.py:14
  25.9 28.2 %collective-permute-start.1 = (bf16[2,512,512]{2,1,0:T(8,128)(2,1)}, bf16[2,512,512]{2,1,0:T(8,128)(2,1)}, u32[]{:S(2)}, u32[]{:S(2)}) collective-permute-start(bf16[2,512,512]{2,1,0:T(8,128)(2,1)} %collective-permute-done), channel_id=1, source_target_pairs={{0,1},{1,0},{2,3},{3,2},{4,5},{5,4},{6,7},{7,6},{8,9},{9,8},{10,11... | collective-permute-start | bytes 3145736 | tf_op jit(solution)/shard_map/ppermute | solution.py:97
  33.1 19.6 %collective-permute-start.3 = (bf16[2,8,128,128]{3,2,1,0:T(8,128)(2,1)S(1)}, bf16[2,8,128,128]{3,2,1,0:T(8,128)(2,1)S(1)}, u32[]{:S(2)}, u32[]{:S(2)}) collective-permute-start(bf16[2,8,128,128]{3,2,1,0:T(8,128)(2,1)S(1)} %pad_maximum_fusion.2), channel_id=1, source_target_pairs={{0,8},{4,12},{8,16},{12,20},{16,24},{20,28},{24,32},{28,36},{32,40... | collective-permute-start | bytes 1572872 | tf_op jit(solution)/shard_map/ppermute | solution.py:14
  53.7 27.3 %collective-permute-start.5 = (bf16[4,8,128,128]{3,2,1,0:T(8,128)(2,1)S(1)}, bf16[4,8,128,128]{3,2,1,0:T(8,128)(2,1)S(1)}, u32[]{:S(2)}, u32[]{:S(2)}) collective-permute-start(bf16[4,8,128,128]{3,2,1,0:T(8,128)(2,1)S(1)} %pad_maximum_fusion.1), channel_id=1, source_target_pairs={{0,16},{4,20},{8,24},{12,28},{16,32},{20,36},{24,40},{28,44},{32,4... | collective-permute-start | bytes 3145736 | tf_op jit(solution)/shard_map/ppermute | solution.py:14
  54.1 3.2 %copy-start.1 = (bf16[2,512,512]{2,1,0:T(8,128)(2,1)S(1)}, bf16[2,512,512]{2,1,0:T(8,128)(2,1)}, u32[]{:S(2)}) copy-start(bf16[2,512,512]{2,1,0:T(8,128)(2,1)} %local_ref.1) | copy-start | bytes 3145732
  79.5 1.3 %copy-start = (f32[8,512,128]{2,1,0:T(8,128)}, f32[8,512,128]{2,1,0:T(8,128)S(1)}, u32[]{:S(2)}) copy-start(f32[8,512,128]{2,1,0:T(8,128)S(1)} %get-tuple-element.5.early_ref) | copy-start | bytes 6291460
  81.1 1.0 copy-start.2
  87.8 8.1 %collective-permute-start.6 = (bf16[4,2,128,128]{3,2,0,1:T(8,128)(2,1)S(1)}, bf16[4,2,128,128]{3,2,0,1:T(8,128)(2,1)S(1)}, u32[]{:S(2)}, u32[]{:S(2)}) collective-permute-start(bf16[4,2,128,128]{3,2,0,1:T(8,128)(2,1)S(1)} %fusion), channel_id=1, source_target_pairs={{0,1},{1,0},{2,3},{3,2},{4,5},{5,4},{6,7},{7,6},{8,9},{9,8},{10,11... | collective-permute-start | bytes 786440 | tf_op jit(solution)/shard_map/ppermute | solution.py:66
  89.8 6.1 %copy-start.3 = (f32[4,512,128]{2,1,0:T(8,128)S(1)}, f32[4,512,128]{2,1,0:T(8,128)}, u32[]{:S(2)}) copy-start(f32[4,512,128]{2,1,0:T(8,128)} %shard_map.78) | copy-start | bytes 3145732
  94.6 2.8 %copy-start.4 = (f32[4,512,128]{2,1,0:T(8,128)S(1)}, f32[4,512,128]{2,1,0:T(8,128)}, u32[]{:S(2)}) copy-start(f32[4,512,128]{2,1,0:T(8,128)} %shard_map.79) | copy-start | bytes 3145732
  95.8 1.6 %collective-permute-start.8 = (bf16[4,2,128,128]{3,2,0,1:T(8,128)(2,1)S(1)}, bf16[4,2,128,128]{3,2,0,1:T(8,128)(2,1)S(1)}, u32[]{:S(2)}, u32[]{:S(2)}) collective-permute-start(bf16[4,2,128,128]{3,2,0,1:T(8,128)(2,1)S(1)} %fusion.1), channel_id=1, source_target_pairs={{0,1},{1,0},{2,3},{3,2},{4,5},{5,4},{6,7},{7,6},{8,9},{9,8},{10,11... | collective-permute-start | bytes 786440 | tf_op jit(solution)/shard_map/ppermute | solution.py:66
  96.0 4.7 %collective-permute-start.7 = (bf16[4,128,128]{2,1,0:T(8,128)(2,1)S(1)}, bf16[4,128,128]{2,1,0:T(8,128)(2,1)S(1)}, u32[]{:S(2)}, u32[]{:S(2)}) collective-permute-start(bf16[4,128,128]{2,1,0:T(8,128)(2,1)S(1)} %fusion.4), channel_id=1, source_target_pairs={{0,2},{1,3},{2,0},{3,1},{4,6},{5,7},{6,4},{7,5},{8,10},{9,11},{10,... | collective-permute-start | bytes 393224 | tf_op jit(solution)/shard_map/ppermute | solution.py:72
  97.5 6.0 %collective-permute-start.9 = (bf16[4,128,128]{2,1,0:T(8,128)(2,1)S(1)}, bf16[4,128,128]{2,1,0:T(8,128)(2,1)S(1)}, u32[]{:S(2)}, u32[]{:S(2)}) collective-permute-start(bf16[4,128,128]{2,1,0:T(8,128)(2,1)S(1)} %fusion.5), channel_id=1, source_target_pairs={{0,2},{1,3},{2,0},{3,1},{4,6},{5,7},{6,4},{7,5},{8,10},{9,11},{10,... | collective-permute-start | bytes 393224 | tf_op jit(solution)/shard_map/ppermute | solution.py:72

commit v13 on v10

--- a/solution.py
+++ b/solution.py
@@ -50,9 +50,10 @@
 
 def product_kernel(ham_ref, early_ref, third_ref, part_ref):
     count = third_ref.shape[0]
-    wide = jnp.concatenate([ham_ref[0, 3 + s] for s in range(count)], axis=1)
-    tall = jnp.concatenate([third_ref[s, 0] for s in range(count)], axis=0)
-    part_ref[0] = early_ref[0] + jnp.dot(wide, tall, preferred_element_type=jnp.float32)
+    for k in range(ham_ref.shape[0]):
+        wide = jnp.concatenate([ham_ref[k, 3 + s] for s in range(count)], axis=1)
+        tall = jnp.concatenate([third_ref[s, k] for s in range(count)], axis=0)
+        part_ref[k] = early_ref[k] + jnp.dot(wide, tall, preferred_element_type=jnp.float32)
 
 
 def on_device(coarse_kernel, interp_index, interp_weight, stop_order, intersection, trial_vectors):
@@ -137,13 +138,14 @@
       first, second, last)
     partial_value = pl.pallas_call(
         product_kernel,
-        grid=(fine_dev,),
+        grid=(2,),
         in_specs=[
-            pl.BlockSpec((1, stop_count, block_order, column_count), lambda k: (k, 0, 0, 0)),
-            pl.BlockSpec((1, block_order, vector_count), lambda k: (k, 0, 0)),
-            pl.BlockSpec((4, 1, column_count, vector_count), lambda k: (0, k, 0, 0)),
+            pl.BlockSpec((fine_dev // 2, stop_count, block_order, column_count),
+                         lambda k: (k, 0, 0, 0)),
+            pl.BlockSpec((fine_dev // 2, block_order, vector_count), lambda k: (k, 0, 0)),
+            pl.BlockSpec((4, fine_dev // 2, column_count, vector_count), lambda k: (0, k, 0, 0)),
         ],
-        out_specs=pl.BlockSpec((1, block_order, vector_count), lambda k: (k, 0, 0)),
+        out_specs=pl.BlockSpec((fine_dev // 2, block_order, vector_count), lambda k: (k, 0, 0)),
         out_shape=jax.ShapeDtypeStruct((fine_dev, block_order, vector_count), jnp.float32),
         cost_estimate=pl.CostEstimate(
             flops=2 * fine_dev * stop_count * block_order * column_count * vector_count,

time: 105 us -> 102 us (0.971)
  Pallas kernels: 30.5 us -> 28.2 us
    pallas_call x1, Pallas kernels: 8.33 us -> 6.01 us  [on_device(): pl.pallas_call(product_kernel, grid=(2,), in_specs=[pl.BlockSpec((fine_de...]
  transfers between devices with their start and end apart: 8 -> 8, of which waited for: 5 -> 5; matrix products, arithmetic and copies ran while one was open for 9% -> 9% of each run, Pallas kernels for 21% -> 22%
where the time goes in v13:
time: 102 us
  waiting for transfers between devices  38.4 us (38%)
  Pallas kernels  28.2 us (28%)
  starting transfers between devices  20.1 us (20%)
  other arithmetic  8.47 us (8%)
  local copies, waits for them, and re-layouts  5.91 us (6%)
    pallas_call x1, Pallas kernels, on_device(): pl.pallas_call(kernel, grid_spec=grid_spec, out_shape=[jax.ShapeDtypeStru...  22.2 us
    ppermute x4, waiting for transfers between devices, shifted(): return lax.ppermute(value, axis, pairs)  17 us
    ppermute x1, waiting for transfers between devices, on_device(): near = lax.ppermute(coarse_kernel, ('blk', 'band'), pairs)  13.6 us
    ppermute x1, starting transfers between devices, on_device(): near = lax.ppermute(coarse_kernel, ('blk', 'band'), pairs)  9.47 us
    ppermute x2, waiting for transfers between devices, on_device(): lax.ppermute(send.astype(jnp.bfloat16), 'band', swap).astype(jnp.float32)  7.73 us
    ppermute x1, starting transfers between devices, on_device(): far = lax.ppermute(near, 'band', [(b, b ^ 1) for b in range(band_count)])  6.24 us
    pallas_call x1, Pallas kernels, on_device(): pl.pallas_call(product_kernel, grid=(2,), in_specs=[pl.BlockSpec((fine_de...  6.01 us
    ppermute x2, starting transfers between devices, on_device(): lax.ppermute(send.astype(jnp.bfloat16), 'band', swap).astype(jnp.float32)  3.4 us
  transfers between devices with their start and end apart: 8, of which 5 were waited for; matrix products, arithmetic and copies ran while one was open for 9% of the time, Pallas kernels for 22%

profile of v13, /device:TPU:1, one launch (start us, length us, event | category | flops | bytes accessed | tf_op | source)
XLA Modules:
  0.0 101.8 jit_solution(8979636373961895073)
XLA Ops:
  0.6 9.5 %collective-permute-start = (bf16[2,512,512]{2,1,0:T(8,128)(2,1)}, bf16[2,512,512]{2,1,0:T(8,128)(2,1)S(1)}, u32[]{:S(2)}, u32[]{:S(2)}) collective-permute-start(bf16[2,512,512]{2,1,0:T(8,128)(2,1)} %local_ref.1), channel_id=1, source_target_pairs={{0,4},{1,125},{2,6},{3,127},{4,8},{5,1},{6,10},{7,3},{8,12},{9,5},... | collective-permute-start | bytes 3145736 | tf_op jit(solution)/shard_map/ppermute | solution.py:79
  10.1 0.7 compare_select_fusion
  10.8 0.8 copy.10
  11.6 0.7 compare_and_fusion
  12.2 13.6 %collective-permute-done = bf16[2,512,512]{2,1,0:T(8,128)(2,1)S(1)} collective-permute-done((bf16[2,512,512]{2,1,0:T(8,128)(2,1)}, bf16[2,512,512]{2,1,0:T(8,128)(2,1)S(1)}, u32[]{:S(2)}, u32[]{:S(2)}) %collective-permute-start) | collective-permute-done | bytes 1048608 | tf_op jit(solution)/shard_map/ppermute | solution.py:79
  25.8 6.2 %collective-permute-start.1 = (bf16[2,512,512]{2,1,0:T(8,128)(2,1)S(1)}, bf16[2,512,512]{2,1,0:T(8,128)(2,1)}, u32[]{:S(2)}, u32[]{:S(2)}) collective-permute-start(bf16[2,512,512]{2,1,0:T(8,128)(2,1)S(1)} %collective-permute-done), channel_id=1, source_target_pairs={{0,1},{1,0},{2,3},{3,2},{4,5},{5,4},{6,7},{7,6},{8,9},{9,8},{10,11... | collective-permute-start | bytes 3145736 | tf_op jit(solution)/shard_map/ppermute | solution.py:80
  32.1 1.0 pad_maximum_fusion.2
  33.1 0.9 collective-permute-start.3
  34.9 0.8 copy.12
  35.7 0.6 gather_fusion.1
  36.4 16.3 %collective-permute-done.3.second_ref = bf16[2,8,128,128]{3,2,1,0:T(8,128)(2,1)S(1)} collective-permute-done((bf16[2,8,128,128]{3,2,1,0:T(8,128)(2,1)S(1)}, bf16[2,8,128,128]{3,2,1,0:T(8,128)(2,1)S(1)}, u32[]{:S(2)}, u32[]{:S(2)}) %collective-permute-start.3) | collective-permute-done | bytes 524320 | tf_op jit(solution)/shard_map/ppermute | solution.py:14
  52.7 1.1 %pad_maximum_fusion.1 = bf16[4,8,128,128]{3,2,1,0:T(8,128)(2,1)S(1)} fusion(bf16[2,8,128,128]{3,2,1,0:T(8,128)(2,1)S(1)} %collective-permute-done.3.second_ref, bf16[1,8,128,128]{3,2,1,0:T(8,128)(2,1)S(1)} %bitcast.19, bf16[1,8,128,128]{3,2,1,0:T(8,128)(2,1)} %bitcast.23), kind=kLoop, calls=%fused_computation.3 | loop fusion | flops 1048576 | bytes 2097152 | tf_op jit(solution)/shard_map/stack | solution.py:86
  54.1 2.8 %pad_maximum_fusion.halo_ref = bf16[4,512,512]{2,1,0:T(8,128)(2,1)} fusion(bf16[2,512,512]{2,1,0:T(8,128)(2,1)} %collective-permute-done.1, bf16[2,512,512]{2,1,0:T(8,128)(2,1)S(1)} %collective-permute-done), kind=kLoop, calls=%fused_computation.2 | loop fusion | flops 1048576 | bytes 4194304 | tf_op jit(solution)/shard_map/concatenate | solution.py:81
  57.0 22.2 %shard_map.77 = (bf16[8,8,512,128]{3,2,1,0:T(8,128)(2,1)}, f32[8,512,128]{2,1,0:T(8,128)S(1)}) custom-call(s32[256]{0:T(256)S(1)} %fusion.5.slot_ref, s32[1]{0:T(128)} %bitcast.1.band_ref, f32[256]{0:T(256)S(1)} %select_n.82.weight_ref, bf16[4,512,512]{2,1,0:T(8,128)(2,1)} %pad_maximum_fusion.halo_ref, bf16[2,512,512]{2,1,0:T(8,128)(2,1)S(1)} %copy-done.1, ...), custom_call_target="tpu_custom_call" | custom-call | flops 7516192768 | bytes 12582912 | tf_op jit(solution)/shard_map/pallas_call | solution.py:124
  79.1 1.3 %copy-done = f32[8,512,128]{2,1,0:T(8,128)} copy-done((f32[8,512,128]{2,1,0:T(8,128)}, f32[8,512,128]{2,1,0:T(8,128)S(1)}, u32[]{:S(2)}) %copy-start) | copy-done | bytes 2097176
  80.5 0.7 collective-permute-done.5.third_ref
  81.2 6.0 %shard_map.78 = f32[8,512,128]{2,1,0:T(8,128)} custom-call(bf16[8,8,512,128]{3,2,1,0:T(8,128)(2,1)} %get-tuple-element.2.ham_ref, f32[8,512,128]{2,1,0:T(8,128)} %copy-done, bf16[4,8,128,128]{3,2,1,0:T(8,128)(2,1)} %collective-permute-done.5.third_ref), custom_call_target="tpu_custom_call" | custom-call | flops 1073741824 | bytes 8388608 | tf_op jit(solution)/shard_map/pallas_call | solution.py:139
  87.2 1.3 %fusion = bf16[8,2,128,128]{3,2,0,1:T(8,128)(2,1)S(1)} fusion(f32[8,2,2,128,128]{4,3,2,1,0:T(8,128)} %bitcast.20, s32[]{:T(128)S(6)} %select_n.84), kind=kLoop, calls=%fused_computation.6 | loop fusion | bytes 1048580 | tf_op jit(solution)/shard_map/convert_element_type | solution.py:160
  88.5 2.0 %collective-permute-start.6 = (bf16[8,2,128,128]{3,2,0,1:T(8,128)(2,1)S(1)}, bf16[8,2,128,128]{3,2,0,1:T(8,128)(2,1)S(1)}, u32[]{:S(2)}, u32[]{:S(2)}) collective-permute-start(bf16[8,2,128,128]{3,2,0,1:T(8,128)(2,1)S(1)} %fusion), channel_id=1, source_target_pairs={{0,1},{1,0},{2,3},{3,2},{4,5},{5,4},{6,7},{7,6},{8,9},{9,8},{10,11... | collective-permute-start | bytes 1572872 | tf_op jit(solution)/shard_map/ppermute | solution.py:160
  90.5 1.5 %collective-permute-done.6 = bf16[8,2,128,128]{3,2,0,1:T(8,128)(2,1)S(1)} collective-permute-done((bf16[8,2,128,128]{3,2,0,1:T(8,128)(2,1)S(1)}, bf16[8,2,128,128]{3,2,0,1:T(8,128)(2,1)S(1)}, u32[]{:S(2)}, u32[]{:S(2)}) %collective-permute-start.6) | collective-permute-done | bytes 524320 | tf_op jit(solution)/shard_map/ppermute | solution.py:160
  92.1 1.3 %bitcast_add_fusion = f32[8,2,128,128]{3,2,0,1:T(8,128)S(1)} fusion(bf16[8,2,128,128]{3,2,0,1:T(8,128)(2,1)S(1)} %collective-permute-done.6, f32[8,2,2,128,128]{4,3,2,1,0:T(8,128)} %bitcast.21, s32[]{:T(128)S(6)} %select_n.83), kind=kLoop, calls=%fused_computation.5 | loop fusion | flops 524288 | bytes 2621444 | tf_op jit(solution)/shard_map/add | solution.py:160
  93.5 1.4 %collective-permute-start.7 = (bf16[8,128,128]{2,1,0:T(8,128)(2,1)S(1)}, bf16[8,128,128]{2,1,0:T(8,128)(2,1)S(1)}, u32[]{:S(2)}, u32[]{:S(2)}) collective-permute-start(bf16[8,128,128]{2,1,0:T(8,128)(2,1)S(1)} %fusion.2), channel_id=1, source_target_pairs={{0,2},{1,3},{2,0},{3,1},{4,6},{5,7},{6,4},{7,5},{8,10},{9,11},{10,... | collective-permute-start | bytes 786440 | tf_op jit(solution)/shard_map/ppermute | solution.py:166
  94.8 6.2 %collective-permute-done.7 = bf16[8,128,128]{2,1,0:T(8,128)(2,1)S(1)} collective-permute-done((bf16[8,128,128]{2,1,0:T(8,128)(2,1)S(1)}, bf16[8,128,128]{2,1,0:T(8,128)(2,1)S(1)}, u32[]{:S(2)}, u32[]{:S(2)}) %collective-permute-start.7) | collective-permute-done | bytes 262176 | tf_op jit(solution)/shard_map/ppermute | solution.py:166
  101.0 0.8 fusion.1
  (19 shorter events, 1.4 us)
Async XLA Ops:
  0.6 25.2 %collective-permute-start = (bf16[2,512,512]{2,1,0:T(8,128)(2,1)}, bf16[2,512,512]{2,1,0:T(8,128)(2,1)S(1)}, u32[]{:S(2)}, u32[]{:S(2)}) collective-permute-start(bf16[2,512,512]{2,1,0:T(8,128)(2,1)} %local_ref.1), channel_id=1, source_target_pairs={{0,4},{1,125},{2,6},{3,127},{4,8},{5,1},{6,10},{7,3},{8,12},{9,5},... | collective-permute-start | bytes 3145736 | tf_op jit(solution)/shard_map/ppermute | solution.py:79
  10.1 22.0 %collective-permute-start.2 = (bf16[8,128,128]{2,1,0:T(8,128)(2,1)}, bf16[8,128,128]{2,1,0:T(8,128)(2,1)S(1)}, u32[]{:S(2)}, u32[]{:S(2)}) collective-permute-start(bf16[8,128,128]{2,1,0:T(8,128)(2,1)} %param.11), channel_id=1, source_target_pairs={{0,4},{4,8},{8,12},{12,16},{16,20},{20,24},{24,28},{28,32},{32,36}... | collective-permute-start | bytes 786440 | tf_op jit(solution)/shard_map/ppermute | solution.py:14
  10.1 46.9 %collective-permute-start.4 = (bf16[8,128,128]{2,1,0:T(8,128)(2,1)}, bf16[8,128,128]{2,1,0:T(8,128)(2,1)S(1)}, u32[]{:S(2)}, u32[]{:S(2)}) collective-permute-start(bf16[8,128,128]{2,1,0:T(8,128)(2,1)} %param.11), channel_id=1, source_target_pairs={{0,32},{4,36},{8,40},{12,44},{16,48},{20,52},{24,56},{28,60},{32,6... | collective-permute-start | bytes 786440 | tf_op jit(solution)/shard_map/ppermute | solution.py:14
  25.8 28.3 %collective-permute-start.1 = (bf16[2,512,512]{2,1,0:T(8,128)(2,1)S(1)}, bf16[2,512,512]{2,1,0:T(8,128)(2,1)}, u32[]{:S(2)}, u32[]{:S(2)}) collective-permute-start(bf16[2,512,512]{2,1,0:T(8,128)(2,1)S(1)} %collective-permute-done), channel_id=1, source_target_pairs={{0,1},{1,0},{2,3},{3,2},{4,5},{5,4},{6,7},{7,6},{8,9},{9,8},{10,11... | collective-permute-start | bytes 3145736 | tf_op jit(solution)/shard_map/ppermute | solution.py:80
  33.1 19.6 %collective-permute-start.3 = (bf16[2,8,128,128]{3,2,1,0:T(8,128)(2,1)S(1)}, bf16[2,8,128,128]{3,2,1,0:T(8,128)(2,1)S(1)}, u32[]{:S(2)}, u32[]{:S(2)}) collective-permute-start(bf16[2,8,128,128]{3,2,1,0:T(8,128)(2,1)S(1)} %pad_maximum_fusion.2), channel_id=1, source_target_pairs={{0,8},{4,12},{8,16},{12,20},{16,24},{20,28},{24,32},{28,36},{32,40... | collective-permute-start | bytes 1572872 | tf_op jit(solution)/shard_map/ppermute | solution.py:14
  53.7 27.4 %collective-permute-start.5 = (bf16[4,8,128,128]{3,2,1,0:T(8,128)(2,1)S(1)}, bf16[4,8,128,128]{3,2,1,0:T(8,128)(2,1)}, u32[]{:S(2)}, u32[]{:S(2)}) collective-permute-start(bf16[4,8,128,128]{3,2,1,0:T(8,128)(2,1)S(1)} %pad_maximum_fusion.1), channel_id=1, source_target_pairs={{0,16},{4,20},{8,24},{12,28},{16,32},{20,36},{24,40},{28,44},{32,4... | collective-permute-start | bytes 3145736 | tf_op jit(solution)/shard_map/ppermute | solution.py:14
  54.1 2.9 %copy-start.1 = (bf16[2,512,512]{2,1,0:T(8,128)(2,1)S(1)}, bf16[2,512,512]{2,1,0:T(8,128)(2,1)}, u32[]{:S(2)}) copy-start(bf16[2,512,512]{2,1,0:T(8,128)(2,1)} %local_ref.1) | copy-start | bytes 3145732
  79.1 1.3 %copy-start = (f32[8,512,128]{2,1,0:T(8,128)}, f32[8,512,128]{2,1,0:T(8,128)S(1)}, u32[]{:S(2)}) copy-start(f32[8,512,128]{2,1,0:T(8,128)S(1)} %get-tuple-element.5.early_ref) | copy-start | bytes 6291460
  88.5 3.6 %collective-permute-start.6 = (bf16[8,2,128,128]{3,2,0,1:T(8,128)(2,1)S(1)}, bf16[8,2,128,128]{3,2,0,1:T(8,128)(2,1)S(1)}, u32[]{:S(2)}, u32[]{:S(2)}) collective-permute-start(bf16[8,2,128,128]{3,2,0,1:T(8,128)(2,1)S(1)} %fusion), channel_id=1, source_target_pairs={{0,1},{1,0},{2,3},{3,2},{4,5},{5,4},{6,7},{7,6},{8,9},{9,8},{10,11... | collective-permute-start | bytes 1572872 | tf_op jit(solution)/shard_map/ppermute | solution.py:160
  93.5 7.6 %collective-permute-start.7 = (bf16[8,128,128]{2,1,0:T(8,128)(2,1)S(1)}, bf16[8,128,128]{2,1,0:T(8,128)(2,1)S(1)}, u32[]{:S(2)}, u32[]{:S(2)}) collective-permute-start(bf16[8,128,128]{2,1,0:T(8,128)(2,1)S(1)} %fusion.2), channel_id=1, source_target_pairs={{0,2},{1,3},{2,0},{3,1},{4,6},{5,7},{6,4},{7,5},{8,10},{9,11},{10,... | collective-permute-start | bytes 786440 | tf_op jit(solution)/shard_map/ppermute | solution.py:166

commit v14 on v13

--- a/solution.py
+++ b/solution.py
@@ -48,12 +48,19 @@
     early_ref[0] = early
 
 
-def product_kernel(ham_ref, early_ref, third_ref, part_ref):
+def product_kernel(band_ref, ham_ref, early_ref, third_ref, send_ref, keep_ref, part_ref):
     count = third_ref.shape[0]
+    rows = keep_ref.shape[2]
+    core = band_ref[0] % 2
     for k in range(ham_ref.shape[0]):
         wide = jnp.concatenate([ham_ref[k, 3 + s] for s in range(count)], axis=1)
         tall = jnp.concatenate([third_ref[s, k] for s in range(count)], axis=0)
-        part_ref[k] = early_ref[k] + jnp.dot(wide, tall, preferred_element_type=jnp.float32)
+        part_ref[...] = early_ref[k] + jnp.dot(wide, tall, preferred_element_type=jnp.float32)
+        for level in range(2):
+            own = pl.multiple_of((level * 2 + core) * rows, rows)
+            other = pl.multiple_of((level * 2 + 1 - core) * rows, rows)
+            keep_ref[k, level] = part_ref[pl.ds(own, rows), :]
+            send_ref[k, level] = part_ref[pl.ds(other, rows), :].astype(jnp.bfloat16)
 
 
 def on_device(coarse_kernel, interp_index, interp_weight, stop_order, intersection, trial_vectors):
@@ -136,28 +143,37 @@
             bytes_accessed=2 * fine_dev * block_order * (block_order + stop_count * column_count)),
     )(slot_index, band_index, weights, halo, coarse_kernel, intersection, intersection,
       first, second, last)
-    partial_value = pl.pallas_call(
+    row_block = block_order // band_count
+    half_fine = fine_dev // 2
+    send, keep = pl.pallas_call(
         product_kernel,
-        grid=(2,),
-        in_specs=[
-            pl.BlockSpec((fine_dev // 2, stop_count, block_order, column_count),
-                         lambda k: (k, 0, 0, 0)),
-            pl.BlockSpec((fine_dev // 2, block_order, vector_count), lambda k: (k, 0, 0)),
-            pl.BlockSpec((4, fine_dev // 2, column_count, vector_count), lambda k: (0, k, 0, 0)),
-        ],
-        out_specs=pl.BlockSpec((fine_dev // 2, block_order, vector_count), lambda k: (k, 0, 0)),
-        out_shape=jax.ShapeDtypeStruct((fine_dev, block_order, vector_count), jnp.float32),
+        grid_spec=pltpu.PrefetchScalarGridSpec(
+            num_scalar_prefetch=1,
+            grid=(2,),
+            in_specs=[
+                pl.BlockSpec((half_fine, stop_count, block_order, column_count),
+                             lambda k, bd: (k, 0, 0, 0)),
+                pl.BlockSpec((half_fine, block_order, vector_count), lambda k, bd: (k, 0, 0)),
+                pl.BlockSpec((4, half_fine, column_count, vector_count),
+                             lambda k, bd: (0, k, 0, 0)),
+            ],
+            out_specs=[
+                pl.BlockSpec((half_fine, 2, row_block, vector_count), lambda k, bd: (k, 0, 0, 0)),
+                pl.BlockSpec((half_fine, 2, row_block, vector_count), lambda k, bd: (k, 0, 0, 0)),
+            ],
+            scratch_shapes=[pltpu.VMEM((block_order, vector_count), jnp.float32)],
+        ),
+        out_shape=[
+            jax.ShapeDtypeStruct((fine_dev, 2, row_block, vector_count), jnp.bfloat16),
+            jax.ShapeDtypeStruct((fine_dev, 2, row_block, vector_count), jnp.float32),
+        ],
         cost_estimate=pl.CostEstimate(
             flops=2 * fine_dev * stop_count * block_order * column_count * vector_count,
             transcendentals=0,
             bytes_accessed=2 * fine_dev * stop_count * block_order * column_count),
-    )(hamiltonian, early_value, third)
-    row_block = block_order // band_count
-    halves = partial_value.reshape(fine_dev, 2, 2, row_block, vector_count)
-    send = lax.dynamic_index_in_dim(halves, 1 - core, 2, keepdims=False)
-    keep = lax.dynamic_index_in_dim(halves, core, 2, keepdims=False)
+    )(band_index, hamiltonian, early_value, third)
     swap = [(b, b ^ 1) for b in range(band_count)]
-    pair_sum = keep + lax.ppermute(send.astype(jnp.bfloat16), "band", swap).astype(jnp.float32)
+    pair_sum = keep + lax.ppermute(send, "band", swap).astype(jnp.float32)
     level = band // 2
     send = lax.dynamic_index_in_dim(pair_sum, 1 - level, 1, keepdims=False)
     keep = lax.dynamic_index_in_dim(pair_sum, level, 1, keepdims=False)

time: 102 us -> 102 us (level)
    ppermute x2 -> x1, starting transfers between devices: 3.4 us -> 1.38 us  [on_device(): lax.ppermute(send.astype(jnp.bfloat16), 'band', swap).astype(jnp.float32)]
    ppermute x0 -> x1, starting transfers between devices: none -> 1.94 us  [on_device(): pair_sum = keep + lax.ppermute(send, 'band', swap).astype(jnp.float32)]
    ppermute x0 -> x1, waiting for transfers between devices: none -> 1.75 us  [on_device(): pair_sum = keep + lax.ppermute(send, 'band', swap).astype(jnp.float32)]
    ppermute x2 -> x1, waiting for transfers between devices: 7.73 us -> 6.2 us  [on_device(): lax.ppermute(send.astype(jnp.bfloat16), 'band', swap).astype(jnp.float32)]
    convert_element_type x2 -> x1, local copies, waits for them, and re-layouts: 1.36 us -> 0.05 us  [on_device(): send.astype(jnp.bfloat16)]
    unnamed x6 -> x8, local copies, waits for them, and re-layouts: 2.93 us -> 3.9 us
  transfers between devices with their start and end apart: 8 -> 8, of which waited for: 5 -> 5; matrix products, arithmetic and copies ran while one was open for 9% -> 10% of each run, Pallas kernels for 22% -> 22%
where the time goes in v14:
time: 102 us; the launch traced here: 101 us
  waiting for transfers between devices  38.3 us (38%)
  Pallas kernels  28.1 us (28%)
  starting transfers between devices  19.9 us (20%)
  other arithmetic  8.78 us (9%)
  local copies, waits for them, and re-layouts  5.57 us (5%)
    pallas_call x1, Pallas kernels, on_device(): pl.pallas_call(kernel, grid_spec=grid_spec, out_shape=[jax.ShapeDtypeStru...  22.2 us
    ppermute x4, waiting for transfers between devices, shifted(): return lax.ppermute(value, axis, pairs)  16.6 us
    ppermute x1, waiting for transfers between devices, on_device(): near = lax.ppermute(coarse_kernel, ('blk', 'band'), pairs)  13.7 us
    ppermute x1, starting transfers between devices, on_device(): near = lax.ppermute(coarse_kernel, ('blk', 'band'), pairs)  9.47 us
    ppermute x1, waiting for transfers between devices, on_device(): lax.ppermute(send.astype(jnp.bfloat16), 'band', swap).astype(jnp.float32)  6.2 us
    ppermute x1, starting transfers between devices, on_device(): far = lax.ppermute(near, 'band', [(b, b ^ 1) for b in range(band_count)])  6.13 us
    pallas_call x1, Pallas kernels, on_device(): pl.pallas_call(product_kernel, grid_spec=pltpu.PrefetchScalarGridSpec(num...  5.95 us
    unnamed x8, local copies, waits for them, and re-layouts  3.9 us
  transfers between devices with their start and end apart: 8, of which 5 were waited for; matrix products, arithmetic and copies ran while one was open for 10% of the time, Pallas kernels for 22%

profile of v14, /device:TPU:1, one launch (start us, length us, event | category | flops | bytes accessed | tf_op | source)
XLA Modules:
  0.0 101.4 jit_solution(4541411749116770726)
XLA Ops:
  0.6 9.5 %collective-permute-start = (bf16[2,512,512]{2,1,0:T(8,128)(2,1)}, bf16[2,512,512]{2,1,0:T(8,128)(2,1)}, u32[]{:S(2)}, u32[]{:S(2)}) collective-permute-start(bf16[2,512,512]{2,1,0:T(8,128)(2,1)} %local_ref.1), channel_id=1, source_target_pairs={{0,4},{1,125},{2,6},{3,127},{4,8},{5,1},{6,10},{7,3},{8,12},{9,5},... | collective-permute-start | bytes 3145736 | tf_op jit(solution)/shard_map/ppermute | solution.py:86
  10.1 0.7 compare_select_fusion
  10.8 0.8 copy.8
  11.6 0.7 compare_and_fusion
  12.2 13.7 %collective-permute-done = bf16[2,512,512]{2,1,0:T(8,128)(2,1)} collective-permute-done((bf16[2,512,512]{2,1,0:T(8,128)(2,1)}, bf16[2,512,512]{2,1,0:T(8,128)(2,1)}, u32[]{:S(2)}, u32[]{:S(2)}) %collective-permute-start) | collective-permute-done | bytes 1048608 | tf_op jit(solution)/shard_map/ppermute | solution.py:86
  25.9 6.1 %collective-permute-start.1 = (bf16[2,512,512]{2,1,0:T(8,128)(2,1)}, bf16[2,512,512]{2,1,0:T(8,128)(2,1)}, u32[]{:S(2)}, u32[]{:S(2)}) collective-permute-start(bf16[2,512,512]{2,1,0:T(8,128)(2,1)} %collective-permute-done), channel_id=1, source_target_pairs={{0,1},{1,0},{2,3},{3,2},{4,5},{5,4},{6,7},{7,6},{8,9},{9,8},{10,11... | collective-permute-start | bytes 3145736 | tf_op jit(solution)/shard_map/ppermute | solution.py:87
  32.1 1.0 pad_maximum_fusion.2
  33.1 0.9 collective-permute-start.3
  34.0 0.6 gather_fusion
  34.9 0.8 copy.10
  35.7 0.6 gather_fusion.1
  36.4 16.3 %collective-permute-done.3.second_ref = bf16[2,8,128,128]{3,2,1,0:T(8,128)(2,1)S(1)} collective-permute-done((bf16[2,8,128,128]{3,2,1,0:T(8,128)(2,1)S(1)}, bf16[2,8,128,128]{3,2,1,0:T(8,128)(2,1)S(1)}, u32[]{:S(2)}, u32[]{:S(2)}) %collective-permute-start.3) | collective-permute-done | bytes 524320 | tf_op jit(solution)/shard_map/ppermute | solution.py:14
  52.7 1.1 %pad_maximum_fusion.1 = bf16[4,8,128,128]{3,2,1,0:T(8,128)(2,1)S(1)} fusion(bf16[2,8,128,128]{3,2,1,0:T(8,128)(2,1)S(1)} %collective-permute-done.3.second_ref, bf16[1,8,128,128]{3,2,1,0:T(8,128)(2,1)S(1)} %bitcast.14, bf16[1,8,128,128]{3,2,1,0:T(8,128)(2,1)} %bitcast.16), kind=kLoop, calls=%fused_computation.3 | loop fusion | flops 1048576 | bytes 2097152 | tf_op jit(solution)/shard_map/stack | solution.py:93
  54.1 3.1 %pad_maximum_fusion.halo_ref = bf16[4,512,512]{2,1,0:T(8,128)(2,1)} fusion(bf16[2,512,512]{2,1,0:T(8,128)(2,1)} %collective-permute-done.1, bf16[2,512,512]{2,1,0:T(8,128)(2,1)} %collective-permute-done), kind=kLoop, calls=%fused_computation.2 | loop fusion | flops 1048576 | bytes 4194304 | tf_op jit(solution)/shard_map/concatenate | solution.py:88
  57.3 22.2 %shard_map.77 = (bf16[8,8,512,128]{3,2,1,0:T(8,128)(2,1)}, f32[8,512,128]{2,1,0:T(8,128)S(1)}) custom-call(s32[256]{0:T(256)S(1)} %fusion.4.slot_ref, s32[1]{0:T(128)} %bitcast.1.band_ref, f32[256]{0:T(256)S(1)} %select_n.75.weight_ref, bf16[4,512,512]{2,1,0:T(8,128)(2,1)} %pad_maximum_fusion.halo_ref, bf16[2,512,512]{2,1,0:T(8,128)(2,1)S(1)} %copy-done.1, ...), custom_call_target="tpu_custom_call" | custom-call | flops 7516192768 | bytes 12582912 | tf_op jit(solution)/shard_map/pallas_call | solution.py:131
  79.4 1.3 %copy-done = f32[8,512,128]{2,1,0:T(8,128)} copy-done((f32[8,512,128]{2,1,0:T(8,128)}, f32[8,512,128]{2,1,0:T(8,128)S(1)}, u32[]{:S(2)}) %copy-start) | copy-done | bytes 2097176
  81.1 1.0 copy-done.2
  82.0 5.9 %shard_map.78 = (bf16[8,2,128,128]{3,2,1,0:T(8,128)(2,1)}, f32[8,2,128,128]{3,2,1,0:T(8,128)}) custom-call(s32[1]{0:T(128)} %bitcast.1.band_ref, bf16[8,8,512,128]{3,2,1,0:T(8,128)(2,1)} %get-tuple-element.4.ham_ref, f32[8,512,128]{2,1,0:T(8,128)} %copy-done, bf16[4,8,128,128]{3,2,1,0:T(8,128)(2,1)} %copy-done.2), custom_call_target="tpu_custom_call" | custom-call | flops 1073741824 | bytes 8388608 | tf_op jit(solution)/shard_map/pallas_call | solution.py:148
  88.0 1.9 %collective-permute-start.6 = (bf16[8,2,128,128]{3,2,1,0:T(8,128)(2,1)}, bf16[8,2,128,128]{3,2,1,0:T(8,128)(2,1)S(1)}, u32[]{:S(2)}, u32[]{:S(2)}) collective-permute-start(bf16[8,2,128,128]{3,2,1,0:T(8,128)(2,1)} %get-tuple-element.9), channel_id=1, source_target_pairs={{0,1},{1,0},{2,3},{3,2},{4,5},{5,4},{6,7},{7,6},{8,9},{9,8},{10,11... | collective-permute-start | bytes 1572872 | tf_op jit(solution)/shard_map/ppermute | solution.py:176
  89.9 1.7 %collective-permute-done.6 = bf16[8,2,128,128]{3,2,1,0:T(8,128)(2,1)S(1)} collective-permute-done((bf16[8,2,128,128]{3,2,1,0:T(8,128)(2,1)}, bf16[8,2,128,128]{3,2,1,0:T(8,128)(2,1)S(1)}, u32[]{:S(2)}, u32[]{:S(2)}) %collective-permute-start.6) | collective-permute-done | bytes 524320 | tf_op jit(solution)/shard_map/ppermute | solution.py:176
  91.7 1.3 %convert_add_fusion = f32[8,2,128,128]{3,2,1,0:T(8,128)S(1)} fusion(f32[8,2,128,128]{3,2,1,0:T(8,128)} %get-tuple-element.8, bf16[8,2,128,128]{3,2,1,0:T(8,128)(2,1)S(1)} %collective-permute-done.6), kind=kLoop, calls=%fused_computation.4 | loop fusion | flops 524288 | bytes 2621440 | tf_op jit(solution)/shard_map/add | solution.py:176
  93.1 1.4 %collective-permute-start.7 = (bf16[8,128,128]{2,1,0:T(8,128)(2,1)S(1)}, bf16[8,128,128]{2,1,0:T(8,128)(2,1)S(1)}, u32[]{:S(2)}, u32[]{:S(2)}) collective-permute-start(bf16[8,128,128]{2,1,0:T(8,128)(2,1)S(1)} %fusion.1), channel_id=1, source_target_pairs={{0,2},{1,3},{2,0},{3,1},{4,6},{5,7},{6,4},{7,5},{8,10},{9,11},{10,... | collective-permute-start | bytes 786440 | tf_op jit(solution)/shard_map/ppermute | solution.py:182
  94.4 6.2 %collective-permute-done.7 = bf16[8,128,128]{2,1,0:T(8,128)(2,1)S(1)} collective-permute-done((bf16[8,128,128]{2,1,0:T(8,128)(2,1)S(1)}, bf16[8,128,128]{2,1,0:T(8,128)(2,1)S(1)}, u32[]{:S(2)}, u32[]{:S(2)}) %collective-permute-start.7) | collective-permute-done | bytes 262176 | tf_op jit(solution)/shard_map/ppermute | solution.py:182
  100.6 0.8 fusion
  (20 shorter events, 1.1 us)
Async XLA Ops:
  0.6 25.3 %collective-permute-start = (bf16[2,512,512]{2,1,0:T(8,128)(2,1)}, bf16[2,512,512]{2,1,0:T(8,128)(2,1)}, u32[]{:S(2)}, u32[]{:S(2)}) collective-permute-start(bf16[2,512,512]{2,1,0:T(8,128)(2,1)} %local_ref.1), channel_id=1, source_target_pairs={{0,4},{1,125},{2,6},{3,127},{4,8},{5,1},{6,10},{7,3},{8,12},{9,5},... | collective-permute-start | bytes 3145736 | tf_op jit(solution)/shard_map/ppermute | solution.py:86
  10.1 22.0 %collective-permute-start.2 = (bf16[8,128,128]{2,1,0:T(8,128)(2,1)}, bf16[8,128,128]{2,1,0:T(8,128)(2,1)S(1)}, u32[]{:S(2)}, u32[]{:S(2)}) collective-permute-start(bf16[8,128,128]{2,1,0:T(8,128)(2,1)} %param.11), channel_id=1, source_target_pairs={{0,4},{4,8},{8,12},{12,16},{16,20},{20,24},{24,28},{28,32},{32,36}... | collective-permute-start | bytes 786440 | tf_op jit(solution)/shard_map/ppermute | solution.py:14
  10.1 47.2 %collective-permute-start.4 = (bf16[8,128,128]{2,1,0:T(8,128)(2,1)}, bf16[8,128,128]{2,1,0:T(8,128)(2,1)S(1)}, u32[]{:S(2)}, u32[]{:S(2)}) collective-permute-start(bf16[8,128,128]{2,1,0:T(8,128)(2,1)} %param.11), channel_id=1, source_target_pairs={{0,32},{4,36},{8,40},{12,44},{16,48},{20,52},{24,56},{28,60},{32,6... | collective-permute-start | bytes 786440 | tf_op jit(solution)/shard_map/ppermute | solution.py:14
  25.9 28.2 %collective-permute-start.1 = (bf16[2,512,512]{2,1,0:T(8,128)(2,1)}, bf16[2,512,512]{2,1,0:T(8,128)(2,1)}, u32[]{:S(2)}, u32[]{:S(2)}) collective-permute-start(bf16[2,512,512]{2,1,0:T(8,128)(2,1)} %collective-permute-done), channel_id=1, source_target_pairs={{0,1},{1,0},{2,3},{3,2},{4,5},{5,4},{6,7},{7,6},{8,9},{9,8},{10,11... | collective-permute-start | bytes 3145736 | tf_op jit(solution)/shard_map/ppermute | solution.py:87
  33.1 19.6 %collective-permute-start.3 = (bf16[2,8,128,128]{3,2,1,0:T(8,128)(2,1)S(1)}, bf16[2,8,128,128]{3,2,1,0:T(8,128)(2,1)S(1)}, u32[]{:S(2)}, u32[]{:S(2)}) collective-permute-start(bf16[2,8,128,128]{3,2,1,0:T(8,128)(2,1)S(1)} %pad_maximum_fusion.2), channel_id=1, source_target_pairs={{0,8},{4,12},{8,16},{12,20},{16,24},{20,28},{24,32},{28,36},{32,40... | collective-permute-start | bytes 1572872 | tf_op jit(solution)/shard_map/ppermute | solution.py:14
  53.7 27.3 %collective-permute-start.5 = (bf16[4,8,128,128]{3,2,1,0:T(8,128)(2,1)S(1)}, bf16[4,8,128,128]{3,2,1,0:T(8,128)(2,1)S(1)}, u32[]{:S(2)}, u32[]{:S(2)}) collective-permute-start(bf16[4,8,128,128]{3,2,1,0:T(8,128)(2,1)S(1)} %pad_maximum_fusion.1), channel_id=1, source_target_pairs={{0,16},{4,20},{8,24},{12,28},{16,32},{20,36},{24,40},{28,44},{32,4... | collective-permute-start | bytes 3145736 | tf_op jit(solution)/shard_map/ppermute | solution.py:14
  54.1 3.2 %copy-start.1 = (bf16[2,512,512]{2,1,0:T(8,128)(2,1)S(1)}, bf16[2,512,512]{2,1,0:T(8,128)(2,1)}, u32[]{:S(2)}) copy-start(bf16[2,512,512]{2,1,0:T(8,128)(2,1)} %local_ref.1) | copy-start | bytes 3145732
  79.4 1.3 %copy-start = (f32[8,512,128]{2,1,0:T(8,128)}, f32[8,512,128]{2,1,0:T(8,128)S(1)}, u32[]{:S(2)}) copy-start(f32[8,512,128]{2,1,0:T(8,128)S(1)} %get-tuple-element.7.early_ref) | copy-start | bytes 6291460
  81.1 1.0 copy-start.2
  88.0 3.7 %collective-permute-start.6 = (bf16[8,2,128,128]{3,2,1,0:T(8,128)(2,1)}, bf16[8,2,128,128]{3,2,1,0:T(8,128)(2,1)S(1)}, u32[]{:S(2)}, u32[]{:S(2)}) collective-permute-start(bf16[8,2,128,128]{3,2,1,0:T(8,128)(2,1)} %get-tuple-element.9), channel_id=1, source_target_pairs={{0,1},{1,0},{2,3},{3,2},{4,5},{5,4},{6,7},{7,6},{8,9},{9,8},{10,11... | collective-permute-start | bytes 1572872 | tf_op jit(solution)/shard_map/ppermute | solution.py:176
  93.1 7.6 %collective-permute-start.7 = (bf16[8,128,128]{2,1,0:T(8,128)(2,1)S(1)}, bf16[8,128,128]{2,1,0:T(8,128)(2,1)S(1)}, u32[]{:S(2)}, u32[]{:S(2)}) collective-permute-start(bf16[8,128,128]{2,1,0:T(8,128)(2,1)S(1)} %fusion.1), channel_id=1, source_target_pairs={{0,2},{1,3},{2,0},{3,1},{4,6},{5,7},{6,4},{7,5},{8,10},{9,11},{10,... | collective-permute-start | bytes 786440 | tf_op jit(solution)/shard_map/ppermute | solution.py:182

commit v15 on v14

--- a/solution.py
+++ b/solution.py
@@ -79,11 +79,16 @@
     band_count = lax.axis_size("band")
     core = band % 2
     pairs = []
+    cross = []
     for i in range(cycle_length):
         for b in range(band_count):
             target = (i + 1) % cycle_length if b % 2 == 0 else (i - 1) % cycle_length
-            pairs.append((i * band_count + b, target * band_count + b))
-    near = lax.ppermute(coarse_kernel, ("blk", "band"), pairs)
+            pairs.append((i * band_count + b, target * band_count + (b ^ 2)))
+            target = (i + 1) % cycle_length if b % 2 == 1 else (i - 1) % cycle_length
+            cross.append((i * band_count + b, target * band_count + (b ^ 3)))
+    near = jnp.concatenate([
+        lax.ppermute(coarse_kernel[:1], ("blk", "band"), pairs),
+        lax.ppermute(coarse_kernel[1:], ("blk", "band"), cross)], axis=0)
     far = lax.ppermute(near, "band", [(b, b ^ 1) for b in range(band_count)])
     halo = jnp.concatenate([near, far], axis=0)
     assert stop_count == 8

time: 102 us -> 103 us (level)
  waiting for transfers between devices: 38.3 us -> 48.3 us
  starting transfers between devices: 19.9 us -> 12.4 us
  other arithmetic: 8.78 us -> 7.32 us
    ppermute x1 -> x2, waiting for transfers between devices: 13.7 us -> 23.8 us  [the longest x1 16.1 us: on_device(): lax.ppermute(coarse_kernel[:1], ('blk', 'band'), pairs)]
    ppermute x1, starting transfers between devices: 6.13 us -> 0.01 us  [on_device(): far = lax.ppermute(near, 'band', [(b, b ^ 1) for b in range(band_count)])]
    ppermute x4, waiting for transfers between devices: 16.6 us -> 15.2 us  [shifted(): return lax.ppermute(value, axis, pairs)]
    unnamed x8 -> x16, local copies, waits for them, and re-layouts: 3.9 us -> 2.5 us
    slice x0 -> x1, local copies, waits for them, and re-layouts: none -> 1.31 us  [on_device(): coarse_kernel[:1]]
    ppermute x1, starting transfers between devices: 1.38 us -> 0.1 us  [on_device(): lax.ppermute(send.astype(jnp.bfloat16), 'band', swap).astype(jnp.float32)]
    ppermute x1, waiting for transfers between devices: 6.2 us -> 7.47 us  [on_device(): lax.ppermute(send.astype(jnp.bfloat16), 'band', swap).astype(jnp.float32)]
    concatenate x0 -> x1, other arithmetic: none -> 1.06 us  [on_device(): jnp.concatenate([lax.ppermute(coarse_kernel[:1], ('blk', 'band'), pairs),...]
  transfers between devices with their start and end apart: 8 -> 9, of which waited for: 5 -> 6; matrix products, arithmetic and copies ran while one was open for 10% -> 7% of each run, Pallas kernels for 22% -> 22%
where the time goes in v15:
time: 103 us; the launch traced here: 102 us
  waiting for transfers between devices  48.3 us (47%)
  Pallas kernels  28.2 us (27%)
  starting transfers between devices  12.4 us (12%)
  other arithmetic  7.32 us (7%)
  local copies, waits for them, and re-layouts  5.48 us (5%)
    pallas_call x1, Pallas kernels, on_device(): pl.pallas_call(kernel, grid_spec=grid_spec, out_shape=[jax.ShapeDtypeStru...  22.2 us
    ppermute x1, waiting for transfers between devices, on_device(): lax.ppermute(coarse_kernel[:1], ('blk', 'band'), pairs)  16.1 us
    ppermute x4, waiting for transfers between devices, shifted(): return lax.ppermute(value, axis, pairs)  15.2 us
    ppermute x1, starting transfers between devices, on_device(): lax.ppermute(coarse_kernel[:1], ('blk', 'band'), pairs)  9.29 us
    ppermute x1, waiting for transfers between devices, on_device(): lax.ppermute(coarse_kernel[1:], ('blk', 'band'), cross)  7.74 us
    ppermute x1, waiting for transfers between devices, on_device(): lax.ppermute(send.astype(jnp.bfloat16), 'band', swap).astype(jnp.float32)  7.47 us
    pallas_call x1, Pallas kernels, on_device(): pl.pallas_call(product_kernel, grid_spec=pltpu.PrefetchScalarGridSpec(num...  5.97 us
    concatenate x1, other arithmetic, on_device(): halo = jnp.concatenate([near, far], axis=0)  2.85 us
  transfers between devices with their start and end apart: 9, of which 6 were waited for; matrix products, arithmetic and copies ran while one was open for 7% of the time, Pallas kernels for 22%

profile of v15, /device:TPU:1, one launch (start us, length us, event | category | flops | bytes accessed | tf_op | source)
XLA Modules:
  0.0 102.5 jit_solution(9641390270712008920)
XLA Ops:
  0.7 1.3 %fusion.6 = (bf16[1,512,512]{2,1,0:T(8,128)(2,1)S(1)}, bf16[1,512,512]{2,1,0:T(8,128)(2,1)S(1)}) fusion(bf16[2,512,512]{2,1,0:T(8,128)(2,1)} %local_ref.1), kind=kLoop, calls=%fused_computation.29 | loop fusion | bytes 2097152 | tf_op jit(solution)/shard_map/slice | solution.py:90
  2.0 9.3 %collective-permute-start = (bf16[1,512,512]{2,1,0:T(8,128)(2,1)S(1)}, bf16[1,512,512]{2,1,0:T(8,128)(2,1)S(1)}, u32[]{:S(2)}, u32[]{:S(2)}) collective-permute-start(bf16[1,512,512]{2,1,0:T(8,128)(2,1)S(1)} %get-tuple-element.10), channel_id=1, source_target_pairs={{0,6},{1,127},{2,4},{3,125},{4,10},{5,3},{6,8},{7,1},{8,14},{9,7},... | collective-permute-start | bytes 1572872 | tf_op jit(solution)/shard_map/ppermute | solution.py:90
  11.5 16.1 %collective-permute-done = bf16[1,512,512]{2,1,0:T(8,128)(2,1)S(1)} collective-permute-done((bf16[1,512,512]{2,1,0:T(8,128)(2,1)S(1)}, bf16[1,512,512]{2,1,0:T(8,128)(2,1)S(1)}, u32[]{:S(2)}, u32[]{:S(2)}) %collective-permute-start) | collective-permute-done | bytes 524320 | tf_op jit(solution)/shard_map/ppermute | solution.py:90
  27.6 7.7 %collective-permute-done.1 = bf16[1,512,512]{2,1,0:T(8,128)(2,1)S(1)} collective-permute-done((bf16[1,512,512]{2,1,0:T(8,128)(2,1)S(1)}, bf16[1,512,512]{2,1,0:T(8,128)(2,1)S(1)}, u32[]{:S(2)}, u32[]{:S(2)}) %collective-permute-start.1) | collective-permute-done | bytes 524320 | tf_op jit(solution)/shard_map/ppermute | solution.py:91
  35.3 1.1 %pad_maximum_fusion.1 = bf16[2,512,512]{2,1,0:T(8,128)(2,1)} fusion(bf16[1,512,512]{2,1,0:T(8,128)(2,1)S(1)} %collective-permute-done.1, bf16[1,512,512]{2,1,0:T(8,128)(2,1)S(1)} %collective-permute-done), kind=kLoop, calls=%fused_computation.3 | loop fusion | flops 524288 | bytes 2097152 | tf_op jit(solution)/shard_map/concatenate | solution.py:89
  36.5 1.0 collective-permute-start.4
  37.5 0.6 gather_fusion
  38.1 0.1 copy.9
  38.3 0.1 sub.33
  38.5 0.6 gather_fusion.1
  39.1 14.5 %collective-permute-done.4.second_ref = bf16[2,8,128,128]{3,2,1,0:T(8,128)(2,1)S(1)} collective-permute-done((bf16[2,8,128,128]{3,2,1,0:T(8,128)(2,1)S(1)}, bf16[2,8,128,128]{3,2,1,0:T(8,128)(2,1)S(1)}, u32[]{:S(2)}, u32[]{:S(2)}) %collective-permute-start.4) | collective-permute-done | bytes 524320 | tf_op jit(solution)/shard_map/ppermute | solution.py:14
  53.6 1.1 %pad_maximum_fusion.2 = bf16[4,8,128,128]{3,2,1,0:T(8,128)(2,1)} fusion(bf16[2,8,128,128]{3,2,1,0:T(8,128)(2,1)S(1)} %collective-permute-done.4.second_ref, bf16[1,8,128,128]{3,2,1,0:T(8,128)(2,1)S(1)} %bitcast.14, bf16[1,8,128,128]{3,2,1,0:T(8,128)(2,1)S(1)} %bitcast.16), kind=kLoop, calls=%fused_computation.4 | loop fusion | flops 1048576 | bytes 2097152 | tf_op jit(solution)/shard_map/stack | solution.py:98
  54.7 0.1 copy.11
  54.9 2.9 %pad_maximum_fusion.halo_ref = bf16[4,512,512]{2,1,0:T(8,128)(2,1)} fusion(bf16[2,512,512]{2,1,0:T(8,128)(2,1)} %collective-permute-done.2, bf16[1,512,512]{2,1,0:T(8,128)(2,1)S(1)} %collective-permute-done.1, bf16[1,512,512]{2,1,0:T(8,128)(2,1)S(1)} %collective-permute-done), kind=kLoop, calls=%fused_computation.2 | loop fusion | flops 2097152 | bytes 4194304 | tf_op jit(solution)/shard_map/concatenate | solution.py:93
  57.8 22.2 %shard_map.77 = (bf16[8,8,512,128]{3,2,1,0:T(8,128)(2,1)}, f32[8,512,128]{2,1,0:T(8,128)S(1)}) custom-call(s32[256]{0:T(256)S(1)} %fusion.4.slot_ref, s32[1]{0:T(128)} %bitcast.1.band_ref, f32[256]{0:T(256)S(1)} %select_n.75.weight_ref, bf16[4,512,512]{2,1,0:T(8,128)(2,1)} %pad_maximum_fusion.halo_ref, bf16[2,512,512]{2,1,0:T(8,128)(2,1)S(1)} %copy-done.1, ...), custom_call_target="tpu_custom_call" | custom-call | flops 7516192768 | bytes 12582912 | tf_op jit(solution)/shard_map/pallas_call | solution.py:136
  80.0 1.3 %copy-done = f32[8,512,128]{2,1,0:T(8,128)} copy-done((f32[8,512,128]{2,1,0:T(8,128)}, f32[8,512,128]{2,1,0:T(8,128)S(1)}, u32[]{:S(2)}) %copy-start) | copy-done | bytes 2097176
  81.4 0.8 collective-permute-done.6.third_ref
  82.1 1.0 copy-done.2
  83.1 6.0 %shard_map.78 = (bf16[8,2,128,128]{3,2,1,0:T(8,128)(2,1)}, f32[8,2,128,128]{3,2,1,0:T(8,128)}) custom-call(s32[1]{0:T(128)} %bitcast.1.band_ref, bf16[8,8,512,128]{3,2,1,0:T(8,128)(2,1)} %get-tuple-element.4.ham_ref, f32[8,512,128]{2,1,0:T(8,128)} %copy-done, bf16[4,8,128,128]{3,2,1,0:T(8,128)(2,1)} %copy-done.2), custom_call_target="tpu_custom_call" | custom-call | flops 1073741824 | bytes 8388608 | tf_op jit(solution)/shard_map/pallas_call | solution.py:153
  89.1 1.9 %collective-permute-start.7 = (bf16[8,2,128,128]{3,2,1,0:T(8,128)(2,1)}, bf16[8,2,128,128]{3,2,1,0:T(8,128)(2,1)S(1)}, u32[]{:S(2)}, u32[]{:S(2)}) collective-permute-start(bf16[8,2,128,128]{3,2,1,0:T(8,128)(2,1)} %get-tuple-element.9), channel_id=1, source_target_pairs={{0,1},{1,0},{2,3},{3,2},{4,5},{5,4},{6,7},{7,6},{8,9},{9,8},{10,11... | collective-permute-start | bytes 1572872 | tf_op jit(solution)/shard_map/ppermute | solution.py:181
  91.0 1.7 %collective-permute-done.7 = bf16[8,2,128,128]{3,2,1,0:T(8,128)(2,1)S(1)} collective-permute-done((bf16[8,2,128,128]{3,2,1,0:T(8,128)(2,1)}, bf16[8,2,128,128]{3,2,1,0:T(8,128)(2,1)S(1)}, u32[]{:S(2)}, u32[]{:S(2)}) %collective-permute-start.7) | collective-permute-done | bytes 524320 | tf_op jit(solution)/shard_map/ppermute | solution.py:181
  92.7 1.3 %convert_add_fusion = f32[8,2,128,128]{3,2,1,0:T(8,128)S(1)} fusion(f32[8,2,128,128]{3,2,1,0:T(8,128)} %get-tuple-element.8, bf16[8,2,128,128]{3,2,1,0:T(8,128)(2,1)S(1)} %collective-permute-done.7), kind=kLoop, calls=%fused_computation.5 | loop fusion | flops 524288 | bytes 2621440 | tf_op jit(solution)/shard_map/add | solution.py:181
  94.2 7.5 %collective-permute-done.8 = bf16[8,128,128]{2,1,0:T(8,128)(2,1)S(1)} collective-permute-done((bf16[8,128,128]{2,1,0:T(8,128)(2,1)S(1)}, bf16[8,128,128]{2,1,0:T(8,128)(2,1)S(1)}, u32[]{:S(2)}, u32[]{:S(2)}) %collective-permute-start.8) | collective-permute-done | bytes 262176 | tf_op jit(solution)/shard_map/ppermute | solution.py:187
  101.7 0.8 fusion
  (32 shorter events, 0.8 us)
Async XLA Ops:
  0.6 10.6 %copy-start.3 = (bf16[8,128,128]{2,1,0:T(8,128)(2,1)S(1)}, bf16[8,128,128]{2,1,0:T(8,128)(2,1)}, u32[]{:S(2)}) copy-start(bf16[8,128,128]{2,1,0:T(8,128)(2,1)} %param.11) | copy-start | bytes 786436
  0.6 10.7 %copy-start.4 = (s32[8,8,4]{1,2,0:T(4,128)S(1)}, s32[8,8,4]{1,2,0:T(4,128)}, u32[]{:S(2)}) copy-start(s32[8,8,4]{1,2,0:T(4,128)} %param.7) | copy-start | bytes 3076
  0.7 10.8 %copy-start.6 = (s32[8]{0:T(128)S(1)}, s32[8]{0:T(128)}, u32[]{:S(2)}) copy-start(s32[8]{0:T(128)} %param.9) | copy-start | bytes 100
  2.0 36.4 %copy-start.5 = (f32[8,8,4]{1,2,0:T(4,128)S(1)}, f32[8,8,4]{1,2,0:T(4,128)}, u32[]{:S(2)}) copy-start(f32[8,8,4]{1,2,0:T(4,128)} %param.8) | copy-start | bytes 3076
  2.0 25.6 %collective-permute-start = (bf16[1,512,512]{2,1,0:T(8,128)(2,1)S(1)}, bf16[1,512,512]{2,1,0:T(8,128)(2,1)S(1)}, u32[]{:S(2)}, u32[]{:S(2)}) collective-permute-start(bf16[1,512,512]{2,1,0:T(8,128)(2,1)S(1)} %get-tuple-element.10), channel_id=1, source_target_pairs={{0,6},{1,127},{2,4},{3,125},{4,10},{5,3},{6,8},{7,1},{8,14},{9,7},... | collective-permute-start | bytes 1572872 | tf_op jit(solution)/shard_map/ppermute | solution.py:90
  11.3 24.1 %collective-permute-start.1 = (bf16[1,512,512]{2,1,0:T(8,128)(2,1)S(1)}, bf16[1,512,512]{2,1,0:T(8,128)(2,1)S(1)}, u32[]{:S(2)}, u32[]{:S(2)}) collective-permute-start(bf16[1,512,512]{2,1,0:T(8,128)(2,1)S(1)} %get-tuple-element.11), channel_id=1, source_target_pairs={{0,127},{1,6},{2,125},{3,4},{4,3},{5,10},{6,1},{7,8},{8,7},{9,14},... | collective-permute-start | bytes 1572872 | tf_op jit(solution)/shard_map/ppermute | solution.py:91
  11.3 25.1 %collective-permute-start.3 = (bf16[8,128,128]{2,1,0:T(8,128)(2,1)S(1)}, bf16[8,128,128]{2,1,0:T(8,128)(2,1)S(1)}, u32[]{:S(2)}, u32[]{:S(2)}) collective-permute-start(bf16[8,128,128]{2,1,0:T(8,128)(2,1)S(1)} %copy-done.3), channel_id=1, source_target_pairs={{0,4},{4,8},{8,12},{12,16},{16,20},{20,24},{24,28},{28,32},{32,36}... | collective-permute-start | bytes 786440 | tf_op jit(solution)/shard_map/ppermute | solution.py:14
  11.3 46.5 %collective-permute-start.5 = (bf16[8,128,128]{2,1,0:T(8,128)(2,1)S(1)}, bf16[8,128,128]{2,1,0:T(8,128)(2,1)S(1)}, u32[]{:S(2)}, u32[]{:S(2)}) collective-permute-start(bf16[8,128,128]{2,1,0:T(8,128)(2,1)S(1)} %copy-done.3), channel_id=1, source_target_pairs={{0,32},{4,36},{8,40},{12,44},{16,48},{20,52},{24,56},{28,60},{32,6... | collective-permute-start | bytes 786440 | tf_op jit(solution)/shard_map/ppermute | solution.py:14
  36.4 18.5 %collective-permute-start.2 = (bf16[2,512,512]{2,1,0:T(8,128)(2,1)}, bf16[2,512,512]{2,1,0:T(8,128)(2,1)}, u32[]{:S(2)}, u32[]{:S(2)}) collective-permute-start(bf16[2,512,512]{2,1,0:T(8,128)(2,1)} %pad_maximum_fusion.1), channel_id=1, source_target_pairs={{0,1},{1,0},{2,3},{3,2},{4,5},{5,4},{6,7},{7,6},{8,9},{9,8},{10,11... | collective-permute-start | bytes 3145736 | tf_op jit(solution)/shard_map/ppermute | solution.py:92
  36.5 17.1 %collective-permute-start.4 = (bf16[2,8,128,128]{3,2,1,0:T(8,128)(2,1)S(1)}, bf16[2,8,128,128]{3,2,1,0:T(8,128)(2,1)S(1)}, u32[]{:S(2)}, u32[]{:S(2)}) collective-permute-start(bf16[2,8,128,128]{3,2,1,0:T(8,128)(2,1)S(1)} %pad_maximum_fusion.3), channel_id=1, source_target_pairs={{0,8},{4,12},{8,16},{12,20},{16,24},{20,28},{24,32},{28,36},{32,40... | collective-permute-start | bytes 1572872 | tf_op jit(solution)/shard_map/ppermute | solution.py:14
  54.7 27.5 %collective-permute-start.6 = (bf16[4,8,128,128]{3,2,1,0:T(8,128)(2,1)}, bf16[4,8,128,128]{3,2,1,0:T(8,128)(2,1)S(1)}, u32[]{:S(2)}, u32[]{:S(2)}) collective-permute-start(bf16[4,8,128,128]{3,2,1,0:T(8,128)(2,1)} %pad_maximum_fusion.2), channel_id=1, source_target_pairs={{0,16},{4,20},{8,24},{12,28},{16,32},{20,36},{24,40},{28,44},{32,4... | collective-permute-start | bytes 3145736 | tf_op jit(solution)/shard_map/ppermute | solution.py:14
  54.9 2.9 %copy-start.1 = (bf16[2,512,512]{2,1,0:T(8,128)(2,1)S(1)}, bf16[2,512,512]{2,1,0:T(8,128)(2,1)}, u32[]{:S(2)}) copy-start(bf16[2,512,512]{2,1,0:T(8,128)(2,1)} %local_ref.1) | copy-start | bytes 3145732
  80.0 1.3 %copy-start = (f32[8,512,128]{2,1,0:T(8,128)}, f32[8,512,128]{2,1,0:T(8,128)S(1)}, u32[]{:S(2)}) copy-start(f32[8,512,128]{2,1,0:T(8,128)S(1)} %get-tuple-element.7.early_ref) | copy-start | bytes 6291460
  82.1 1.0 copy-start.2
  89.1 3.7 %collective-permute-start.7 = (bf16[8,2,128,128]{3,2,1,0:T(8,128)(2,1)}, bf16[8,2,128,128]{3,2,1,0:T(8,128)(2,1)S(1)}, u32[]{:S(2)}, u32[]{:S(2)}) collective-permute-start(bf16[8,2,128,128]{3,2,1,0:T(8,128)(2,1)} %get-tuple-element.9), channel_id=1, source_target_pairs={{0,1},{1,0},{2,3},{3,2},{4,5},{5,4},{6,7},{7,6},{8,9},{9,8},{10,11... | collective-permute-start | bytes 1572872 | tf_op jit(solution)/shard_map/ppermute | solution.py:181
  94.1 7.6 %collective-permute-start.8 = (bf16[8,128,128]{2,1,0:T(8,128)(2,1)S(1)}, bf16[8,128,128]{2,1,0:T(8,128)(2,1)S(1)}, u32[]{:S(2)}, u32[]{:S(2)}) collective-permute-start(bf16[8,128,128]{2,1,0:T(8,128)(2,1)S(1)} %fusion.1), channel_id=1, source_target_pairs={{0,2},{1,3},{2,0},{3,1},{4,6},{5,7},{6,4},{7,5},{8,10},{9,11},{10,... | collective-permute-start | bytes 786440 | tf_op jit(solution)/shard_map/ppermute | solution.py:187

commit v16 on v14

--- a/solution.py
+++ b/solution.py
@@ -48,12 +48,14 @@
     early_ref[0] = early
 
 
-def product_kernel(band_ref, ham_ref, early_ref, third_ref, send_ref, keep_ref, part_ref):
+def product_kernel(band_ref, head_ref, middle_ref, tail_ref, early_ref, third_ref, send_ref,
+                   keep_ref, part_ref):
     count = third_ref.shape[0]
     rows = keep_ref.shape[2]
     core = band_ref[0] % 2
-    for k in range(ham_ref.shape[0]):
-        wide = jnp.concatenate([ham_ref[k, 3 + s] for s in range(count)], axis=1)
+    for k in range(head_ref.shape[0]):
+        pieces = [head_ref[k, 0], middle_ref[k, 0], middle_ref[k, 1], tail_ref[k, 0]]
+        wide = jnp.concatenate(pieces, axis=1)
         tall = jnp.concatenate([third_ref[s, k] for s in range(count)], axis=0)
         part_ref[...] = early_ref[k] + jnp.dot(wide, tall, preferred_element_type=jnp.float32)
         for level in range(2):
@@ -151,8 +153,12 @@
             num_scalar_prefetch=1,
             grid=(2,),
             in_specs=[
-                pl.BlockSpec((half_fine, stop_count, block_order, column_count),
-                             lambda k, bd: (k, 0, 0, 0)),
+                pl.BlockSpec((half_fine, 1, block_order, column_count),
+                             lambda k, bd: (k, 3, 0, 0)),
+                pl.BlockSpec((half_fine, 2, block_order, column_count),
+                             lambda k, bd: (k, 2, 0, 0)),
+                pl.BlockSpec((half_fine, 1, block_order, column_count),
+                             lambda k, bd: (k, 6, 0, 0)),
                 pl.BlockSpec((half_fine, block_order, vector_count), lambda k, bd: (k, 0, 0)),
                 pl.BlockSpec((4, half_fine, column_count, vector_count),
                              lambda k, bd: (0, k, 0, 0)),
@@ -171,7 +177,7 @@
             flops=2 * fine_dev * stop_count * block_order * column_count * vector_count,
             transcendentals=0,
             bytes_accessed=2 * fine_dev * stop_count * block_order * column_count),
-    )(band_index, hamiltonian, early_value, third)
+    )(band_index, hamiltonian, hamiltonian, hamiltonian, early_value, third)
     swap = [(b, b ^ 1) for b in range(band_count)]
     pair_sum = keep + lax.ppermute(send, "band", swap).astype(jnp.float32)
     level = band // 2

time: 102 us -> 99.7 us (0.977)
  Pallas kernels: 28.1 us -> 27 us
    pallas_call x1, Pallas kernels: 5.95 us -> 4.79 us  [on_device(): pl.pallas_call(product_kernel, grid_spec=pltpu.PrefetchScalarGridSpec(num...]
    unnamed x8 -> x6, local copies, waits for them, and re-layouts: 3.9 us -> 2.92 us
where the time goes in v16:
time: 99.7 us; the launch traced here: 99.4 us
  waiting for transfers between devices  38.6 us (39%)
  Pallas kernels  27 us (27%)
  starting transfers between devices  20 us (20%)
  other arithmetic  8.47 us (8%)
  local copies, waits for them, and re-layouts  4.59 us (5%)
    pallas_call x1, Pallas kernels, on_device(): pl.pallas_call(kernel, grid_spec=grid_spec, out_shape=[jax.ShapeDtypeStru...  22.2 us
    ppermute x4, waiting for transfers between devices, shifted(): return lax.ppermute(value, axis, pairs)  17.1 us
    ppermute x1, waiting for transfers between devices, on_device(): near = lax.ppermute(coarse_kernel, ('blk', 'band'), pairs)  13.6 us
    ppermute x1, starting transfers between devices, on_device(): near = lax.ppermute(coarse_kernel, ('blk', 'band'), pairs)  9.47 us
    ppermute x1, starting transfers between devices, on_device(): far = lax.ppermute(near, 'band', [(b, b ^ 1) for b in range(band_count)])  6.24 us
    ppermute x1, waiting for transfers between devices, on_device(): lax.ppermute(send.astype(jnp.bfloat16), 'band', swap).astype(jnp.float32)  6.2 us
    pallas_call x1, Pallas kernels, on_device(): pl.pallas_call(product_kernel, grid_spec=pltpu.PrefetchScalarGridSpec(num...  4.79 us
    unnamed x6, local copies, waits for them, and re-layouts  2.92 us
  transfers between devices with their start and end apart: 8, of which 5 were waited for; matrix products, arithmetic and copies ran while one was open for 10% of the time, Pallas kernels for 22%

profile of v16, /device:TPU:1, one launch (start us, length us, event | category | flops | bytes accessed | tf_op | source)
XLA Modules:
  0.0 99.4 jit_solution(15016066792377058728)
XLA Ops:
  0.6 9.5 %collective-permute-start = (bf16[2,512,512]{2,1,0:T(8,128)(2,1)}, bf16[2,512,512]{2,1,0:T(8,128)(2,1)S(1)}, u32[]{:S(2)}, u32[]{:S(2)}) collective-permute-start(bf16[2,512,512]{2,1,0:T(8,128)(2,1)} %local_ref.1), channel_id=1, source_target_pairs={{0,4},{1,125},{2,6},{3,127},{4,8},{5,1},{6,10},{7,3},{8,12},{9,5},... | collective-permute-start | bytes 3145736 | tf_op jit(solution)/shard_map/ppermute | solution.py:88
  10.1 0.7 compare_select_fusion
  10.8 0.8 copy.8
  11.6 0.7 compare_and_fusion
  12.2 13.6 %collective-permute-done = bf16[2,512,512]{2,1,0:T(8,128)(2,1)S(1)} collective-permute-done((bf16[2,512,512]{2,1,0:T(8,128)(2,1)}, bf16[2,512,512]{2,1,0:T(8,128)(2,1)S(1)}, u32[]{:S(2)}, u32[]{:S(2)}) %collective-permute-start) | collective-permute-done | bytes 1048608 | tf_op jit(solution)/shard_map/ppermute | solution.py:88
  25.8 6.2 %collective-permute-start.1 = (bf16[2,512,512]{2,1,0:T(8,128)(2,1)S(1)}, bf16[2,512,512]{2,1,0:T(8,128)(2,1)}, u32[]{:S(2)}, u32[]{:S(2)}) collective-permute-start(bf16[2,512,512]{2,1,0:T(8,128)(2,1)S(1)} %collective-permute-done), channel_id=1, source_target_pairs={{0,1},{1,0},{2,3},{3,2},{4,5},{5,4},{6,7},{7,6},{8,9},{9,8},{10,11... | collective-permute-start | bytes 3145736 | tf_op jit(solution)/shard_map/ppermute | solution.py:89
  32.1 1.0 %pad_maximum_fusion.2 = bf16[2,8,128,128]{3,2,1,0:T(8,128)(2,1)S(1)} fusion(bf16[1,8,128,128]{3,2,1,0:T(8,128)(2,1)S(1)} %bitcast.13, bf16[1,8,128,128]{3,2,1,0:T(8,128)(2,1)} %bitcast.15), kind=kLoop, calls=%fused_computation.5 | loop fusion | flops 262144 | bytes 1048576 | tf_op jit(solution)/shard_map/stack | solution.py:94
  33.1 0.9 collective-permute-start.3
  34.0 0.6 gather_fusion
  34.9 0.8 copy.10
  35.7 0.6 gather_fusion.1
  36.4 16.3 %collective-permute-done.3.second_ref = bf16[2,8,128,128]{3,2,1,0:T(8,128)(2,1)S(1)} collective-permute-done((bf16[2,8,128,128]{3,2,1,0:T(8,128)(2,1)S(1)}, bf16[2,8,128,128]{3,2,1,0:T(8,128)(2,1)S(1)}, u32[]{:S(2)}, u32[]{:S(2)}) %collective-permute-start.3) | collective-permute-done | bytes 524320 | tf_op jit(solution)/shard_map/ppermute | solution.py:14
  52.7 1.1 %pad_maximum_fusion.1 = bf16[4,8,128,128]{3,2,1,0:T(8,128)(2,1)S(1)} fusion(bf16[2,8,128,128]{3,2,1,0:T(8,128)(2,1)S(1)} %collective-permute-done.3.second_ref, bf16[1,8,128,128]{3,2,1,0:T(8,128)(2,1)S(1)} %bitcast.14, bf16[1,8,128,128]{3,2,1,0:T(8,128)(2,1)} %bitcast.16), kind=kLoop, calls=%fused_computation.3 | loop fusion | flops 1048576 | bytes 2097152 | tf_op jit(solution)/shard_map/stack | solution.py:95
  54.1 2.8 %pad_maximum_fusion.halo_ref = bf16[4,512,512]{2,1,0:T(8,128)(2,1)} fusion(bf16[2,512,512]{2,1,0:T(8,128)(2,1)} %collective-permute-done.1, bf16[2,512,512]{2,1,0:T(8,128)(2,1)S(1)} %collective-permute-done), kind=kLoop, calls=%fused_computation.2 | loop fusion | flops 1048576 | bytes 4194304 | tf_op jit(solution)/shard_map/concatenate | solution.py:90
  56.9 22.2 %shard_map.77 = (bf16[8,8,512,128]{3,2,1,0:T(8,128)(2,1)}, f32[8,512,128]{2,1,0:T(8,128)S(1)}) custom-call(s32[256]{0:T(256)S(1)} %fusion.4.slot_ref, s32[1]{0:T(128)} %bitcast.1.band_ref, f32[256]{0:T(256)S(1)} %select_n.75.weight_ref, bf16[4,512,512]{2,1,0:T(8,128)(2,1)} %pad_maximum_fusion.halo_ref, bf16[2,512,512]{2,1,0:T(8,128)(2,1)S(1)} %copy-done.1, ...), custom_call_target="tpu_custom_call" | custom-call | flops 7516192768 | bytes 12582912 | tf_op jit(solution)/shard_map/pallas_call | solution.py:133
  79.1 1.3 %copy-done = f32[8,512,128]{2,1,0:T(8,128)} copy-done((f32[8,512,128]{2,1,0:T(8,128)}, f32[8,512,128]{2,1,0:T(8,128)S(1)}, u32[]{:S(2)}) %copy-start) | copy-done | bytes 2097176
  80.5 0.7 collective-permute-done.5.third_ref
  81.2 4.8 %shard_map.78 = (bf16[8,2,128,128]{3,2,1,0:T(8,128)(2,1)}, f32[8,2,128,128]{3,2,1,0:T(8,128)}) custom-call(s32[1]{0:T(128)} %bitcast.1.band_ref, bf16[8,8,512,128]{3,2,1,0:T(8,128)(2,1)} %get-tuple-element.4.head_ref.middle_ref.tail_ref, bf16[8,8,512,128]{3,2,1,0:T(8,128)(2,1)} %get-tuple-element.4.head_ref.middle_ref.tail_ref, ...), custom_call_target="tpu_custom_call" | custom-call | flops 1073741824 | bytes 8388608 | tf_op jit(solution)/shard_map/pallas_call | solution.py:150
  86.0 1.9 %collective-permute-start.6 = (bf16[8,2,128,128]{3,2,1,0:T(8,128)(2,1)}, bf16[8,2,128,128]{3,2,1,0:T(8,128)(2,1)S(1)}, u32[]{:S(2)}, u32[]{:S(2)}) collective-permute-start(bf16[8,2,128,128]{3,2,1,0:T(8,128)(2,1)} %get-tuple-element.9), channel_id=1, source_target_pairs={{0,1},{1,0},{2,3},{3,2},{4,5},{5,4},{6,7},{7,6},{8,9},{9,8},{10,11... | collective-permute-start | bytes 1572872 | tf_op jit(solution)/shard_map/ppermute | solution.py:182
  87.9 1.7 %collective-permute-done.6 = bf16[8,2,128,128]{3,2,1,0:T(8,128)(2,1)S(1)} collective-permute-done((bf16[8,2,128,128]{3,2,1,0:T(8,128)(2,1)}, bf16[8,2,128,128]{3,2,1,0:T(8,128)(2,1)S(1)}, u32[]{:S(2)}, u32[]{:S(2)}) %collective-permute-start.6) | collective-permute-done | bytes 524320 | tf_op jit(solution)/shard_map/ppermute | solution.py:182
  89.6 1.3 %convert_add_fusion = f32[8,2,128,128]{3,2,1,0:T(8,128)S(1)} fusion(f32[8,2,128,128]{3,2,1,0:T(8,128)} %get-tuple-element.8, bf16[8,2,128,128]{3,2,1,0:T(8,128)(2,1)S(1)} %collective-permute-done.6), kind=kLoop, calls=%fused_computation.4 | loop fusion | flops 524288 | bytes 2621440 | tf_op jit(solution)/shard_map/add | solution.py:182
  91.0 1.4 %collective-permute-start.7 = (bf16[8,128,128]{2,1,0:T(8,128)(2,1)S(1)}, bf16[8,128,128]{2,1,0:T(8,128)(2,1)S(1)}, u32[]{:S(2)}, u32[]{:S(2)}) collective-permute-start(bf16[8,128,128]{2,1,0:T(8,128)(2,1)S(1)} %fusion.1), channel_id=1, source_target_pairs={{0,2},{1,3},{2,0},{3,1},{4,6},{5,7},{6,4},{7,5},{8,10},{9,11},{10,... | collective-permute-start | bytes 786440 | tf_op jit(solution)/shard_map/ppermute | solution.py:188
  92.4 6.2 %collective-permute-done.7 = bf16[8,128,128]{2,1,0:T(8,128)(2,1)S(1)} collective-permute-done((bf16[8,128,128]{2,1,0:T(8,128)(2,1)S(1)}, bf16[8,128,128]{2,1,0:T(8,128)(2,1)S(1)}, u32[]{:S(2)}, u32[]{:S(2)}) %collective-permute-start.7) | collective-permute-done | bytes 262176 | tf_op jit(solution)/shard_map/ppermute | solution.py:188
  98.6 0.8 fusion
  (18 shorter events, 0.8 us)
Async XLA Ops:
  0.6 25.2 %collective-permute-start = (bf16[2,512,512]{2,1,0:T(8,128)(2,1)}, bf16[2,512,512]{2,1,0:T(8,128)(2,1)S(1)}, u32[]{:S(2)}, u32[]{:S(2)}) collective-permute-start(bf16[2,512,512]{2,1,0:T(8,128)(2,1)} %local_ref.1), channel_id=1, source_target_pairs={{0,4},{1,125},{2,6},{3,127},{4,8},{5,1},{6,10},{7,3},{8,12},{9,5},... | collective-permute-start | bytes 3145736 | tf_op jit(solution)/shard_map/ppermute | solution.py:88
  10.1 22.0 %collective-permute-start.2 = (bf16[8,128,128]{2,1,0:T(8,128)(2,1)}, bf16[8,128,128]{2,1,0:T(8,128)(2,1)S(1)}, u32[]{:S(2)}, u32[]{:S(2)}) collective-permute-start(bf16[8,128,128]{2,1,0:T(8,128)(2,1)} %param.11), channel_id=1, source_target_pairs={{0,4},{4,8},{8,12},{12,16},{16,20},{20,24},{24,28},{28,32},{32,36}... | collective-permute-start | bytes 786440 | tf_op jit(solution)/shard_map/ppermute | solution.py:14
  10.1 46.8 %collective-permute-start.4 = (bf16[8,128,128]{2,1,0:T(8,128)(2,1)}, bf16[8,128,128]{2,1,0:T(8,128)(2,1)S(1)}, u32[]{:S(2)}, u32[]{:S(2)}) collective-permute-start(bf16[8,128,128]{2,1,0:T(8,128)(2,1)} %param.11), channel_id=1, source_target_pairs={{0,32},{4,36},{8,40},{12,44},{16,48},{20,52},{24,56},{28,60},{32,6... | collective-permute-start | bytes 786440 | tf_op jit(solution)/shard_map/ppermute | solution.py:14
  25.8 28.3 %collective-permute-start.1 = (bf16[2,512,512]{2,1,0:T(8,128)(2,1)S(1)}, bf16[2,512,512]{2,1,0:T(8,128)(2,1)}, u32[]{:S(2)}, u32[]{:S(2)}) collective-permute-start(bf16[2,512,512]{2,1,0:T(8,128)(2,1)S(1)} %collective-permute-done), channel_id=1, source_target_pairs={{0,1},{1,0},{2,3},{3,2},{4,5},{5,4},{6,7},{7,6},{8,9},{9,8},{10,11... | collective-permute-start | bytes 3145736 | tf_op jit(solution)/shard_map/ppermute | solution.py:89
  33.1 19.6 %collective-permute-start.3 = (bf16[2,8,128,128]{3,2,1,0:T(8,128)(2,1)S(1)}, bf16[2,8,128,128]{3,2,1,0:T(8,128)(2,1)S(1)}, u32[]{:S(2)}, u32[]{:S(2)}) collective-permute-start(bf16[2,8,128,128]{3,2,1,0:T(8,128)(2,1)S(1)} %pad_maximum_fusion.2), channel_id=1, source_target_pairs={{0,8},{4,12},{8,16},{12,20},{16,24},{20,28},{24,32},{28,36},{32,40... | collective-permute-start | bytes 1572872 | tf_op jit(solution)/shard_map/ppermute | solution.py:14
  53.7 27.4 %collective-permute-start.5 = (bf16[4,8,128,128]{3,2,1,0:T(8,128)(2,1)S(1)}, bf16[4,8,128,128]{3,2,1,0:T(8,128)(2,1)}, u32[]{:S(2)}, u32[]{:S(2)}) collective-permute-start(bf16[4,8,128,128]{3,2,1,0:T(8,128)(2,1)S(1)} %pad_maximum_fusion.1), channel_id=1, source_target_pairs={{0,16},{4,20},{8,24},{12,28},{16,32},{20,36},{24,40},{28,44},{32,4... | collective-permute-start | bytes 3145736 | tf_op jit(solution)/shard_map/ppermute | solution.py:14
  54.1 2.9 %copy-start.1 = (bf16[2,512,512]{2,1,0:T(8,128)(2,1)S(1)}, bf16[2,512,512]{2,1,0:T(8,128)(2,1)}, u32[]{:S(2)}) copy-start(bf16[2,512,512]{2,1,0:T(8,128)(2,1)} %local_ref.1) | copy-start | bytes 3145732
  79.1 1.3 %copy-start = (f32[8,512,128]{2,1,0:T(8,128)}, f32[8,512,128]{2,1,0:T(8,128)S(1)}, u32[]{:S(2)}) copy-start(f32[8,512,128]{2,1,0:T(8,128)S(1)} %get-tuple-element.7.early_ref) | copy-start | bytes 6291460
  86.0 3.7 %collective-permute-start.6 = (bf16[8,2,128,128]{3,2,1,0:T(8,128)(2,1)}, bf16[8,2,128,128]{3,2,1,0:T(8,128)(2,1)S(1)}, u32[]{:S(2)}, u32[]{:S(2)}) collective-permute-start(bf16[8,2,128,128]{3,2,1,0:T(8,128)(2,1)} %get-tuple-element.9), channel_id=1, source_target_pairs={{0,1},{1,0},{2,3},{3,2},{4,5},{5,4},{6,7},{7,6},{8,9},{9,8},{10,11... | collective-permute-start | bytes 1572872 | tf_op jit(solution)/shard_map/ppermute | solution.py:182
  91.0 7.6 %collective-permute-start.7 = (bf16[8,128,128]{2,1,0:T(8,128)(2,1)S(1)}, bf16[8,128,128]{2,1,0:T(8,128)(2,1)S(1)}, u32[]{:S(2)}, u32[]{:S(2)}) collective-permute-start(bf16[8,128,128]{2,1,0:T(8,128)(2,1)S(1)} %fusion.1), channel_id=1, source_target_pairs={{0,2},{1,3},{2,0},{3,1},{4,6},{5,7},{6,4},{7,5},{8,10},{9,11},{10,... | collective-permute-start | bytes 786440 | tf_op jit(solution)/shard_map/ppermute | solution.py:188

commit v17 on v16

--- a/solution.py
+++ b/solution.py
@@ -147,46 +147,50 @@
       first, second, last)
     row_block = block_order // band_count
     half_fine = fine_dev // 2
-    send, keep = pl.pallas_call(
-        product_kernel,
-        grid_spec=pltpu.PrefetchScalarGridSpec(
-            num_scalar_prefetch=1,
-            grid=(2,),
-            in_specs=[
-                pl.BlockSpec((half_fine, 1, block_order, column_count),
-                             lambda k, bd: (k, 3, 0, 0)),
-                pl.BlockSpec((half_fine, 2, block_order, column_count),
-                             lambda k, bd: (k, 2, 0, 0)),
-                pl.BlockSpec((half_fine, 1, block_order, column_count),
-                             lambda k, bd: (k, 6, 0, 0)),
-                pl.BlockSpec((half_fine, block_order, vector_count), lambda k, bd: (k, 0, 0)),
-                pl.BlockSpec((4, half_fine, column_count, vector_count),
-                             lambda k, bd: (0, k, 0, 0)),
+    shares = []
+    for offset in (0, half_fine):
+        send, keep = pl.pallas_call(
+            product_kernel,
+            grid_spec=pltpu.PrefetchScalarGridSpec(
+                num_scalar_prefetch=1,
+                grid=(1,),
+                in_specs=[
+                    pl.BlockSpec((half_fine, 1, block_order, column_count),
+                                 lambda k, bd, o=offset // half_fine: (k + o, 3, 0, 0)),
+                    pl.BlockSpec((half_fine, 2, block_order, column_count),
+                                 lambda k, bd, o=offset // half_fine: (k + o, 2, 0, 0)),
+                    pl.BlockSpec((half_fine, 1, block_order, column_count),
+                                 lambda k, bd, o=offset // half_fine: (k + o, 6, 0, 0)),
+                    pl.BlockSpec((half_fine, block_order, vector_count), lambda k, bd, o=offset // half_fine: (k + o, 0, 0)),
+                    pl.BlockSpec((4, half_fine, column_count, vector_count),
+                                 lambda k, bd, o=offset // half_fine: (0, k + o, 0, 0)),
+                ],
+                out_specs=[
+                    pl.BlockSpec((half_fine, 2, row_block, vector_count), lambda k, bd: (k, 0, 0, 0)),
+                    pl.BlockSpec((half_fine, 2, row_block, vector_count), lambda k, bd: (k, 0, 0, 0)),
+                ],
+                scratch_shapes=[pltpu.VMEM((block_order, vector_count), jnp.float32)],
+            ),
+            out_shape=[
+                jax.ShapeDtypeStruct((half_fine, 2, row_block, vector_count), jnp.bfloat16),
+                jax.ShapeDtypeStruct((half_fine, 2, row_block, vector_count), jnp.float32),
             ],
-            out_specs=[
-                pl.BlockSpec((half_fine, 2, row_block, vector_count), lambda k, bd: (k, 0, 0, 0)),
-                pl.BlockSpec((half_fine, 2, row_block, vector_count), lambda k, bd: (k, 0, 0, 0)),
-            ],
-            scratch_shapes=[pltpu.VMEM((block_order, vector_count), jnp.float32)],
-        ),
-        out_shape=[
-            jax.ShapeDtypeStruct((fine_dev, 2, row_block, vector_count), jnp.bfloat16),
-            jax.ShapeDtypeStruct((fine_dev, 2, row_block, vector_count), jnp.float32),
-        ],
-        cost_estimate=pl.CostEstimate(
-            flops=2 * fine_dev * stop_count * block_order * column_count * vector_count,
-            transcendentals=0,
-            bytes_accessed=2 * fine_dev * stop_count * block_order * column_count),
-    )(band_index, hamiltonian, hamiltonian, hamiltonian, early_value, third)
-    swap = [(b, b ^ 1) for b in range(band_count)]
-    pair_sum = keep + lax.ppermute(send, "band", swap).astype(jnp.float32)
-    level = band // 2
-    send = lax.dynamic_index_in_dim(pair_sum, 1 - level, 1, keepdims=False)
-    keep = lax.dynamic_index_in_dim(pair_sum, level, 1, keepdims=False)
-    swap = [(b, b ^ 2) for b in range(band_count)]
-    product_share = (
-        keep + lax.ppermute(send.astype(jnp.bfloat16), "band", swap).astype(jnp.float32)
-    ).astype(jnp.bfloat16)
+            cost_estimate=pl.CostEstimate(
+                flops=2 * half_fine * stop_count * block_order * column_count * vector_count,
+                transcendentals=0,
+                bytes_accessed=2 * half_fine * stop_count * block_order * column_count),
+        )(band_index, hamiltonian, hamiltonian, hamiltonian, early_value, third)
+        swap = [(b, b ^ 1) for b in range(band_count)]
+        pair_sum = keep + lax.ppermute(send, "band", swap).astype(jnp.float32)
+        level = band // 2
+        send = lax.dynamic_index_in_dim(pair_sum, 1 - level, 1, keepdims=False)
+        keep = lax.dynamic_index_in_dim(pair_sum, level, 1, keepdims=False)
+        swap = [(b, b ^ 2) for b in range(band_count)]
+        product_share = (
+            keep + lax.ppermute(send.astype(jnp.bfloat16), "band", swap).astype(jnp.float32)
+        ).astype(jnp.bfloat16)
+        shares.append(product_share)
+    product_share = jnp.concatenate(shares, axis=0)
     return (hamiltonian, product_share)
 
 

time: 99.7 us -> 101 us (1.013)
  waiting for transfers between devices: 38.6 us -> 33.9 us
  Pallas kernels: 27 us -> 29.6 us
  local copies, waits for them, and re-layouts: 4.59 us -> 6.54 us
  starting transfers between devices: 20 us -> 21.4 us
    ppermute x1 -> x2, waiting for transfers between devices: 6.2 us -> 3.34 us  [on_device(): lax.ppermute(send.astype(jnp.bfloat16), 'band', swap).astype(jnp.float32)]
    pallas_call x1 -> x2, Pallas kernels: 4.79 us -> 7.38 us  [on_device(): pl.pallas_call(product_kernel, grid_spec=pltpu.PrefetchScalarGridSpec(num...]
    ppermute x1 -> x2, waiting for transfers between devices: 1.75 us -> 0.23 us  [on_device(): pair_sum = keep + lax.ppermute(send, 'band', swap).astype(jnp.float32)]
    ppermute x1 -> x2, starting transfers between devices: 1.38 us -> 2.75 us  [on_device(): lax.ppermute(send.astype(jnp.bfloat16), 'band', swap).astype(jnp.float32)]
    unnamed x6 -> x10, local copies, waits for them, and re-layouts: 2.92 us -> 3.89 us
    ppermute x1 -> x2, starting transfers between devices: 1.94 us -> 2.07 us  [on_device(): pair_sum = keep + lax.ppermute(send, 'band', swap).astype(jnp.float32)]
  transfers between devices with their start and end apart: 8 -> 10, of which waited for: 5 -> 6; matrix products, arithmetic and copies ran while one was open for 10% -> 11% of each run, Pallas kernels for 22% -> 26%
where the time goes in v17:
time: 101 us
  waiting for transfers between devices  33.9 us (34%)
  Pallas kernels  29.6 us (29%)
  starting transfers between devices  21.4 us (21%)
  other arithmetic  8.63 us (9%)
  local copies, waits for them, and re-layouts  6.54 us (6%)
    pallas_call x1, Pallas kernels, on_device(): pl.pallas_call(kernel, grid_spec=grid_spec, out_shape=[jax.ShapeDtypeStru...  22.2 us
    ppermute x4, waiting for transfers between devices, shifted(): return lax.ppermute(value, axis, pairs)  16.6 us
    ppermute x1, waiting for transfers between devices, on_device(): near = lax.ppermute(coarse_kernel, ('blk', 'band'), pairs)  13.7 us
    ppermute x1, starting transfers between devices, on_device(): near = lax.ppermute(coarse_kernel, ('blk', 'band'), pairs)  9.47 us
    pallas_call x2, Pallas kernels, on_device(): pl.pallas_call(product_kernel, grid_spec=pltpu.PrefetchScalarGridSpec(num...  7.38 us
    ppermute x1, starting transfers between devices, on_device(): far = lax.ppermute(near, 'band', [(b, b ^ 1) for b in range(band_count)])  6.13 us
    unnamed x10, local copies, waits for them, and re-layouts  3.89 us
    ppermute x2, waiting for transfers between devices, on_device(): lax.ppermute(send.astype(jnp.bfloat16), 'band', swap).astype(jnp.float32)  3.34 us
  transfers between devices with their start and end apart: 10, of which 6 were waited for; matrix products, arithmetic and copies ran while one was open for 11% of the time, Pallas kernels for 26%

profile of v17, /device:TPU:1, one launch (start us, length us, event | category | flops | bytes accessed | tf_op | source)
XLA Modules:
  0.0 100.8 jit_solution(11546114450597628393)
XLA Ops:
  0.6 9.5 %collective-permute-start = (bf16[2,512,512]{2,1,0:T(8,128)(2,1)}, bf16[2,512,512]{2,1,0:T(8,128)(2,1)}, u32[]{:S(2)}, u32[]{:S(2)}) collective-permute-start(bf16[2,512,512]{2,1,0:T(8,128)(2,1)} %local_ref.1), channel_id=1, source_target_pairs={{0,4},{1,125},{2,6},{3,127},{4,8},{5,1},{6,10},{7,3},{8,12},{9,5},... | collective-permute-start | bytes 3145736 | tf_op jit(solution)/shard_map/ppermute | solution.py:88
  10.1 0.7 compare_select_fusion
  10.8 0.8 copy.10
  11.6 0.7 compare_and_fusion
  12.2 13.7 %collective-permute-done = bf16[2,512,512]{2,1,0:T(8,128)(2,1)} collective-permute-done((bf16[2,512,512]{2,1,0:T(8,128)(2,1)}, bf16[2,512,512]{2,1,0:T(8,128)(2,1)}, u32[]{:S(2)}, u32[]{:S(2)}) %collective-permute-start) | collective-permute-done | bytes 1048608 | tf_op jit(solution)/shard_map/ppermute | solution.py:88
  25.9 6.1 %collective-permute-start.1 = (bf16[2,512,512]{2,1,0:T(8,128)(2,1)}, bf16[2,512,512]{2,1,0:T(8,128)(2,1)}, u32[]{:S(2)}, u32[]{:S(2)}) collective-permute-start(bf16[2,512,512]{2,1,0:T(8,128)(2,1)} %collective-permute-done), channel_id=1, source_target_pairs={{0,1},{1,0},{2,3},{3,2},{4,5},{5,4},{6,7},{7,6},{8,9},{9,8},{10,11... | collective-permute-start | bytes 3145736 | tf_op jit(solution)/shard_map/ppermute | solution.py:89
  32.1 1.0 pad_maximum_fusion.2
  33.1 0.9 collective-permute-start.3
  34.9 0.8 copy.12
  36.4 16.3 %collective-permute-done.3.second_ref = bf16[2,8,128,128]{3,2,1,0:T(8,128)(2,1)S(1)} collective-permute-done((bf16[2,8,128,128]{3,2,1,0:T(8,128)(2,1)S(1)}, bf16[2,8,128,128]{3,2,1,0:T(8,128)(2,1)S(1)}, u32[]{:S(2)}, u32[]{:S(2)}) %collective-permute-start.3) | collective-permute-done | bytes 524320 | tf_op jit(solution)/shard_map/ppermute | solution.py:14
  52.7 1.1 %pad_maximum_fusion.1 = bf16[4,8,128,128]{3,2,1,0:T(8,128)(2,1)S(1)} fusion(bf16[2,8,128,128]{3,2,1,0:T(8,128)(2,1)S(1)} %collective-permute-done.3.second_ref, bf16[1,8,128,128]{3,2,1,0:T(8,128)(2,1)S(1)} %bitcast.20, bf16[1,8,128,128]{3,2,1,0:T(8,128)(2,1)} %bitcast.22), kind=kLoop, calls=%fused_computation.3 | loop fusion | flops 1048576 | bytes 2097152 | tf_op jit(solution)/shard_map/stack | solution.py:95
  54.1 3.1 %pad_maximum_fusion.halo_ref = bf16[4,512,512]{2,1,0:T(8,128)(2,1)} fusion(bf16[2,512,512]{2,1,0:T(8,128)(2,1)} %collective-permute-done.1, bf16[2,512,512]{2,1,0:T(8,128)(2,1)} %collective-permute-done), kind=kLoop, calls=%fused_computation.2 | loop fusion | flops 1048576 | bytes 4194304 | tf_op jit(solution)/shard_map/concatenate | solution.py:90
  57.3 22.2 %shard_map.77 = (bf16[8,8,512,128]{3,2,1,0:T(8,128)(2,1)}, f32[8,512,128]{2,1,0:T(8,128)S(1)}) custom-call(s32[256]{0:T(256)S(1)} %fusion.6.slot_ref, s32[1]{0:T(128)} %bitcast.1.band_ref, f32[256]{0:T(256)S(1)} %select_n.78.weight_ref, bf16[4,512,512]{2,1,0:T(8,128)(2,1)} %pad_maximum_fusion.halo_ref, bf16[2,512,512]{2,1,0:T(8,128)(2,1)S(1)} %copy-done.1, ...), custom_call_target="tpu_custom_call" | custom-call | flops 7516192768 | bytes 12582912 | tf_op jit(solution)/shard_map/pallas_call | solution.py:133
  79.4 1.3 %copy-done = f32[8,512,128]{2,1,0:T(8,128)} copy-done((f32[8,512,128]{2,1,0:T(8,128)}, f32[8,512,128]{2,1,0:T(8,128)S(1)}, u32[]{:S(2)}) %copy-start) | copy-done | bytes 2097176
  81.1 1.0 copy-done.2
  82.0 3.7 %shard_map.78 = (bf16[4,2,128,128]{3,2,1,0:T(8,128)(2,1)}, f32[4,2,128,128]{3,2,1,0:T(8,128)}) custom-call(s32[1]{0:T(128)} %bitcast.1.band_ref, bf16[8,8,512,128]{3,2,1,0:T(8,128)(2,1)} %get-tuple-element.6.head_ref.middle_ref.tail_ref, bf16[8,8,512,128]{3,2,1,0:T(8,128)(2,1)} %get-tuple-element.6.head_ref.middle_ref.tail_ref, ...), custom_call_target="tpu_custom_call" | custom-call | flops 536870912 | bytes 4194304 | tf_op jit(solution)/shard_map/pallas_call | solution.py:152
  85.7 1.0 copy.14
  86.7 2.0 %collective-permute-start.6 = (bf16[4,2,128,128]{3,2,0,1:T(8,128)(2,1)S(1)}, bf16[4,2,128,128]{3,2,0,1:T(8,128)(2,1)S(1)}, u32[]{:S(2)}, u32[]{:S(2)}) collective-permute-start(bf16[4,2,128,128]{3,2,0,1:T(8,128)(2,1)S(1)} %copy.14), channel_id=1, source_target_pairs={{0,1},{1,0},{2,3},{3,2},{4,5},{5,4},{6,7},{7,6},{8,9},{9,8},{10,11... | collective-permute-start | bytes 786440 | tf_op jit(solution)/shard_map/ppermute | solution.py:184
  88.7 3.7 %shard_map.79 = (bf16[4,2,128,128]{3,2,1,0:T(8,128)(2,1)}, f32[4,2,128,128]{3,2,1,0:T(8,128)}) custom-call(s32[1]{0:T(128)} %bitcast.1.band_ref, bf16[8,8,512,128]{3,2,1,0:T(8,128)(2,1)} %get-tuple-element.6.head_ref.middle_ref.tail_ref, bf16[8,8,512,128]{3,2,1,0:T(8,128)(2,1)} %get-tuple-element.6.head_ref.middle_ref.tail_ref, ...), custom_call_target="tpu_custom_call" | custom-call | flops 536870912 | bytes 4194304 | tf_op jit(solution)/shard_map/pallas_call | solution.py:152
  92.5 1.4 %collective-permute-start.7 = (bf16[4,128,128]{2,1,0:T(8,128)(2,1)S(1)}, bf16[4,128,128]{2,1,0:T(8,128)(2,1)S(1)}, u32[]{:S(2)}, u32[]{:S(2)}) collective-permute-start(bf16[4,128,128]{2,1,0:T(8,128)(2,1)S(1)} %fusion.2), channel_id=1, source_target_pairs={{0,2},{1,3},{2,0},{3,1},{4,6},{5,7},{6,4},{7,5},{8,10},{9,11},{10,... | collective-permute-start | bytes 393224 | tf_op jit(solution)/shard_map/ppermute | solution.py:190
  94.2 1.1 %convert_add_fusion = f32[4,2,128,128]{3,2,1,0:T(8,128)S(1)} fusion(f32[4,2,128,128]{3,2,1,0:T(8,128)} %get-tuple-element.12, bf16[4,2,128,128]{3,2,1,0:T(8,128)(2,1)S(1)} %collective-permute-done.8), kind=kLoop, calls=%fused_computation.6 | loop fusion | flops 262144 | bytes 1310720 | tf_op jit(solution)/shard_map/add | solution.py:184
  95.3 1.4 %collective-permute-start.9 = (bf16[4,128,128]{2,1,0:T(8,128)(2,1)S(1)}, bf16[4,128,128]{2,1,0:T(8,128)(2,1)S(1)}, u32[]{:S(2)}, u32[]{:S(2)}) collective-permute-start(bf16[4,128,128]{2,1,0:T(8,128)(2,1)S(1)} %fusion.3), channel_id=1, source_target_pairs={{0,2},{1,3},{2,0},{3,1},{4,6},{5,7},{6,4},{7,5},{8,10},{9,11},{10,... | collective-permute-start | bytes 393224 | tf_op jit(solution)/shard_map/ppermute | solution.py:190
  97.3 2.8 %collective-permute-done.9 = bf16[4,128,128]{2,1,0:T(8,128)(2,1)S(1)} collective-permute-done((bf16[4,128,128]{2,1,0:T(8,128)(2,1)S(1)}, bf16[4,128,128]{2,1,0:T(8,128)(2,1)S(1)}, u32[]{:S(2)}, u32[]{:S(2)}) %collective-permute-start.9) | collective-permute-done | bytes 131104 | tf_op jit(solution)/shard_map/ppermute | solution.py:190
  100.1 0.7 pad_maximum_fusion.3
  (32 shorter events, 3.2 us)
Async XLA Ops:
  0.6 25.3 %collective-permute-start = (bf16[2,512,512]{2,1,0:T(8,128)(2,1)}, bf16[2,512,512]{2,1,0:T(8,128)(2,1)}, u32[]{:S(2)}, u32[]{:S(2)}) collective-permute-start(bf16[2,512,512]{2,1,0:T(8,128)(2,1)} %local_ref.1), channel_id=1, source_target_pairs={{0,4},{1,125},{2,6},{3,127},{4,8},{5,1},{6,10},{7,3},{8,12},{9,5},... | collective-permute-start | bytes 3145736 | tf_op jit(solution)/shard_map/ppermute | solution.py:88
  10.1 22.0 %collective-permute-start.2 = (bf16[8,128,128]{2,1,0:T(8,128)(2,1)}, bf16[8,128,128]{2,1,0:T(8,128)(2,1)S(1)}, u32[]{:S(2)}, u32[]{:S(2)}) collective-permute-start(bf16[8,128,128]{2,1,0:T(8,128)(2,1)} %param.11), channel_id=1, source_target_pairs={{0,4},{4,8},{8,12},{12,16},{16,20},{20,24},{24,28},{28,32},{32,36}... | collective-permute-start | bytes 786440 | tf_op jit(solution)/shard_map/ppermute | solution.py:14
  10.1 47.2 %collective-permute-start.4 = (bf16[8,128,128]{2,1,0:T(8,128)(2,1)}, bf16[8,128,128]{2,1,0:T(8,128)(2,1)S(1)}, u32[]{:S(2)}, u32[]{:S(2)}) collective-permute-start(bf16[8,128,128]{2,1,0:T(8,128)(2,1)} %param.11), channel_id=1, source_target_pairs={{0,32},{4,36},{8,40},{12,44},{16,48},{20,52},{24,56},{28,60},{32,6... | collective-permute-start | bytes 786440 | tf_op jit(solution)/shard_map/ppermute | solution.py:14
  25.9 28.2 %collective-permute-start.1 = (bf16[2,512,512]{2,1,0:T(8,128)(2,1)}, bf16[2,512,512]{2,1,0:T(8,128)(2,1)}, u32[]{:S(2)}, u32[]{:S(2)}) collective-permute-start(bf16[2,512,512]{2,1,0:T(8,128)(2,1)} %collective-permute-done), channel_id=1, source_target_pairs={{0,1},{1,0},{2,3},{3,2},{4,5},{5,4},{6,7},{7,6},{8,9},{9,8},{10,11... | collective-permute-start | bytes 3145736 | tf_op jit(solution)/shard_map/ppermute | solution.py:89
  33.1 19.6 %collective-permute-start.3 = (bf16[2,8,128,128]{3,2,1,0:T(8,128)(2,1)S(1)}, bf16[2,8,128,128]{3,2,1,0:T(8,128)(2,1)S(1)}, u32[]{:S(2)}, u32[]{:S(2)}) collective-permute-start(bf16[2,8,128,128]{3,2,1,0:T(8,128)(2,1)S(1)} %pad_maximum_fusion.2), channel_id=1, source_target_pairs={{0,8},{4,12},{8,16},{12,20},{16,24},{20,28},{24,32},{28,36},{32,40... | collective-permute-start | bytes 1572872 | tf_op jit(solution)/shard_map/ppermute | solution.py:14
  53.7 27.3 %collective-permute-start.5 = (bf16[4,8,128,128]{3,2,1,0:T(8,128)(2,1)S(1)}, bf16[4,8,128,128]{3,2,1,0:T(8,128)(2,1)S(1)}, u32[]{:S(2)}, u32[]{:S(2)}) collective-permute-start(bf16[4,8,128,128]{3,2,1,0:T(8,128)(2,1)S(1)} %pad_maximum_fusion.1), channel_id=1, source_target_pairs={{0,16},{4,20},{8,24},{12,28},{16,32},{20,36},{24,40},{28,44},{32,4... | collective-permute-start | bytes 3145736 | tf_op jit(solution)/shard_map/ppermute | solution.py:14
  54.1 3.2 %copy-start.1 = (bf16[2,512,512]{2,1,0:T(8,128)(2,1)S(1)}, bf16[2,512,512]{2,1,0:T(8,128)(2,1)}, u32[]{:S(2)}) copy-start(bf16[2,512,512]{2,1,0:T(8,128)(2,1)} %local_ref.1) | copy-start | bytes 3145732
  79.4 1.3 %copy-start = (f32[8,512,128]{2,1,0:T(8,128)}, f32[8,512,128]{2,1,0:T(8,128)S(1)}, u32[]{:S(2)}) copy-start(f32[8,512,128]{2,1,0:T(8,128)S(1)} %get-tuple-element.9.early_ref) | copy-start | bytes 6291460
  81.1 1.0 copy-start.2
  86.7 5.8 %collective-permute-start.6 = (bf16[4,2,128,128]{3,2,0,1:T(8,128)(2,1)S(1)}, bf16[4,2,128,128]{3,2,0,1:T(8,128)(2,1)S(1)}, u32[]{:S(2)}, u32[]{:S(2)}) collective-permute-start(bf16[4,2,128,128]{3,2,0,1:T(8,128)(2,1)S(1)} %copy.14), channel_id=1, source_target_pairs={{0,1},{1,0},{2,3},{3,2},{4,5},{5,4},{6,7},{7,6},{8,9},{9,8},{10,11... | collective-permute-start | bytes 786440 | tf_op jit(solution)/shard_map/ppermute | solution.py:184
  88.7 3.8 %copy-start.3 = (f32[4,2,128,128]{3,2,1,0:T(8,128)S(1)}, f32[4,2,128,128]{3,2,1,0:T(8,128)}, u32[]{:S(2)}) copy-start(f32[4,2,128,128]{3,2,1,0:T(8,128)} %get-tuple-element.10) | copy-start | bytes 1572868
  92.4 1.7 %collective-permute-start.8 = (bf16[4,2,128,128]{3,2,1,0:T(8,128)(2,1)}, bf16[4,2,128,128]{3,2,1,0:T(8,128)(2,1)S(1)}, u32[]{:S(2)}, u32[]{:S(2)}) collective-permute-start(bf16[4,2,128,128]{3,2,1,0:T(8,128)(2,1)} %get-tuple-element.13), channel_id=1, source_target_pairs={{0,1},{1,0},{2,3},{3,2},{4,5},{5,4},{6,7},{7,6},{8,9},{9,8},{10,11... | collective-permute-start | bytes 786440 | tf_op jit(solution)/shard_map/ppermute | solution.py:184
  92.5 4.7 %collective-permute-start.7 = (bf16[4,128,128]{2,1,0:T(8,128)(2,1)S(1)}, bf16[4,128,128]{2,1,0:T(8,128)(2,1)S(1)}, u32[]{:S(2)}, u32[]{:S(2)}) collective-permute-start(bf16[4,128,128]{2,1,0:T(8,128)(2,1)S(1)} %fusion.2), channel_id=1, source_target_pairs={{0,2},{1,3},{2,0},{3,1},{4,6},{5,7},{6,4},{7,5},{8,10},{9,11},{10,... | collective-permute-start | bytes 393224 | tf_op jit(solution)/shard_map/ppermute | solution.py:190
  95.3 4.7 %collective-permute-start.9 = (bf16[4,128,128]{2,1,0:T(8,128)(2,1)S(1)}, bf16[4,128,128]{2,1,0:T(8,128)(2,1)S(1)}, u32[]{:S(2)}, u32[]{:S(2)}) collective-permute-start(bf16[4,128,128]{2,1,0:T(8,128)(2,1)S(1)} %fusion.3), channel_id=1, source_target_pairs={{0,2},{1,3},{2,0},{3,1},{4,6},{5,7},{6,4},{7,5},{8,10},{9,11},{10,... | collective-permute-start | bytes 393224 | tf_op jit(solution)/shard_map/ppermute | solution.py:190

commit v18 on v16

--- a/solution.py
+++ b/solution.py
@@ -15,7 +15,7 @@
 
 
 def sandwich_kernel(slot_ref, band_ref, weight_ref, halo_ref, local_ref, inter_ref, right_ref,
-                    first_ref, second_ref, last_ref, ham_ref, early_ref, prod_ref, rot_ref,
+                    first_ref, last_ref, ham_ref, early_ref, prod_ref, rot_ref,
                     *, blocks_dev, stop_count, corner_count):
     k = pl.program_id(0)
     column_count = right_ref.shape[2]
@@ -40,23 +40,23 @@
         for s in range(half):
             ham_ref[0, part * half + s] = ham[:, s * column_count:(s + 1) * column_count]
         if part == 0:
-            tall = jnp.concatenate([first_ref[0], second_ref[0, 0], second_ref[1, 0]], axis=0)
-            early = jnp.dot(ham[:, :3 * column_count], tall, preferred_element_type=jnp.float32)
+            early = jnp.dot(ham[:, :column_count], first_ref[0], preferred_element_type=jnp.float32)
         else:
             early = early + jnp.dot(ham[:, (half - 1) * column_count:], last_ref[0],
                                     preferred_element_type=jnp.float32)
     early_ref[0] = early
 
 
-def product_kernel(band_ref, head_ref, middle_ref, tail_ref, early_ref, third_ref, send_ref,
-                   keep_ref, part_ref):
-    count = third_ref.shape[0]
+def product_kernel(band_ref, head_ref, low_ref, high_ref, tail_ref, early_ref, two_ref, four_ref,
+                   six_ref, send_ref, keep_ref, part_ref):
     rows = keep_ref.shape[2]
     core = band_ref[0] % 2
     for k in range(head_ref.shape[0]):
-        pieces = [head_ref[k, 0], middle_ref[k, 0], middle_ref[k, 1], tail_ref[k, 0]]
+        pieces = [head_ref[k, 0], low_ref[k, 0], low_ref[k, 1], high_ref[k, 0], high_ref[k, 1],
+                  tail_ref[k, 0]]
         wide = jnp.concatenate(pieces, axis=1)
-        tall = jnp.concatenate([third_ref[s, k] for s in range(count)], axis=0)
+        tall = jnp.concatenate([ref[j, k] for ref in (two_ref, four_ref, six_ref) for j in range(2)],
+                               axis=0)
         part_ref[...] = early_ref[k] + jnp.dot(wide, tall, preferred_element_type=jnp.float32)
         for level in range(2):
             own = pl.multiple_of((level * 2 + core) * rows, rows)
@@ -91,8 +91,10 @@
     assert stop_count == 8
     first = shifted(trial_vectors, "blk", 1)
     last = shifted(trial_vectors, "blk", 8)
-    second = shifted(jnp.stack([trial_vectors, first]), "blk", 2)
-    third = shifted(jnp.stack([trial_vectors, first, second[0], second[1]]), "blk", 4)
+    pair = jnp.stack([trial_vectors, first])
+    two = shifted(pair, "blk", 2)
+    four = shifted(pair, "blk", 4)
+    six = shifted(pair, "blk", 6)
 
     order_index = jnp.take(interp_index, stop_order, axis=1)
     order_weight = jnp.take(interp_weight, stop_order, axis=1)
@@ -117,7 +119,6 @@
             pl.BlockSpec((1, block_order, block_order), lambda k, sl, bd: (k, 0, 0)),
             pl.BlockSpec((1, block_order, column_count), lambda k, sl, bd: (k, 0, bd[0])),
             pl.BlockSpec((1, column_count, vector_count), lambda k, sl, bd: (k, 0, 0)),
-            pl.BlockSpec((2, 1, column_count, vector_count), lambda k, sl, bd: (0, k, 0, 0)),
             pl.BlockSpec((1, column_count, vector_count), lambda k, sl, bd: (k, 0, 0)),
         ],
         out_specs=[
@@ -144,7 +145,7 @@
             transcendentals=0,
             bytes_accessed=2 * fine_dev * block_order * (block_order + stop_count * column_count)),
     )(slot_index, band_index, weights, halo, coarse_kernel, intersection, intersection,
-      first, second, last)
+      first, last)
     row_block = block_order // band_count
     half_fine = fine_dev // 2
     send, keep = pl.pallas_call(
@@ -154,14 +155,16 @@
             grid=(2,),
             in_specs=[
                 pl.BlockSpec((half_fine, 1, block_order, column_count),
-                             lambda k, bd: (k, 3, 0, 0)),
+                             lambda k, bd: (k, 1, 0, 0)),
+                pl.BlockSpec((half_fine, 2, block_order, column_count),
+                             lambda k, bd: (k, 1, 0, 0)),
                 pl.BlockSpec((half_fine, 2, block_order, column_count),
                              lambda k, bd: (k, 2, 0, 0)),
                 pl.BlockSpec((half_fine, 1, block_order, column_count),
                              lambda k, bd: (k, 6, 0, 0)),
                 pl.BlockSpec((half_fine, block_order, vector_count), lambda k, bd: (k, 0, 0)),
-                pl.BlockSpec((4, half_fine, column_count, vector_count),
-                             lambda k, bd: (0, k, 0, 0)),
+            ] + [pl.BlockSpec((2, half_fine, column_count, vector_count),
+                              lambda k, bd: (0, k, 0, 0))] * 3 + [
             ],
             out_specs=[
                 pl.BlockSpec((half_fine, 2, row_block, vector_count), lambda k, bd: (k, 0, 0, 0)),
@@ -177,7 +180,7 @@
             flops=2 * fine_dev * stop_count * block_order * column_count * vector_count,
             transcendentals=0,
             bytes_accessed=2 * fine_dev * stop_count * block_order * column_count),
-    )(band_index, hamiltonian, hamiltonian, hamiltonian, early_value, third)
+    )(band_index, hamiltonian, hamiltonian, hamiltonian, hamiltonian, early_value, two, four, six)
     swap = [(b, b ^ 1) for b in range(band_count)]
     pair_sum = keep + lax.ppermute(send, "band", swap).astype(jnp.float32)
     level = band // 2

time: 99.7 us -> 111 us (1.11)
  the two profiles are of different devices: /device:TPU:1 before, /device:TPU:78 now
where the time goes in v18:
time: 111 us
  waiting for transfers between devices  60.9 us (55%)
  Pallas kernels  27.7 us (25%)
  starting transfers between devices  12.4 us (11%)
  other arithmetic  4.78 us (4%)
  local copies, waits for them, and re-layouts  4.6 us (4%)
    ppermute x5, waiting for transfers between devices, shifted(): return lax.ppermute(value, axis, pairs)  28 us
    ppermute x1, waiting for transfers between devices, on_device(): near = lax.ppermute(coarse_kernel, ('blk', 'band'), pairs)  22.9 us
    pallas_call x1, Pallas kernels, on_device(): pl.pallas_call(kernel, grid_spec=grid_spec, out_shape=[jax.ShapeDtypeStru...  21.9 us
    ppermute x5, starting transfers between devices, shifted(): return lax.ppermute(value, axis, pairs)  9.45 us
    ppermute x1, waiting for transfers between devices, on_device(): lax.ppermute(send.astype(jnp.bfloat16), 'band', swap).astype(jnp.float32)  7.9 us
    pallas_call x1, Pallas kernels, on_device(): pl.pallas_call(product_kernel, grid_spec=pltpu.PrefetchScalarGridSpec(num...  5.84 us
    unnamed x8, local copies, waits for them, and re-layouts  2.92 us
    ppermute x1, starting transfers between devices, on_device(): near = lax.ppermute(coarse_kernel, ('blk', 'band'), pairs)  2.36 us
  transfers between devices with their start and end apart: 9, of which 4 were waited for; matrix products, arithmetic and copies ran while one was open for 5% of the time, Pallas kernels for 20%

profile of v18, /device:TPU:78, one launch (start us, length us, event | category | flops | bytes accessed | tf_op | source)
XLA Modules:
  0.0 111.2 jit_solution(12248265034596777847)
XLA Ops:
  0.6 2.4 %collective-permute-start = (bf16[2,512,512]{2,1,0:T(8,128)(2,1)}, bf16[2,512,512]{2,1,0:T(8,128)(2,1)S(1)}, u32[]{:S(2)}, u32[]{:S(2)}) collective-permute-start(bf16[2,512,512]{2,1,0:T(8,128)(2,1)} %local_ref.1), channel_id=1, source_target_pairs={{0,4},{1,125},{2,6},{3,127},{4,8},{5,1},{6,10},{7,3},{8,12},{9,5},... | collective-permute-start | bytes 3145736 | tf_op jit(solution)/shard_map/ppermute | solution.py:88
  3.0 2.3 %collective-permute-start.2 = (bf16[8,128,128]{2,1,0:T(8,128)(2,1)}, bf16[8,128,128]{2,1,0:T(8,128)(2,1)S(1)}, u32[]{:S(2)}, u32[]{:S(2)}) collective-permute-start(bf16[8,128,128]{2,1,0:T(8,128)(2,1)} %param.11), channel_id=1, source_target_pairs={{0,4},{4,8},{8,12},{12,16},{16,20},{20,24},{24,28},{28,32},{32,36}... | collective-permute-start | bytes 786440 | tf_op jit(solution)/shard_map/ppermute | solution.py:14
  5.3 0.5 collective-permute-start.3
  5.8 0.7 compare_select_fusion
  6.4 22.9 %collective-permute-done = bf16[2,512,512]{2,1,0:T(8,128)(2,1)S(1)} collective-permute-done((bf16[2,512,512]{2,1,0:T(8,128)(2,1)}, bf16[2,512,512]{2,1,0:T(8,128)(2,1)S(1)}, u32[]{:S(2)}, u32[]{:S(2)}) %collective-permute-start) | collective-permute-done | bytes 1048608 | tf_op jit(solution)/shard_map/ppermute | solution.py:88
  29.4 0.8 copy.8
  30.2 0.8 copy.10
  30.9 0.6 gather_fusion
  31.5 0.6 gather_fusion.1
  32.1 0.7 compare_and_fusion
  32.9 0.1 copy.9
  33.4 1.0 pad_maximum_fusion.1
  34.5 5.2 %collective-permute-start.4 = (bf16[2,8,128,128]{3,2,1,0:T(8,128)(2,1)S(1)}, bf16[2,8,128,128]{3,2,1,0:T(8,128)(2,1)S(1)}, u32[]{:S(2)}, u32[]{:S(2)}) collective-permute-start(bf16[2,8,128,128]{3,2,1,0:T(8,128)(2,1)S(1)} %pad_maximum_fusion.1), channel_id=1, source_target_pairs={{0,8},{4,12},{8,16},{12,20},{16,24},{20,28},{24,32},{28,36},{32,40... | collective-permute-start | bytes 1572872 | tf_op jit(solution)/shard_map/ppermute | solution.py:14
  39.7 1.5 %collective-permute-start.6 = (bf16[2,8,128,128]{3,2,1,0:T(8,128)(2,1)S(1)}, bf16[2,8,128,128]{3,2,1,0:T(8,128)(2,1)}, u32[]{:S(2)}, u32[]{:S(2)}) collective-permute-start(bf16[2,8,128,128]{3,2,1,0:T(8,128)(2,1)S(1)} %pad_maximum_fusion.1), channel_id=1, source_target_pairs={{0,24},{4,28},{8,32},{12,36},{16,40},{20,44},{24,48},{28,52},{32,5... | collective-permute-start | bytes 1572872 | tf_op jit(solution)/shard_map/ppermute | solution.py:14
  41.2 0.2 pad_maximum_fusion.halo_ref
  41.4 21.9 %shard_map.77 = (bf16[8,8,512,128]{3,2,1,0:T(8,128)(2,1)}, f32[8,512,128]{2,1,0:T(8,128)S(1)}) custom-call(s32[256]{0:T(256)S(1)} %fusion.4.slot_ref, s32[1]{0:T(128)} %bitcast.1.band_ref, f32[256]{0:T(256)S(1)} %select_n.75.weight_ref, bf16[4,512,512]{2,1,0:T(8,128)(2,1)S(1)} %pad_maximum_fusion.halo_ref, bf16[2,512,512]{2,1,0:T(8,128)(2,1)S(1)} %copy-done.1, ...), custom_call_target="tpu_custom_call" | custom-call | flops 7516192768 | bytes 12582912 | tf_op jit(solution)/shard_map/pallas_call | solution.py:134
  63.2 1.3 %copy-done = f32[8,512,128]{2,1,0:T(8,128)} copy-done((f32[8,512,128]{2,1,0:T(8,128)}, f32[8,512,128]{2,1,0:T(8,128)S(1)}, u32[]{:S(2)}) %copy-start) | copy-done | bytes 2097176
  64.6 28.0 %collective-permute-done.6.six_ref = bf16[2,8,128,128]{3,2,1,0:T(8,128)(2,1)} collective-permute-done((bf16[2,8,128,128]{3,2,1,0:T(8,128)(2,1)S(1)}, bf16[2,8,128,128]{3,2,1,0:T(8,128)(2,1)}, u32[]{:S(2)}, u32[]{:S(2)}) %collective-permute-start.6) | collective-permute-done | bytes 524320 | tf_op jit(solution)/shard_map/ppermute | solution.py:14
  92.5 5.8 %shard_map.78 = (bf16[8,2,128,128]{3,2,1,0:T(8,128)(2,1)}, f32[8,2,128,128]{3,2,1,0:T(8,128)}) custom-call(s32[1]{0:T(128)} %bitcast.1.band_ref, bf16[8,8,512,128]{3,2,1,0:T(8,128)(2,1)} %get-tuple-element.4.head_ref.low_ref.high_ref.tail_ref, bf16[8,8,512,128]{3,2,1,0:T(8,128)(2,1)} %get-tuple-element.4.head_ref.low_ref.high_ref.tail_ref, ...), custom_call_target="tpu_custom_call" | custom-call | flops 1073741824 | bytes 8388608 | tf_op jit(solution)/shard_map/pallas_call | solution.py:151
  98.5 2.1 %collective-permute-done.7 = bf16[8,2,128,128]{3,2,1,0:T(8,128)(2,1)S(1)} collective-permute-done((bf16[8,2,128,128]{3,2,1,0:T(8,128)(2,1)}, bf16[8,2,128,128]{3,2,1,0:T(8,128)(2,1)S(1)}, u32[]{:S(2)}, u32[]{:S(2)}) %collective-permute-start.7) | collective-permute-done | bytes 524320 | tf_op jit(solution)/shard_map/ppermute | solution.py:185
  100.6 1.3 %convert_add_fusion = f32[8,2,128,128]{3,2,1,0:T(8,128)S(1)} fusion(f32[8,2,128,128]{3,2,1,0:T(8,128)} %get-tuple-element.8, bf16[8,2,128,128]{3,2,1,0:T(8,128)(2,1)S(1)} %collective-permute-done.7), kind=kLoop, calls=%fused_computation.3 | loop fusion | flops 524288 | bytes 2621440 | tf_op jit(solution)/shard_map/add | solution.py:185
  102.0 0.5 collective-permute-start.8
  102.5 7.9 %collective-permute-done.8 = bf16[8,128,128]{2,1,0:T(8,128)(2,1)S(1)} collective-permute-done((bf16[8,128,128]{2,1,0:T(8,128)(2,1)S(1)}, bf16[8,128,128]{2,1,0:T(8,128)(2,1)S(1)}, u32[]{:S(2)}, u32[]{:S(2)}) %collective-permute-start.8) | collective-permute-done | bytes 262176 | tf_op jit(solution)/shard_map/ppermute | solution.py:191
  110.4 0.8 fusion
  (21 shorter events, 0.7 us)
Async XLA Ops:
  0.6 28.7 %collective-permute-start = (bf16[2,512,512]{2,1,0:T(8,128)(2,1)}, bf16[2,512,512]{2,1,0:T(8,128)(2,1)S(1)}, u32[]{:S(2)}, u32[]{:S(2)}) collective-permute-start(bf16[2,512,512]{2,1,0:T(8,128)(2,1)} %local_ref.1), channel_id=1, source_target_pairs={{0,4},{1,125},{2,6},{3,127},{4,8},{5,1},{6,10},{7,3},{8,12},{9,5},... | collective-permute-start | bytes 3145736 | tf_op jit(solution)/shard_map/ppermute | solution.py:88
  3.0 30.4 %collective-permute-start.2 = (bf16[8,128,128]{2,1,0:T(8,128)(2,1)}, bf16[8,128,128]{2,1,0:T(8,128)(2,1)S(1)}, u32[]{:S(2)}, u32[]{:S(2)}) collective-permute-start(bf16[8,128,128]{2,1,0:T(8,128)(2,1)} %param.11), channel_id=1, source_target_pairs={{0,4},{4,8},{8,12},{12,16},{16,20},{20,24},{24,28},{28,32},{32,36}... | collective-permute-start | bytes 786440 | tf_op jit(solution)/shard_map/ppermute | solution.py:14
  5.3 36.1 %collective-permute-start.3 = (bf16[8,128,128]{2,1,0:T(8,128)(2,1)}, bf16[8,128,128]{2,1,0:T(8,128)(2,1)S(1)}, u32[]{:S(2)}, u32[]{:S(2)}) collective-permute-start(bf16[8,128,128]{2,1,0:T(8,128)(2,1)} %param.11), channel_id=1, source_target_pairs={{0,32},{4,36},{8,40},{12,44},{16,48},{20,52},{24,56},{28,60},{32,6... | collective-permute-start | bytes 786440 | tf_op jit(solution)/shard_map/ppermute | solution.py:14
  29.3 11.8 %collective-permute-start.1 = (bf16[2,512,512]{2,1,0:T(8,128)(2,1)S(1)}, bf16[2,512,512]{2,1,0:T(8,128)(2,1)S(1)}, u32[]{:S(2)}, u32[]{:S(2)}) collective-permute-start(bf16[2,512,512]{2,1,0:T(8,128)(2,1)S(1)} %collective-permute-done), channel_id=1, source_target_pairs={{0,1},{1,0},{2,3},{3,2},{4,5},{5,4},{6,7},{7,6},{8,9},{9,8},{10,11... | collective-permute-start | bytes 3145736 | tf_op jit(solution)/shard_map/ppermute | solution.py:89
  34.5 6.9 %copy-start.1 = (bf16[2,512,512]{2,1,0:T(8,128)(2,1)S(1)}, bf16[2,512,512]{2,1,0:T(8,128)(2,1)}, u32[]{:S(2)}) copy-start(bf16[2,512,512]{2,1,0:T(8,128)(2,1)} %local_ref.1) | copy-start | bytes 3145732
  34.5 30.1 %collective-permute-start.4 = (bf16[2,8,128,128]{3,2,1,0:T(8,128)(2,1)S(1)}, bf16[2,8,128,128]{3,2,1,0:T(8,128)(2,1)S(1)}, u32[]{:S(2)}, u32[]{:S(2)}) collective-permute-start(bf16[2,8,128,128]{3,2,1,0:T(8,128)(2,1)S(1)} %pad_maximum_fusion.1), channel_id=1, source_target_pairs={{0,8},{4,12},{8,16},{12,20},{16,24},{20,28},{24,32},{28,36},{32,40... | collective-permute-start | bytes 1572872 | tf_op jit(solution)/shard_map/ppermute | solution.py:14
  39.7 24.9 %collective-permute-start.5 = (bf16[2,8,128,128]{3,2,1,0:T(8,128)(2,1)S(1)}, bf16[2,8,128,128]{3,2,1,0:T(8,128)(2,1)}, u32[]{:S(2)}, u32[]{:S(2)}) collective-permute-start(bf16[2,8,128,128]{3,2,1,0:T(8,128)(2,1)S(1)} %pad_maximum_fusion.1), channel_id=1, source_target_pairs={{0,16},{4,20},{8,24},{12,28},{16,32},{20,36},{24,40},{28,44},{32,4... | collective-permute-start | bytes 1572872 | tf_op jit(solution)/shard_map/ppermute | solution.py:14
  39.7 52.9 %collective-permute-start.6 = (bf16[2,8,128,128]{3,2,1,0:T(8,128)(2,1)S(1)}, bf16[2,8,128,128]{3,2,1,0:T(8,128)(2,1)}, u32[]{:S(2)}, u32[]{:S(2)}) collective-permute-start(bf16[2,8,128,128]{3,2,1,0:T(8,128)(2,1)S(1)} %pad_maximum_fusion.1), channel_id=1, source_target_pairs={{0,24},{4,28},{8,32},{12,36},{16,40},{20,44},{24,48},{28,52},{32,5... | collective-permute-start | bytes 1572872 | tf_op jit(solution)/shard_map/ppermute | solution.py:14
  63.2 1.3 %copy-start = (f32[8,512,128]{2,1,0:T(8,128)}, f32[8,512,128]{2,1,0:T(8,128)S(1)}, u32[]{:S(2)}) copy-start(f32[8,512,128]{2,1,0:T(8,128)S(1)} %get-tuple-element.7.early_ref) | copy-start | bytes 6291460
  64.6 28.0 %copy-start.2 = (bf16[2,8,128,128]{3,2,1,0:T(8,128)(2,1)}, bf16[2,8,128,128]{3,2,1,0:T(8,128)(2,1)S(1)}, u32[]{:S(2)}) copy-start(bf16[2,8,128,128]{3,2,1,0:T(8,128)(2,1)S(1)} %collective-permute-done.4.two_ref) | copy-start | bytes 1572868
  98.4 2.2 %collective-permute-start.7 = (bf16[8,2,128,128]{3,2,1,0:T(8,128)(2,1)}, bf16[8,2,128,128]{3,2,1,0:T(8,128)(2,1)S(1)}, u32[]{:S(2)}, u32[]{:S(2)}) collective-permute-start(bf16[8,2,128,128]{3,2,1,0:T(8,128)(2,1)} %get-tuple-element.9), channel_id=1, source_target_pairs={{0,1},{1,0},{2,3},{3,2},{4,5},{5,4},{6,7},{7,6},{8,9},{9,8},{10,11... | collective-permute-start | bytes 1572872 | tf_op jit(solution)/shard_map/ppermute | solution.py:185
  102.0 8.4 %collective-permute-start.8 = (bf16[8,128,128]{2,1,0:T(8,128)(2,1)S(1)}, bf16[8,128,128]{2,1,0:T(8,128)(2,1)S(1)}, u32[]{:S(2)}, u32[]{:S(2)}) collective-permute-start(bf16[8,128,128]{2,1,0:T(8,128)(2,1)S(1)} %fusion.1), channel_id=1, source_target_pairs={{0,2},{1,3},{2,0},{3,1},{4,6},{5,7},{6,4},{7,5},{8,10},{9,11},{10,... | collective-permute-start | bytes 786440 | tf_op jit(solution)/shard_map/ppermute | solution.py:191

commit v19 on v16

--- a/solution.py
+++ b/solution.py
@@ -146,12 +146,12 @@
     )(slot_index, band_index, weights, halo, coarse_kernel, intersection, intersection,
       first, second, last)
     row_block = block_order // band_count
-    half_fine = fine_dev // 2
+    half_fine = fine_dev // 4
     send, keep = pl.pallas_call(
         product_kernel,
         grid_spec=pltpu.PrefetchScalarGridSpec(
             num_scalar_prefetch=1,
-            grid=(2,),
+            grid=(4,),
             in_specs=[
                 pl.BlockSpec((half_fine, 1, block_order, column_count),
                              lambda k, bd: (k, 3, 0, 0)),

time: 99.7 us -> 101 us (1.013)
  no operation moved by 1% of the time
where the time goes in v19:
time: 101 us; the launch traced here: 100 us
  waiting for transfers between devices  38.6 us (38%)
  Pallas kernels  27.7 us (27%)
  starting transfers between devices  20 us (20%)
  other arithmetic  8.47 us (8%)
  local copies, waits for them, and re-layouts  4.59 us (5%)
    pallas_call x1, Pallas kernels, on_device(): pl.pallas_call(kernel, grid_spec=grid_spec, out_shape=[jax.ShapeDtypeStru...  22.2 us
    ppermute x4, waiting for transfers between devices, shifted(): return lax.ppermute(value, axis, pairs)  17.1 us
    ppermute x1, waiting for transfers between devices, on_device(): near = lax.ppermute(coarse_kernel, ('blk', 'band'), pairs)  13.6 us
    ppermute x1, starting transfers between devices, on_device(): near = lax.ppermute(coarse_kernel, ('blk', 'band'), pairs)  9.47 us
    ppermute x1, starting transfers between devices, on_device(): far = lax.ppermute(near, 'band', [(b, b ^ 1) for b in range(band_count)])  6.24 us
    ppermute x1, waiting for transfers between devices, on_device(): lax.ppermute(send.astype(jnp.bfloat16), 'band', swap).astype(jnp.float32)  6.2 us
    pallas_call x1, Pallas kernels, on_device(): pl.pallas_call(product_kernel, grid_spec=pltpu.PrefetchScalarGridSpec(num...  5.52 us
    unnamed x6, local copies, waits for them, and re-layouts  2.92 us
  transfers between devices with their start and end apart: 8, of which 5 were waited for; matrix products, arithmetic and copies ran while one was open for 10% of the time, Pallas kernels for 22%

profile of v19, /device:TPU:1, one launch (start us, length us, event | category | flops | bytes accessed | tf_op | source)
XLA Modules:
  0.0 100.1 jit_solution(18391296185266016302)
XLA Ops:
  0.6 9.5 %collective-permute-start = (bf16[2,512,512]{2,1,0:T(8,128)(2,1)}, bf16[2,512,512]{2,1,0:T(8,128)(2,1)S(1)}, u32[]{:S(2)}, u32[]{:S(2)}) collective-permute-start(bf16[2,512,512]{2,1,0:T(8,128)(2,1)} %local_ref.1), channel_id=1, source_target_pairs={{0,4},{1,125},{2,6},{3,127},{4,8},{5,1},{6,10},{7,3},{8,12},{9,5},... | collective-permute-start | bytes 3145736 | tf_op jit(solution)/shard_map/ppermute | solution.py:88
  10.1 0.7 compare_select_fusion
  10.8 0.8 copy.8
  11.6 0.7 compare_and_fusion
  12.2 13.6 %collective-permute-done = bf16[2,512,512]{2,1,0:T(8,128)(2,1)S(1)} collective-permute-done((bf16[2,512,512]{2,1,0:T(8,128)(2,1)}, bf16[2,512,512]{2,1,0:T(8,128)(2,1)S(1)}, u32[]{:S(2)}, u32[]{:S(2)}) %collective-permute-start) | collective-permute-done | bytes 1048608 | tf_op jit(solution)/shard_map/ppermute | solution.py:88
  25.8 6.2 %collective-permute-start.1 = (bf16[2,512,512]{2,1,0:T(8,128)(2,1)S(1)}, bf16[2,512,512]{2,1,0:T(8,128)(2,1)}, u32[]{:S(2)}, u32[]{:S(2)}) collective-permute-start(bf16[2,512,512]{2,1,0:T(8,128)(2,1)S(1)} %collective-permute-done), channel_id=1, source_target_pairs={{0,1},{1,0},{2,3},{3,2},{4,5},{5,4},{6,7},{7,6},{8,9},{9,8},{10,11... | collective-permute-start | bytes 3145736 | tf_op jit(solution)/shard_map/ppermute | solution.py:89
  32.1 1.0 pad_maximum_fusion.2
  33.1 0.9 collective-permute-start.3
  34.0 0.6 gather_fusion
  34.9 0.8 copy.10
  35.7 0.6 gather_fusion.1
  36.4 16.3 %collective-permute-done.3.second_ref = bf16[2,8,128,128]{3,2,1,0:T(8,128)(2,1)S(1)} collective-permute-done((bf16[2,8,128,128]{3,2,1,0:T(8,128)(2,1)S(1)}, bf16[2,8,128,128]{3,2,1,0:T(8,128)(2,1)S(1)}, u32[]{:S(2)}, u32[]{:S(2)}) %collective-permute-start.3) | collective-permute-done | bytes 524320 | tf_op jit(solution)/shard_map/ppermute | solution.py:14
  52.7 1.1 %pad_maximum_fusion.1 = bf16[4,8,128,128]{3,2,1,0:T(8,128)(2,1)S(1)} fusion(bf16[2,8,128,128]{3,2,1,0:T(8,128)(2,1)S(1)} %collective-permute-done.3.second_ref, bf16[1,8,128,128]{3,2,1,0:T(8,128)(2,1)S(1)} %bitcast.14, bf16[1,8,128,128]{3,2,1,0:T(8,128)(2,1)} %bitcast.16), kind=kLoop, calls=%fused_computation.3 | loop fusion | flops 1048576 | bytes 2097152 | tf_op jit(solution)/shard_map/stack | solution.py:95
  54.1 2.8 %pad_maximum_fusion.halo_ref = bf16[4,512,512]{2,1,0:T(8,128)(2,1)} fusion(bf16[2,512,512]{2,1,0:T(8,128)(2,1)} %collective-permute-done.1, bf16[2,512,512]{2,1,0:T(8,128)(2,1)S(1)} %collective-permute-done), kind=kLoop, calls=%fused_computation.2 | loop fusion | flops 1048576 | bytes 4194304 | tf_op jit(solution)/shard_map/concatenate | solution.py:90
  56.9 22.2 %shard_map.77 = (bf16[8,8,512,128]{3,2,1,0:T(8,128)(2,1)}, f32[8,512,128]{2,1,0:T(8,128)S(1)}) custom-call(s32[256]{0:T(256)S(1)} %fusion.4.slot_ref, s32[1]{0:T(128)} %bitcast.1.band_ref, f32[256]{0:T(256)S(1)} %select_n.75.weight_ref, bf16[4,512,512]{2,1,0:T(8,128)(2,1)} %pad_maximum_fusion.halo_ref, bf16[2,512,512]{2,1,0:T(8,128)(2,1)S(1)} %copy-done.1, ...), custom_call_target="tpu_custom_call" | custom-call | flops 7516192768 | bytes 12582912 | tf_op jit(solution)/shard_map/pallas_call | solution.py:133
  79.1 1.3 %copy-done = f32[8,512,128]{2,1,0:T(8,128)} copy-done((f32[8,512,128]{2,1,0:T(8,128)}, f32[8,512,128]{2,1,0:T(8,128)S(1)}, u32[]{:S(2)}) %copy-start) | copy-done | bytes 2097176
  80.5 0.7 collective-permute-done.5.third_ref
  81.2 5.5 %shard_map.78 = (bf16[8,2,128,128]{3,2,1,0:T(8,128)(2,1)}, f32[8,2,128,128]{3,2,1,0:T(8,128)}) custom-call(s32[1]{0:T(128)} %bitcast.1.band_ref, bf16[8,8,512,128]{3,2,1,0:T(8,128)(2,1)} %get-tuple-element.4.head_ref.middle_ref.tail_ref, bf16[8,8,512,128]{3,2,1,0:T(8,128)(2,1)} %get-tuple-element.4.head_ref.middle_ref.tail_ref, ...), custom_call_target="tpu_custom_call" | custom-call | flops 1073741824 | bytes 8388608 | tf_op jit(solution)/shard_map/pallas_call | solution.py:150
  86.7 1.9 %collective-permute-start.6 = (bf16[8,2,128,128]{3,2,1,0:T(8,128)(2,1)}, bf16[8,2,128,128]{3,2,1,0:T(8,128)(2,1)S(1)}, u32[]{:S(2)}, u32[]{:S(2)}) collective-permute-start(bf16[8,2,128,128]{3,2,1,0:T(8,128)(2,1)} %get-tuple-element.9), channel_id=1, source_target_pairs={{0,1},{1,0},{2,3},{3,2},{4,5},{5,4},{6,7},{7,6},{8,9},{9,8},{10,11... | collective-permute-start | bytes 1572872 | tf_op jit(solution)/shard_map/ppermute | solution.py:182
  88.6 1.7 %collective-permute-done.6 = bf16[8,2,128,128]{3,2,1,0:T(8,128)(2,1)S(1)} collective-permute-done((bf16[8,2,128,128]{3,2,1,0:T(8,128)(2,1)}, bf16[8,2,128,128]{3,2,1,0:T(8,128)(2,1)S(1)}, u32[]{:S(2)}, u32[]{:S(2)}) %collective-permute-start.6) | collective-permute-done | bytes 524320 | tf_op jit(solution)/shard_map/ppermute | solution.py:182
  90.4 1.3 %convert_add_fusion = f32[8,2,128,128]{3,2,1,0:T(8,128)S(1)} fusion(f32[8,2,128,128]{3,2,1,0:T(8,128)} %get-tuple-element.8, bf16[8,2,128,128]{3,2,1,0:T(8,128)(2,1)S(1)} %collective-permute-done.6), kind=kLoop, calls=%fused_computation.4 | loop fusion | flops 524288 | bytes 2621440 | tf_op jit(solution)/shard_map/add | solution.py:182
  91.8 1.4 %collective-permute-start.7 = (bf16[8,128,128]{2,1,0:T(8,128)(2,1)S(1)}, bf16[8,128,128]{2,1,0:T(8,128)(2,1)S(1)}, u32[]{:S(2)}, u32[]{:S(2)}) collective-permute-start(bf16[8,128,128]{2,1,0:T(8,128)(2,1)S(1)} %fusion.1), channel_id=1, source_target_pairs={{0,2},{1,3},{2,0},{3,1},{4,6},{5,7},{6,4},{7,5},{8,10},{9,11},{10,... | collective-permute-start | bytes 786440 | tf_op jit(solution)/shard_map/ppermute | solution.py:188
  93.1 6.2 %collective-permute-done.7 = bf16[8,128,128]{2,1,0:T(8,128)(2,1)S(1)} collective-permute-done((bf16[8,128,128]{2,1,0:T(8,128)(2,1)S(1)}, bf16[8,128,128]{2,1,0:T(8,128)(2,1)S(1)}, u32[]{:S(2)}, u32[]{:S(2)}) %collective-permute-start.7) | collective-permute-done | bytes 262176 | tf_op jit(solution)/shard_map/ppermute | solution.py:188
  99.3 0.8 fusion
  (18 shorter events, 0.8 us)
Async XLA Ops:
  0.6 25.2 %collective-permute-start = (bf16[2,512,512]{2,1,0:T(8,128)(2,1)}, bf16[2,512,512]{2,1,0:T(8,128)(2,1)S(1)}, u32[]{:S(2)}, u32[]{:S(2)}) collective-permute-start(bf16[2,512,512]{2,1,0:T(8,128)(2,1)} %local_ref.1), channel_id=1, source_target_pairs={{0,4},{1,125},{2,6},{3,127},{4,8},{5,1},{6,10},{7,3},{8,12},{9,5},... | collective-permute-start | bytes 3145736 | tf_op jit(solution)/shard_map/ppermute | solution.py:88
  10.1 22.0 %collective-permute-start.2 = (bf16[8,128,128]{2,1,0:T(8,128)(2,1)}, bf16[8,128,128]{2,1,0:T(8,128)(2,1)S(1)}, u32[]{:S(2)}, u32[]{:S(2)}) collective-permute-start(bf16[8,128,128]{2,1,0:T(8,128)(2,1)} %param.11), channel_id=1, source_target_pairs={{0,4},{4,8},{8,12},{12,16},{16,20},{20,24},{24,28},{28,32},{32,36}... | collective-permute-start | bytes 786440 | tf_op jit(solution)/shard_map/ppermute | solution.py:14
  10.1 46.8 %collective-permute-start.4 = (bf16[8,128,128]{2,1,0:T(8,128)(2,1)}, bf16[8,128,128]{2,1,0:T(8,128)(2,1)S(1)}, u32[]{:S(2)}, u32[]{:S(2)}) collective-permute-start(bf16[8,128,128]{2,1,0:T(8,128)(2,1)} %param.11), channel_id=1, source_target_pairs={{0,32},{4,36},{8,40},{12,44},{16,48},{20,52},{24,56},{28,60},{32,6... | collective-permute-start | bytes 786440 | tf_op jit(solution)/shard_map/ppermute | solution.py:14
  25.8 28.3 %collective-permute-start.1 = (bf16[2,512,512]{2,1,0:T(8,128)(2,1)S(1)}, bf16[2,512,512]{2,1,0:T(8,128)(2,1)}, u32[]{:S(2)}, u32[]{:S(2)}) collective-permute-start(bf16[2,512,512]{2,1,0:T(8,128)(2,1)S(1)} %collective-permute-done), channel_id=1, source_target_pairs={{0,1},{1,0},{2,3},{3,2},{4,5},{5,4},{6,7},{7,6},{8,9},{9,8},{10,11... | collective-permute-start | bytes 3145736 | tf_op jit(solution)/shard_map/ppermute | solution.py:89
  33.1 19.6 %collective-permute-start.3 = (bf16[2,8,128,128]{3,2,1,0:T(8,128)(2,1)S(1)}, bf16[2,8,128,128]{3,2,1,0:T(8,128)(2,1)S(1)}, u32[]{:S(2)}, u32[]{:S(2)}) collective-permute-start(bf16[2,8,128,128]{3,2,1,0:T(8,128)(2,1)S(1)} %pad_maximum_fusion.2), channel_id=1, source_target_pairs={{0,8},{4,12},{8,16},{12,20},{16,24},{20,28},{24,32},{28,36},{32,40... | collective-permute-start | bytes 1572872 | tf_op jit(solution)/shard_map/ppermute | solution.py:14
  53.7 27.4 %collective-permute-start.5 = (bf16[4,8,128,128]{3,2,1,0:T(8,128)(2,1)S(1)}, bf16[4,8,128,128]{3,2,1,0:T(8,128)(2,1)}, u32[]{:S(2)}, u32[]{:S(2)}) collective-permute-start(bf16[4,8,128,128]{3,2,1,0:T(8,128)(2,1)S(1)} %pad_maximum_fusion.1), channel_id=1, source_target_pairs={{0,16},{4,20},{8,24},{12,28},{16,32},{20,36},{24,40},{28,44},{32,4... | collective-permute-start | bytes 3145736 | tf_op jit(solution)/shard_map/ppermute | solution.py:14
  54.1 2.9 %copy-start.1 = (bf16[2,512,512]{2,1,0:T(8,128)(2,1)S(1)}, bf16[2,512,512]{2,1,0:T(8,128)(2,1)}, u32[]{:S(2)}) copy-start(bf16[2,512,512]{2,1,0:T(8,128)(2,1)} %local_ref.1) | copy-start | bytes 3145732
  79.1 1.3 %copy-start = (f32[8,512,128]{2,1,0:T(8,128)}, f32[8,512,128]{2,1,0:T(8,128)S(1)}, u32[]{:S(2)}) copy-start(f32[8,512,128]{2,1,0:T(8,128)S(1)} %get-tuple-element.7.early_ref) | copy-start | bytes 6291460
  86.7 3.7 %collective-permute-start.6 = (bf16[8,2,128,128]{3,2,1,0:T(8,128)(2,1)}, bf16[8,2,128,128]{3,2,1,0:T(8,128)(2,1)S(1)}, u32[]{:S(2)}, u32[]{:S(2)}) collective-permute-start(bf16[8,2,128,128]{3,2,1,0:T(8,128)(2,1)} %get-tuple-element.9), channel_id=1, source_target_pairs={{0,1},{1,0},{2,3},{3,2},{4,5},{5,4},{6,7},{7,6},{8,9},{9,8},{10,11... | collective-permute-start | bytes 1572872 | tf_op jit(solution)/shard_map/ppermute | solution.py:182
  91.8 7.6 %collective-permute-start.7 = (bf16[8,128,128]{2,1,0:T(8,128)(2,1)S(1)}, bf16[8,128,128]{2,1,0:T(8,128)(2,1)S(1)}, u32[]{:S(2)}, u32[]{:S(2)}) collective-permute-start(bf16[8,128,128]{2,1,0:T(8,128)(2,1)S(1)} %fusion.1), channel_id=1, source_target_pairs={{0,2},{1,3},{2,0},{3,1},{4,6},{5,7},{6,4},{7,5},{8,10},{9,11},{10,... | collective-permute-start | bytes 786440 | tf_op jit(solution)/shard_map/ppermute | solution.py:188

commit v20 on v16

--- a/solution.py
+++ b/solution.py
@@ -49,10 +49,11 @@
 
 
 def product_kernel(band_ref, head_ref, middle_ref, tail_ref, early_ref, third_ref, send_ref,
-                   keep_ref, part_ref):
+                   own_ref, other_ref, part_ref):
     count = third_ref.shape[0]
-    rows = keep_ref.shape[2]
+    rows = own_ref.shape[1]
     core = band_ref[0] % 2
+    level_own = band_ref[0] // 2
     for k in range(head_ref.shape[0]):
         pieces = [head_ref[k, 0], middle_ref[k, 0], middle_ref[k, 1], tail_ref[k, 0]]
         wide = jnp.concatenate(pieces, axis=1)
@@ -61,8 +62,11 @@
         for level in range(2):
             own = pl.multiple_of((level * 2 + core) * rows, rows)
             other = pl.multiple_of((level * 2 + 1 - core) * rows, rows)
-            keep_ref[k, level] = part_ref[pl.ds(own, rows), :]
             send_ref[k, level] = part_ref[pl.ds(other, rows), :].astype(jnp.bfloat16)
+        own = pl.multiple_of((level_own * 2 + core) * rows, rows)
+        other = pl.multiple_of(((1 - level_own) * 2 + core) * rows, rows)
+        own_ref[k] = part_ref[pl.ds(own, rows), :]
+        other_ref[k] = part_ref[pl.ds(other, rows), :]
 
 
 def on_device(coarse_kernel, interp_index, interp_weight, stop_order, intersection, trial_vectors):
@@ -147,7 +151,7 @@
       first, second, last)
     row_block = block_order // band_count
     half_fine = fine_dev // 2
-    send, keep = pl.pallas_call(
+    send, keep_own, keep_other = pl.pallas_call(
         product_kernel,
         grid_spec=pltpu.PrefetchScalarGridSpec(
             num_scalar_prefetch=1,
@@ -165,13 +169,15 @@
             ],
             out_specs=[
                 pl.BlockSpec((half_fine, 2, row_block, vector_count), lambda k, bd: (k, 0, 0, 0)),
-                pl.BlockSpec((half_fine, 2, row_block, vector_count), lambda k, bd: (k, 0, 0, 0)),
+                pl.BlockSpec((half_fine, row_block, vector_count), lambda k, bd: (k, 0, 0)),
+                pl.BlockSpec((half_fine, row_block, vector_count), lambda k, bd: (k, 0, 0)),
             ],
             scratch_shapes=[pltpu.VMEM((block_order, vector_count), jnp.float32)],
         ),
         out_shape=[
             jax.ShapeDtypeStruct((fine_dev, 2, row_block, vector_count), jnp.bfloat16),
-            jax.ShapeDtypeStruct((fine_dev, 2, row_block, vector_count), jnp.float32),
+            jax.ShapeDtypeStruct((fine_dev, row_block, vector_count), jnp.float32),
+            jax.ShapeDtypeStruct((fine_dev, row_block, vector_count), jnp.float32),
         ],
         cost_estimate=pl.CostEstimate(
             flops=2 * fine_dev * stop_count * block_order * column_count * vector_count,
@@ -179,10 +185,10 @@
             bytes_accessed=2 * fine_dev * stop_count * block_order * column_count),
     )(band_index, hamiltonian, hamiltonian, hamiltonian, early_value, third)
     swap = [(b, b ^ 1) for b in range(band_count)]
-    pair_sum = keep + lax.ppermute(send, "band", swap).astype(jnp.float32)
+    received = lax.ppermute(send, "band", swap).astype(jnp.float32)
     level = band // 2
-    send = lax.dynamic_index_in_dim(pair_sum, 1 - level, 1, keepdims=False)
-    keep = lax.dynamic_index_in_dim(pair_sum, level, 1, keepdims=False)
+    send = keep_other + lax.dynamic_index_in_dim(received, 1 - level, 1, keepdims=False)
+    keep = keep_own + lax.dynamic_index_in_dim(received, level, 1, keepdims=False)
     swap = [(b, b ^ 2) for b in range(band_count)]
     product_share = (
         keep + lax.ppermute(send.astype(jnp.bfloat16), "band", swap).astype(jnp.float32)

time: 99.7 us -> 99.6 us (level)
    add x1 -> x0, other arithmetic: 1.33 us -> none  [on_device(): pair_sum = keep + lax.ppermute(send, 'band', swap).astype(jnp.float32)]
    convert_element_type x0 -> x2, other arithmetic: none -> 1.2 us  [the longest x1 1.11 us: on_device(): send.astype(jnp.bfloat16)]
    unnamed x6 -> x8, local copies, waits for them, and re-layouts: 2.92 us -> 2.93 us
where the time goes in v20:
time: 99.6 us; the launch traced here: 99.2 us
  waiting for transfers between devices  38.6 us (39%)
  Pallas kernels  26.9 us (27%)
  starting transfers between devices  20.1 us (20%)
  other arithmetic  8.37 us (8%)
  local copies, waits for them, and re-layouts  4.55 us (5%)
    pallas_call x1, Pallas kernels, on_device(): pl.pallas_call(kernel, grid_spec=grid_spec, out_shape=[jax.ShapeDtypeStru...  22.2 us
    ppermute x4, waiting for transfers between devices, shifted(): return lax.ppermute(value, axis, pairs)  17.1 us
    ppermute x1, waiting for transfers between devices, on_device(): near = lax.ppermute(coarse_kernel, ('blk', 'band'), pairs)  13.6 us
    ppermute x1, starting transfers between devices, on_device(): near = lax.ppermute(coarse_kernel, ('blk', 'band'), pairs)  9.47 us
    ppermute x1, starting transfers between devices, on_device(): far = lax.ppermute(near, 'band', [(b, b ^ 1) for b in range(band_count)])  6.24 us
    ppermute x1, waiting for transfers between devices, on_device(): lax.ppermute(send.astype(jnp.bfloat16), 'band', swap).astype(jnp.float32)  6.2 us
    pallas_call x1, Pallas kernels, on_device(): pl.pallas_call(product_kernel, grid_spec=pltpu.PrefetchScalarGridSpec(num...  4.71 us
    unnamed x8, local copies, waits for them, and re-layouts  2.93 us
  transfers between devices with their start and end apart: 8, of which 5 were waited for; matrix products, arithmetic and copies ran while one was open for 10% of the time, Pallas kernels for 22%

profile of v20, /device:TPU:1, one launch (start us, length us, event | category | flops | bytes accessed | tf_op | source)
XLA Modules:
  0.0 99.2 jit_solution(15480228426637492953)
XLA Ops:
  0.6 9.5 %collective-permute-start = (bf16[2,512,512]{2,1,0:T(8,128)(2,1)}, bf16[2,512,512]{2,1,0:T(8,128)(2,1)S(1)}, u32[]{:S(2)}, u32[]{:S(2)}) collective-permute-start(bf16[2,512,512]{2,1,0:T(8,128)(2,1)} %local_ref.1), channel_id=1, source_target_pairs={{0,4},{1,125},{2,6},{3,127},{4,8},{5,1},{6,10},{7,3},{8,12},{9,5},... | collective-permute-start | bytes 3145736 | tf_op jit(solution)/shard_map/ppermute | solution.py:92
  10.1 0.7 compare_select_fusion
  10.8 0.8 copy.8
  11.6 0.7 compare_and_fusion
  12.2 13.6 %collective-permute-done = bf16[2,512,512]{2,1,0:T(8,128)(2,1)S(1)} collective-permute-done((bf16[2,512,512]{2,1,0:T(8,128)(2,1)}, bf16[2,512,512]{2,1,0:T(8,128)(2,1)S(1)}, u32[]{:S(2)}, u32[]{:S(2)}) %collective-permute-start) | collective-permute-done | bytes 1048608 | tf_op jit(solution)/shard_map/ppermute | solution.py:92
  25.8 6.2 %collective-permute-start.1 = (bf16[2,512,512]{2,1,0:T(8,128)(2,1)S(1)}, bf16[2,512,512]{2,1,0:T(8,128)(2,1)}, u32[]{:S(2)}, u32[]{:S(2)}) collective-permute-start(bf16[2,512,512]{2,1,0:T(8,128)(2,1)S(1)} %collective-permute-done), channel_id=1, source_target_pairs={{0,1},{1,0},{2,3},{3,2},{4,5},{5,4},{6,7},{7,6},{8,9},{9,8},{10,11... | collective-permute-start | bytes 3145736 | tf_op jit(solution)/shard_map/ppermute | solution.py:93
  32.1 1.0 %pad_maximum_fusion.2 = bf16[2,8,128,128]{3,2,1,0:T(8,128)(2,1)S(1)} fusion(bf16[1,8,128,128]{3,2,1,0:T(8,128)(2,1)S(1)} %bitcast.17, bf16[1,8,128,128]{3,2,1,0:T(8,128)(2,1)} %bitcast.19), kind=kLoop, calls=%fused_computation.4 | loop fusion | flops 262144 | bytes 1048576 | tf_op jit(solution)/shard_map/stack | solution.py:98
  33.1 0.9 collective-permute-start.3
  34.0 0.6 gather_fusion
  34.9 0.8 copy.10
  35.7 0.6 gather_fusion.1
  36.4 16.3 %collective-permute-done.3.second_ref = bf16[2,8,128,128]{3,2,1,0:T(8,128)(2,1)S(1)} collective-permute-done((bf16[2,8,128,128]{3,2,1,0:T(8,128)(2,1)S(1)}, bf16[2,8,128,128]{3,2,1,0:T(8,128)(2,1)S(1)}, u32[]{:S(2)}, u32[]{:S(2)}) %collective-permute-start.3) | collective-permute-done | bytes 524320 | tf_op jit(solution)/shard_map/ppermute | solution.py:14
  52.7 1.1 %pad_maximum_fusion.1 = bf16[4,8,128,128]{3,2,1,0:T(8,128)(2,1)S(1)} fusion(bf16[2,8,128,128]{3,2,1,0:T(8,128)(2,1)S(1)} %collective-permute-done.3.second_ref, bf16[1,8,128,128]{3,2,1,0:T(8,128)(2,1)S(1)} %bitcast.18, bf16[1,8,128,128]{3,2,1,0:T(8,128)(2,1)} %bitcast.20), kind=kLoop, calls=%fused_computation.3 | loop fusion | flops 1048576 | bytes 2097152 | tf_op jit(solution)/shard_map/stack | solution.py:99
  54.1 2.8 %pad_maximum_fusion.halo_ref = bf16[4,512,512]{2,1,0:T(8,128)(2,1)} fusion(bf16[2,512,512]{2,1,0:T(8,128)(2,1)} %collective-permute-done.1, bf16[2,512,512]{2,1,0:T(8,128)(2,1)S(1)} %collective-permute-done), kind=kLoop, calls=%fused_computation.2 | loop fusion | flops 1048576 | bytes 4194304 | tf_op jit(solution)/shard_map/concatenate | solution.py:94
  56.9 22.2 %shard_map.77 = (bf16[8,8,512,128]{3,2,1,0:T(8,128)(2,1)}, f32[8,512,128]{2,1,0:T(8,128)S(1)}) custom-call(s32[256]{0:T(256)S(1)} %fusion.5.slot_ref, s32[1]{0:T(128)} %bitcast.1.band_ref, f32[256]{0:T(256)S(1)} %select_n.75.weight_ref, bf16[4,512,512]{2,1,0:T(8,128)(2,1)} %pad_maximum_fusion.halo_ref, bf16[2,512,512]{2,1,0:T(8,128)(2,1)S(1)} %copy-done.1, ...), custom_call_target="tpu_custom_call" | custom-call | flops 7516192768 | bytes 12582912 | tf_op jit(solution)/shard_map/pallas_call | solution.py:137
  79.1 1.3 %copy-done = f32[8,512,128]{2,1,0:T(8,128)} copy-done((f32[8,512,128]{2,1,0:T(8,128)}, f32[8,512,128]{2,1,0:T(8,128)S(1)}, u32[]{:S(2)}) %copy-start) | copy-done | bytes 2097176
  80.5 0.7 collective-permute-done.5.third_ref
  81.2 4.7 %shard_map.78 = (bf16[8,2,128,128]{3,2,1,0:T(8,128)(2,1)}, f32[8,128,128]{2,1,0:T(8,128)}, f32[8,128,128]{2,1,0:T(8,128)}) custom-call(s32[1]{0:T(128)} %bitcast.1.band_ref, bf16[8,8,512,128]{3,2,1,0:T(8,128)(2,1)} %get-tuple-element.5.head_ref.middle_ref.tail_ref, bf16[8,8,512,128]{3,2,1,0:T(8,128)(2,1)} %get-tuple-element.5.head_ref.middle_ref.tail_ref, ...), custom_call_target="tpu_custom_call" | custom-call | flops 1073741824 | bytes 8388608 | tf_op jit(solution)/shard_map/pallas_call | solution.py:154
  85.9 2.0 %collective-permute-start.6 = (bf16[8,2,128,128]{3,2,1,0:T(8,128)(2,1)}, bf16[8,2,128,128]{3,2,1,0:T(8,128)(2,1)S(1)}, u32[]{:S(2)}, u32[]{:S(2)}) collective-permute-start(bf16[8,2,128,128]{3,2,1,0:T(8,128)(2,1)} %get-tuple-element.10), channel_id=1, source_target_pairs={{0,1},{1,0},{2,3},{3,2},{4,5},{5,4},{6,7},{7,6},{8,9},{9,8},{10,11... | collective-permute-start | bytes 1572872 | tf_op jit(solution)/shard_map/ppermute | solution.py:188
  87.9 1.7 %collective-permute-done.6 = bf16[8,2,128,128]{3,2,1,0:T(8,128)(2,1)S(1)} collective-permute-done((bf16[8,2,128,128]{3,2,1,0:T(8,128)(2,1)}, bf16[8,2,128,128]{3,2,1,0:T(8,128)(2,1)S(1)}, u32[]{:S(2)}, u32[]{:S(2)}) %collective-permute-start.6) | collective-permute-done | bytes 524320 | tf_op jit(solution)/shard_map/ppermute | solution.py:188
  89.8 1.1 %fusion = bf16[8,128,128]{2,1,0:T(8,128)(2,1)S(1)} fusion(f32[8,128,128]{2,1,0:T(8,128)} %get-tuple-element.11, f32[8,2,128,128]{3,2,1,0:T(8,128)S(1)} %convert_element_type.12, s32[]{:T(128)S(6)} %select_n.78), kind=kLoop, calls=%fused_computation.6 | loop fusion | flops 262144 | bytes 1310724 | tf_op jit(solution)/shard_map/convert_element_type | solution.py:194
  90.9 1.4 %collective-permute-start.7 = (bf16[8,128,128]{2,1,0:T(8,128)(2,1)S(1)}, bf16[8,128,128]{2,1,0:T(8,128)(2,1)S(1)}, u32[]{:S(2)}, u32[]{:S(2)}) collective-permute-start(bf16[8,128,128]{2,1,0:T(8,128)(2,1)S(1)} %fusion), channel_id=1, source_target_pairs={{0,2},{1,3},{2,0},{3,1},{4,6},{5,7},{6,4},{7,5},{8,10},{9,11},{10,... | collective-permute-start | bytes 786440 | tf_op jit(solution)/shard_map/ppermute | solution.py:194
  92.2 6.2 %collective-permute-done.7 = bf16[8,128,128]{2,1,0:T(8,128)(2,1)S(1)} collective-permute-done((bf16[8,128,128]{2,1,0:T(8,128)(2,1)S(1)}, bf16[8,128,128]{2,1,0:T(8,128)(2,1)S(1)}, u32[]{:S(2)}, u32[]{:S(2)}) %collective-permute-start.7) | collective-permute-done | bytes 262176 | tf_op jit(solution)/shard_map/ppermute | solution.py:194
  98.4 0.8 fusion.2
  (20 shorter events, 0.9 us)
Async XLA Ops:
  0.6 25.2 %collective-permute-start = (bf16[2,512,512]{2,1,0:T(8,128)(2,1)}, bf16[2,512,512]{2,1,0:T(8,128)(2,1)S(1)}, u32[]{:S(2)}, u32[]{:S(2)}) collective-permute-start(bf16[2,512,512]{2,1,0:T(8,128)(2,1)} %local_ref.1), channel_id=1, source_target_pairs={{0,4},{1,125},{2,6},{3,127},{4,8},{5,1},{6,10},{7,3},{8,12},{9,5},... | collective-permute-start | bytes 3145736 | tf_op jit(solution)/shard_map/ppermute | solution.py:92
  10.1 22.0 %collective-permute-start.2 = (bf16[8,128,128]{2,1,0:T(8,128)(2,1)}, bf16[8,128,128]{2,1,0:T(8,128)(2,1)S(1)}, u32[]{:S(2)}, u32[]{:S(2)}) collective-permute-start(bf16[8,128,128]{2,1,0:T(8,128)(2,1)} %param.11), channel_id=1, source_target_pairs={{0,4},{4,8},{8,12},{12,16},{16,20},{20,24},{24,28},{28,32},{32,36}... | collective-permute-start | bytes 786440 | tf_op jit(solution)/shard_map/ppermute | solution.py:14
  10.1 46.8 %collective-permute-start.4 = (bf16[8,128,128]{2,1,0:T(8,128)(2,1)}, bf16[8,128,128]{2,1,0:T(8,128)(2,1)S(1)}, u32[]{:S(2)}, u32[]{:S(2)}) collective-permute-start(bf16[8,128,128]{2,1,0:T(8,128)(2,1)} %param.11), channel_id=1, source_target_pairs={{0,32},{4,36},{8,40},{12,44},{16,48},{20,52},{24,56},{28,60},{32,6... | collective-permute-start | bytes 786440 | tf_op jit(solution)/shard_map/ppermute | solution.py:14
  25.8 28.3 %collective-permute-start.1 = (bf16[2,512,512]{2,1,0:T(8,128)(2,1)S(1)}, bf16[2,512,512]{2,1,0:T(8,128)(2,1)}, u32[]{:S(2)}, u32[]{:S(2)}) collective-permute-start(bf16[2,512,512]{2,1,0:T(8,128)(2,1)S(1)} %collective-permute-done), channel_id=1, source_target_pairs={{0,1},{1,0},{2,3},{3,2},{4,5},{5,4},{6,7},{7,6},{8,9},{9,8},{10,11... | collective-permute-start | bytes 3145736 | tf_op jit(solution)/shard_map/ppermute | solution.py:93
  33.1 19.6 %collective-permute-start.3 = (bf16[2,8,128,128]{3,2,1,0:T(8,128)(2,1)S(1)}, bf16[2,8,128,128]{3,2,1,0:T(8,128)(2,1)S(1)}, u32[]{:S(2)}, u32[]{:S(2)}) collective-permute-start(bf16[2,8,128,128]{3,2,1,0:T(8,128)(2,1)S(1)} %pad_maximum_fusion.2), channel_id=1, source_target_pairs={{0,8},{4,12},{8,16},{12,20},{16,24},{20,28},{24,32},{28,36},{32,40... | collective-permute-start | bytes 1572872 | tf_op jit(solution)/shard_map/ppermute | solution.py:14
  53.7 27.4 %collective-permute-start.5 = (bf16[4,8,128,128]{3,2,1,0:T(8,128)(2,1)S(1)}, bf16[4,8,128,128]{3,2,1,0:T(8,128)(2,1)}, u32[]{:S(2)}, u32[]{:S(2)}) collective-permute-start(bf16[4,8,128,128]{3,2,1,0:T(8,128)(2,1)S(1)} %pad_maximum_fusion.1), channel_id=1, source_target_pairs={{0,16},{4,20},{8,24},{12,28},{16,32},{20,36},{24,40},{28,44},{32,4... | collective-permute-start | bytes 3145736 | tf_op jit(solution)/shard_map/ppermute | solution.py:14
  54.1 2.9 %copy-start.1 = (bf16[2,512,512]{2,1,0:T(8,128)(2,1)S(1)}, bf16[2,512,512]{2,1,0:T(8,128)(2,1)}, u32[]{:S(2)}) copy-start(bf16[2,512,512]{2,1,0:T(8,128)(2,1)} %local_ref.1) | copy-start | bytes 3145732
  79.1 1.3 %copy-start = (f32[8,512,128]{2,1,0:T(8,128)}, f32[8,512,128]{2,1,0:T(8,128)S(1)}, u32[]{:S(2)}) copy-start(f32[8,512,128]{2,1,0:T(8,128)S(1)} %get-tuple-element.8.early_ref) | copy-start | bytes 6291460
  85.9 12.6 %copy-start.2 = (f32[8,128,128]{2,1,0:T(8,128)S(1)}, f32[8,128,128]{2,1,0:T(8,128)}, u32[]{:S(2)}) copy-start(f32[8,128,128]{2,1,0:T(8,128)} %get-tuple-element.9) | copy-start | bytes 1572868
  85.9 3.8 %collective-permute-start.6 = (bf16[8,2,128,128]{3,2,1,0:T(8,128)(2,1)}, bf16[8,2,128,128]{3,2,1,0:T(8,128)(2,1)S(1)}, u32[]{:S(2)}, u32[]{:S(2)}) collective-permute-start(bf16[8,2,128,128]{3,2,1,0:T(8,128)(2,1)} %get-tuple-element.10), channel_id=1, source_target_pairs={{0,1},{1,0},{2,3},{3,2},{4,5},{5,4},{6,7},{7,6},{8,9},{9,8},{10,11... | collective-permute-start | bytes 1572872 | tf_op jit(solution)/shard_map/ppermute | solution.py:188
  90.9 7.6 %collective-permute-start.7 = (bf16[8,128,128]{2,1,0:T(8,128)(2,1)S(1)}, bf16[8,128,128]{2,1,0:T(8,128)(2,1)S(1)}, u32[]{:S(2)}, u32[]{:S(2)}) collective-permute-start(bf16[8,128,128]{2,1,0:T(8,128)(2,1)S(1)} %fusion), channel_id=1, source_target_pairs={{0,2},{1,3},{2,0},{3,1},{4,6},{5,7},{6,4},{7,5},{8,10},{9,11},{10,... | collective-permute-start | bytes 786440 | tf_op jit(solution)/shard_map/ppermute | solution.py:194
